TPU v7x, 256 devices: a whole 4x4x8 slice. The times are simulated.
256 devices in a mesh: dp: 16 (over z_lo, y, core), expert: 16 (over z_hi, x).
Axes of the slice: x: 4, y: 4, z: 8 (z_hi: 4, z_lo: 2; z = z_hi * 2 + z_lo), core: 2. Of those that a mesh axis runs over, the one named last changes fastest.
Arguments:
- feats: bfloat16 [16, 64, 128, 512], P('dp', 'expert'), may hold values from -6 to 6
- labels: int32 [16, 64, 128, 1], P('dp', 'expert'), may hold values from 0 to 15; in each aligned block of 512 rows (0 to 511, 512 to 1023, ..., all dimensions but the last counted through in order) at most 64 rows name the same one
- w_first: bfloat16 [16, 512, 2048], P('expert'), may hold values from -0.25 to 0.25
- w_second: bfloat16 [16, 2048, 256], P('expert'), may hold values from -0.125 to 0.125
- kernel: bfloat16 [27, 256, 256], replicated, may hold values from -0.078125 to 0.078125
- cotangent: bfloat16 [16, 64, 128, 256], P('dp', 'expert'), may hold values from -6 to 6
Outputs:
- imitated: bfloat16 [16, 64, 128, 256], P('dp', 'expert')
- feat_grad: bfloat16 [16, 64, 128, 512], P('dp', 'expert')
- grad_first: float32 [16, 512, 2048], P('expert', None, 'dp')
- grad_second: float32 [16, 2048, 256], P('expert', 'dp')
Inputs may be any that keep to these rules, and one draw needn't show every extreme that they name: `labels`: within the 512 patches of one device (aligned blocks of 512 patches in grid order), no label occurs more than 64 times, and some label occurs exactly 64 times.
All inputs are finite; a program needn't handle non-finite values.
Results may differ from a plain program's by a relative error of at most 0.023.
Values may be sent and summed in bfloat16 or wider, within the bound.
No kernel may reach another device: no remote copies, remote signals or barrier semaphores. Data moves between devices by JAX's collectives and lax.ppermute only.
A program may use at most 128 MiB of HBM per device.

v0:
```python
import jax
import jax.numpy as jnp
from jax import lax
from jax.sharding import PartitionSpec as P


def extended(x, sides, width):
    for axis, dim in sides:
        size, length = (lax.axis_size(axis), x.shape[dim])
        up = [(i, (i + 1) % size) for i in range(size - 1)]
        down = [(j, i) for i, j in up]
        last = lax.slice_in_dim(x, length - width, length, axis=dim)
        first = lax.slice_in_dim(x, 0, width, axis=dim)
        before = lax.ppermute(last, axis, up)
        after = lax.ppermute(first, axis, down)
        x = jnp.concatenate([before, x, after], axis=dim)
    return x


def gelu_act(value):
    return jax.nn.gelu(value, approximate=True)


def gelu_back(preact, upstream):
    return jax.vjp(gelu_act, preact)[1](upstream)[0]


def gather_taps(padded, rows_y, depth_cells, flipped):
    pieces = []
    for plane in range(3):
        for across in range(3):
            for along in range(3):
                if flipped:
                    plane_at, across_at, along_at = (2 - plane, 2 - across, 2 - along)
                else:
                    plane_at, across_at, along_at = (plane, across, along)
                pieces.append(
                    padded[
                        plane_at,
                        across_at : across_at + rows_y,
                        along_at : along_at + depth_cells,
                        :,
                    ]
                )
    stacked = jnp.stack(pieces, axis=2)
    return stacked.reshape(rows_y * depth_cells, 27, padded.shape[3])


def per_device(feats, labels, w_first, w_second, kernel, cotangent):
    experts = lax.axis_size("expert")
    rows_y = feats.shape[1]
    depth_cells = feats.shape[2]
    feat_width = feats.shape[3]
    channels = kernel.shape[2]
    hidden = w_first.shape[2]
    patch_count = rows_y * depth_cells
    capacity = 2 * patch_count // experts
    regime = labels.reshape(patch_count)
    onehot = (regime[:, None] == jnp.arange(experts, dtype=jnp.int32)[None, :]).astype(jnp.int32)
    ranking = jnp.cumsum(onehot, axis=0) - 1
    slot_index = jnp.sum(ranking * onehot, axis=1)
    target = regime * capacity + slot_index
    flat_feats = feats.reshape(patch_count, feat_width)
    outbound = jnp.zeros((experts * capacity, feat_width), jnp.bfloat16).at[target].set(flat_feats)
    outbound = outbound.reshape(experts, capacity, feat_width)
    weight_one = w_first[0]
    weight_two = w_second[0]
    received = lax.all_to_all(outbound, "expert", split_axis=0, concat_axis=0, tiled=True)
    groups = received.shape[0]
    slot_count = received.shape[1]
    row_block = received.reshape(groups * slot_count, feat_width)
    preact = jnp.dot(row_block, weight_one, preferred_element_type=jnp.float32)
    activation = gelu_act(preact).astype(jnp.bfloat16)
    result = jnp.dot(activation, weight_two, preferred_element_type=jnp.float32).astype(
        jnp.bfloat16
    )
    result = result.reshape(groups, slot_count, channels)
    returned = lax.all_to_all(result, "expert", split_axis=0, concat_axis=0, tiled=True)
    returned, received, preact, activation = (
        returned,
        received,
        preact.reshape(groups, slot_count, hidden),
        activation.reshape(groups, slot_count, hidden),
    )
    mixed_rows = returned.reshape(experts * capacity, channels)[target]
    patch_grid = mixed_rows.reshape(1, rows_y, depth_cells, channels)
    padded = extended(patch_grid, (("dp", 0), ("expert", 1)), 1)
    padded = jnp.pad(padded, ((0, 0), (0, 0), (1, 1), (0, 0)))
    columns = gather_taps(padded, rows_y, depth_cells, False)
    imitated = jnp.einsum("tki,kio->to", columns, kernel, preferred_element_type=jnp.float32)
    imitated = imitated.astype(jnp.bfloat16).reshape(1, rows_y, depth_cells, channels)
    grad_padded = extended(cotangent, (("dp", 0), ("expert", 1)), 1)
    grad_padded = jnp.pad(grad_padded, ((0, 0), (0, 0), (1, 1), (0, 0)))
    grad_columns = gather_taps(grad_padded, rows_y, depth_cells, True)
    field_grad = jnp.einsum(
        "tko,kio->ti", grad_columns, kernel, preferred_element_type=jnp.float32
    ).astype(jnp.bfloat16)
    grad_outbound = (
        jnp.zeros((experts * capacity, channels), jnp.bfloat16).at[target].set(field_grad)
    )
    grad_outbound = grad_outbound.reshape(experts, capacity, channels)
    grad_inbound = lax.all_to_all(grad_outbound, "expert", split_axis=0, concat_axis=0, tiled=True)
    feat_rows = received.reshape(experts * capacity, feat_width)
    grad_rows = grad_inbound.reshape(experts * capacity, channels)
    preact_rows = preact.reshape(experts * capacity, hidden)
    activation_rows = activation.reshape(experts * capacity, hidden)
    upstream = lax.dot_general(
        grad_rows, weight_two, (((1,), (1,)), ((), ())), preferred_element_type=jnp.float32
    )
    gate_grad = gelu_back(preact_rows, upstream).astype(jnp.bfloat16)
    input_grad = lax.dot_general(
        gate_grad, weight_one, (((1,), (1,)), ((), ())), preferred_element_type=jnp.float32
    )
    input_grad = input_grad.astype(jnp.bfloat16).reshape(experts, capacity, feat_width)
    input_back = lax.all_to_all(input_grad, "expert", split_axis=0, concat_axis=0, tiled=True)
    feat_grad = input_back.reshape(experts * capacity, feat_width)[target].reshape(
        1, rows_y, depth_cells, feat_width
    )
    part_one = lax.dot_general(
        feat_rows, gate_grad, (((0,), (0,)), ((), ())), preferred_element_type=jnp.float32
    )
    part_two = lax.dot_general(
        activation_rows, grad_rows, (((0,), (0,)), ((), ())), preferred_element_type=jnp.float32
    )
    grad_one, grad_two = (
        lax.psum_scatter(
            part_one.astype(jnp.bfloat16), "dp", scatter_dimension=1, tiled=True
        ).astype(jnp.float32),
        lax.psum_scatter(
            part_two.astype(jnp.bfloat16), "dp", scatter_dimension=0, tiled=True
        ).astype(jnp.float32),
    )
    return (imitated, feat_grad, grad_one[None], grad_two[None])


def solution(mesh):
    in_specs = (
        P("dp", "expert", None, None),
        P("dp", "expert", None, None),
        P("expert", None, None),
        P("expert", None, None),
        P(),
        P("dp", "expert", None, None),
    )
    out_specs = (
        P("dp", "expert", None, None),
        P("dp", "expert", None, None),
        P("expert", None, "dp"),
        P("expert", "dp", None),
    )
    return jax.shard_map(
        per_device, mesh=mesh, in_specs=in_specs, out_specs=out_specs, check_vma=False
    )
```

profile of v0, /device:TPU:70, one launch (start us, length us, event | category | flops | bytes accessed | tf_op | source)
XLA Modules:
  0.0 252.7 jit_solution(14375182021403696367)
XLA Ops:
  7.2 2.7 %collective-permute-start.4 = (bf16[1,4,128,256]{3,2,1,0:T(8,128)(2,1)}, bf16[1,4,128,256]{3,2,1,0:T(8,128)(2,1)}, u32[]{:S(2)}, u32[]{:S(2)}) collective-permute-start(bf16[1,4,128,256]{3,2,1,0:T(8,128)(2,1)} %param.11), channel_id=1, source_target_pairs={{0,16},{16,32},{32,48},{48,64},{64,80},{80,96},{96,112},{112,128},... | collective-permute-start | bytes 786440 | tf_op jit(solution)/shard_map/ppermute | solution.py:14
  12.5 3.1 %reduce-window.6 = s32[16,4,128]{2,0,1:T(8,128)} reduce-window(s32[16,4,128]{2,0,1:T(8,128)} %fusion.30, s32[]{:T(128)} %constant.6.clone.1), window={size=1x1x128 pad=0_0x0_0x127_0}, to_apply=%region_0.0 | reduce-window | flops 1040384 | bytes 65540 | tf_op jit(solution)/shard_map/reduce-window
  22.2 6.3 %collective-permute-start.6 = (bf16[3,1,128,256]{3,2,1,0:T(8,128)(2,1)}, bf16[3,1,128,256]{3,2,1,0:T(8,128)(2,1)}, u32[]{:S(2)}, u32[]{:S(2)}) collective-permute-start(bf16[3,1,128,256]{3,2,1,0:T(8,128)(2,1)} %get-tuple-element.55), channel_id=1, source_target_pairs={{0,1},{1,2},{2,3},{3,4},{4,5},{5,6},{6,7},{7,8},{8,9},{9,10},{10,1... | collective-permute-start | bytes 589832 | tf_op jit(solution)/shard_map/ppermute | solution.py:14
  28.5 1.9 collective-permute-start.7
  31.1 4.0 %scatter_custom_fusion = bf16[1024,512]{1,0:T(8,128)(2,1)} fusion(s32[512]{0:T(512)S(1)} %bitcast.198, bf16[512,512]{1,0:T(8,128)(2,1)} %bitcast.202, bf16[]{:T(256)} %constant.11.clone.1), kind=kCustom, calls=%fused_computation.40 | custom fusion | bytes 1049088 | tf_op jit(solution)/shard_map/scatter | solution.py:64
  35.0 9.9 %all-to-all-start = ((bf16[16,64,512]{2,1,0:T(8,128)(2,1)}), bf16[16,64,512]{2,1,0:T(8,128)(2,1)}, u32[]{:S(2)}, u32[]{:S(2)}) async-start(bf16[16,64,512]{2,1,0:T(8,128)(2,1)} %bitcast.141), calls=%async_computation | async-start | bytes 2097152 | tf_op jit(solution)/shard_map/all_to_all | solution.py:68
  46.3 1.7 select_maximum_fusion
  52.7 2.7 %fusion.21 = bf16[512,256]{1,0:T(8,128)(2,1)} fusion(bf16[512,27,256]{2,0,1:T(8,128)(2,1)S(1)} %constant_dynamic-update-slice_fusion.29, bf16[27,256,256]{2,1,0:T(8,128)(2,1)S(1)} %copy-done), kind=kOutput, calls=%fused_computation.37 | convolution fusion | flops 1812070400 | bytes 10878976 | tf_op jit(solution)/shard_map/tko,kio->ti/dot_general | solution.py:95
  55.5 3.5 %scatter_custom_fusion.1 = bf16[1024,256]{1,0:T(8,128)(2,1)} fusion(s32[512]{0:T(512)S(1)} %bitcast.199, bf16[512,256]{1,0:T(8,128)(2,1)} %fusion.21, bf16[]{:T(256)} %constant.11.clone.1), kind=kCustom, calls=%fused_computation.59 | custom fusion | bytes 524800 | tf_op jit(solution)/shard_map/scatter | solution.py:99
  59.0 14.1 %all-to-all-done = bf16[16,64,512]{2,1,0:T(8,128)(2,1)} async-done(((bf16[16,64,512]{2,1,0:T(8,128)(2,1)}), bf16[16,64,512]{2,1,0:T(8,128)(2,1)}, u32[]{:S(2)}, u32[]{:S(2)}) %all-to-all-start) | async-done | bytes 1048608 | tf_op jit(solution)/shard_map/all_to_all | solution.py:68
  73.1 7.2 %all-to-all-start.2 = ((bf16[16,64,256]{2,1,0:T(8,128)(2,1)}), bf16[16,64,256]{2,1,0:T(8,128)(2,1)}, u32[]{:S(2)}, u32[]{:S(2)}) async-start(bf16[16,64,256]{2,1,0:T(8,128)(2,1)} %bitcast.142), calls=%async_computation.2 | async-start | bytes 1048576 | tf_op jit(solution)/shard_map/all_to_all | solution.py:102
  80.6 9.9 %multiply_convert_fusion = (bf16[1024,2048]{1,0:T(8,128)(2,1)}, f32[1024,2048]{1,0:T(8,128)}) fusion(bf16[1024,512]{1,0:T(8,128)(2,1)} %bitcast.8, bf16[1,512,2048]{2,1,0:T(8,128)(2,1)} %param.8), kind=kOutput, calls=%fused_computation.13 | convolution fusion | flops 2166358016 | bytes 15728640 | tf_op jit(solution)/shard_map/dot_general | solution.py:72
  90.5 3.1 %all-to-all-done.2 = bf16[16,64,256]{2,1,0:T(8,128)(2,1)} async-done(((bf16[16,64,256]{2,1,0:T(8,128)(2,1)}), bf16[16,64,256]{2,1,0:T(8,128)(2,1)}, u32[]{:S(2)}, u32[]{:S(2)}) %all-to-all-start.2) | async-done | bytes 524320 | tf_op jit(solution)/shard_map/all_to_all | solution.py:102
  93.6 4.7 %convolution_convert_fusion.1 = bf16[2048,256]{1,0:T(8,128)(2,1)} fusion(bf16[1024,2048]{1,0:T(8,128)(2,1)} %get-tuple-element.59, bf16[1024,256]{1,0:T(8,128)(2,1)} %bitcast.72), kind=kOutput, calls=%fused_computation.17 | convolution fusion | flops 1074266112 | bytes 5767168 | tf_op jit(solution)/shard_map/dot_general | solution.py:122
  98.3 4.5 %convolution_convert_fusion.2 = bf16[1024,256]{1,0:T(8,128)(2,1)} fusion(bf16[1024,2048]{1,0:T(8,128)(2,1)} %get-tuple-element.59, bf16[1,2048,256]{2,1,0:T(8,128)(2,1)} %param.9), kind=kOutput, calls=%fused_computation.24 | convolution fusion | flops 1074003968 | bytes 5767168 | tf_op jit(solution)/shard_map/dot_general | solution.py:74
  102.8 7.7 %all-to-all-start.1 = ((bf16[16,64,256]{2,1,0:T(8,128)(2,1)}), bf16[16,64,256]{2,1,0:T(8,128)(2,1)}, u32[]{:S(2)}, u32[]{:S(2)}) async-start(bf16[16,64,256]{2,1,0:T(8,128)(2,1)} %bitcast.194), calls=%async_computation.1 | async-start | bytes 1048576 | tf_op jit(solution)/shard_map/all_to_all | solution.py:78
  110.5 10.0 %fusion.6 = bf16[1024,2048]{1,0:T(8,128)(2,1)} fusion(f32[1024,2048]{1,0:T(8,128)} %get-tuple-element.60, bf16[1024,256]{1,0:T(8,128)(2,1)} %bitcast.72, bf16[1,2048,256]{2,1,0:T(8,128)(2,1)} %param.9), kind=kOutput, calls=%fused_computation.12 | convolution fusion | flops 1115684864 | bytes 14155776 | tf_op jit(solution)/shard_map/dot_general | solution.py:107
  120.4 3.7 %all-to-all-done.1 = bf16[16,64,256]{2,1,0:T(8,128)(2,1)} async-done(((bf16[16,64,256]{2,1,0:T(8,128)(2,1)}), bf16[16,64,256]{2,1,0:T(8,128)(2,1)}, u32[]{:S(2)}, u32[]{:S(2)}) %all-to-all-start.1) | async-done | bytes 524320 | tf_op jit(solution)/shard_map/all_to_all | solution.py:78
  124.1 3.3 %gather_fusion = bf16[512,256]{1,0:T(8,128)(2,1)} fusion(bf16[1024,256]{1,0:T(8,128)(2,1)} %bitcast.12, s32[1024]{0:T(1024)S(1)} %pad_clamp_fusion), kind=kCustom, calls=%fused_computation | custom fusion | bytes 526336 | tf_op jit(solution)/shard_map/gather | solution.py:85
  130.3 6.2 %fusion.12 = bf16[1024,512]{1,0:T(8,128)(2,1)} fusion(bf16[1024,2048]{1,0:T(8,128)(2,1)} %fusion.6, bf16[1,512,2048]{2,1,0:T(8,128)(2,1)} %param.8), kind=kOutput, calls=%fused_computation.23 | convolution fusion | flops 2148007936 | bytes 7340032 | tf_op jit(solution)/shard_map/dot_general | solution.py:111
  137.5 5.4 %collective-permute-start.2 = (bf16[3,1,128,256]{3,2,1,0:T(8,128)(2,1)}, bf16[3,1,128,256]{3,2,1,0:T(8,128)(2,1)}, u32[]{:S(2)}, u32[]{:S(2)}) collective-permute-start(bf16[3,1,128,256]{3,2,1,0:T(8,128)(2,1)} %get-tuple-element.57), channel_id=1, source_target_pairs={{0,1},{1,2},{2,3},{3,4},{4,5},{5,6},{6,7},{7,8},{8,9},{9,10},{10,1... | collective-permute-start | bytes 589832 | tf_op jit(solution)/shard_map/ppermute | solution.py:14
  142.8 2.1 collective-permute-start.3
  145.0 5.0 %convolution_convert_fusion = bf16[512,2048]{1,0:T(8,128)(2,1)} fusion(bf16[1024,512]{1,0:T(8,128)(2,1)} %bitcast.8, bf16[1024,2048]{1,0:T(8,128)(2,1)S(1)} %copy-done.10), kind=kOutput, calls=%fused_computation.16 | convolution fusion | flops 2148532224 | bytes 7340032 | tf_op jit(solution)/shard_map/dot_general | solution.py:119
  150.0 4.0 %copy.12 = bf16[512,2048]{0,1:T(8,128)(2,1)} copy(bf16[512,2048]{1,0:T(8,128)(2,1)} %convolution_convert_fusion) | data formatting | bytes 4194304
  154.0 9.9 %all-to-all-start.3 = ((bf16[16,64,512]{2,1,0:T(8,128)(2,1)}), bf16[16,64,512]{2,1,0:T(8,128)(2,1)}, u32[]{:S(2)}, u32[]{:S(2)}) async-start(bf16[16,64,512]{2,1,0:T(8,128)(2,1)} %bitcast.185), calls=%async_computation.3 | async-start | bytes 2097152 | tf_op jit(solution)/shard_map/all_to_all | solution.py:115
  164.7 1.9 select_maximum_fusion.2
  170.2 2.7 %fusion.20 = bf16[512,256]{1,0:T(8,128)(2,1)} fusion(bf16[512,27,256]{2,0,1:T(8,128)(2,1)S(1)} %constant_dynamic-update-slice_fusion, bf16[27,256,256]{2,1,0:T(8,128)(2,1)S(1)} %copy-done), kind=kOutput, calls=%fused_computation.36 | convolution fusion | flops 1812070400 | bytes 10878976 | tf_op jit(solution)/shard_map/tki,kio->to/dot_general | solution.py:90
  172.9 15.1 %all-to-all-done.3 = bf16[16,64,512]{2,1,0:T(8,128)(2,1)} async-done(((bf16[16,64,512]{2,1,0:T(8,128)(2,1)}), bf16[16,64,512]{2,1,0:T(8,128)(2,1)}, u32[]{:S(2)}, u32[]{:S(2)}) %all-to-all-start.3) | async-done | bytes 1048608 | tf_op jit(solution)/shard_map/all_to_all | solution.py:115
  188.0 4.0 %gather_fusion.1 = bf16[512,512]{1,0:T(8,128)(2,1)} fusion(bf16[1024,512]{1,0:T(8,128)(2,1)} %bitcast.74, s32[1024]{0:T(1024)S(1)} %pad_clamp_fusion), kind=kCustom, calls=%fused_computation.1 | custom fusion | bytes 1050624 | tf_op jit(solution)/shard_map/gather | solution.py:116
  193.5 49.1 %reduce-scatter.7.cloned.1.call-done = bf16[128,512]{1,0:T(8,128)(2,1)} async-done(((bf16[2048,512]{1,0:T(8,128)(2,1)}), bf16[128,512]{1,0:T(8,128)(2,1)}) %reduce-scatter.7.cloned.1.call-update) | async-done | bytes 131088
  242.6 1.7 copy.13
  244.2 1.6 bitcast_convert_fusion
  (110 shorter events, 25.3 us)
Async XLA Ops:
  7.2 45.6 %copy-start = (bf16[27,256,256]{2,1,0:T(8,128)(2,1)S(1)}, bf16[27,256,256]{2,1,0:T(8,128)(2,1)}, u32[]{:S(2)}) copy-start(bf16[27,256,256]{2,1,0:T(8,128)(2,1)} %param.10) | copy-start | bytes 10616836
  7.2 10.4 %collective-permute-start.4 = (bf16[1,4,128,256]{3,2,1,0:T(8,128)(2,1)}, bf16[1,4,128,256]{3,2,1,0:T(8,128)(2,1)}, u32[]{:S(2)}, u32[]{:S(2)}) collective-permute-start(bf16[1,4,128,256]{3,2,1,0:T(8,128)(2,1)} %param.11), channel_id=1, source_target_pairs={{0,16},{16,32},{32,48},{48,64},{64,80},{80,96},{96,112},{112,128},... | collective-permute-start | bytes 786440 | tf_op jit(solution)/shard_map/ppermute | solution.py:14
  9.9 9.6 %collective-permute-start.5 = (bf16[1,4,128,256]{3,2,1,0:T(8,128)(2,1)}, bf16[1,4,128,256]{3,2,1,0:T(8,128)(2,1)}, u32[]{:S(2)}, u32[]{:S(2)}) collective-permute-start(bf16[1,4,128,256]{3,2,1,0:T(8,128)(2,1)} %param.11), channel_id=1, source_target_pairs={{16,0},{32,16},{48,32},{64,48},{80,64},{96,80},{112,96},{128,112},... | collective-permute-start | bytes 786440 | tf_op jit(solution)/shard_map/ppermute | solution.py:15
  20.5 0.9 copy-start.7
  22.2 22.8 %collective-permute-start.6 = (bf16[3,1,128,256]{3,2,1,0:T(8,128)(2,1)}, bf16[3,1,128,256]{3,2,1,0:T(8,128)(2,1)}, u32[]{:S(2)}, u32[]{:S(2)}) collective-permute-start(bf16[3,1,128,256]{3,2,1,0:T(8,128)(2,1)} %get-tuple-element.55), channel_id=1, source_target_pairs={{0,1},{1,2},{2,3},{3,4},{4,5},{5,6},{6,7},{7,8},{8,9},{9,10},{10,1... | collective-permute-start | bytes 589832 | tf_op jit(solution)/shard_map/ppermute | solution.py:14
  28.5 17.8 %collective-permute-start.7 = (bf16[3,1,128,256]{3,2,1,0:T(8,128)(2,1)}, bf16[3,1,128,256]{3,2,1,0:T(8,128)(2,1)}, u32[]{:S(2)}, u32[]{:S(2)}) collective-permute-start(bf16[3,1,128,256]{3,2,1,0:T(8,128)(2,1)} %get-tuple-element.56), channel_id=1, source_target_pairs={{1,0},{2,1},{3,2},{4,3},{5,4},{6,5},{7,6},{8,7},{9,8},{10,9},{11,1... | collective-permute-start | bytes 589832 | tf_op jit(solution)/shard_map/ppermute | solution.py:15
  35.0 38.1 %all-to-all-start = ((bf16[16,64,512]{2,1,0:T(8,128)(2,1)}), bf16[16,64,512]{2,1,0:T(8,128)(2,1)}, u32[]{:S(2)}, u32[]{:S(2)}) async-start(bf16[16,64,512]{2,1,0:T(8,128)(2,1)} %bitcast.141), calls=%async_computation | async-start | bytes 2097152 | tf_op jit(solution)/shard_map/all_to_all | solution.py:68
  44.9 4.0 %copy-start.8 = (bf16[3,4,128,256]{3,2,1,0:T(8,128)(2,1)S(1)}, bf16[3,4,128,256]{3,2,1,0:T(8,128)(2,1)}, u32[]{:S(2)}) copy-start(bf16[3,4,128,256]{3,2,1,0:T(8,128)(2,1)} %copy-done.7) | copy-start | bytes 2359300
  48.9 2.5 copy-start.9
  73.1 20.4 %all-to-all-start.2 = ((bf16[16,64,256]{2,1,0:T(8,128)(2,1)}), bf16[16,64,256]{2,1,0:T(8,128)(2,1)}, u32[]{:S(2)}, u32[]{:S(2)}) async-start(bf16[16,64,256]{2,1,0:T(8,128)(2,1)} %bitcast.142), calls=%async_computation.2 | async-start | bytes 1048576 | tf_op jit(solution)/shard_map/all_to_all | solution.py:102
  80.3 111.7 %reduce-scatter.5.cloned.1.call-start = ((), (), s32[]{:S(2)}) async-start(), calls=%async_computation.6 | async-start | bytes 1114112 | tf_op jit(solution)/shard_map/reduce_scatter | solution.py:129
  102.8 21.3 %all-to-all-start.1 = ((bf16[16,64,256]{2,1,0:T(8,128)(2,1)}), bf16[16,64,256]{2,1,0:T(8,128)(2,1)}, u32[]{:S(2)}, u32[]{:S(2)}) async-start(bf16[16,64,256]{2,1,0:T(8,128)(2,1)} %bitcast.194), calls=%async_computation.1 | async-start | bytes 1048576 | tf_op jit(solution)/shard_map/all_to_all | solution.py:78
  127.4 9.1 %copy-start.1 = (bf16[512,256]{1,0:T(8,128)(2,1)S(1)}, bf16[512,256]{1,0:T(8,128)(2,1)}, u32[]{:S(2)}) copy-start(bf16[512,256]{1,0:T(8,128)(2,1)} %gather_fusion) | copy-start | bytes 786436
  127.4 17.6 %copy-start.10 = (bf16[1024,2048]{1,0:T(8,128)(2,1)S(1)}, bf16[1024,2048]{1,0:T(8,128)(2,1)}, u32[]{:S(2)}) copy-start(bf16[1024,2048]{1,0:T(8,128)(2,1)} %fusion.6) | copy-start | bytes 12582916
  127.4 9.1 %collective-permute-start = (bf16[1,4,128,256]{3,2,1,0:T(8,128)(2,1)}, bf16[1,4,128,256]{3,2,1,0:T(8,128)(2,1)S(1)}, u32[]{:S(2)}, u32[]{:S(2)}) collective-permute-start(bf16[1,4,128,256]{3,2,1,0:T(8,128)(2,1)} %bitcast.132), channel_id=1, source_target_pairs={{0,16},{16,32},{32,48},{48,64},{64,80},{80,96},{96,112},{112,128},... | collective-permute-start | bytes 786440 | tf_op jit(solution)/shard_map/ppermute | solution.py:14
  129.0 7.5 %collective-permute-start.1 = (bf16[1,4,128,256]{3,2,1,0:T(8,128)(2,1)}, bf16[1,4,128,256]{3,2,1,0:T(8,128)(2,1)S(1)}, u32[]{:S(2)}, u32[]{:S(2)}) collective-permute-start(bf16[1,4,128,256]{3,2,1,0:T(8,128)(2,1)} %bitcast.133), channel_id=1, source_target_pairs={{16,0},{32,16},{48,32},{64,48},{80,64},{96,80},{112,96},{128,112},... | collective-permute-start | bytes 786440 | tf_op jit(solution)/shard_map/ppermute | solution.py:15
  136.5 1.0 copy-start.5
  136.5 0.9 copy-start.3
  137.5 27.2 %collective-permute-start.2 = (bf16[3,1,128,256]{3,2,1,0:T(8,128)(2,1)}, bf16[3,1,128,256]{3,2,1,0:T(8,128)(2,1)}, u32[]{:S(2)}, u32[]{:S(2)}) collective-permute-start(bf16[3,1,128,256]{3,2,1,0:T(8,128)(2,1)} %get-tuple-element.57), channel_id=1, source_target_pairs={{0,1},{1,2},{2,3},{3,4},{4,5},{5,6},{6,7},{7,8},{8,9},{9,10},{10,1... | collective-permute-start | bytes 589832 | tf_op jit(solution)/shard_map/ppermute | solution.py:14
  142.8 21.8 %collective-permute-start.3 = (bf16[3,1,128,256]{3,2,1,0:T(8,128)(2,1)}, bf16[3,1,128,256]{3,2,1,0:T(8,128)(2,1)}, u32[]{:S(2)}, u32[]{:S(2)}) collective-permute-start(bf16[3,1,128,256]{3,2,1,0:T(8,128)(2,1)} %get-tuple-element.58), channel_id=1, source_target_pairs={{1,0},{2,1},{3,2},{4,3},{5,4},{6,5},{7,6},{8,7},{9,8},{10,9},{11,1... | collective-permute-start | bytes 589832 | tf_op jit(solution)/shard_map/ppermute | solution.py:15
  154.0 34.0 %all-to-all-start.3 = ((bf16[16,64,512]{2,1,0:T(8,128)(2,1)}), bf16[16,64,512]{2,1,0:T(8,128)(2,1)}, u32[]{:S(2)}, u32[]{:S(2)}) async-start(bf16[16,64,512]{2,1,0:T(8,128)(2,1)} %bitcast.185), calls=%async_computation.3 | async-start | bytes 2097152 | tf_op jit(solution)/shard_map/all_to_all | solution.py:115
  163.8 78.7 %reduce-scatter.7.cloned.1.call-start = ((), (), s32[]{:S(2)}) async-start(), calls=%async_computation.7 | async-start | bytes 2228224
  164.6 2.8 %copy-start.2 = (bf16[512,256]{1,0:T(8,128)(2,1)S(1)}, bf16[512,256]{1,0:T(8,128)(2,1)}, u32[]{:S(2)}) copy-start(bf16[512,256]{1,0:T(8,128)(2,1)} %gather_fusion) | copy-start | bytes 786436
  164.6 2.8 %copy-start.4 = (bf16[1,4,128,256]{3,2,1,0:T(8,128)(2,1)S(1)}, bf16[1,4,128,256]{3,2,1,0:T(8,128)(2,1)}, u32[]{:S(2)}) copy-start(bf16[1,4,128,256]{3,2,1,0:T(8,128)(2,1)} %copy-done.3) | copy-start | bytes 786436
  164.6 2.8 %copy-start.6 = (bf16[1,4,128,256]{3,2,1,0:T(8,128)(2,1)S(1)}, bf16[1,4,128,256]{3,2,1,0:T(8,128)(2,1)}, u32[]{:S(2)}) copy-start(bf16[1,4,128,256]{3,2,1,0:T(8,128)(2,1)} %copy-done.5) | copy-start | bytes 786436
Sparse Core Ops, SparseCore 0:
  98.4 68.5 reduce-scatter.4
  169.7 72.8 reduce-scatter.6
where the time goes:
time: 254 us; the launch traced here: 253 us
  waiting for transfers between devices  87.1 us (34%)
  starting transfers between devices  57.5 us (23%)
  matrix products  45.7 us (18%)
  local copies, waits for them, and re-layouts  30.8 us (12%)
  other arithmetic  16.9 us (7%)
  between operations  14.7 us (6%)
    unnamed x3, waiting for transfers between devices  49.8 us
    ppermute x4, starting transfers between devices, extended(): before = lax.ppermute(last, axis, up)  16 us
    all_to_all x1, waiting for transfers between devices, per_device(): lax.all_to_all(input_grad, 'expert', split_axis=0, concat_axis=0, tiled=T...  15.1 us
    all_to_all x1, waiting for transfers between devices, per_device(): lax.all_to_all(outbound, 'expert', split_axis=0, concat_axis=0, tiled=True)  14.1 us
    unnamed x78, local copies, waits for them, and re-layouts  11.4 us
    dot_general x1, matrix products, per_device(): lax.dot_general(grad_rows, weight_two, (((1,), (1,)), ((), ())), preferre...  9.96 us
    dot_general x1, matrix products, per_device(): preact = jnp.dot(row_block, weight_one, preferred_element_type=jnp.float32)  9.93 us
    all_to_all x1, starting transfers between devices, per_device(): lax.all_to_all(outbound, 'expert', split_axis=0, concat_axis=0, tiled=True)  9.88 us
  transfers between devices with their start and end apart: 14, of which 6 were waited for; matrix products, arithmetic and copies ran while one was open for 33% of the time, Pallas kernels for 0%

commit v1 on v0

--- a/solution.py
+++ b/solution.py
@@ -23,6 +23,24 @@
 
 def gelu_back(preact, upstream):
     return jax.vjp(gelu_act, preact)[1](upstream)[0]
+
+
+def tree_scatter(blocks, order):
+    count = blocks.shape[0]
+    me = lax.axis_index("dp")
+    bits = count.bit_length() - 1
+    x = blocks.reshape((2,) * bits + blocks.shape[1:])
+    remaining = list(range(bits - 1, -1, -1))
+    for bit in order:
+        axis = remaining.index(bit)
+        mine = (me >> bit) & 1
+        keep = lax.dynamic_index_in_dim(x, mine, axis=axis, keepdims=False)
+        send = lax.dynamic_index_in_dim(x, 1 - mine, axis=axis, keepdims=False)
+        pairs = [(i, i ^ (1 << bit)) for i in range(count)]
+        got = lax.ppermute(send.astype(jnp.bfloat16), "dp", pairs)
+        x = keep + got.astype(jnp.float32)
+        remaining.pop(axis)
+    return x
 
 
 def gather_taps(padded, rows_y, depth_cells, flipped):
@@ -116,20 +134,16 @@
     feat_grad = input_back.reshape(experts * capacity, feat_width)[target].reshape(
         1, rows_y, depth_cells, feat_width
     )
+    slabs = lax.axis_size("dp")
     part_one = lax.dot_general(
-        feat_rows, gate_grad, (((0,), (0,)), ((), ())), preferred_element_type=jnp.float32
+        gate_grad, feat_rows, (((0,), (0,)), ((), ())), preferred_element_type=jnp.float32
     )
     part_two = lax.dot_general(
         activation_rows, grad_rows, (((0,), (0,)), ((), ())), preferred_element_type=jnp.float32
     )
-    grad_one, grad_two = (
-        lax.psum_scatter(
-            part_one.astype(jnp.bfloat16), "dp", scatter_dimension=1, tiled=True
-        ).astype(jnp.float32),
-        lax.psum_scatter(
-            part_two.astype(jnp.bfloat16), "dp", scatter_dimension=0, tiled=True
-        ).astype(jnp.float32),
-    )
+    grad_one = tree_scatter(part_one.reshape(slabs, hidden // slabs, feat_width), (0, 1, 3, 2))
+    grad_one = grad_one.T
+    grad_two = tree_scatter(part_two.reshape(slabs, hidden // slabs, channels), (0, 3, 1, 2))
     return (imitated, feat_grad, grad_one[None], grad_two[None])
 
 

time: 254 us -> 263 us (1.035)
  the two profiles are of different devices: /device:TPU:70 before, /device:TPU:95 now
where the time goes in v1:
time: 263 us; the launch traced here: 258 us
  starting transfers between devices  75.1 us (29%)
  waiting for transfers between devices  65.9 us (25%)
  matrix products  50.1 us (19%)
  local copies, waits for them, and re-layouts  46.3 us (18%)
  other arithmetic  19.1 us (7%)
    ppermute x4, waiting for transfers between devices, extended(): before = lax.ppermute(last, axis, up)  21.1 us
    ppermute x4, starting transfers between devices, extended(): before = lax.ppermute(last, axis, up)  20.5 us
    ppermute x8, waiting for transfers between devices, tree_scatter(): got = lax.ppermute(send.astype(jnp.bfloat16), 'dp', pairs)  14.2 us
    dot_general x1, matrix products, per_device(): preact = jnp.dot(row_block, weight_one, preferred_element_type=jnp.float32)  13.3 us
    ppermute x4, waiting for transfers between devices, extended(): after = lax.ppermute(first, axis, down)  13 us
    ppermute x8, starting transfers between devices, tree_scatter(): got = lax.ppermute(send.astype(jnp.bfloat16), 'dp', pairs)  12.5 us
    unnamed x71, local copies, waits for them, and re-layouts  11.4 us
    all_to_all x1, waiting for transfers between devices, per_device(): lax.all_to_all(outbound, 'expert', split_axis=0, concat_axis=0, tiled=True)  11.2 us
  transfers between devices with their start and end apart: 20, of which 9 were waited for; matrix products, arithmetic and copies ran while one was open for 29% of the time, Pallas kernels for 0%

profile of v1, /device:TPU:95, one launch (start us, length us, event | category | flops | bytes accessed | tf_op | source)
XLA Modules:
  0.0 257.9 jit_solution(1028851559864735803)
XLA Ops:
  3.5 5.1 %collective-permute-start.4 = (bf16[1,4,128,256]{3,2,1,0:T(8,128)(2,1)}, bf16[1,4,128,256]{3,2,1,0:T(8,128)(2,1)}, u32[]{:S(2)}, u32[]{:S(2)}) collective-permute-start(bf16[1,4,128,256]{3,2,1,0:T(8,128)(2,1)} %param.11), channel_id=1, source_target_pairs={{0,16},{16,32},{32,48},{48,64},{64,80},{80,96},{96,112},{112,128},... | collective-permute-start | bytes 786440 | tf_op jit(solution)/shard_map/ppermute | solution.py:14
  9.9 3.1 %reduce-window.6 = s32[16,4,128]{2,0,1:T(8,128)} reduce-window(s32[16,4,128]{2,0,1:T(8,128)} %fusion.57, s32[]{:T(128)} %constant.79.clone.1), window={size=1x1x128 pad=0_0x0_0x127_0}, to_apply=%region_0.0 | reduce-window | flops 1040384 | bytes 65540 | tf_op jit(solution)/shard_map/reduce-window
  17.9 6.0 %collective-permute-start.6 = (bf16[3,1,128,256]{3,2,1,0:T(8,128)(2,1)S(1)}, bf16[3,1,128,256]{3,2,1,0:T(8,128)(2,1)S(1)}, u32[]{:S(2)}, u32[]{:S(2)}) collective-permute-start(bf16[3,1,128,256]{3,2,1,0:T(8,128)(2,1)S(1)} %get-tuple-element.65), channel_id=1, source_target_pairs={{0,1},{1,2},{2,3},{3,4},{4,5},{5,6},{6,7},{7,8},{8,9},{9,10},{10,1... | collective-permute-start | bytes 589832 | tf_op jit(solution)/shard_map/ppermute | solution.py:14
  26.6 3.6 %collective-permute-done.6 = bf16[3,1,128,256]{3,2,1,0:T(8,128)(2,1)S(1)} collective-permute-done((bf16[3,1,128,256]{3,2,1,0:T(8,128)(2,1)S(1)}, bf16[3,1,128,256]{3,2,1,0:T(8,128)(2,1)S(1)}, u32[]{:S(2)}, u32[]{:S(2)}) %collective-permute-start.6) | collective-permute-done | bytes 196640 | tf_op jit(solution)/shard_map/ppermute | solution.py:14
  30.2 8.1 %collective-permute-done.7 = bf16[3,1,128,256]{3,2,1,0:T(8,128)(2,1)S(1)} collective-permute-done((bf16[3,1,128,256]{3,2,1,0:T(8,128)(2,1)S(1)}, bf16[3,1,128,256]{3,2,1,0:T(8,128)(2,1)S(1)}, u32[]{:S(2)}, u32[]{:S(2)}) %collective-permute-start.7) | collective-permute-done | bytes 196640 | tf_op jit(solution)/shard_map/ppermute | solution.py:15
  45.3 3.5 %scatter_custom_fusion.1 = bf16[1024,256]{1,0:T(8,128)(2,1)} fusion(s32[512]{0:T(512)S(1)} %bitcast.266, bf16[512,256]{1,0:T(8,128)(2,1)} %fusion.37, bf16[]{:T(256)} %constant.77.clone.1), kind=kCustom, calls=%fused_computation.95 | custom fusion | bytes 524800 | tf_op jit(solution)/shard_map/scatter | solution.py:117
  48.8 5.8 %all-to-all-start.2 = ((bf16[16,64,256]{2,1,0:T(8,128)(2,1)}), bf16[16,64,256]{2,1,0:T(8,128)(2,1)}, u32[]{:S(2)}, u32[]{:S(2)}) async-start(bf16[16,64,256]{2,1,0:T(8,128)(2,1)} %bitcast.211), calls=%async_computation.2 | async-start | bytes 1048576 | tf_op jit(solution)/shard_map/all_to_all | solution.py:120
  54.6 4.0 %scatter_custom_fusion = bf16[1024,512]{1,0:T(8,128)(2,1)} fusion(s32[512]{0:T(512)S(1)} %bitcast.267, bf16[512,512]{1,0:T(8,128)(2,1)} %bitcast.270, bf16[]{:T(256)} %constant.77.clone.1), kind=kCustom, calls=%fused_computation.69 | custom fusion | bytes 1049088 | tf_op jit(solution)/shard_map/scatter | solution.py:82
  58.6 6.4 %all-to-all-done.2 = bf16[16,64,256]{2,1,0:T(8,128)(2,1)} async-done(((bf16[16,64,256]{2,1,0:T(8,128)(2,1)}), bf16[16,64,256]{2,1,0:T(8,128)(2,1)}, u32[]{:S(2)}, u32[]{:S(2)}) %all-to-all-start.2) | async-done | bytes 524320 | tf_op jit(solution)/shard_map/all_to_all | solution.py:120
  65.0 10.1 %all-to-all-start = ((bf16[16,64,512]{2,1,0:T(8,128)(2,1)}), bf16[16,64,512]{2,1,0:T(8,128)(2,1)}, u32[]{:S(2)}, u32[]{:S(2)}) async-start(bf16[16,64,512]{2,1,0:T(8,128)(2,1)} %bitcast.210), calls=%async_computation | async-start | bytes 2097152 | tf_op jit(solution)/shard_map/all_to_all | solution.py:86
  75.2 5.9 %fusion.39 = f32[1024,2048]{1,0:T(8,128)} fusion(bf16[1024,256]{1,0:T(8,128)(2,1)} %bitcast.72, bf16[1,2048,256]{2,1,0:T(8,128)(2,1)} %param.9), kind=kOutput, calls=%fused_computation.58 | convolution fusion | flops 1073741824 | bytes 9961472 | tf_op jit(solution)/shard_map/dot_general | solution.py:125
  81.1 11.2 %all-to-all-done = bf16[16,64,512]{2,1,0:T(8,128)(2,1)} async-done(((bf16[16,64,512]{2,1,0:T(8,128)(2,1)}), bf16[16,64,512]{2,1,0:T(8,128)(2,1)}, u32[]{:S(2)}, u32[]{:S(2)}) %all-to-all-start) | async-done | bytes 1048608 | tf_op jit(solution)/shard_map/all_to_all | solution.py:86
  92.2 13.3 %fusion.14 = (bf16[2048,1024]{0,1:T(8,128)(2,1)}, bf16[2048,1024]{0,1:T(8,128)(2,1)}, f32[1024,2048]{1,0:T(8,128)}) fusion(f32[1024,2048]{1,0:T(8,128)} %fusion.39, bf16[1024,512]{1,0:T(8,128)(2,1)} %bitcast.8, bf16[1,512,2048]{2,1,0:T(8,128)(2,1)} %param.8), kind=kOutput, calls=%fused_computation.24 | convolution fusion | flops 2193620992 | bytes 28311552 | tf_op jit(solution)/shard_map/dot_general | solution.py:90
  105.5 6.3 %copy.20 = bf16[2048,1024]{1,0:T(8,128)(2,1)} copy(bf16[2048,1024]{0,1:T(8,128)(2,1)} %get-tuple-element.12) | data formatting | bytes 8388608 | tf_op jit(solution)/shard_map/dot_general | solution.py:141
  111.8 3.7 %fusion.72 = f32[2,2,2,2,128,256]{5,4,3,2,1,0:T(8,128)S(1)} fusion(bf16[2,2,2,2,128,1024]{5,4,3,2,1,0:T(8,128)(2,1)} %bitcast.209, bf16[1024,256,1,1,1,1]{1,0,5,4,3,2:T(8,128)(2,1)} %bitcast.93), kind=kOutput, calls=%fused_computation.187 | convolution fusion | flops 1073741824 | bytes 6815744 | tf_op jit(solution)/shard_map/dot_general | solution.py:141
  117.8 3.9 %collective-permute-start.12 = (bf16[2,2,2,128,256]{4,3,2,1,0:T(8,128)(2,1)}, bf16[2,2,2,128,256]{4,3,2,1,0:T(8,128)(2,1)}, u32[]{:S(2)}, u32[]{:S(2)}) collective-permute-start(bf16[2,2,2,128,256]{4,3,2,1,0:T(8,128)(2,1)} %fusion.43), channel_id=1, source_target_pairs={{0,16},{16,0},{32,48},{48,32},{64,80},{80,64},{96,112},{112,96},{1... | collective-permute-start | bytes 1572872 | tf_op jit(solution)/shard_map/ppermute | solution.py:40
  121.7 6.0 %fusion.30 = bf16[1024,256]{1,0:T(8,128)(2,1)} fusion(f32[1024,2048]{1,0:T(8,128)} %get-tuple-element.69, bf16[1,2048,256]{2,1,0:T(8,128)(2,1)S(1)} %copy-done.5), kind=kOutput, calls=%fused_computation.41 | convolution fusion | flops 1092878336 | bytes 9961472 | tf_op jit(solution)/shard_map/dot_general | solution.py:92
  127.6 9.7 %all-to-all-start.1 = ((bf16[16,64,256]{2,1,0:T(8,128)(2,1)}), bf16[16,64,256]{2,1,0:T(8,128)(2,1)}, u32[]{:S(2)}, u32[]{:S(2)}) async-start(bf16[16,64,256]{2,1,0:T(8,128)(2,1)} %bitcast.263), calls=%async_computation.1 | async-start | bytes 1048576 | tf_op jit(solution)/shard_map/all_to_all | solution.py:96
  137.4 6.5 %copy.19 = bf16[2048,1024]{1,0:T(8,128)(2,1)} copy(bf16[2048,1024]{0,1:T(8,128)(2,1)} %get-tuple-element.13) | data formatting | bytes 8388608 | tf_op jit(solution)/shard_map/dot_general | solution.py:138
  147.5 4.8 %fusion.71 = f32[2,2,2,2,128,512]{5,4,3,2,1,0:T(8,128)S(1)} fusion(bf16[2,2,2,2,128,1024]{5,4,3,2,1,0:T(8,128)(2,1)} %bitcast.208, bf16[1024,512,1,1,1,1]{1,0,5,4,3,2:T(8,128)(2,1)} %bitcast.80), kind=kOutput, calls=%fused_computation.186 | convolution fusion | flops 2147483648 | bytes 9437184 | tf_op jit(solution)/shard_map/dot_general | solution.py:138
  152.4 5.0 %collective-permute-done.13 = bf16[2,2,128,256]{3,2,1,0:T(8,128)(2,1)S(1)} collective-permute-done((bf16[2,2,128,256]{3,2,1,0:T(8,128)(2,1)S(1)}, bf16[2,2,128,256]{3,2,1,0:T(8,128)(2,1)S(1)}, u32[]{:S(2)}, u32[]{:S(2)}) %collective-permute-start.13) | collective-permute-done | bytes 262176 | tf_op jit(solution)/shard_map/ppermute | solution.py:40
  163.4 4.3 %collective-permute-start.15 = (bf16[128,256]{1,0:T(8,128)(2,1)}, bf16[128,256]{1,0:T(8,128)(2,1)}, u32[]{:S(2)}, u32[]{:S(2)}) collective-permute-start(bf16[128,256]{1,0:T(8,128)(2,1)} %fusion.54), channel_id=1, source_target_pairs={{0,64},{16,80},{32,96},{48,112},{64,0},{80,16},{96,32},{112,48},{1... | collective-permute-start | bytes 196616 | tf_op jit(solution)/shard_map/ppermute | solution.py:40
  167.7 3.3 %gather_fusion = bf16[512,256]{1,0:T(8,128)(2,1)} fusion(bf16[1024,256]{1,0:T(8,128)(2,1)} %bitcast.12, s32[1024]{0:T(1024)S(1)} %pad_clamp_fusion), kind=kCustom, calls=%fused_computation | custom fusion | bytes 526336 | tf_op jit(solution)/shard_map/gather | solution.py:103
  171.1 3.5 %collective-permute-start.1 = (bf16[1,4,128,256]{3,2,1,0:T(8,128)(2,1)}, bf16[1,4,128,256]{3,2,1,0:T(8,128)(2,1)}, u32[]{:S(2)}, u32[]{:S(2)}) collective-permute-start(bf16[1,4,128,256]{3,2,1,0:T(8,128)(2,1)} %bitcast.202), channel_id=1, source_target_pairs={{16,0},{32,16},{48,32},{64,48},{80,64},{96,80},{112,96},{128,112},... | collective-permute-start | bytes 786440 | tf_op jit(solution)/shard_map/ppermute | solution.py:15
  174.6 4.1 %collective-permute-start = (bf16[1,4,128,256]{3,2,1,0:T(8,128)(2,1)}, bf16[1,4,128,256]{3,2,1,0:T(8,128)(2,1)}, u32[]{:S(2)}, u32[]{:S(2)}) collective-permute-start(bf16[1,4,128,256]{3,2,1,0:T(8,128)(2,1)} %bitcast.203), channel_id=1, source_target_pairs={{0,16},{16,32},{32,48},{48,64},{64,80},{80,96},{96,112},{112,128},... | collective-permute-start | bytes 786440 | tf_op jit(solution)/shard_map/ppermute | solution.py:14
  178.7 10.9 %fusion.25 = bf16[1024,512]{1,0:T(8,128)(2,1)} fusion(bf16[1,512,2048]{2,1,0:T(8,128)(2,1)} %param.8, f32[1024,2048]{1,0:T(8,128)} %get-tuple-element.69, f32[1024,2048]{1,0:T(8,128)} %fusion.39), kind=kOutput, calls=%fused_computation.40 | convolution fusion | flops 2189950976 | bytes 19922944 | tf_op jit(solution)/shard_map/dot_general | solution.py:129
  189.7 6.3 %all-to-all-start.3 = ((bf16[16,64,512]{2,1,0:T(8,128)(2,1)}), bf16[16,64,512]{2,1,0:T(8,128)(2,1)}, u32[]{:S(2)}, u32[]{:S(2)}) async-start(bf16[16,64,512]{2,1,0:T(8,128)(2,1)} %bitcast.254), calls=%async_computation.3 | async-start | bytes 2097152 | tf_op jit(solution)/shard_map/all_to_all | solution.py:133
  198.7 5.2 %collective-permute-start.2 = (bf16[3,1,128,256]{3,2,1,0:T(8,128)(2,1)S(1)}, bf16[3,1,128,256]{3,2,1,0:T(8,128)(2,1)S(1)}, u32[]{:S(2)}, u32[]{:S(2)}) collective-permute-start(bf16[3,1,128,256]{3,2,1,0:T(8,128)(2,1)S(1)} %get-tuple-element.67), channel_id=1, source_target_pairs={{0,1},{1,2},{2,3},{3,4},{4,5},{5,6},{6,7},{7,8},{8,9},{9,10},{10,1... | collective-permute-start | bytes 589832 | tf_op jit(solution)/shard_map/ppermute | solution.py:14
  208.6 17.5 %collective-permute-done.2 = bf16[3,1,128,256]{3,2,1,0:T(8,128)(2,1)S(1)} collective-permute-done((bf16[3,1,128,256]{3,2,1,0:T(8,128)(2,1)S(1)}, bf16[3,1,128,256]{3,2,1,0:T(8,128)(2,1)S(1)}, u32[]{:S(2)}, u32[]{:S(2)}) %collective-permute-start.2) | collective-permute-done | bytes 196640 | tf_op jit(solution)/shard_map/ppermute | solution.py:14
  226.1 4.9 %collective-permute-done.3 = bf16[3,1,128,256]{3,2,1,0:T(8,128)(2,1)S(1)} collective-permute-done((bf16[3,1,128,256]{3,2,1,0:T(8,128)(2,1)S(1)}, bf16[3,1,128,256]{3,2,1,0:T(8,128)(2,1)S(1)}, u32[]{:S(2)}, u32[]{:S(2)}) %collective-permute-start.3) | collective-permute-done | bytes 196640 | tf_op jit(solution)/shard_map/ppermute | solution.py:15
  238.7 7.4 %collective-permute-done.10 = bf16[2,128,512]{2,1,0:T(8,128)(2,1)S(1)} collective-permute-done((bf16[2,128,512]{2,1,0:T(8,128)(2,1)S(1)}, bf16[2,128,512]{2,1,0:T(8,128)(2,1)S(1)}, u32[]{:S(2)}, u32[]{:S(2)}) %collective-permute-start.10) | collective-permute-done | bytes 262176 | tf_op jit(solution)/shard_map/ppermute | solution.py:40
  250.3 4.0 %gather_fusion.1 = bf16[512,512]{1,0:T(8,128)(2,1)} fusion(bf16[1024,512]{1,0:T(8,128)(2,1)} %bitcast.74, s32[1024]{0:T(1024)S(1)} %pad_clamp_fusion), kind=kCustom, calls=%fused_computation.1 | custom fusion | bytes 1050624 | tf_op jit(solution)/shard_map/gather | solution.py:134
  (129 shorter events, 52.9 us)
Async XLA Ops:
  0.6 41.9 %copy-start = (bf16[27,256,256]{2,1,0:T(8,128)(2,1)S(1)}, bf16[27,256,256]{2,1,0:T(8,128)(2,1)}, u32[]{:S(2)}) copy-start(bf16[27,256,256]{2,1,0:T(8,128)(2,1)} %param.10) | copy-start | bytes 10616836
  0.6 16.2 %collective-permute-start.5 = (bf16[1,4,128,256]{3,2,1,0:T(8,128)(2,1)}, bf16[1,4,128,256]{3,2,1,0:T(8,128)(2,1)}, u32[]{:S(2)}, u32[]{:S(2)}) collective-permute-start(bf16[1,4,128,256]{3,2,1,0:T(8,128)(2,1)} %param.11), channel_id=1, source_target_pairs={{16,0},{32,16},{48,32},{64,48},{80,64},{96,80},{112,96},{128,112},... | collective-permute-start | bytes 786440 | tf_op jit(solution)/shard_map/ppermute | solution.py:15
  3.5 11.4 %collective-permute-start.4 = (bf16[1,4,128,256]{3,2,1,0:T(8,128)(2,1)}, bf16[1,4,128,256]{3,2,1,0:T(8,128)(2,1)}, u32[]{:S(2)}, u32[]{:S(2)}) collective-permute-start(bf16[1,4,128,256]{3,2,1,0:T(8,128)(2,1)} %param.11), channel_id=1, source_target_pairs={{0,16},{16,32},{32,48},{48,64},{64,80},{80,96},{96,112},{112,128},... | collective-permute-start | bytes 786440 | tf_op jit(solution)/shard_map/ppermute | solution.py:14
  17.9 12.3 %collective-permute-start.6 = (bf16[3,1,128,256]{3,2,1,0:T(8,128)(2,1)S(1)}, bf16[3,1,128,256]{3,2,1,0:T(8,128)(2,1)S(1)}, u32[]{:S(2)}, u32[]{:S(2)}) collective-permute-start(bf16[3,1,128,256]{3,2,1,0:T(8,128)(2,1)S(1)} %get-tuple-element.65), channel_id=1, source_target_pairs={{0,1},{1,2},{2,3},{3,4},{4,5},{5,6},{6,7},{7,8},{8,9},{9,10},{10,1... | collective-permute-start | bytes 589832 | tf_op jit(solution)/shard_map/ppermute | solution.py:14
  23.9 14.3 %collective-permute-start.7 = (bf16[3,1,128,256]{3,2,1,0:T(8,128)(2,1)S(1)}, bf16[3,1,128,256]{3,2,1,0:T(8,128)(2,1)S(1)}, u32[]{:S(2)}, u32[]{:S(2)}) collective-permute-start(bf16[3,1,128,256]{3,2,1,0:T(8,128)(2,1)S(1)} %get-tuple-element.66), channel_id=1, source_target_pairs={{1,0},{2,1},{3,2},{4,3},{5,4},{6,5},{7,6},{8,7},{9,8},{10,9},{11,1... | collective-permute-start | bytes 589832 | tf_op jit(solution)/shard_map/ppermute | solution.py:15
  39.7 1.5 copy-start.6
  48.8 16.2 %all-to-all-start.2 = ((bf16[16,64,256]{2,1,0:T(8,128)(2,1)}), bf16[16,64,256]{2,1,0:T(8,128)(2,1)}, u32[]{:S(2)}, u32[]{:S(2)}) async-start(bf16[16,64,256]{2,1,0:T(8,128)(2,1)} %bitcast.211), calls=%async_computation.2 | async-start | bytes 1048576 | tf_op jit(solution)/shard_map/all_to_all | solution.py:120
  65.0 27.2 %all-to-all-start = ((bf16[16,64,512]{2,1,0:T(8,128)(2,1)}), bf16[16,64,512]{2,1,0:T(8,128)(2,1)}, u32[]{:S(2)}, u32[]{:S(2)}) async-start(bf16[16,64,512]{2,1,0:T(8,128)(2,1)} %bitcast.210), calls=%async_computation | async-start | bytes 2097152 | tf_op jit(solution)/shard_map/all_to_all | solution.py:86
  111.8 9.8 %copy-start.5 = (bf16[1,2048,256]{2,1,0:T(8,128)(2,1)S(1)}, bf16[1,2048,256]{2,1,0:T(8,128)(2,1)}, u32[]{:S(2)}) copy-start(bf16[1,2048,256]{2,1,0:T(8,128)(2,1)} %param.9) | copy-start | bytes 3145732
  115.5 1.4 copy-start.4
  117.8 26.1 %collective-permute-start.12 = (bf16[2,2,2,128,256]{4,3,2,1,0:T(8,128)(2,1)}, bf16[2,2,2,128,256]{4,3,2,1,0:T(8,128)(2,1)}, u32[]{:S(2)}, u32[]{:S(2)}) collective-permute-start(bf16[2,2,2,128,256]{4,3,2,1,0:T(8,128)(2,1)} %fusion.43), channel_id=1, source_target_pairs={{0,16},{16,0},{32,48},{48,32},{64,80},{80,64},{96,112},{112,96},{1... | collective-permute-start | bytes 1572872 | tf_op jit(solution)/shard_map/ppermute | solution.py:40
  127.6 40.1 %all-to-all-start.1 = ((bf16[16,64,256]{2,1,0:T(8,128)(2,1)}), bf16[16,64,256]{2,1,0:T(8,128)(2,1)}, u32[]{:S(2)}, u32[]{:S(2)}) async-start(bf16[16,64,256]{2,1,0:T(8,128)(2,1)} %bitcast.263), calls=%async_computation.1 | async-start | bytes 1048576 | tf_op jit(solution)/shard_map/all_to_all | solution.py:96
  145.4 12.0 %collective-permute-start.13 = (bf16[2,2,128,256]{3,2,1,0:T(8,128)(2,1)S(1)}, bf16[2,2,128,256]{3,2,1,0:T(8,128)(2,1)S(1)}, u32[]{:S(2)}, u32[]{:S(2)}) collective-permute-start(bf16[2,2,128,256]{3,2,1,0:T(8,128)(2,1)S(1)} %fusion.47), channel_id=1, source_target_pairs={{0,128},{16,144},{32,160},{48,176},{64,192},{80,208},{96,224},{112... | collective-permute-start | bytes 786440 | tf_op jit(solution)/shard_map/ppermute | solution.py:40
  152.4 5.7 %copy-start.2 = (f32[2,2,2,2,128,512]{5,4,3,2,1,0:T(8,128)}, f32[2,2,2,2,128,512]{5,4,3,2,1,0:T(8,128)S(1)}, u32[]{:S(2)}) copy-start(f32[2,2,2,2,128,512]{5,4,3,2,1,0:T(8,128)S(1)} %fusion.71) | copy-start | bytes 12582916
  157.5 4.5 %collective-permute-start.14 = (bf16[2,128,256]{2,1,0:T(8,128)(2,1)S(1)}, bf16[2,128,256]{2,1,0:T(8,128)(2,1)S(1)}, u32[]{:S(2)}, u32[]{:S(2)}) collective-permute-start(bf16[2,128,256]{2,1,0:T(8,128)(2,1)S(1)} %fusion.52), channel_id=1, source_target_pairs={{0,32},{16,48},{32,0},{48,16},{64,96},{80,112},{96,64},{112,80},{1... | collective-permute-start | bytes 393224 | tf_op jit(solution)/shard_map/ppermute | solution.py:40
  159.1 46.7 %collective-permute-start.8 = (bf16[2,2,2,128,512]{4,3,2,1,0:T(8,128)(2,1)}, bf16[2,2,2,128,512]{4,3,2,1,0:T(8,128)(2,1)}, u32[]{:S(2)}, u32[]{:S(2)}) collective-permute-start(bf16[2,2,2,128,512]{4,3,2,1,0:T(8,128)(2,1)} %fusion.38), channel_id=1, source_target_pairs={{0,16},{16,0},{32,48},{48,32},{64,80},{80,64},{96,112},{112,96},{1... | collective-permute-start | bytes 3145736 | tf_op jit(solution)/shard_map/ppermute | solution.py:40
  162.1 0.7 copy-start.7
  163.4 32.6 %collective-permute-start.15 = (bf16[128,256]{1,0:T(8,128)(2,1)}, bf16[128,256]{1,0:T(8,128)(2,1)}, u32[]{:S(2)}, u32[]{:S(2)}) collective-permute-start(bf16[128,256]{1,0:T(8,128)(2,1)} %fusion.54), channel_id=1, source_target_pairs={{0,64},{16,80},{32,96},{48,112},{64,0},{80,16},{96,32},{112,48},{1... | collective-permute-start | bytes 196616 | tf_op jit(solution)/shard_map/ppermute | solution.py:40
  171.1 26.6 %collective-permute-start.1 = (bf16[1,4,128,256]{3,2,1,0:T(8,128)(2,1)}, bf16[1,4,128,256]{3,2,1,0:T(8,128)(2,1)}, u32[]{:S(2)}, u32[]{:S(2)}) collective-permute-start(bf16[1,4,128,256]{3,2,1,0:T(8,128)(2,1)} %bitcast.202), channel_id=1, source_target_pairs={{16,0},{32,16},{48,32},{64,48},{80,64},{96,80},{112,96},{128,112},... | collective-permute-start | bytes 786440 | tf_op jit(solution)/shard_map/ppermute | solution.py:15
  174.6 23.0 %collective-permute-start = (bf16[1,4,128,256]{3,2,1,0:T(8,128)(2,1)}, bf16[1,4,128,256]{3,2,1,0:T(8,128)(2,1)}, u32[]{:S(2)}, u32[]{:S(2)}) collective-permute-start(bf16[1,4,128,256]{3,2,1,0:T(8,128)(2,1)} %bitcast.203), channel_id=1, source_target_pairs={{0,16},{16,32},{32,48},{48,64},{64,80},{80,96},{96,112},{112,128},... | collective-permute-start | bytes 786440 | tf_op jit(solution)/shard_map/ppermute | solution.py:14
  189.7 60.7 %all-to-all-start.3 = ((bf16[16,64,512]{2,1,0:T(8,128)(2,1)}), bf16[16,64,512]{2,1,0:T(8,128)(2,1)}, u32[]{:S(2)}, u32[]{:S(2)}) async-start(bf16[16,64,512]{2,1,0:T(8,128)(2,1)} %bitcast.254), calls=%async_computation.3 | async-start | bytes 2097152 | tf_op jit(solution)/shard_map/all_to_all | solution.py:133
  195.9 35.1 %copy-start.1 = (bf16[512,256]{1,0:T(8,128)(2,1)S(1)}, bf16[512,256]{1,0:T(8,128)(2,1)}, u32[]{:S(2)}) copy-start(bf16[512,256]{1,0:T(8,128)(2,1)} %gather_fusion) | copy-start | bytes 786436
  198.7 27.4 %collective-permute-start.2 = (bf16[3,1,128,256]{3,2,1,0:T(8,128)(2,1)S(1)}, bf16[3,1,128,256]{3,2,1,0:T(8,128)(2,1)S(1)}, u32[]{:S(2)}, u32[]{:S(2)}) collective-permute-start(bf16[3,1,128,256]{3,2,1,0:T(8,128)(2,1)S(1)} %get-tuple-element.67), channel_id=1, source_target_pairs={{0,1},{1,2},{2,3},{3,4},{4,5},{5,6},{6,7},{7,8},{8,9},{9,10},{10,1... | collective-permute-start | bytes 589832 | tf_op jit(solution)/shard_map/ppermute | solution.py:14
  203.9 27.1 %collective-permute-start.3 = (bf16[3,1,128,256]{3,2,1,0:T(8,128)(2,1)S(1)}, bf16[3,1,128,256]{3,2,1,0:T(8,128)(2,1)S(1)}, u32[]{:S(2)}, u32[]{:S(2)}) collective-permute-start(bf16[3,1,128,256]{3,2,1,0:T(8,128)(2,1)S(1)} %get-tuple-element.68), channel_id=1, source_target_pairs={{1,0},{2,1},{3,2},{4,3},{5,4},{6,5},{7,6},{8,7},{9,8},{10,9},{11,1... | collective-permute-start | bytes 589832 | tf_op jit(solution)/shard_map/ppermute | solution.py:15
  208.2 30.1 %collective-permute-start.9 = (bf16[2,2,128,512]{3,2,1,0:T(8,128)(2,1)S(1)}, bf16[2,2,128,512]{3,2,1,0:T(8,128)(2,1)S(1)}, u32[]{:S(2)}, u32[]{:S(2)}) collective-permute-start(bf16[2,2,128,512]{3,2,1,0:T(8,128)(2,1)S(1)} %fusion.42), channel_id=1, source_target_pairs={{0,32},{16,48},{32,0},{48,16},{64,96},{80,112},{96,64},{112,80},{1... | collective-permute-start | bytes 1572872 | tf_op jit(solution)/shard_map/ppermute | solution.py:40
  238.5 7.5 %collective-permute-start.10 = (bf16[2,128,512]{2,1,0:T(8,128)(2,1)S(1)}, bf16[2,128,512]{2,1,0:T(8,128)(2,1)S(1)}, u32[]{:S(2)}, u32[]{:S(2)}) collective-permute-start(bf16[2,128,512]{2,1,0:T(8,128)(2,1)S(1)} %fusion.46), channel_id=1, source_target_pairs={{0,128},{16,144},{32,160},{48,176},{64,192},{80,208},{96,224},{112... | collective-permute-start | bytes 786440 | tf_op jit(solution)/shard_map/ppermute | solution.py:40
  246.1 0.8 copy-start.3
  247.6 6.7 %collective-permute-start.11 = (bf16[128,512]{1,0:T(8,128)(2,1)}, bf16[128,512]{1,0:T(8,128)(2,1)}, u32[]{:S(2)}, u32[]{:S(2)}) collective-permute-start(bf16[128,512]{1,0:T(8,128)(2,1)} %fusion.51), channel_id=1, source_target_pairs={{0,64},{16,80},{32,96},{48,112},{64,0},{80,16},{96,32},{112,48},{1... | collective-permute-start | bytes 393224 | tf_op jit(solution)/shard_map/ppermute | solution.py:40

commit v2 on v1

v2 whole, which is shorter than its diff:
```python
import jax
import jax.numpy as jnp
from jax import lax
from jax.sharding import PartitionSpec as P


def extended(x, sides, width):
    for axis, dim in sides:
        size, length = (lax.axis_size(axis), x.shape[dim])
        up = [(i, (i + 1) % size) for i in range(size - 1)]
        down = [(j, i) for i, j in up]
        last = lax.slice_in_dim(x, length - width, length, axis=dim)
        first = lax.slice_in_dim(x, 0, width, axis=dim)
        before = lax.ppermute(last, axis, up)
        after = lax.ppermute(first, axis, down)
        x = jnp.concatenate([before, x, after], axis=dim)
    return x


def gelu_act(value):
    return jax.nn.gelu(value, approximate=True)


def gelu_back(preact, upstream):
    return jax.vjp(gelu_act, preact)[1](upstream)[0]


def tree_scatter(blocks, order):
    count = blocks.shape[0]
    me = lax.axis_index("dp")
    bits = count.bit_length() - 1
    x = blocks.reshape((2,) * bits + blocks.shape[1:])
    remaining = list(range(bits - 1, -1, -1))
    for bit in order:
        axis = remaining.index(bit)
        mine = (me >> bit) & 1
        keep = lax.dynamic_index_in_dim(x, mine, axis=axis, keepdims=False)
        send = lax.dynamic_index_in_dim(x, 1 - mine, axis=axis, keepdims=False)
        pairs = [(i, i ^ (1 << bit)) for i in range(count)]
        got = lax.ppermute(send.astype(jnp.bfloat16), "dp", pairs)
        x = keep + got.astype(jnp.float32)
        remaining.pop(axis)
    return x


def conv_block(grid, taps):
    padded = extended(grid, (("dp", 0), ("expert", 1)), 1)
    padded = jnp.pad(padded, ((0, 0), (0, 0), (1, 1), (0, 0)))
    out = lax.conv_general_dilated(
        padded[None],
        taps,
        (1, 1, 1),
        "VALID",
        dimension_numbers=("NDHWC", "DHWIO", "NDHWC"),
        preferred_element_type=jnp.float32,
    )
    return out[0].astype(jnp.bfloat16)


def per_device(feats, labels, w_first, w_second, kernel, cotangent):
    experts = lax.axis_size("expert")
    rows_y = feats.shape[1]
    depth_cells = feats.shape[2]
    feat_width = feats.shape[3]
    channels = kernel.shape[2]
    hidden = w_first.shape[2]
    patch_count = rows_y * depth_cells
    capacity = 2 * patch_count // experts
    slots = experts * capacity
    regime = labels.reshape(patch_count)
    onehot = (regime[:, None] == jnp.arange(experts, dtype=jnp.int32)[None, :]).astype(
        jnp.bfloat16
    )
    lower = (
        jnp.arange(patch_count)[:, None] >= jnp.arange(patch_count)[None, :]
    ).astype(jnp.bfloat16)
    ranking = jnp.dot(lower, onehot, preferred_element_type=jnp.float32)
    slot_index = jnp.sum(ranking * onehot.astype(jnp.float32), axis=1).astype(jnp.int32) - 1
    target = regime * capacity + slot_index
    route = (target[None, :] == jnp.arange(slots, dtype=jnp.int32)[:, None]).astype(jnp.bfloat16)
    flat_feats = feats.reshape(patch_count, feat_width)
    outbound = jnp.dot(route, flat_feats, preferred_element_type=jnp.float32).astype(jnp.bfloat16)
    outbound = outbound.reshape(experts, capacity, feat_width)
    received = lax.all_to_all(outbound, "expert", split_axis=0, concat_axis=0, tiled=True)

    taps = kernel.reshape(3, 3, 3, channels, channels)
    flipped = taps[::-1, ::-1, ::-1]
    field_grad = conv_block(cotangent, jnp.swapaxes(flipped, 3, 4))
    field_rows = field_grad.reshape(patch_count, channels)
    grad_outbound = jnp.dot(route, field_rows, preferred_element_type=jnp.float32).astype(
        jnp.bfloat16
    )
    grad_outbound = grad_outbound.reshape(experts, capacity, channels)
    grad_inbound = lax.all_to_all(grad_outbound, "expert", split_axis=0, concat_axis=0, tiled=True)

    weight_one = w_first[0]
    weight_two = w_second[0]
    row_block = received.reshape(slots, feat_width)
    preact = jnp.dot(row_block, weight_one, preferred_element_type=jnp.float32)
    activation = gelu_act(preact).astype(jnp.bfloat16)
    result = jnp.dot(activation, weight_two, preferred_element_type=jnp.float32).astype(
        jnp.bfloat16
    )
    returned = lax.all_to_all(
        result.reshape(experts, capacity, channels), "expert", split_axis=0, concat_axis=0, tiled=True
    )
    mixed_rows = lax.dot_general(
        route,
        returned.reshape(slots, channels),
        (((0,), (0,)), ((), ())),
        preferred_element_type=jnp.float32,
    ).astype(jnp.bfloat16)
    patch_grid = mixed_rows.reshape(1, rows_y, depth_cells, channels)
    imitated = conv_block(patch_grid, taps)

    grad_rows = grad_inbound.reshape(slots, channels)
    upstream = lax.dot_general(
        grad_rows, weight_two, (((1,), (1,)), ((), ())), preferred_element_type=jnp.float32
    )
    gate_grad = gelu_back(preact, upstream).astype(jnp.bfloat16)
    input_grad = lax.dot_general(
        gate_grad, weight_one, (((1,), (1,)), ((), ())), preferred_element_type=jnp.float32
    )
    input_grad = input_grad.astype(jnp.bfloat16).reshape(experts, capacity, feat_width)
    input_back = lax.all_to_all(input_grad, "expert", split_axis=0, concat_axis=0, tiled=True)
    feat_grad = lax.dot_general(
        route,
        input_back.reshape(slots, feat_width),
        (((0,), (0,)), ((), ())),
        preferred_element_type=jnp.float32,
    ).astype(jnp.bfloat16)
    feat_grad = feat_grad.reshape(1, rows_y, depth_cells, feat_width)

    slabs = lax.axis_size("dp")
    part_one = lax.dot_general(
        gate_grad, row_block, (((0,), (0,)), ((), ())), preferred_element_type=jnp.float32
    )
    part_two = lax.dot_general(
        activation, grad_rows, (((0,), (0,)), ((), ())), preferred_element_type=jnp.float32
    )
    grad_one = tree_scatter(part_one.reshape(slabs, hidden // slabs, feat_width), (0, 1, 3, 2))
    grad_one = grad_one.T
    grad_two = tree_scatter(part_two.reshape(slabs, hidden // slabs, channels), (0, 3, 1, 2))
    return (imitated, feat_grad, grad_one[None], grad_two[None])


def solution(mesh):
    in_specs = (
        P("dp", "expert", None, None),
        P("dp", "expert", None, None),
        P("expert", None, None),
        P("expert", None, None),
        P(),
        P("dp", "expert", None, None),
    )
    out_specs = (
        P("dp", "expert", None, None),
        P("dp", "expert", None, None),
        P("expert", None, "dp"),
        P("expert", "dp", None),
    )
    return jax.shard_map(
        per_device, mesh=mesh, in_specs=in_specs, out_specs=out_specs, check_vma=False
    )
```

time: 263 us -> 253 us (0.962)
  other arithmetic: 19.1 us -> 10.3 us
  local copies, waits for them, and re-layouts: 46.3 us -> 38.2 us
  matrix products: 50.1 us -> 57 us
    ppermute x4, waiting for transfers between devices: 13 us -> 35.8 us  [extended(): after = lax.ppermute(first, axis, down)]
    ppermute x4, waiting for transfers between devices: 21.1 us -> 4.48 us  [extended(): before = lax.ppermute(last, axis, up)]
    conv_general_dilated x0 -> x6, local copies, waits for them, and re-layouts: none -> 10.3 us  [conv_block(): lax.conv_general_dilated(padded[None], taps, (1, 1, 1), 'VALID', dimensio...]
    scatter x2 -> x0, local copies, waits for them, and re-layouts: 7.56 us -> none  [the longest x1 4.03 us: per_device(): jnp.zeros((experts * capacity, feat_width), jnp.bfloat16).at[target]]
    gather x2 -> x0, local copies, waits for them, and re-layouts: 7.31 us -> none  [the longest x1 4.01 us: per_device(): input_back.reshape(experts * capacity, feat_width)[target]]
    ppermute x8, waiting for transfers between devices: 14.2 us -> 7.88 us  [tree_scatter(): got = lax.ppermute(send.astype(jnp.bfloat16), 'dp', pairs)]
    concatenate x5 -> x0, other arithmetic: 4.51 us -> none  [extended(): x = jnp.concatenate([before, x, after], axis=dim)]
    dot_general x4 -> x7, matrix products: 13.9 us -> 18.3 us  [the longest x1 4.97 us: per_device(): lax.dot_general(gate_grad, row_block, (((0,), (0,)), ((), ())), preferred...]
  transfers between devices with their start and end apart: 20 -> 20, of which waited for: 9 -> 12; matrix products, arithmetic and copies ran while one was open for 29% -> 25% of each run, Pallas kernels for 0% -> 0%
where the time goes in v2:
time: 253 us; the launch traced here: 248 us
  starting transfers between devices  74.3 us (29%)
  waiting for transfers between devices  67.1 us (27%)
  matrix products  57 us (23%)
  local copies, waits for them, and re-layouts  38.2 us (15%)
  other arithmetic  10.3 us (4%)
    ppermute x4, waiting for transfers between devices, extended(): after = lax.ppermute(first, axis, down)  35.8 us
    ppermute x4, starting transfers between devices, extended(): before = lax.ppermute(last, axis, up)  23.1 us
    dot_general x1, matrix products, per_device(): preact = jnp.dot(row_block, weight_one, preferred_element_type=jnp.float32)  13.3 us
    ppermute x8, starting transfers between devices, tree_scatter(): got = lax.ppermute(send.astype(jnp.bfloat16), 'dp', pairs)  11 us
    all_to_all x1, waiting for transfers between devices, per_device(): lax.all_to_all(outbound, 'expert', split_axis=0, concat_axis=0, tiled=True)  10.8 us
    conv_general_dilated x6, local copies, waits for them, and re-layouts, conv_block(): lax.conv_general_dilated(padded[None], taps, (1, 1, 1), 'VALID', dimensio...  10.3 us
    ppermute x4, starting transfers between devices, extended(): after = lax.ppermute(first, axis, down)  9.52 us
    all_to_all x1, starting transfers between devices, per_device(): lax.all_to_all(result.reshape(experts, capacity, channels), 'expert', spl...  9.46 us
  transfers between devices with their start and end apart: 20, of which 12 were waited for; matrix products, arithmetic and copies ran while one was open for 25% of the time, Pallas kernels for 0%

profile of v2, /device:TPU:95, one launch (start us, length us, event | category | flops | bytes accessed | tf_op | source)
XLA Modules:
  0.0 248.0 jit_solution(17613640505664253628)
XLA Ops:
  0.6 4.0 %collective-permute-start.4 = (bf16[1,4,128,256]{3,2,1,0:T(8,128)(2,1)}, bf16[1,4,128,256]{3,2,1,0:T(8,128)(2,1)S(1)}, u32[]{:S(2)}, u32[]{:S(2)}) collective-permute-start(bf16[1,4,128,256]{3,2,1,0:T(8,128)(2,1)} %param.11), channel_id=1, source_target_pairs={{0,16},{16,32},{32,48},{48,64},{64,80},{80,96},{96,112},{112,128},... | collective-permute-start | bytes 786440 | tf_op jit(solution)/shard_map/ppermute | solution.py:14
  9.3 5.4 %collective-permute-done.5 = bf16[1,4,128,256]{3,2,1,0:T(8,128)(2,1)S(1)} collective-permute-done((bf16[1,4,128,256]{3,2,1,0:T(8,128)(2,1)}, bf16[1,4,128,256]{3,2,1,0:T(8,128)(2,1)S(1)}, u32[]{:S(2)}, u32[]{:S(2)}) %collective-permute-start.5) | collective-permute-done | bytes 262176 | tf_op jit(solution)/shard_map/ppermute | solution.py:15
  14.8 5.1 %collective-permute-start.6 = (bf16[3,1,128,256]{3,2,1,0:T(8,128)(2,1)S(1)}, bf16[3,1,128,256]{3,2,1,0:T(8,128)(2,1)S(1)}, u32[]{:S(2)}, u32[]{:S(2)}) collective-permute-start(bf16[3,1,128,256]{3,2,1,0:T(8,128)(2,1)S(1)} %get-tuple-element.18), channel_id=1, source_target_pairs={{0,1},{1,2},{2,3},{3,4},{4,5},{5,6},{6,7},{7,8},{8,9},{9,10},{10,1... | collective-permute-start | bytes 589832 | tf_op jit(solution)/shard_map/ppermute | solution.py:14
  24.6 8.3 %collective-permute-done.7 = bf16[3,1,128,256]{3,2,1,0:T(8,128)(2,1)S(1)} collective-permute-done((bf16[3,1,128,256]{3,2,1,0:T(8,128)(2,1)S(1)}, bf16[3,1,128,256]{3,2,1,0:T(8,128)(2,1)S(1)}, u32[]{:S(2)}, u32[]{:S(2)}) %collective-permute-start.7) | collective-permute-done | bytes 196640 | tf_op jit(solution)/shard_map/ppermute | solution.py:15
  34.6 3.3 %reshape.109 = bf16[3,6,1,8,17,256]{5,4,3,1,0,2:T(8,128)(2,1)} reshape(bf16[3,6,1,136,256]{4,3,1,0,2:T(8,128)(2,1)} %pad.11) | data formatting | bytes 2506752 | tf_op jit(solution)/shard_map/conv_general_dilated | solution.py:49
  43.4 5.8 %all-to-all-start.2 = ((bf16[16,64,256]{2,1,0:T(8,128)(2,1)}), bf16[16,64,256]{2,1,0:T(8,128)(2,1)}, u32[]{:S(2)}, u32[]{:S(2)}) async-start(bf16[16,64,256]{2,1,0:T(8,128)(2,1)} %bitcast.163), calls=%async_computation.2 | async-start | bytes 1048576 | tf_op jit(solution)/shard_map/all_to_all | solution.py:94
  49.2 2.8 %fusion.36 = bf16[1024,512]{1,0:T(8,128)(2,1)} fusion(bf16[512,512]{1,0:T(8,128)(2,1)} %bitcast.167, s32[512]{0:T(512)S(1)} %add_add_fusion), kind=kOutput, calls=%fused_computation.45 | convolution fusion | flops 537919488 | bytes 1574912 | tf_op jit(solution)/shard_map/dot_general | solution.py:82
  52.0 8.1 %all-to-all-done.2 = bf16[16,64,256]{2,1,0:T(8,128)(2,1)} async-done(((bf16[16,64,256]{2,1,0:T(8,128)(2,1)}), bf16[16,64,256]{2,1,0:T(8,128)(2,1)}, u32[]{:S(2)}, u32[]{:S(2)}) %all-to-all-start.2) | async-done | bytes 524320 | tf_op jit(solution)/shard_map/all_to_all | solution.py:94
  60.1 9.4 %all-to-all-start = ((bf16[16,64,512]{2,1,0:T(8,128)(2,1)}), bf16[16,64,512]{2,1,0:T(8,128)(2,1)}, u32[]{:S(2)}, u32[]{:S(2)}) async-start(bf16[16,64,512]{2,1,0:T(8,128)(2,1)} %bitcast.157), calls=%async_computation | async-start | bytes 2097152 | tf_op jit(solution)/shard_map/all_to_all | solution.py:84
  69.5 6.0 %fusion.76 = f32[1024,2048]{1,0:T(8,128)} fusion(bf16[1024,256]{1,0:T(8,128)(2,1)} %bitcast.19, bf16[1,2048,256]{2,1,0:T(8,128)(2,1)} %param.9), kind=kOutput, calls=%fused_computation.82 | convolution fusion | flops 1073741824 | bytes 9961472 | tf_op jit(solution)/shard_map/dot_general | solution.py:117
  75.5 10.8 %all-to-all-done = bf16[16,64,512]{2,1,0:T(8,128)(2,1)} async-done(((bf16[16,64,512]{2,1,0:T(8,128)(2,1)}), bf16[16,64,512]{2,1,0:T(8,128)(2,1)}, u32[]{:S(2)}, u32[]{:S(2)}) %all-to-all-start) | async-done | bytes 1048608 | tf_op jit(solution)/shard_map/all_to_all | solution.py:84
  86.3 13.3 %fusion.14 = (bf16[2048,1024]{0,1:T(8,128)(2,1)}, bf16[2048,1024]{0,1:T(8,128)(2,1)}, f32[1024,2048]{1,0:T(8,128)}) fusion(f32[1024,2048]{1,0:T(8,128)} %fusion.76, bf16[1024,512]{1,0:T(8,128)(2,1)} %bitcast.3, bf16[1,512,2048]{2,1,0:T(8,128)(2,1)} %param.8), kind=kOutput, calls=%fused_computation.20 | convolution fusion | flops 2193620992 | bytes 28311552 | tf_op jit(solution)/shard_map/dot_general | solution.py:99
  99.6 6.4 %copy.37 = bf16[2048,1024]{1,0:T(8,128)(2,1)} copy(bf16[2048,1024]{0,1:T(8,128)(2,1)} %get-tuple-element.16) | data formatting | bytes 8388608 | tf_op jit(solution)/shard_map/dot_general | solution.py:138
  106.0 3.7 %fusion.114 = f32[2,2,2,2,128,256]{5,4,3,2,1,0:T(8,128)S(1)} fusion(bf16[2,2,2,2,128,1024]{5,4,3,2,1,0:T(8,128)(2,1)} %bitcast.153, bf16[1024,256,1,1,1,1]{1,0,5,4,3,2:T(8,128)(2,1)} %bitcast.40), kind=kOutput, calls=%fused_computation.142 | convolution fusion | flops 1073741824 | bytes 6815744 | tf_op jit(solution)/shard_map/dot_general | solution.py:138
  111.9 4.5 %collective-permute-start.12 = (bf16[2,2,2,128,256]{4,3,2,1,0:T(8,128)(2,1)}, bf16[2,2,2,128,256]{4,3,2,1,0:T(8,128)(2,1)}, u32[]{:S(2)}, u32[]{:S(2)}) collective-permute-start(bf16[2,2,2,128,256]{4,3,2,1,0:T(8,128)(2,1)} %fusion.86), channel_id=1, source_target_pairs={{0,16},{16,0},{32,48},{48,32},{64,80},{80,64},{96,112},{112,96},{1... | collective-permute-start | bytes 1572872 | tf_op jit(solution)/shard_map/ppermute | solution.py:40
  116.5 6.0 %fusion.52 = bf16[1024,256]{1,0:T(8,128)(2,1)} fusion(f32[1024,2048]{1,0:T(8,128)} %get-tuple-element.22, bf16[1,2048,256]{2,1,0:T(8,128)(2,1)S(1)} %copy-done.7), kind=kOutput, calls=%fused_computation.59 | convolution fusion | flops 1092878336 | bytes 9961472 | tf_op jit(solution)/shard_map/dot_general | solution.py:101
  122.5 9.5 %all-to-all-start.1 = ((bf16[16,64,256]{2,1,0:T(8,128)(2,1)}), bf16[16,64,256]{2,1,0:T(8,128)(2,1)}, u32[]{:S(2)}, u32[]{:S(2)}) async-start(bf16[16,64,256]{2,1,0:T(8,128)(2,1)} %bitcast.162), calls=%async_computation.1 | async-start | bytes 1048576 | tf_op jit(solution)/shard_map/all_to_all | solution.py:104
  131.9 6.5 %copy.36 = bf16[2048,1024]{1,0:T(8,128)(2,1)} copy(bf16[2048,1024]{0,1:T(8,128)(2,1)} %get-tuple-element.17) | data formatting | bytes 8388608 | tf_op jit(solution)/shard_map/dot_general | solution.py:135
  142.2 5.0 %fusion.113 = f32[2,2,2,2,128,512]{5,4,3,2,1,0:T(8,128)S(1)} fusion(bf16[2,2,2,2,128,1024]{5,4,3,2,1,0:T(8,128)(2,1)} %bitcast.152, bf16[1024,512,1,1,1,1]{1,0,5,4,3,2:T(8,128)(2,1)} %bitcast.27), kind=kOutput, calls=%fused_computation.141 | convolution fusion | flops 2147483648 | bytes 9437184 | tf_op jit(solution)/shard_map/dot_general | solution.py:135
  148.9 3.0 %collective-permute-done.13 = bf16[2,2,128,256]{3,2,1,0:T(8,128)(2,1)S(1)} collective-permute-done((bf16[2,2,128,256]{3,2,1,0:T(8,128)(2,1)S(1)}, bf16[2,2,128,256]{3,2,1,0:T(8,128)(2,1)S(1)}, u32[]{:S(2)}, u32[]{:S(2)}) %collective-permute-start.13) | collective-permute-done | bytes 262176 | tf_op jit(solution)/shard_map/ppermute | solution.py:40
  152.0 3.7 %collective-permute-start.14 = (bf16[2,128,256]{2,1,0:T(8,128)(2,1)S(1)}, bf16[2,128,256]{2,1,0:T(8,128)(2,1)S(1)}, u32[]{:S(2)}, u32[]{:S(2)}) collective-permute-start(bf16[2,128,256]{2,1,0:T(8,128)(2,1)S(1)} %fusion.91), channel_id=1, source_target_pairs={{0,32},{16,48},{32,0},{48,16},{64,96},{80,112},{96,64},{112,80},{1... | collective-permute-start | bytes 393224 | tf_op jit(solution)/shard_map/ppermute | solution.py:40
  155.7 9.1 %fusion.31 = bf16[1024,512]{1,0:T(8,128)(2,1)} fusion(bf16[1,512,2048]{2,1,0:T(8,128)(2,1)S(1)} %copy-done.10, f32[1024,2048]{1,0:T(8,128)} %get-tuple-element.22, f32[1024,2048]{1,0:T(8,128)S(1)} %bitcast.151), kind=kOutput, calls=%fused_computation.44 | convolution fusion | flops 2189950976 | bytes 19922944 | tf_op jit(solution)/shard_map/dot_general | solution.py:121
  166.2 6.1 %all-to-all-start.3 = ((bf16[16,64,512]{2,1,0:T(8,128)(2,1)}), bf16[16,64,512]{2,1,0:T(8,128)(2,1)}, u32[]{:S(2)}, u32[]{:S(2)}) async-start(bf16[16,64,512]{2,1,0:T(8,128)(2,1)} %bitcast.156), calls=%async_computation.3 | async-start | bytes 2097152 | tf_op jit(solution)/shard_map/all_to_all | solution.py:125
  174.1 3.8 %collective-permute-start.1 = (bf16[1,4,128,256]{3,2,1,0:T(8,128)(2,1)S(1)}, bf16[1,4,128,256]{3,2,1,0:T(8,128)(2,1)S(1)}, u32[]{:S(2)}, u32[]{:S(2)}) collective-permute-start(bf16[1,4,128,256]{3,2,1,0:T(8,128)(2,1)S(1)} %bitcast.158), channel_id=1, source_target_pairs={{16,0},{32,16},{48,32},{64,48},{80,64},{96,80},{112,96},{128,112},... | collective-permute-start | bytes 786440 | tf_op jit(solution)/shard_map/ppermute | solution.py:15
  177.9 5.4 %collective-permute-start = (bf16[1,4,128,256]{3,2,1,0:T(8,128)(2,1)S(1)}, bf16[1,4,128,256]{3,2,1,0:T(8,128)(2,1)S(1)}, u32[]{:S(2)}, u32[]{:S(2)}) collective-permute-start(bf16[1,4,128,256]{3,2,1,0:T(8,128)(2,1)S(1)} %bitcast.159), channel_id=1, source_target_pairs={{0,16},{16,32},{32,48},{48,64},{64,80},{80,96},{96,112},{112,128},... | collective-permute-start | bytes 786440 | tf_op jit(solution)/shard_map/ppermute | solution.py:14
  183.4 2.2 bitcast_add_fusion
  187.8 14.9 %collective-permute-done.1 = bf16[1,4,128,256]{3,2,1,0:T(8,128)(2,1)S(1)} collective-permute-done((bf16[1,4,128,256]{3,2,1,0:T(8,128)(2,1)S(1)}, bf16[1,4,128,256]{3,2,1,0:T(8,128)(2,1)S(1)}, u32[]{:S(2)}, u32[]{:S(2)}) %collective-permute-start.1) | collective-permute-done | bytes 262176 | tf_op jit(solution)/shard_map/ppermute | solution.py:15
  204.5 8.5 %collective-permute-start.2 = (bf16[3,1,128,256]{3,2,1,0:T(8,128)(2,1)S(1)}, bf16[3,1,128,256]{3,2,1,0:T(8,128)(2,1)S(1)}, u32[]{:S(2)}, u32[]{:S(2)}) collective-permute-start(bf16[3,1,128,256]{3,2,1,0:T(8,128)(2,1)S(1)} %get-tuple-element.20), channel_id=1, source_target_pairs={{0,1},{1,2},{2,3},{3,4},{4,5},{5,6},{6,7},{7,8},{8,9},{9,10},{10,1... | collective-permute-start | bytes 589832 | tf_op jit(solution)/shard_map/ppermute | solution.py:14
  216.5 7.2 %collective-permute-done.3 = bf16[3,1,128,256]{3,2,1,0:T(8,128)(2,1)S(1)} collective-permute-done((bf16[3,1,128,256]{3,2,1,0:T(8,128)(2,1)S(1)}, bf16[3,1,128,256]{3,2,1,0:T(8,128)(2,1)S(1)}, u32[]{:S(2)}, u32[]{:S(2)}) %collective-permute-start.3) | collective-permute-done | bytes 196640 | tf_op jit(solution)/shard_map/ppermute | solution.py:15
  225.4 3.3 %reshape.102 = bf16[3,6,1,8,17,256]{5,4,3,1,0,2:T(8,128)(2,1)} reshape(bf16[3,6,1,136,256]{4,3,1,0,2:T(8,128)(2,1)} %pad.9) | data formatting | bytes 2506752 | tf_op jit(solution)/shard_map/conv_general_dilated | solution.py:49
  238.9 2.8 %fusion.51 = bf16[512,512]{1,0:T(8,128)(2,1)} fusion(bf16[1024,512]{1,0:T(8,128)(2,1)} %bitcast.21, s32[512]{0:T(512)S(1)} %add_add_fusion), kind=kOutput, calls=%fused_computation.58 | convolution fusion | flops 537657344 | bytes 1574912 | tf_op jit(solution)/shard_map/dot_general | solution.py:126
  241.8 2.8 %collective-permute-done.11 = bf16[128,512]{1,0:T(8,128)(2,1)} collective-permute-done((bf16[128,512]{1,0:T(8,128)(2,1)}, bf16[128,512]{1,0:T(8,128)(2,1)}, u32[]{:S(2)}, u32[]{:S(2)}) %collective-permute-start.11) | collective-permute-done | bytes 131104 | tf_op jit(solution)/shard_map/ppermute | solution.py:40
  (91 shorter events, 50.4 us)
Async XLA Ops:
  0.6 39.1 %copy-start = (bf16[27,256,256]{2,1,0:T(8,128)(2,1)S(1)}, bf16[27,256,256]{2,1,0:T(8,128)(2,1)}, u32[]{:S(2)}) copy-start(bf16[27,256,256]{2,1,0:T(8,128)(2,1)} %param.10) | copy-start | bytes 10616836
  0.6 7.6 %collective-permute-start.4 = (bf16[1,4,128,256]{3,2,1,0:T(8,128)(2,1)}, bf16[1,4,128,256]{3,2,1,0:T(8,128)(2,1)S(1)}, u32[]{:S(2)}, u32[]{:S(2)}) collective-permute-start(bf16[1,4,128,256]{3,2,1,0:T(8,128)(2,1)} %param.11), channel_id=1, source_target_pairs={{0,16},{16,32},{32,48},{48,64},{64,80},{80,96},{96,112},{112,128},... | collective-permute-start | bytes 786440 | tf_op jit(solution)/shard_map/ppermute | solution.py:14
  4.7 10.0 %collective-permute-start.5 = (bf16[1,4,128,256]{3,2,1,0:T(8,128)(2,1)}, bf16[1,4,128,256]{3,2,1,0:T(8,128)(2,1)S(1)}, u32[]{:S(2)}, u32[]{:S(2)}) collective-permute-start(bf16[1,4,128,256]{3,2,1,0:T(8,128)(2,1)} %param.11), channel_id=1, source_target_pairs={{16,0},{32,16},{48,32},{64,48},{80,64},{96,80},{112,96},{128,112},... | collective-permute-start | bytes 786440 | tf_op jit(solution)/shard_map/ppermute | solution.py:15
  14.8 9.9 %collective-permute-start.6 = (bf16[3,1,128,256]{3,2,1,0:T(8,128)(2,1)S(1)}, bf16[3,1,128,256]{3,2,1,0:T(8,128)(2,1)S(1)}, u32[]{:S(2)}, u32[]{:S(2)}) collective-permute-start(bf16[3,1,128,256]{3,2,1,0:T(8,128)(2,1)S(1)} %get-tuple-element.18), channel_id=1, source_target_pairs={{0,1},{1,2},{2,3},{3,4},{4,5},{5,6},{6,7},{7,8},{8,9},{9,10},{10,1... | collective-permute-start | bytes 589832 | tf_op jit(solution)/shard_map/ppermute | solution.py:14
  19.9 13.0 %collective-permute-start.7 = (bf16[3,1,128,256]{3,2,1,0:T(8,128)(2,1)S(1)}, bf16[3,1,128,256]{3,2,1,0:T(8,128)(2,1)S(1)}, u32[]{:S(2)}, u32[]{:S(2)}) collective-permute-start(bf16[3,1,128,256]{3,2,1,0:T(8,128)(2,1)S(1)} %get-tuple-element.19), channel_id=1, source_target_pairs={{1,0},{2,1},{3,2},{4,3},{5,4},{6,5},{7,6},{8,7},{9,8},{10,9},{11,1... | collective-permute-start | bytes 589832 | tf_op jit(solution)/shard_map/ppermute | solution.py:15
  34.6 5.1 %copy-start.11 = (pred[8,17]{0,1:T(8,128)(4,1)S(1)}, pred[8,17]{0,1:T(8,128)(4,1)}, u32[]{:S(2)}) copy-start(pred[8,17]{0,1:T(8,128)(4,1)} %constant.103) | copy-start | bytes 412
  43.4 16.6 %all-to-all-start.2 = ((bf16[16,64,256]{2,1,0:T(8,128)(2,1)}), bf16[16,64,256]{2,1,0:T(8,128)(2,1)}, u32[]{:S(2)}, u32[]{:S(2)}) async-start(bf16[16,64,256]{2,1,0:T(8,128)(2,1)} %bitcast.163), calls=%async_computation.2 | async-start | bytes 1048576 | tf_op jit(solution)/shard_map/all_to_all | solution.py:94
  60.1 26.2 %all-to-all-start = ((bf16[16,64,512]{2,1,0:T(8,128)(2,1)}), bf16[16,64,512]{2,1,0:T(8,128)(2,1)}, u32[]{:S(2)}, u32[]{:S(2)}) async-start(bf16[16,64,512]{2,1,0:T(8,128)(2,1)} %bitcast.157), calls=%async_computation | async-start | bytes 2097152 | tf_op jit(solution)/shard_map/all_to_all | solution.py:84
  106.0 10.5 %copy-start.7 = (bf16[1,2048,256]{2,1,0:T(8,128)(2,1)S(1)}, bf16[1,2048,256]{2,1,0:T(8,128)(2,1)}, u32[]{:S(2)}) copy-start(bf16[1,2048,256]{2,1,0:T(8,128)(2,1)} %param.9) | copy-start | bytes 3145732
  109.7 1.4 copy-start.6
  111.9 26.5 %collective-permute-start.12 = (bf16[2,2,2,128,256]{4,3,2,1,0:T(8,128)(2,1)}, bf16[2,2,2,128,256]{4,3,2,1,0:T(8,128)(2,1)}, u32[]{:S(2)}, u32[]{:S(2)}) collective-permute-start(bf16[2,2,2,128,256]{4,3,2,1,0:T(8,128)(2,1)} %fusion.86), channel_id=1, source_target_pairs={{0,16},{16,0},{32,48},{48,32},{64,80},{80,64},{96,112},{112,96},{1... | collective-permute-start | bytes 1572872 | tf_op jit(solution)/shard_map/ppermute | solution.py:40
  122.5 43.8 %all-to-all-start.1 = ((bf16[16,64,256]{2,1,0:T(8,128)(2,1)}), bf16[16,64,256]{2,1,0:T(8,128)(2,1)}, u32[]{:S(2)}, u32[]{:S(2)}) async-start(bf16[16,64,256]{2,1,0:T(8,128)(2,1)} %bitcast.162), calls=%async_computation.1 | async-start | bytes 1048576 | tf_op jit(solution)/shard_map/all_to_all | solution.py:104
  138.4 17.3 %slice-start = ((s8[8388608]{0:T(1024)(128)(4,1)}), s8[4194304]{0:T(1024)(128)(4,1)S(1)}, s32[]{:S(2)}) async-start(s8[8388608]{0:T(1024)(128)(4,1)} %bitcast.150), calls=%async_computation.4 | async-start | bytes 8388608
  140.1 11.8 %collective-permute-start.13 = (bf16[2,2,128,256]{3,2,1,0:T(8,128)(2,1)S(1)}, bf16[2,2,128,256]{3,2,1,0:T(8,128)(2,1)S(1)}, u32[]{:S(2)}, u32[]{:S(2)}) collective-permute-start(bf16[2,2,128,256]{3,2,1,0:T(8,128)(2,1)S(1)} %fusion.88), channel_id=1, source_target_pairs={{0,128},{16,144},{32,160},{48,176},{64,192},{80,208},{96,224},{112... | collective-permute-start | bytes 786440 | tf_op jit(solution)/shard_map/ppermute | solution.py:40
  142.2 13.5 %slice-start.1 = ((s8[8388608]{0:T(1024)(128)(4,1)}), s8[4194304]{0:T(1024)(128)(4,1)S(1)}, s32[]{:S(2)}) async-start(s8[8388608]{0:T(1024)(128)(4,1)} %bitcast.150), calls=%async_computation.5 | async-start | bytes 8388608
  147.2 4.7 %copy-start.3 = (f32[2,2,2,2,128,512]{5,4,3,2,1,0:T(8,128)}, f32[2,2,2,2,128,512]{5,4,3,2,1,0:T(8,128)S(1)}, u32[]{:S(2)}) copy-start(f32[2,2,2,2,128,512]{5,4,3,2,1,0:T(8,128)S(1)} %fusion.113) | copy-start | bytes 12582916
  147.2 8.5 %copy-start.10 = (bf16[1,512,2048]{2,1,0:T(8,128)(2,1)S(1)}, bf16[1,512,2048]{2,1,0:T(8,128)(2,1)}, u32[]{:S(2)}) copy-start(bf16[1,512,2048]{2,1,0:T(8,128)(2,1)} %param.8) | copy-start | bytes 6291460
  148.4 35.0 %collective-permute-start.8 = (bf16[2,2,2,128,512]{4,3,2,1,0:T(8,128)(2,1)}, bf16[2,2,2,128,512]{4,3,2,1,0:T(8,128)(2,1)}, u32[]{:S(2)}, u32[]{:S(2)}) collective-permute-start(bf16[2,2,2,128,512]{4,3,2,1,0:T(8,128)(2,1)} %fusion.75), channel_id=1, source_target_pairs={{0,16},{16,0},{32,48},{48,32},{64,80},{80,64},{96,112},{112,96},{1... | collective-permute-start | bytes 3145736 | tf_op jit(solution)/shard_map/ppermute | solution.py:40
  152.0 12.9 %collective-permute-start.14 = (bf16[2,128,256]{2,1,0:T(8,128)(2,1)S(1)}, bf16[2,128,256]{2,1,0:T(8,128)(2,1)S(1)}, u32[]{:S(2)}, u32[]{:S(2)}) collective-permute-start(bf16[2,128,256]{2,1,0:T(8,128)(2,1)S(1)} %fusion.91), channel_id=1, source_target_pairs={{0,32},{16,48},{32,0},{48,16},{64,96},{80,112},{96,64},{112,80},{1... | collective-permute-start | bytes 393224 | tf_op jit(solution)/shard_map/ppermute | solution.py:40
  166.2 48.7 %collective-permute-start.15 = (bf16[128,256]{1,0:T(8,128)(2,1)}, bf16[128,256]{1,0:T(8,128)(2,1)}, u32[]{:S(2)}, u32[]{:S(2)}) collective-permute-start(bf16[128,256]{1,0:T(8,128)(2,1)} %fusion.93), channel_id=1, source_target_pairs={{0,64},{16,80},{32,96},{48,112},{64,0},{80,16},{96,32},{112,48},{1... | collective-permute-start | bytes 196616 | tf_op jit(solution)/shard_map/ppermute | solution.py:40
  166.2 72.7 %all-to-all-start.3 = ((bf16[16,64,512]{2,1,0:T(8,128)(2,1)}), bf16[16,64,512]{2,1,0:T(8,128)(2,1)}, u32[]{:S(2)}, u32[]{:S(2)}) async-start(bf16[16,64,512]{2,1,0:T(8,128)(2,1)} %bitcast.156), calls=%async_computation.3 | async-start | bytes 2097152 | tf_op jit(solution)/shard_map/all_to_all | solution.py:125
  174.1 40.8 %copy-start.9 = (f32[2,128,256]{2,1,0:T(8,128)S(1)}, f32[2,128,256]{2,1,0:T(8,128)}, u32[]{:S(2)}) copy-start(f32[2,128,256]{2,1,0:T(8,128)} %copy-done.8) | copy-start | bytes 786436
  174.1 28.6 %collective-permute-start.1 = (bf16[1,4,128,256]{3,2,1,0:T(8,128)(2,1)S(1)}, bf16[1,4,128,256]{3,2,1,0:T(8,128)(2,1)S(1)}, u32[]{:S(2)}, u32[]{:S(2)}) collective-permute-start(bf16[1,4,128,256]{3,2,1,0:T(8,128)(2,1)S(1)} %bitcast.158), channel_id=1, source_target_pairs={{16,0},{32,16},{48,32},{64,48},{80,64},{96,80},{112,96},{128,112},... | collective-permute-start | bytes 786440 | tf_op jit(solution)/shard_map/ppermute | solution.py:15
  177.9 26.5 %collective-permute-start = (bf16[1,4,128,256]{3,2,1,0:T(8,128)(2,1)S(1)}, bf16[1,4,128,256]{3,2,1,0:T(8,128)(2,1)S(1)}, u32[]{:S(2)}, u32[]{:S(2)}) collective-permute-start(bf16[1,4,128,256]{3,2,1,0:T(8,128)(2,1)S(1)} %bitcast.159), channel_id=1, source_target_pairs={{0,16},{16,32},{32,48},{48,64},{64,80},{80,96},{96,112},{112,128},... | collective-permute-start | bytes 786440 | tf_op jit(solution)/shard_map/ppermute | solution.py:14
  185.6 1.4 copy-start.1
  187.8 42.8 %collective-permute-start.9 = (bf16[2,2,128,512]{3,2,1,0:T(8,128)(2,1)}, bf16[2,2,128,512]{3,2,1,0:T(8,128)(2,1)}, u32[]{:S(2)}, u32[]{:S(2)}) collective-permute-start(bf16[2,2,128,512]{3,2,1,0:T(8,128)(2,1)} %fusion.85), channel_id=1, source_target_pairs={{0,32},{16,48},{32,0},{48,16},{64,96},{80,112},{96,64},{112,80},{1... | collective-permute-start | bytes 1572872 | tf_op jit(solution)/shard_map/ppermute | solution.py:40
  204.5 12.0 %collective-permute-start.2 = (bf16[3,1,128,256]{3,2,1,0:T(8,128)(2,1)S(1)}, bf16[3,1,128,256]{3,2,1,0:T(8,128)(2,1)S(1)}, u32[]{:S(2)}, u32[]{:S(2)}) collective-permute-start(bf16[3,1,128,256]{3,2,1,0:T(8,128)(2,1)S(1)} %get-tuple-element.20), channel_id=1, source_target_pairs={{0,1},{1,2},{2,3},{3,4},{4,5},{5,6},{6,7},{7,8},{8,9},{9,10},{10,1... | collective-permute-start | bytes 589832 | tf_op jit(solution)/shard_map/ppermute | solution.py:14
  213.0 10.6 %collective-permute-start.3 = (bf16[3,1,128,256]{3,2,1,0:T(8,128)(2,1)S(1)}, bf16[3,1,128,256]{3,2,1,0:T(8,128)(2,1)S(1)}, u32[]{:S(2)}, u32[]{:S(2)}) collective-permute-start(bf16[3,1,128,256]{3,2,1,0:T(8,128)(2,1)S(1)} %get-tuple-element.21), channel_id=1, source_target_pairs={{1,0},{2,1},{3,2},{4,3},{5,4},{6,5},{7,6},{8,7},{9,8},{10,9},{11,1... | collective-permute-start | bytes 589832 | tf_op jit(solution)/shard_map/ppermute | solution.py:15
  228.6 2.1 copy-start.2
  232.1 5.3 %collective-permute-start.10 = (bf16[2,128,512]{2,1,0:T(8,128)(2,1)S(1)}, bf16[2,128,512]{2,1,0:T(8,128)(2,1)S(1)}, u32[]{:S(2)}, u32[]{:S(2)}) collective-permute-start(bf16[2,128,512]{2,1,0:T(8,128)(2,1)S(1)} %fusion.87), channel_id=1, source_target_pairs={{0,128},{16,144},{32,160},{48,176},{64,192},{80,208},{96,224},{112... | collective-permute-start | bytes 786440 | tf_op jit(solution)/shard_map/ppermute | solution.py:40
  238.9 5.6 %collective-permute-start.11 = (bf16[128,512]{1,0:T(8,128)(2,1)}, bf16[128,512]{1,0:T(8,128)(2,1)}, u32[]{:S(2)}, u32[]{:S(2)}) collective-permute-start(bf16[128,512]{1,0:T(8,128)(2,1)} %fusion.90), channel_id=1, source_target_pairs={{0,64},{16,80},{32,96},{48,112},{64,0},{80,16},{96,32},{112,48},{1... | collective-permute-start | bytes 393224 | tf_op jit(solution)/shard_map/ppermute | solution.py:40
  238.9 5.6 %copy-start.5 = (f32[2,128,512]{2,1,0:T(8,128)S(1)}, f32[2,128,512]{2,1,0:T(8,128)}, u32[]{:S(2)}) copy-start(f32[2,128,512]{2,1,0:T(8,128)} %copy-done.4) | copy-start | bytes 1572868
  (2 other events, 1.5 us)

commit v3 on v2

v3 whole, which is shorter than its diff:
```python
import functools

import jax
import jax.numpy as jnp
from jax import lax
from jax.experimental import pallas as pl
from jax.experimental.pallas import tpu as pltpu
from jax.sharding import PartitionSpec as P


def extended(x, sides, width):
    for axis, dim in sides:
        size, length = (lax.axis_size(axis), x.shape[dim])
        up = [(i, (i + 1) % size) for i in range(size - 1)]
        down = [(j, i) for i, j in up]
        last = lax.slice_in_dim(x, length - width, length, axis=dim)
        first = lax.slice_in_dim(x, 0, width, axis=dim)
        before = lax.ppermute(last, axis, up)
        after = lax.ppermute(first, axis, down)
        x = jnp.concatenate([before, x, after], axis=dim)
    return x


def gelu_act(value):
    return jax.nn.gelu(value, approximate=True)


def gelu_back(preact, upstream):
    return jax.vjp(gelu_act, preact)[1](upstream)[0]


def tree_scatter(blocks, order):
    count = blocks.shape[0]
    me = lax.axis_index("dp")
    bits = count.bit_length() - 1
    x = blocks.reshape((2,) * bits + blocks.shape[1:])
    remaining = list(range(bits - 1, -1, -1))
    for bit in order:
        axis = remaining.index(bit)
        mine = (me >> bit) & 1
        keep = lax.dynamic_index_in_dim(x, mine, axis=axis, keepdims=False)
        send = lax.dynamic_index_in_dim(x, 1 - mine, axis=axis, keepdims=False)
        pairs = [(i, i ^ (1 << bit)) for i in range(count)]
        got = lax.ppermute(send.astype(jnp.bfloat16), "dp", pairs)
        x = keep + got.astype(jnp.float32)
        remaining.pop(axis)
    return x


def conv_block(grid, taps):
    padded = extended(grid, (("dp", 0), ("expert", 1)), 1)
    padded = jnp.pad(padded, ((0, 0), (0, 0), (1, 1), (0, 0)))
    out = lax.conv_general_dilated(
        padded[None],
        taps,
        (1, 1, 1),
        "VALID",
        dimension_numbers=("NDHWC", "DHWIO", "NDHWC"),
        preferred_element_type=jnp.float32,
    )
    return out[0].astype(jnp.bfloat16)


def expert_kernel(
    cols, rows_ref, first_ref, second_ref, back_ref, part_ref, result_acc, input_acc
):
    step = pl.program_id(0)

    @pl.when(step == 0)
    def _():
        result_acc[...] = jnp.zeros_like(result_acc)
        input_acc[...] = jnp.zeros_like(input_acc)

    rows = rows_ref[:, :cols]
    grads = rows_ref[:, cols:]
    first = first_ref[...]
    second = second_ref[...]
    preact = jnp.dot(rows, first, preferred_element_type=jnp.float32)
    activation = gelu_act(preact).astype(jnp.bfloat16)
    result_acc[...] += jnp.dot(activation, second, preferred_element_type=jnp.float32)
    upstream = lax.dot_general(
        grads, second, (((1,), (1,)), ((), ())), preferred_element_type=jnp.float32
    )
    gate_grad = gelu_back(preact, upstream).astype(jnp.bfloat16)
    input_acc[...] += lax.dot_general(
        gate_grad, first, (((1,), (1,)), ((), ())), preferred_element_type=jnp.float32
    )
    part_ref[:, :cols] = lax.dot_general(
        gate_grad, rows, (((0,), (0,)), ((), ())), preferred_element_type=jnp.float32
    )
    part_ref[:, cols:] = lax.dot_general(
        activation, grads, (((0,), (0,)), ((), ())), preferred_element_type=jnp.float32
    )

    @pl.when(step == pl.num_programs(0) - 1)
    def _():
        width = result_acc.shape[1]
        back_ref[:, :width] = result_acc[...].astype(back_ref.dtype)
        back_ref[:, width:] = input_acc[...].astype(back_ref.dtype)


def expert(inbound, weight_one, weight_two, chunk):
    slots, both = inbound.shape
    cols, hidden = weight_one.shape
    channels = weight_two.shape[1]
    flops = 2 * slots * hidden * (3 * cols + 3 * channels)
    return pl.pallas_call(
        functools.partial(expert_kernel, cols),
        grid=(hidden // chunk,),
        in_specs=[
            pl.BlockSpec((slots, both), lambda h: (0, 0)),
            pl.BlockSpec((cols, chunk), lambda h: (0, h)),
            pl.BlockSpec((chunk, channels), lambda h: (h, 0)),
        ],
        out_specs=[
            pl.BlockSpec((slots, both), lambda h: (0, 0)),
            pl.BlockSpec((chunk, both), lambda h: (h, 0)),
        ],
        out_shape=[
            jax.ShapeDtypeStruct((slots, both), jnp.bfloat16),
            jax.ShapeDtypeStruct((hidden, both), jnp.float32),
        ],
        scratch_shapes=[
            pltpu.VMEM((slots, channels), jnp.float32),
            pltpu.VMEM((slots, cols), jnp.float32),
        ],
        compiler_params=pltpu.CompilerParams(
            dimension_semantics=("arbitrary",), vmem_limit_bytes=56 * 1024 * 1024
        ),
        cost_estimate=pl.CostEstimate(
            flops=flops,
            transcendentals=slots * hidden,
            bytes_accessed=2 * (2 * slots * both + hidden * (cols + channels)) + 4 * hidden * both,
        ),
    )(inbound, weight_one, weight_two)


def per_device(feats, labels, w_first, w_second, kernel, cotangent):
    experts = lax.axis_size("expert")
    slabs = lax.axis_size("dp")
    rows_y = feats.shape[1]
    depth_cells = feats.shape[2]
    feat_width = feats.shape[3]
    channels = kernel.shape[2]
    hidden = w_first.shape[2]
    patch_count = rows_y * depth_cells
    capacity = 2 * patch_count // experts
    slots = experts * capacity
    regime = labels.reshape(patch_count)
    onehot = (regime[:, None] == jnp.arange(experts, dtype=jnp.int32)[None, :]).astype(
        jnp.bfloat16
    )
    lower = (
        jnp.arange(patch_count)[:, None] >= jnp.arange(patch_count)[None, :]
    ).astype(jnp.bfloat16)
    ranking = jnp.dot(lower, onehot, preferred_element_type=jnp.float32)
    slot_index = jnp.sum(ranking * onehot.astype(jnp.float32), axis=1).astype(jnp.int32) - 1
    target = regime * capacity + slot_index
    route = (target[None, :] == jnp.arange(slots, dtype=jnp.int32)[:, None]).astype(jnp.bfloat16)

    taps = kernel.reshape(3, 3, 3, channels, channels)
    flipped = taps[::-1, ::-1, ::-1]
    field_grad = conv_block(cotangent, jnp.swapaxes(flipped, 3, 4))
    field_rows = field_grad.reshape(patch_count, channels)
    flat_feats = feats.reshape(patch_count, feat_width)
    local = jnp.concatenate([flat_feats, field_rows], axis=1)
    outbound = jnp.dot(route, local, preferred_element_type=jnp.float32).astype(jnp.bfloat16)
    both = feat_width + channels
    inbound = lax.all_to_all(
        outbound.reshape(experts, capacity, both), "expert", split_axis=0, concat_axis=0, tiled=True
    )
    back, part = expert(inbound.reshape(slots, both), w_first[0], w_second[0], 512)
    returned = lax.all_to_all(
        back.reshape(experts, capacity, both), "expert", split_axis=0, concat_axis=0, tiled=True
    )
    mixed = lax.dot_general(
        route,
        returned.reshape(slots, both),
        (((0,), (0,)), ((), ())),
        preferred_element_type=jnp.float32,
    ).astype(jnp.bfloat16)
    patch_grid = mixed[:, :channels].reshape(1, rows_y, depth_cells, channels)
    imitated = conv_block(patch_grid, taps)
    feat_grad = mixed[:, channels:].reshape(1, rows_y, depth_cells, feat_width)

    grads = tree_scatter(part.reshape(slabs, hidden // slabs, both), (0, 1, 3, 2))
    grad_one = grads[:, :feat_width].T
    grad_two = grads[:, feat_width:]
    return (imitated, feat_grad, grad_one[None], grad_two[None])


def solution(mesh):
    in_specs = (
        P("dp", "expert", None, None),
        P("dp", "expert", None, None),
        P("expert", None, None),
        P("expert", None, None),
        P(),
        P("dp", "expert", None, None),
    )
    out_specs = (
        P("dp", "expert", None, None),
        P("dp", "expert", None, None),
        P("expert", None, "dp"),
        P("expert", "dp", None),
    )
    return jax.shard_map(
        per_device, mesh=mesh, in_specs=in_specs, out_specs=out_specs, check_vma=False
    )
```

time: 253 us -> 222 us (0.88); the launches traced: 248 us -> 221 us
  matrix products: 57 us -> 18.4 us
  starting transfers between devices: 74.3 us -> 53.5 us
  waiting for transfers between devices: 67.1 us -> 87.7 us
  Pallas kernels: 0 us -> 17.1 us
  local copies, waits for them, and re-layouts: 38.2 us -> 33.2 us
    dot_general x10 -> x2, matrix products: 51.7 us -> 4.92 us  [the longest x1 2.7 us: per_device(): lax.dot_general(route, returned.reshape(slots, both), (((0,), (0,)), ((),...]
    ppermute x8 -> x4, waiting for transfers between devices: 7.88 us -> 27.7 us  [tree_scatter(): got = lax.ppermute(send.astype(jnp.bfloat16), 'dp', pairs)]
    all_to_all x4 -> x2, starting transfers between devices: 30.7 us -> 13.4 us  [the longest x1 7.67 us: per_device(): lax.all_to_all(back.reshape(experts, capacity, both), 'expert', split_axi...]
    pallas_call x0 -> x1, Pallas kernels: none -> 17.1 us  [expert(): pl.pallas_call(functools.partial(expert_kernel, cols), grid=(hidden // ch...]
    dot_general x2 -> x0, local copies, waits for them, and re-layouts: 12.9 us -> none  [the longest x1 6.49 us: per_device(): lax.dot_general(gate_grad, row_block, (((0,), (0,)), ((), ())), preferred...]
    all_to_all x4 -> x2, waiting for transfers between devices: 18.9 us -> 31 us  [the longest x1 31 us: per_device(): lax.all_to_all(outbound.reshape(experts, capacity, both), 'expert', split...]
    ppermute x4, waiting for transfers between devices: 35.8 us -> 24 us  [extended(): after = lax.ppermute(first, axis, down)]
    dynamic_slice x0 -> x3, local copies, waits for them, and re-layouts: none -> 10.6 us  [the longest x2 7.37 us: tree_scatter(): keep = lax.dynamic_index_in_dim(x, mine, axis=axis, keepdims=False)]
  transfers between devices with their start and end apart: 20 -> 14, of which waited for: 12 -> 9; matrix products, arithmetic and copies ran while one was open for 25% -> 12% of each run, Pallas kernels for 0% -> 0%
where the time goes in v3:
time: 222 us; the launch traced here: 221 us
  waiting for transfers between devices  87.7 us (40%)
  starting transfers between devices  53.5 us (24%)
  local copies, waits for them, and re-layouts  33.2 us (15%)
  matrix products  18.4 us (8%)
  Pallas kernels  17.1 us (8%)
  other arithmetic  9.92 us (4%)
    all_to_all x1, waiting for transfers between devices, per_device(): lax.all_to_all(outbound.reshape(experts, capacity, both), 'expert', split...  31 us
    ppermute x4, waiting for transfers between devices, tree_scatter(): got = lax.ppermute(send.astype(jnp.bfloat16), 'dp', pairs)  27.7 us
    ppermute x4, waiting for transfers between devices, extended(): after = lax.ppermute(first, axis, down)  24 us
    ppermute x4, starting transfers between devices, extended(): before = lax.ppermute(last, axis, up)  17.8 us
    pallas_call x1, Pallas kernels, expert(): pl.pallas_call(functools.partial(expert_kernel, cols), grid=(hidden // ch...  17.1 us
    conv_general_dilated x2, matrix products, conv_block(): lax.conv_general_dilated(padded[None], taps, (1, 1, 1), 'VALID', dimensio...  12.5 us
    ppermute x4, starting transfers between devices, tree_scatter(): got = lax.ppermute(send.astype(jnp.bfloat16), 'dp', pairs)  12 us
    ppermute x4, starting transfers between devices, extended(): after = lax.ppermute(first, axis, down)  10.2 us
  transfers between devices with their start and end apart: 14, of which 9 were waited for; matrix products, arithmetic and copies ran while one was open for 12% of the time, Pallas kernels for 0%

profile of v3, /device:TPU:95, one launch (start us, length us, event | category | flops | bytes accessed | tf_op | source)
XLA Modules:
  0.0 220.8 jit_solution(395195415665366275)
XLA Ops:
  0.7 4.0 %collective-permute-start = (bf16[1,4,128,256]{3,2,1,0:T(8,128)(2,1)}, bf16[1,4,128,256]{3,2,1,0:T(8,128)(2,1)S(1)}, u32[]{:S(2)}, u32[]{:S(2)}) collective-permute-start(bf16[1,4,128,256]{3,2,1,0:T(8,128)(2,1)} %param.11), channel_id=1, source_target_pairs={{0,16},{16,32},{32,48},{48,64},{64,80},{80,96},{96,112},{112,128},... | collective-permute-start | bytes 786440 | tf_op jit(solution)/shard_map/ppermute | solution.py:18
  4.7 1.9 collective-permute-start.1
  9.3 5.4 %collective-permute-done.1 = bf16[1,4,128,256]{3,2,1,0:T(8,128)(2,1)S(1)} collective-permute-done((bf16[1,4,128,256]{3,2,1,0:T(8,128)(2,1)}, bf16[1,4,128,256]{3,2,1,0:T(8,128)(2,1)S(1)}, u32[]{:S(2)}, u32[]{:S(2)}) %collective-permute-start.1) | collective-permute-done | bytes 262176 | tf_op jit(solution)/shard_map/ppermute | solution.py:19
  14.8 5.1 %collective-permute-start.2 = (bf16[3,1,128,256]{3,2,1,0:T(8,128)(2,1)S(1)}, bf16[3,1,128,256]{3,2,1,0:T(8,128)(2,1)S(1)}, u32[]{:S(2)}, u32[]{:S(2)}) collective-permute-start(bf16[3,1,128,256]{3,2,1,0:T(8,128)(2,1)S(1)} %get-tuple-element.14), channel_id=1, source_target_pairs={{0,1},{1,2},{2,3},{3,4},{4,5},{5,6},{6,7},{7,8},{8,9},{9,10},{10,1... | collective-permute-start | bytes 589832 | tf_op jit(solution)/shard_map/ppermute | solution.py:18
  19.9 1.9 collective-permute-start.3
  21.9 2.8 %collective-permute-done.2 = bf16[3,1,128,256]{3,2,1,0:T(8,128)(2,1)S(1)} collective-permute-done((bf16[3,1,128,256]{3,2,1,0:T(8,128)(2,1)S(1)}, bf16[3,1,128,256]{3,2,1,0:T(8,128)(2,1)S(1)}, u32[]{:S(2)}, u32[]{:S(2)}) %collective-permute-start.2) | collective-permute-done | bytes 196640 | tf_op jit(solution)/shard_map/ppermute | solution.py:18
  24.6 8.3 %collective-permute-done.3 = bf16[3,1,128,256]{3,2,1,0:T(8,128)(2,1)S(1)} collective-permute-done((bf16[3,1,128,256]{3,2,1,0:T(8,128)(2,1)S(1)}, bf16[3,1,128,256]{3,2,1,0:T(8,128)(2,1)S(1)}, u32[]{:S(2)}, u32[]{:S(2)}) %collective-permute-start.3) | collective-permute-done | bytes 196640 | tf_op jit(solution)/shard_map/ppermute | solution.py:19
  33.5 10.4 %fusion.27 = bf16[1,1,4,128,256]{4,0,3,2,1:T(2,128)(2,1)S(1)} fusion(bf16[3,3,3,256,256]{4,3,2,1,0:T(8,128)(2,1)S(1)} %bitcast.57, bf16[1,3,6,130,256]{4,3,2,1,0:T(8,128)(2,1)S(1)} %fusion.24), kind=kOutput, calls=%fused_computation.36 | convolution fusion | flops 1812070400 | bytes 4999168 | tf_op jit(solution)/shard_map/conv_general_dilated | solution.py:53
  43.9 2.2 %fusion.6 = bf16[1024,768]{1,0:T(8,128)(2,1)} fusion(s32[512]{0:T(512)S(1)} %add_add_fusion, bf16[512,256]{1,0:T(8,128)(2,1)S(1)} %bitcast.66, bf16[512,512]{1,0:T(8,128)(2,1)S(1)} %bitcast.71), kind=kOutput, calls=%fused_computation.11 | convolution fusion | flops 808189952 | bytes 2361344 | tf_op jit(solution)/shard_map/dot_general | solution.py:167
  46.1 5.8 %all-to-all-start = ((bf16[16,64,768]{2,1,0:T(8,128)(2,1)}), bf16[16,64,768]{2,1,0:T(8,128)(2,1)}, u32[]{:S(2)}, u32[]{:S(2)}) async-start(bf16[16,64,768]{2,1,0:T(8,128)(2,1)} %bitcast.63), calls=%async_computation | async-start | bytes 3145728 | tf_op jit(solution)/shard_map/all_to_all | solution.py:169
  51.9 31.0 %all-to-all-done = bf16[16,64,768]{2,1,0:T(8,128)(2,1)} async-done(((bf16[16,64,768]{2,1,0:T(8,128)(2,1)}), bf16[16,64,768]{2,1,0:T(8,128)(2,1)}, u32[]{:S(2)}, u32[]{:S(2)}) %all-to-all-start) | async-done | bytes 1572896 | tf_op jit(solution)/shard_map/all_to_all | solution.py:169
  82.9 17.1 %shard_map.93 = (bf16[1024,768]{1,0:T(8,128)(2,1)}, f32[2048,768]{1,0:T(8,128)}) custom-call(bf16[1024,768]{1,0:T(8,128)(2,1)} %bitcast.5.rows_ref, bf16[512,2048]{1,0:T(8,128)(2,1)} %bitcast.69, bf16[2048,256]{1,0:T(8,128)(2,1)} %bitcast.70), custom_call_target="tpu_custom_call" | custom-call | flops 9663676416 | bytes 12582912 | tf_op jit(solution)/shard_map/pallas_call | solution.py:107
  99.9 3.2 %constant_dynamic-slice_fusion = bf16[2,2,2,1,128,768]{5,4,3,2,1,0:T(8,128)(2,1)} fusion(f32[2,2,2,2,128,768]{5,4,3,2,1,0:T(8,128)} %bitcast.59, s32[]{:T(128)S(6)} %select_n.29), kind=kLoop, calls=%fused_computation.67 | loop fusion | bytes 3145732 | tf_op jit(solution)/shard_map/jit(dynamic_index_in_dim)/dynamic_slice | solution.py:42
  103.2 2.6 %copy.21 = bf16[2,2,2,1,128,768]{4,5,1,0,2,3:T(8,128)(2,1)} copy(bf16[2,2,2,1,128,768]{5,4,3,2,1,0:T(8,128)(2,1)} %constant_dynamic-slice_fusion) | data formatting | bytes 3145728
  105.7 2.2 %collective-permute-start.8 = (bf16[2,2,2,128,768]{3,4,1,0,2:T(8,128)(2,1)}, bf16[2,2,2,128,768]{3,4,1,0,2:T(8,128)(2,1)}, u32[]{:S(2)}, u32[]{:S(2)}) collective-permute-start(bf16[2,2,2,128,768]{3,4,1,0,2:T(8,128)(2,1)} %bitcast.62), channel_id=1, source_target_pairs={{0,16},{16,0},{32,48},{48,32},{64,80},{80,64},{96,112},{112,96},{1... | collective-permute-start | bytes 4718600 | tf_op jit(solution)/shard_map/ppermute | solution.py:44
  108.0 7.7 %all-to-all-start.1 = ((bf16[16,64,768]{2,1,0:T(8,128)(2,1)}), bf16[16,64,768]{2,1,0:T(8,128)(2,1)}, u32[]{:S(2)}, u32[]{:S(2)}) async-start(bf16[16,64,768]{2,1,0:T(8,128)(2,1)} %bitcast.61), calls=%async_computation.1 | async-start | bytes 3145728 | tf_op jit(solution)/shard_map/all_to_all | solution.py:173
  115.6 3.9 %constant_dynamic-slice_fusion.1 = f32[2,2,2,1,128,768]{5,4,3,2,1,0:T(8,128)} fusion(f32[2,2,2,2,128,768]{5,4,3,2,1,0:T(8,128)} %bitcast.60, s32[]{:T(128)S(6)} %select_n.28), kind=kLoop, calls=%fused_computation.68 | loop fusion | bytes 6291460 | tf_op jit(solution)/shard_map/jit(dynamic_index_in_dim)/dynamic_slice | solution.py:41
  119.5 3.5 %copy.16 = f32[2,2,2,1,128,768]{4,5,1,0,2,3:T(8,128)} copy(f32[2,2,2,1,128,768]{5,4,3,2,1,0:T(8,128)} %constant_dynamic-slice_fusion.1) | data formatting | bytes 6291456 | tf_op jit(solution)/shard_map/jit(dynamic_index_in_dim)/dynamic_slice | solution.py:41
  123.0 2.6 %bitcast_add_fusion = f32[2,2,2,128,768]{3,4,1,0,2:T(8,128)S(1)} fusion(f32[2,2,2,1,128,768]{4,5,1,0,2,3:T(8,128)} %copy.16, bf16[2,2,2,128,768]{3,4,1,0,2:T(8,128)(2,1)} %collective-permute-done.8), kind=kLoop, calls=%fused_computation.2 | loop fusion | flops 1572864 | bytes 7864320 | tf_op jit(solution)/shard_map/add | solution.py:45
  128.2 8.3 %collective-permute-start.9 = (bf16[2,2,128,768]{2,3,1,0:T(8,128)(2,1)}, bf16[2,2,128,768]{2,3,1,0:T(8,128)(2,1)}, u32[]{:S(2)}, u32[]{:S(2)}) collective-permute-start(bf16[2,2,128,768]{2,3,1,0:T(8,128)(2,1)} %fusion.39), channel_id=1, source_target_pairs={{0,32},{16,48},{32,0},{48,16},{64,96},{80,112},{96,64},{112,80},{1... | collective-permute-start | bytes 2359304 | tf_op jit(solution)/shard_map/ppermute | solution.py:44
  136.5 17.8 %collective-permute-done.9 = bf16[2,2,128,768]{2,3,1,0:T(8,128)(2,1)} collective-permute-done((bf16[2,2,128,768]{2,3,1,0:T(8,128)(2,1)}, bf16[2,2,128,768]{2,3,1,0:T(8,128)(2,1)}, u32[]{:S(2)}, u32[]{:S(2)}) %collective-permute-start.9) | collective-permute-done | bytes 786464 | tf_op jit(solution)/shard_map/ppermute | solution.py:44
  154.3 1.8 bitcast_add_fusion.1
  158.0 9.9 %collective-permute-done.10 = bf16[2,128,768]{1,2,0:T(8,128)(2,1)} collective-permute-done((bf16[2,128,768]{1,2,0:T(8,128)(2,1)}, bf16[2,128,768]{1,2,0:T(8,128)(2,1)}, u32[]{:S(2)}, u32[]{:S(2)}) %collective-permute-start.10) | collective-permute-done | bytes 393248 | tf_op jit(solution)/shard_map/ppermute | solution.py:44
  172.4 2.7 %fusion.14 = bf16[512,768]{1,0:T(8,128)(2,1)S(1)} fusion(bf16[1024,768]{1,0:T(8,128)(2,1)} %bitcast.9, s32[512]{0:T(512)S(1)} %add_add_fusion), kind=kOutput, calls=%fused_computation.21 | convolution fusion | flops 806223872 | bytes 2361344 | tf_op jit(solution)/shard_map/dot_general | solution.py:176
  175.8 4.2 %collective-permute-start.5 = (bf16[1,4,128,256]{3,2,1,0:T(8,128)(2,1)}, bf16[1,4,128,256]{3,2,1,0:T(8,128)(2,1)}, u32[]{:S(2)}, u32[]{:S(2)}) collective-permute-start(bf16[1,4,128,256]{3,2,1,0:T(8,128)(2,1)} %bitcast.10), channel_id=1, source_target_pairs={{16,0},{32,16},{48,32},{64,48},{80,64},{96,80},{112,96},{128,112},... | collective-permute-start | bytes 786440 | tf_op jit(solution)/shard_map/ppermute | solution.py:19
  180.0 3.4 %collective-permute-start.4 = (bf16[1,4,128,256]{3,2,1,0:T(8,128)(2,1)}, bf16[1,4,128,256]{3,2,1,0:T(8,128)(2,1)}, u32[]{:S(2)}, u32[]{:S(2)}) collective-permute-start(bf16[1,4,128,256]{3,2,1,0:T(8,128)(2,1)} %bitcast.10), channel_id=1, source_target_pairs={{0,16},{16,32},{32,48},{48,64},{64,80},{80,96},{96,112},{112,128},... | collective-permute-start | bytes 786440 | tf_op jit(solution)/shard_map/ppermute | solution.py:18
  188.8 5.2 %collective-permute-start.6 = (bf16[3,1,128,256]{3,2,1,0:T(8,128)(2,1)S(1)}, bf16[3,1,128,256]{3,2,1,0:T(8,128)(2,1)S(1)}, u32[]{:S(2)}, u32[]{:S(2)}) collective-permute-start(bf16[3,1,128,256]{3,2,1,0:T(8,128)(2,1)S(1)} %get-tuple-element.12), channel_id=1, source_target_pairs={{0,1},{1,2},{2,3},{3,4},{4,5},{5,6},{6,7},{7,8},{8,9},{9,10},{10,1... | collective-permute-start | bytes 589832 | tf_op jit(solution)/shard_map/ppermute | solution.py:18
  194.1 2.1 collective-permute-start.7
  199.5 10.3 %collective-permute-done.7 = bf16[3,1,128,256]{3,2,1,0:T(8,128)(2,1)S(1)} collective-permute-done((bf16[3,1,128,256]{3,2,1,0:T(8,128)(2,1)S(1)}, bf16[3,1,128,256]{3,2,1,0:T(8,128)(2,1)S(1)}, u32[]{:S(2)}, u32[]{:S(2)}) %collective-permute-start.7) | collective-permute-done | bytes 196640 | tf_op jit(solution)/shard_map/ppermute | solution.py:19
  212.6 3.2 %reshape.80 = bf16[3,6,1,8,17,256]{5,4,3,1,0,2:T(8,128)(2,1)} reshape(bf16[3,6,1,136,256]{4,3,1,0,2:T(8,128)(2,1)} %pad.9) | data formatting | bytes 2506752 | tf_op jit(solution)/shard_map/conv_general_dilated | solution.py:53
  215.8 1.8 copy.14
  217.7 2.1 fusion.33
  (52 shorter events, 25.5 us)
Async XLA Ops:
  0.6 32.8 %copy-start = (bf16[27,256,256]{2,1,0:T(8,128)(2,1)S(1)}, bf16[27,256,256]{2,1,0:T(8,128)(2,1)}, u32[]{:S(2)}) copy-start(bf16[27,256,256]{2,1,0:T(8,128)(2,1)} %param.10) | copy-start | bytes 10616836
  0.6 21.2 %copy-start.6 = (s32[1,4,128,1]{2,3,1,0:T(1,128)S(1)}, s32[1,4,128,1]{2,3,1,0:T(1,128)}, u32[]{:S(2)}) copy-start(s32[1,4,128,1]{2,3,1,0:T(1,128)} %param.7) | copy-start | bytes 6148
  0.7 7.6 %collective-permute-start = (bf16[1,4,128,256]{3,2,1,0:T(8,128)(2,1)}, bf16[1,4,128,256]{3,2,1,0:T(8,128)(2,1)S(1)}, u32[]{:S(2)}, u32[]{:S(2)}) collective-permute-start(bf16[1,4,128,256]{3,2,1,0:T(8,128)(2,1)} %param.11), channel_id=1, source_target_pairs={{0,16},{16,32},{32,48},{48,64},{64,80},{80,96},{96,112},{112,128},... | collective-permute-start | bytes 786440 | tf_op jit(solution)/shard_map/ppermute | solution.py:18
  4.7 10.0 %collective-permute-start.1 = (bf16[1,4,128,256]{3,2,1,0:T(8,128)(2,1)}, bf16[1,4,128,256]{3,2,1,0:T(8,128)(2,1)S(1)}, u32[]{:S(2)}, u32[]{:S(2)}) collective-permute-start(bf16[1,4,128,256]{3,2,1,0:T(8,128)(2,1)} %param.11), channel_id=1, source_target_pairs={{16,0},{32,16},{48,32},{64,48},{80,64},{96,80},{112,96},{128,112},... | collective-permute-start | bytes 786440 | tf_op jit(solution)/shard_map/ppermute | solution.py:19
  14.8 9.9 %collective-permute-start.2 = (bf16[3,1,128,256]{3,2,1,0:T(8,128)(2,1)S(1)}, bf16[3,1,128,256]{3,2,1,0:T(8,128)(2,1)S(1)}, u32[]{:S(2)}, u32[]{:S(2)}) collective-permute-start(bf16[3,1,128,256]{3,2,1,0:T(8,128)(2,1)S(1)} %get-tuple-element.14), channel_id=1, source_target_pairs={{0,1},{1,2},{2,3},{3,4},{4,5},{5,6},{6,7},{7,8},{8,9},{9,10},{10,1... | collective-permute-start | bytes 589832 | tf_op jit(solution)/shard_map/ppermute | solution.py:18
  19.9 13.0 %collective-permute-start.3 = (bf16[3,1,128,256]{3,2,1,0:T(8,128)(2,1)S(1)}, bf16[3,1,128,256]{3,2,1,0:T(8,128)(2,1)S(1)}, u32[]{:S(2)}, u32[]{:S(2)}) collective-permute-start(bf16[3,1,128,256]{3,2,1,0:T(8,128)(2,1)S(1)} %get-tuple-element.15), channel_id=1, source_target_pairs={{1,0},{2,1},{3,2},{4,3},{5,4},{6,5},{7,6},{8,7},{9,8},{10,9},{11,1... | collective-permute-start | bytes 589832 | tf_op jit(solution)/shard_map/ppermute | solution.py:19
  33.5 10.4 %copy-start.7 = (bf16[1,4,128,512]{3,2,1,0:T(8,128)(2,1)S(1)}, bf16[1,4,128,512]{3,2,1,0:T(8,128)(2,1)}, u32[]{:S(2)}) copy-start(bf16[1,4,128,512]{3,2,1,0:T(8,128)(2,1)} %param.6) | copy-start | bytes 1572868
  46.1 36.7 %all-to-all-start = ((bf16[16,64,768]{2,1,0:T(8,128)(2,1)}), bf16[16,64,768]{2,1,0:T(8,128)(2,1)}, u32[]{:S(2)}, u32[]{:S(2)}) async-start(bf16[16,64,768]{2,1,0:T(8,128)(2,1)} %bitcast.63), calls=%async_computation | async-start | bytes 3145728 | tf_op jit(solution)/shard_map/all_to_all | solution.py:169
  105.7 17.3 %collective-permute-start.8 = (bf16[2,2,2,128,768]{3,4,1,0,2:T(8,128)(2,1)}, bf16[2,2,2,128,768]{3,4,1,0,2:T(8,128)(2,1)}, u32[]{:S(2)}, u32[]{:S(2)}) collective-permute-start(bf16[2,2,2,128,768]{3,4,1,0,2:T(8,128)(2,1)} %bitcast.62), channel_id=1, source_target_pairs={{0,16},{16,0},{32,48},{48,32},{64,80},{80,64},{96,112},{112,96},{1... | collective-permute-start | bytes 4718600 | tf_op jit(solution)/shard_map/ppermute | solution.py:44
  108.0 64.4 %all-to-all-start.1 = ((bf16[16,64,768]{2,1,0:T(8,128)(2,1)}), bf16[16,64,768]{2,1,0:T(8,128)(2,1)}, u32[]{:S(2)}, u32[]{:S(2)}) async-start(bf16[16,64,768]{2,1,0:T(8,128)(2,1)} %bitcast.61), calls=%async_computation.1 | async-start | bytes 3145728 | tf_op jit(solution)/shard_map/all_to_all | solution.py:173
  125.6 1.6 copy-start.1
  128.2 26.0 %collective-permute-start.9 = (bf16[2,2,128,768]{2,3,1,0:T(8,128)(2,1)}, bf16[2,2,128,768]{2,3,1,0:T(8,128)(2,1)}, u32[]{:S(2)}, u32[]{:S(2)}) collective-permute-start(bf16[2,2,128,768]{2,3,1,0:T(8,128)(2,1)} %fusion.39), channel_id=1, source_target_pairs={{0,32},{16,48},{32,0},{48,16},{64,96},{80,112},{96,64},{112,80},{1... | collective-permute-start | bytes 2359304 | tf_op jit(solution)/shard_map/ppermute | solution.py:44
  156.1 1.2 copy-start.2
  158.0 9.9 %collective-permute-start.10 = (bf16[2,128,768]{1,2,0:T(8,128)(2,1)}, bf16[2,128,768]{1,2,0:T(8,128)(2,1)}, u32[]{:S(2)}, u32[]{:S(2)}) collective-permute-start(bf16[2,128,768]{1,2,0:T(8,128)(2,1)} %fusion.44), channel_id=1, source_target_pairs={{0,128},{16,144},{32,160},{48,176},{64,192},{80,208},{96,224},{112... | collective-permute-start | bytes 1179656 | tf_op jit(solution)/shard_map/ppermute | solution.py:44
  169.2 0.9 copy-start.3
  170.8 12.7 %collective-permute-start.11 = (bf16[128,768]{0,1:T(8,128)(2,1)}, bf16[128,768]{0,1:T(8,128)(2,1)}, u32[]{:S(2)}, u32[]{:S(2)}) collective-permute-start(bf16[128,768]{0,1:T(8,128)(2,1)} %fusion.45), channel_id=1, source_target_pairs={{0,64},{16,80},{32,96},{48,112},{64,0},{80,16},{96,32},{112,48},{1... | collective-permute-start | bytes 589832 | tf_op jit(solution)/shard_map/ppermute | solution.py:44
  172.4 11.1 %copy-start.4 = (f32[2,128,768]{1,2,0:T(8,128)S(1)}, f32[2,128,768]{1,2,0:T(8,128)}, u32[]{:S(2)}) copy-start(f32[2,128,768]{1,2,0:T(8,128)} %copy-done.3) | copy-start | bytes 2359300
  175.8 12.0 %collective-permute-start.5 = (bf16[1,4,128,256]{3,2,1,0:T(8,128)(2,1)}, bf16[1,4,128,256]{3,2,1,0:T(8,128)(2,1)}, u32[]{:S(2)}, u32[]{:S(2)}) collective-permute-start(bf16[1,4,128,256]{3,2,1,0:T(8,128)(2,1)} %bitcast.10), channel_id=1, source_target_pairs={{16,0},{32,16},{48,32},{64,48},{80,64},{96,80},{112,96},{128,112},... | collective-permute-start | bytes 786440 | tf_op jit(solution)/shard_map/ppermute | solution.py:19
  180.0 7.7 %collective-permute-start.4 = (bf16[1,4,128,256]{3,2,1,0:T(8,128)(2,1)}, bf16[1,4,128,256]{3,2,1,0:T(8,128)(2,1)}, u32[]{:S(2)}, u32[]{:S(2)}) collective-permute-start(bf16[1,4,128,256]{3,2,1,0:T(8,128)(2,1)} %bitcast.10), channel_id=1, source_target_pairs={{0,16},{16,32},{32,48},{48,64},{64,80},{80,96},{96,112},{112,128},... | collective-permute-start | bytes 786440 | tf_op jit(solution)/shard_map/ppermute | solution.py:18
  184.5 1.0 copy-start.5
  188.8 10.7 %collective-permute-start.6 = (bf16[3,1,128,256]{3,2,1,0:T(8,128)(2,1)S(1)}, bf16[3,1,128,256]{3,2,1,0:T(8,128)(2,1)S(1)}, u32[]{:S(2)}, u32[]{:S(2)}) collective-permute-start(bf16[3,1,128,256]{3,2,1,0:T(8,128)(2,1)S(1)} %get-tuple-element.12), channel_id=1, source_target_pairs={{0,1},{1,2},{2,3},{3,4},{4,5},{5,6},{6,7},{7,8},{8,9},{9,10},{10,1... | collective-permute-start | bytes 589832 | tf_op jit(solution)/shard_map/ppermute | solution.py:18
  194.1 15.8 %collective-permute-start.7 = (bf16[3,1,128,256]{3,2,1,0:T(8,128)(2,1)S(1)}, bf16[3,1,128,256]{3,2,1,0:T(8,128)(2,1)S(1)}, u32[]{:S(2)}, u32[]{:S(2)}) collective-permute-start(bf16[3,1,128,256]{3,2,1,0:T(8,128)(2,1)S(1)} %get-tuple-element.13), channel_id=1, source_target_pairs={{1,0},{2,1},{3,2},{4,3},{5,4},{6,5},{7,6},{8,7},{9,8},{10,9},{11,1... | collective-permute-start | bytes 589832 | tf_op jit(solution)/shard_map/ppermute | solution.py:19
  215.8 1.8 copy-start.8

commit v4 on v3

--- a/solution.py
+++ b/solution.py
@@ -47,18 +47,53 @@
     return x
 
 
-def conv_block(grid, taps):
+def conv_kernel(flip, shifted_ref, taps_ref, out_ref, acc_ref):
+    rows_y = shifted_ref.shape[3] - 2
+    depth_cells = shifted_ref.shape[4]
+    width = shifted_ref.shape[5]
+    acc_ref[...] = jnp.zeros_like(acc_ref)
+    for plane in range(3):
+        for across in range(3):
+            for along in range(3):
+                tap = 9 * plane + 3 * across + along
+                piece = shifted_ref[0, along, plane, across : across + rows_y]
+                piece = piece.reshape(rows_y * depth_cells, width)
+                if flip:
+                    acc_ref[...] += lax.dot_general(
+                        piece,
+                        taps_ref[26 - tap],
+                        (((1,), (1,)), ((), ())),
+                        preferred_element_type=jnp.float32,
+                    )
+                else:
+                    acc_ref[...] += jnp.dot(
+                        piece, taps_ref[tap], preferred_element_type=jnp.float32
+                    )
+    out_ref[...] = acc_ref[...].astype(out_ref.dtype)
+
+
+def conv_block(grid, kernel, flip):
     padded = extended(grid, (("dp", 0), ("expert", 1)), 1)
     padded = jnp.pad(padded, ((0, 0), (0, 0), (1, 1), (0, 0)))
-    out = lax.conv_general_dilated(
-        padded[None],
-        taps,
-        (1, 1, 1),
-        "VALID",
-        dimension_numbers=("NDHWC", "DHWIO", "NDHWC"),
-        preferred_element_type=jnp.float32,
-    )
-    return out[0].astype(jnp.bfloat16)
+    depth_cells = grid.shape[2]
+    shifted = jnp.stack(
+        [padded[:, :, along : along + depth_cells] for along in range(3)], axis=0
+    )[None]
+    count = grid.shape[1] * depth_cells
+    width = kernel.shape[2]
+    return pl.pallas_call(
+        functools.partial(conv_kernel, flip),
+        out_shape=jax.ShapeDtypeStruct((count, width), jnp.bfloat16),
+        in_specs=[pl.BlockSpec(memory_space=pltpu.VMEM)] * 2,
+        out_specs=pl.BlockSpec(memory_space=pltpu.VMEM),
+        scratch_shapes=[pltpu.VMEM((count, width), jnp.float32)],
+        compiler_params=pltpu.CompilerParams(vmem_limit_bytes=48 * 1024 * 1024),
+        cost_estimate=pl.CostEstimate(
+            flops=2 * 27 * count * width * width,
+            transcendentals=0,
+            bytes_accessed=2 * (shifted.size + kernel.size + count * width),
+        ),
+    )(shifted, kernel)
 
 
 def expert_kernel(
@@ -158,18 +193,23 @@
     target = regime * capacity + slot_index
     route = (target[None, :] == jnp.arange(slots, dtype=jnp.int32)[:, None]).astype(jnp.bfloat16)
 
-    taps = kernel.reshape(3, 3, 3, channels, channels)
-    flipped = taps[::-1, ::-1, ::-1]
-    field_grad = conv_block(cotangent, jnp.swapaxes(flipped, 3, 4))
-    field_rows = field_grad.reshape(patch_count, channels)
     flat_feats = feats.reshape(patch_count, feat_width)
-    local = jnp.concatenate([flat_feats, field_rows], axis=1)
-    outbound = jnp.dot(route, local, preferred_element_type=jnp.float32).astype(jnp.bfloat16)
+    outbound = jnp.dot(route, flat_feats, preferred_element_type=jnp.float32).astype(jnp.bfloat16)
+    received = lax.all_to_all(
+        outbound.reshape(experts, capacity, feat_width), "expert", split_axis=0, concat_axis=0, tiled=True
+    )
+    field_rows = conv_block(cotangent, kernel, True)
+    grad_outbound = jnp.dot(route, field_rows, preferred_element_type=jnp.float32).astype(
+        jnp.bfloat16
+    )
+    grad_inbound = lax.all_to_all(
+        grad_outbound.reshape(experts, capacity, channels), "expert", split_axis=0, concat_axis=0, tiled=True
+    )
     both = feat_width + channels
-    inbound = lax.all_to_all(
-        outbound.reshape(experts, capacity, both), "expert", split_axis=0, concat_axis=0, tiled=True
-    )
-    back, part = expert(inbound.reshape(slots, both), w_first[0], w_second[0], 512)
+    inbound = jnp.concatenate(
+        [received.reshape(slots, feat_width), grad_inbound.reshape(slots, channels)], axis=1
+    )
+    back, part = expert(inbound, w_first[0], w_second[0], 512)
     returned = lax.all_to_all(
         back.reshape(experts, capacity, both), "expert", split_axis=0, concat_axis=0, tiled=True
     )
@@ -180,10 +220,10 @@
         preferred_element_type=jnp.float32,
     ).astype(jnp.bfloat16)
     patch_grid = mixed[:, :channels].reshape(1, rows_y, depth_cells, channels)
-    imitated = conv_block(patch_grid, taps)
+    imitated = conv_block(patch_grid, kernel, False).reshape(1, rows_y, depth_cells, channels)
     feat_grad = mixed[:, channels:].reshape(1, rows_y, depth_cells, feat_width)
 
-    grads = tree_scatter(part.reshape(slabs, hidden // slabs, both), (0, 1, 3, 2))
+    grads = tree_scatter(part.reshape(slabs, hidden // slabs, both), (0, 1, 2, 3))
     grad_one = grads[:, :feat_width].T
     grad_two = grads[:, feat_width:]
     return (imitated, feat_grad, grad_one[None], grad_two[None])

time: 222 us -> 208 us (0.937)
  local copies, waits for them, and re-layouts: 33.2 us -> 17.4 us
  starting transfers between devices: 53.5 us -> 67.4 us
  matrix products: 18.4 us -> 6.63 us
  Pallas kernels: 17.1 us -> 25.8 us
  waiting for transfers between devices: 87.7 us -> 81 us
  other arithmetic: 9.92 us -> 6.49 us
    conv_general_dilated x2 -> x0, matrix products: 12.5 us -> none  [conv_block(): lax.conv_general_dilated(padded[None], taps, (1, 1, 1), 'VALID', dimensio...]
    all_to_all x1 -> x2, waiting for transfers between devices: 31 us -> 21 us  [the longest x1 12 us: per_device(): lax.all_to_all(outbound.reshape(experts, capacity, feat_width), 'expert',...]
    all_to_all x1 -> x2, starting transfers between devices: 5.77 us -> 15.2 us  [the longest x1 9.4 us: per_device(): lax.all_to_all(outbound.reshape(experts, capacity, feat_width), 'expert',...]
    pallas_call x0 -> x2, Pallas kernels: none -> 8.72 us  [conv_block(): pl.pallas_call(functools.partial(conv_kernel, flip), out_shape=jax.ShapeD...]
    conv_general_dilated x3 -> x0, local copies, waits for them, and re-layouts: 5.07 us -> none  [conv_block(): lax.conv_general_dilated(padded[None], taps, (1, 1, 1), 'VALID', dimensio...]
    unnamed x24 -> x10, local copies, waits for them, and re-layouts: 9.73 us -> 4.97 us
    ppermute x4, waiting for transfers between devices: 24 us -> 28.6 us  [extended(): after = lax.ppermute(first, axis, down)]
    ppermute x4, starting transfers between devices: 12 us -> 15.1 us  [tree_scatter(): got = lax.ppermute(send.astype(jnp.bfloat16), 'dp', pairs)]
  transfers between devices with their start and end apart: 14 -> 15, of which waited for: 9 -> 11; matrix products, arithmetic and copies ran while one was open for 12% -> 10% of each run, Pallas kernels for 0% -> 0%
where the time goes in v4:
time: 208 us; the launch traced here: 206 us
  waiting for transfers between devices  81 us (39%)
  starting transfers between devices  67.4 us (32%)
  Pallas kernels  25.8 us (12%)
  local copies, waits for them, and re-layouts  17.4 us (8%)
  matrix products  6.63 us (3%)
  other arithmetic  6.49 us (3%)
    ppermute x4, waiting for transfers between devices, extended(): after = lax.ppermute(first, axis, down)  28.6 us
    ppermute x4, waiting for transfers between devices, tree_scatter(): got = lax.ppermute(send.astype(jnp.bfloat16), 'dp', pairs)  27.6 us
    ppermute x4, starting transfers between devices, extended(): before = lax.ppermute(last, axis, up)  19.9 us
    pallas_call x1, Pallas kernels, expert(): pl.pallas_call(functools.partial(expert_kernel, cols), grid=(hidden // ch...  17.1 us
    ppermute x4, starting transfers between devices, tree_scatter(): got = lax.ppermute(send.astype(jnp.bfloat16), 'dp', pairs)  15.1 us
    all_to_all x1, waiting for transfers between devices, per_device(): lax.all_to_all(outbound.reshape(experts, capacity, feat_width), 'expert',...  12 us
    all_to_all x1, starting transfers between devices, per_device(): lax.all_to_all(back.reshape(experts, capacity, both), 'expert', split_axi...  9.49 us
    all_to_all x1, starting transfers between devices, per_device(): lax.all_to_all(outbound.reshape(experts, capacity, feat_width), 'expert',...  9.4 us
  transfers between devices with their start and end apart: 15, of which 11 were waited for; matrix products, arithmetic and copies ran while one was open for 10% of the time, Pallas kernels for 0%

profile of v4, /device:TPU:95, one launch (start us, length us, event | category | flops | bytes accessed | tf_op | source)
XLA Modules:
  0.0 205.7 jit_solution(4153891614900343048)
XLA Ops:
  0.7 3.9 %collective-permute-start = (bf16[1,4,128,256]{3,2,1,0:T(8,128)(2,1)}, bf16[1,4,128,256]{3,2,1,0:T(8,128)(2,1)S(1)}, u32[]{:S(2)}, u32[]{:S(2)}) collective-permute-start(bf16[1,4,128,256]{3,2,1,0:T(8,128)(2,1)} %param.11), channel_id=1, source_target_pairs={{0,16},{16,32},{32,48},{48,64},{64,80},{80,96},{96,112},{112,128},... | collective-permute-start | bytes 786440 | tf_op jit(solution)/shard_map/ppermute | solution.py:18
  4.6 1.9 collective-permute-start.1
  9.2 5.4 %collective-permute-done.1 = bf16[1,4,128,256]{3,2,1,0:T(8,128)(2,1)S(1)} collective-permute-done((bf16[1,4,128,256]{3,2,1,0:T(8,128)(2,1)}, bf16[1,4,128,256]{3,2,1,0:T(8,128)(2,1)S(1)}, u32[]{:S(2)}, u32[]{:S(2)}) %collective-permute-start.1) | collective-permute-done | bytes 262176 | tf_op jit(solution)/shard_map/ppermute | solution.py:19
  14.6 5.1 %collective-permute-start.2 = (bf16[3,1,128,256]{3,2,1,0:T(8,128)(2,1)S(1)}, bf16[3,1,128,256]{3,2,1,0:T(8,128)(2,1)S(1)}, u32[]{:S(2)}, u32[]{:S(2)}) collective-permute-start(bf16[3,1,128,256]{3,2,1,0:T(8,128)(2,1)S(1)} %get-tuple-element.20), channel_id=1, source_target_pairs={{0,1},{1,2},{2,3},{3,4},{4,5},{5,6},{6,7},{7,8},{8,9},{9,10},{10,1... | collective-permute-start | bytes 589832 | tf_op jit(solution)/shard_map/ppermute | solution.py:18
  19.8 1.9 collective-permute-start.3
  21.7 2.8 %collective-permute-done.2 = bf16[3,1,128,256]{3,2,1,0:T(8,128)(2,1)S(1)} collective-permute-done((bf16[3,1,128,256]{3,2,1,0:T(8,128)(2,1)S(1)}, bf16[3,1,128,256]{3,2,1,0:T(8,128)(2,1)S(1)}, u32[]{:S(2)}, u32[]{:S(2)}) %collective-permute-start.2) | collective-permute-done | bytes 196640 | tf_op jit(solution)/shard_map/ppermute | solution.py:18
  24.5 8.3 %collective-permute-done.3 = bf16[3,1,128,256]{3,2,1,0:T(8,128)(2,1)S(1)} collective-permute-done((bf16[3,1,128,256]{3,2,1,0:T(8,128)(2,1)S(1)}, bf16[3,1,128,256]{3,2,1,0:T(8,128)(2,1)S(1)}, u32[]{:S(2)}, u32[]{:S(2)}) %collective-permute-start.3) | collective-permute-done | bytes 196640 | tf_op jit(solution)/shard_map/ppermute | solution.py:19
  34.0 4.0 %shard_map.93 = bf16[512,256]{1,0:T(8,128)(2,1)S(1)} custom-call(bf16[1,3,3,6,128,256]{5,4,3,2,1,0:T(8,128)(2,1)S(1)} %maximum_bitcast_fusion.shifted_ref, bf16[27,256,256]{2,1,0:T(8,128)(2,1)} %taps_ref.3), custom_call_target="tpu_custom_call" | custom-call | flops 1811939328 | bytes 7340032 | tf_op jit(solution)/shard_map/pallas_call | solution.py:84
  39.3 5.8 %all-to-all-start.1 = ((bf16[16,64,256]{2,1,0:T(8,128)(2,1)}), bf16[16,64,256]{2,1,0:T(8,128)(2,1)S(1)}, u32[]{:S(2)}, u32[]{:S(2)}) async-start(bf16[16,64,256]{2,1,0:T(8,128)(2,1)} %bitcast.8), calls=%async_computation.1 | async-start | bytes 1048576 | tf_op jit(solution)/shard_map/all_to_all | solution.py:205
  45.1 1.7 fusion.3
  46.8 9.1 %all-to-all-done.1 = bf16[16,64,256]{2,1,0:T(8,128)(2,1)S(1)} async-done(((bf16[16,64,256]{2,1,0:T(8,128)(2,1)}), bf16[16,64,256]{2,1,0:T(8,128)(2,1)S(1)}, u32[]{:S(2)}, u32[]{:S(2)}) %all-to-all-start.1) | async-done | bytes 524320 | tf_op jit(solution)/shard_map/all_to_all | solution.py:205
  55.9 9.4 %all-to-all-start = ((bf16[16,64,512]{2,1,0:T(8,128)(2,1)}), bf16[16,64,512]{2,1,0:T(8,128)(2,1)S(1)}, u32[]{:S(2)}, u32[]{:S(2)}) async-start(bf16[16,64,512]{2,1,0:T(8,128)(2,1)} %bitcast.2), calls=%async_computation | async-start | bytes 2097152 | tf_op jit(solution)/shard_map/all_to_all | solution.py:198
  65.3 12.0 %all-to-all-done = bf16[16,64,512]{2,1,0:T(8,128)(2,1)S(1)} async-done(((bf16[16,64,512]{2,1,0:T(8,128)(2,1)}), bf16[16,64,512]{2,1,0:T(8,128)(2,1)S(1)}, u32[]{:S(2)}, u32[]{:S(2)}) %all-to-all-start) | async-done | bytes 1048608 | tf_op jit(solution)/shard_map/all_to_all | solution.py:198
  78.5 17.1 %shard_map.94 = (bf16[1024,768]{1,0:T(8,128)(2,1)}, f32[2048,768]{1,0:T(8,128)}) custom-call(bf16[1024,768]{1,0:T(8,128)(2,1)} %pad_maximum_fusion.rows_ref, bf16[512,2048]{1,0:T(8,128)(2,1)} %bitcast.72, bf16[2048,256]{1,0:T(8,128)(2,1)} %bitcast.73), custom_call_target="tpu_custom_call" | custom-call | flops 9663676416 | bytes 12582912 | tf_op jit(solution)/shard_map/pallas_call | solution.py:142
  95.5 2.1 constant_dynamic-slice_fusion
  99.2 9.2 %collective-permute-start.8 = (bf16[2,2,2,128,768]{3,4,0,1,2:T(8,128)(2,1)}, bf16[2,2,2,128,768]{3,4,0,1,2:T(8,128)(2,1)S(1)}, u32[]{:S(2)}, u32[]{:S(2)}) collective-permute-start(bf16[2,2,2,128,768]{3,4,0,1,2:T(8,128)(2,1)} %bitcast.67), channel_id=1, source_target_pairs={{0,16},{16,0},{32,48},{48,32},{64,80},{80,64},{96,112},{112,96},{1... | collective-permute-start | bytes 4718600 | tf_op jit(solution)/shard_map/ppermute | solution.py:44
  108.4 9.5 %all-to-all-start.2 = ((bf16[16,64,768]{2,1,0:T(8,128)(2,1)}), bf16[16,64,768]{2,1,0:T(8,128)(2,1)}, u32[]{:S(2)}, u32[]{:S(2)}) async-start(bf16[16,64,768]{2,1,0:T(8,128)(2,1)} %bitcast.66), calls=%async_computation.2 | async-start | bytes 3145728 | tf_op jit(solution)/shard_map/all_to_all | solution.py:213
  117.9 3.8 %constant_dynamic-slice_fusion.1 = f32[2,2,2,1,128,768]{5,4,3,2,1,0:T(8,128)} fusion(f32[2,2,2,2,128,768]{5,4,3,2,1,0:T(8,128)} %bitcast.64, s32[]{:T(128)S(6)} %select_n.28), kind=kLoop, calls=%fused_computation.45 | loop fusion | bytes 6291460 | tf_op jit(solution)/shard_map/jit(dynamic_index_in_dim)/dynamic_slice | solution.py:41
  121.7 3.5 %copy.12 = f32[2,2,2,1,128,768]{4,5,0,1,2,3:T(8,128)} copy(f32[2,2,2,1,128,768]{5,4,3,2,1,0:T(8,128)} %constant_dynamic-slice_fusion.1) | data formatting | bytes 6291456 | tf_op jit(solution)/shard_map/jit(dynamic_index_in_dim)/dynamic_slice | solution.py:41
  125.2 2.1 %bitcast_add_fusion = f32[2,2,2,128,768]{3,4,0,1,2:T(8,128)S(1)} fusion(f32[2,2,2,1,128,768]{4,5,0,1,2,3:T(8,128)} %copy.12, bf16[2,2,2,128,768]{3,4,0,1,2:T(8,128)(2,1)S(1)} %collective-permute-done.8), kind=kLoop, calls=%fused_computation.2 | loop fusion | flops 1572864 | bytes 7864320 | tf_op jit(solution)/shard_map/add | solution.py:45
  127.4 1.6 copy-done.1
  129.1 4.6 %collective-permute-start.9 = (bf16[2,2,128,768]{2,3,0,1:T(8,128)(2,1)S(1)}, bf16[2,2,128,768]{2,3,0,1:T(8,128)(2,1)S(1)}, u32[]{:S(2)}, u32[]{:S(2)}) collective-permute-start(bf16[2,2,128,768]{2,3,0,1:T(8,128)(2,1)S(1)} %fusion.10), channel_id=1, source_target_pairs={{0,32},{16,48},{32,0},{48,16},{64,96},{80,112},{96,64},{112,80},{1... | collective-permute-start | bytes 2359304 | tf_op jit(solution)/shard_map/ppermute | solution.py:44
  133.7 17.5 %collective-permute-done.9 = bf16[2,2,128,768]{2,3,0,1:T(8,128)(2,1)S(1)} collective-permute-done((bf16[2,2,128,768]{2,3,0,1:T(8,128)(2,1)S(1)}, bf16[2,2,128,768]{2,3,0,1:T(8,128)(2,1)S(1)}, u32[]{:S(2)}, u32[]{:S(2)}) %collective-permute-start.9) | collective-permute-done | bytes 786464 | tf_op jit(solution)/shard_map/ppermute | solution.py:44
  153.9 10.1 %collective-permute-done.10 = bf16[2,128,768]{1,2,0:T(8,128)(2,1)S(1)} collective-permute-done((bf16[2,128,768]{1,2,0:T(8,128)(2,1)S(1)}, bf16[2,128,768]{1,2,0:T(8,128)(2,1)S(1)}, u32[]{:S(2)}, u32[]{:S(2)}) %collective-permute-start.10) | collective-permute-done | bytes 393248 | tf_op jit(solution)/shard_map/ppermute | solution.py:44
  164.4 2.6 %fusion.4 = bf16[512,768]{1,0:T(8,128)(2,1)S(1)} fusion(bf16[1024,768]{1,0:T(8,128)(2,1)} %bitcast.13, s32[512]{0:T(512)S(1)} %add_add_fusion), kind=kOutput, calls=%fused_computation.12 | convolution fusion | flops 806223872 | bytes 2361344 | tf_op jit(solution)/shard_map/dot_general | solution.py:216
  167.1 5.7 %collective-permute-start.4 = (bf16[1,4,128,256]{3,2,1,0:T(8,128)(2,1)S(1)}, bf16[1,4,128,256]{3,2,1,0:T(8,128)(2,1)S(1)}, u32[]{:S(2)}, u32[]{:S(2)}) collective-permute-start(bf16[1,4,128,256]{3,2,1,0:T(8,128)(2,1)S(1)} %bitcast.58), channel_id=1, source_target_pairs={{0,16},{16,32},{32,48},{48,64},{64,80},{80,96},{96,112},{112,128},... | collective-permute-start | bytes 786440 | tf_op jit(solution)/shard_map/ppermute | solution.py:18
  172.8 1.9 collective-permute-start.5
  176.4 6.2 %collective-permute-done.5 = bf16[1,4,128,256]{3,2,1,0:T(8,128)(2,1)S(1)} collective-permute-done((bf16[1,4,128,256]{3,2,1,0:T(8,128)(2,1)S(1)}, bf16[1,4,128,256]{3,2,1,0:T(8,128)(2,1)S(1)}, u32[]{:S(2)}, u32[]{:S(2)}) %collective-permute-start.5) | collective-permute-done | bytes 262176 | tf_op jit(solution)/shard_map/ppermute | solution.py:19
  182.7 5.2 %collective-permute-start.6 = (bf16[3,1,128,256]{3,2,1,0:T(8,128)(2,1)S(1)}, bf16[3,1,128,256]{3,2,1,0:T(8,128)(2,1)S(1)}, u32[]{:S(2)}, u32[]{:S(2)}) collective-permute-start(bf16[3,1,128,256]{3,2,1,0:T(8,128)(2,1)S(1)} %get-tuple-element.18), channel_id=1, source_target_pairs={{0,1},{1,2},{2,3},{3,4},{4,5},{5,6},{6,7},{7,8},{8,9},{9,10},{10,1... | collective-permute-start | bytes 589832 | tf_op jit(solution)/shard_map/ppermute | solution.py:18
  187.9 1.9 collective-permute-start.7
  190.8 8.7 %collective-permute-done.7 = bf16[3,1,128,256]{3,2,1,0:T(8,128)(2,1)S(1)} collective-permute-done((bf16[3,1,128,256]{3,2,1,0:T(8,128)(2,1)S(1)}, bf16[3,1,128,256]{3,2,1,0:T(8,128)(2,1)S(1)}, u32[]{:S(2)}, u32[]{:S(2)}) %collective-permute-start.7) | collective-permute-done | bytes 196640 | tf_op jit(solution)/shard_map/ppermute | solution.py:19
  201.0 4.7 %shard_map.95 = bf16[512,256]{1,0:T(8,128)(2,1)} custom-call(bf16[1,3,3,6,128,256]{5,4,3,2,1,0:T(8,128)(2,1)S(1)} %maximum_bitcast_fusion.1.shifted_ref, bf16[27,256,256]{2,1,0:T(8,128)(2,1)} %taps_ref.3), custom_call_target="tpu_custom_call" | custom-call | flops 1811939328 | bytes 7340032 | tf_op jit(solution)/shard_map/pallas_call | solution.py:84
  (41 shorter events, 15.4 us)
Async XLA Ops:
  0.6 44.5 %copy-start = (bf16[1,4,128,512]{3,2,1,0:T(8,128)(2,1)S(1)}, bf16[1,4,128,512]{3,2,1,0:T(8,128)(2,1)}, u32[]{:S(2)}) copy-start(bf16[1,4,128,512]{3,2,1,0:T(8,128)(2,1)} %param.6) | copy-start | bytes 1572868
  0.6 21.1 %copy-start.2 = (s32[1,4,128,1]{2,3,1,0:T(1,128)S(1)}, s32[1,4,128,1]{2,3,1,0:T(1,128)}, u32[]{:S(2)}) copy-start(s32[1,4,128,1]{2,3,1,0:T(1,128)} %param.7) | copy-start | bytes 6148
  0.7 7.5 %collective-permute-start = (bf16[1,4,128,256]{3,2,1,0:T(8,128)(2,1)}, bf16[1,4,128,256]{3,2,1,0:T(8,128)(2,1)S(1)}, u32[]{:S(2)}, u32[]{:S(2)}) collective-permute-start(bf16[1,4,128,256]{3,2,1,0:T(8,128)(2,1)} %param.11), channel_id=1, source_target_pairs={{0,16},{16,32},{32,48},{48,64},{64,80},{80,96},{96,112},{112,128},... | collective-permute-start | bytes 786440 | tf_op jit(solution)/shard_map/ppermute | solution.py:18
  4.6 10.0 %collective-permute-start.1 = (bf16[1,4,128,256]{3,2,1,0:T(8,128)(2,1)}, bf16[1,4,128,256]{3,2,1,0:T(8,128)(2,1)S(1)}, u32[]{:S(2)}, u32[]{:S(2)}) collective-permute-start(bf16[1,4,128,256]{3,2,1,0:T(8,128)(2,1)} %param.11), channel_id=1, source_target_pairs={{16,0},{32,16},{48,32},{64,48},{80,64},{96,80},{112,96},{128,112},... | collective-permute-start | bytes 786440 | tf_op jit(solution)/shard_map/ppermute | solution.py:19
  14.6 9.9 %collective-permute-start.2 = (bf16[3,1,128,256]{3,2,1,0:T(8,128)(2,1)S(1)}, bf16[3,1,128,256]{3,2,1,0:T(8,128)(2,1)S(1)}, u32[]{:S(2)}, u32[]{:S(2)}) collective-permute-start(bf16[3,1,128,256]{3,2,1,0:T(8,128)(2,1)S(1)} %get-tuple-element.20), channel_id=1, source_target_pairs={{0,1},{1,2},{2,3},{3,4},{4,5},{5,6},{6,7},{7,8},{8,9},{9,10},{10,1... | collective-permute-start | bytes 589832 | tf_op jit(solution)/shard_map/ppermute | solution.py:18
  19.8 13.0 %collective-permute-start.3 = (bf16[3,1,128,256]{3,2,1,0:T(8,128)(2,1)S(1)}, bf16[3,1,128,256]{3,2,1,0:T(8,128)(2,1)S(1)}, u32[]{:S(2)}, u32[]{:S(2)}) collective-permute-start(bf16[3,1,128,256]{3,2,1,0:T(8,128)(2,1)S(1)} %get-tuple-element.21), channel_id=1, source_target_pairs={{1,0},{2,1},{3,2},{4,3},{5,4},{6,5},{7,6},{8,7},{9,8},{10,9},{11,1... | collective-permute-start | bytes 589832 | tf_op jit(solution)/shard_map/ppermute | solution.py:19
  39.3 16.5 %all-to-all-start.1 = ((bf16[16,64,256]{2,1,0:T(8,128)(2,1)}), bf16[16,64,256]{2,1,0:T(8,128)(2,1)S(1)}, u32[]{:S(2)}, u32[]{:S(2)}) async-start(bf16[16,64,256]{2,1,0:T(8,128)(2,1)} %bitcast.8), calls=%async_computation.1 | async-start | bytes 1048576 | tf_op jit(solution)/shard_map/all_to_all | solution.py:205
  55.9 21.4 %all-to-all-start = ((bf16[16,64,512]{2,1,0:T(8,128)(2,1)}), bf16[16,64,512]{2,1,0:T(8,128)(2,1)S(1)}, u32[]{:S(2)}, u32[]{:S(2)}) async-start(bf16[16,64,512]{2,1,0:T(8,128)(2,1)} %bitcast.2), calls=%async_computation | async-start | bytes 2097152 | tf_op jit(solution)/shard_map/all_to_all | solution.py:198
  99.2 26.0 %collective-permute-start.8 = (bf16[2,2,2,128,768]{3,4,0,1,2:T(8,128)(2,1)}, bf16[2,2,2,128,768]{3,4,0,1,2:T(8,128)(2,1)S(1)}, u32[]{:S(2)}, u32[]{:S(2)}) collective-permute-start(bf16[2,2,2,128,768]{3,4,0,1,2:T(8,128)(2,1)} %bitcast.67), channel_id=1, source_target_pairs={{0,16},{16,0},{32,48},{48,32},{64,80},{80,64},{96,112},{112,96},{1... | collective-permute-start | bytes 4718600 | tf_op jit(solution)/shard_map/ppermute | solution.py:44
  108.4 56.1 %all-to-all-start.2 = ((bf16[16,64,768]{2,1,0:T(8,128)(2,1)}), bf16[16,64,768]{2,1,0:T(8,128)(2,1)}, u32[]{:S(2)}, u32[]{:S(2)}) async-start(bf16[16,64,768]{2,1,0:T(8,128)(2,1)} %bitcast.66), calls=%async_computation.2 | async-start | bytes 3145728 | tf_op jit(solution)/shard_map/all_to_all | solution.py:213
  127.4 1.6 copy-start.1
  129.1 22.1 %collective-permute-start.9 = (bf16[2,2,128,768]{2,3,0,1:T(8,128)(2,1)S(1)}, bf16[2,2,128,768]{2,3,0,1:T(8,128)(2,1)S(1)}, u32[]{:S(2)}, u32[]{:S(2)}) collective-permute-start(bf16[2,2,128,768]{2,3,0,1:T(8,128)(2,1)S(1)} %fusion.10), channel_id=1, source_target_pairs={{0,32},{16,48},{32,0},{48,16},{64,96},{80,112},{96,64},{112,80},{1... | collective-permute-start | bytes 2359304 | tf_op jit(solution)/shard_map/ppermute | solution.py:44
  152.8 11.2 %collective-permute-start.10 = (bf16[2,128,768]{1,2,0:T(8,128)(2,1)S(1)}, bf16[2,128,768]{1,2,0:T(8,128)(2,1)S(1)}, u32[]{:S(2)}, u32[]{:S(2)}) collective-permute-start(bf16[2,128,768]{1,2,0:T(8,128)(2,1)S(1)} %fusion.11), channel_id=1, source_target_pairs={{0,64},{16,80},{32,96},{48,112},{64,0},{80,16},{96,32},{112,48},{1... | collective-permute-start | bytes 1179656 | tf_op jit(solution)/shard_map/ppermute | solution.py:44
  164.1 10.6 %collective-permute-start.11 = (bf16[128,768]{0,1:T(8,128)(2,1)S(1)}, bf16[128,768]{0,1:T(8,128)(2,1)S(1)}, u32[]{:S(2)}, u32[]{:S(2)}) collective-permute-start(bf16[128,768]{0,1:T(8,128)(2,1)S(1)} %fusion.12), channel_id=1, source_target_pairs={{0,128},{16,144},{32,160},{48,176},{64,192},{80,208},{96,224},{112... | collective-permute-start | bytes 589832 | tf_op jit(solution)/shard_map/ppermute | solution.py:44
  167.1 9.3 %collective-permute-start.4 = (bf16[1,4,128,256]{3,2,1,0:T(8,128)(2,1)S(1)}, bf16[1,4,128,256]{3,2,1,0:T(8,128)(2,1)S(1)}, u32[]{:S(2)}, u32[]{:S(2)}) collective-permute-start(bf16[1,4,128,256]{3,2,1,0:T(8,128)(2,1)S(1)} %bitcast.58), channel_id=1, source_target_pairs={{0,16},{16,32},{32,48},{48,64},{64,80},{80,96},{96,112},{112,128},... | collective-permute-start | bytes 786440 | tf_op jit(solution)/shard_map/ppermute | solution.py:18
  172.8 9.8 %collective-permute-start.5 = (bf16[1,4,128,256]{3,2,1,0:T(8,128)(2,1)S(1)}, bf16[1,4,128,256]{3,2,1,0:T(8,128)(2,1)S(1)}, u32[]{:S(2)}, u32[]{:S(2)}) collective-permute-start(bf16[1,4,128,256]{3,2,1,0:T(8,128)(2,1)S(1)} %bitcast.59), channel_id=1, source_target_pairs={{16,0},{32,16},{48,32},{64,48},{80,64},{96,80},{112,96},{128,112},... | collective-permute-start | bytes 786440 | tf_op jit(solution)/shard_map/ppermute | solution.py:19
  182.7 8.2 %collective-permute-start.6 = (bf16[3,1,128,256]{3,2,1,0:T(8,128)(2,1)S(1)}, bf16[3,1,128,256]{3,2,1,0:T(8,128)(2,1)S(1)}, u32[]{:S(2)}, u32[]{:S(2)}) collective-permute-start(bf16[3,1,128,256]{3,2,1,0:T(8,128)(2,1)S(1)} %get-tuple-element.18), channel_id=1, source_target_pairs={{0,1},{1,2},{2,3},{3,4},{4,5},{5,6},{6,7},{7,8},{8,9},{9,10},{10,1... | collective-permute-start | bytes 589832 | tf_op jit(solution)/shard_map/ppermute | solution.py:18
  187.9 11.7 %collective-permute-start.7 = (bf16[3,1,128,256]{3,2,1,0:T(8,128)(2,1)S(1)}, bf16[3,1,128,256]{3,2,1,0:T(8,128)(2,1)S(1)}, u32[]{:S(2)}, u32[]{:S(2)}) collective-permute-start(bf16[3,1,128,256]{3,2,1,0:T(8,128)(2,1)S(1)} %get-tuple-element.19), channel_id=1, source_target_pairs={{1,0},{2,1},{3,2},{4,3},{5,4},{6,5},{7,6},{8,7},{9,8},{10,9},{11,1... | collective-permute-start | bytes 589832 | tf_op jit(solution)/shard_map/ppermute | solution.py:19

commit v5 on v4

--- a/solution.py
+++ b/solution.py
@@ -72,8 +72,29 @@
     out_ref[...] = acc_ref[...].astype(out_ref.dtype)
 
 
+def halo(grid):
+    slabs, experts = lax.axis_size("dp"), lax.axis_size("expert")
+    block = grid[0]
+    last, first = block[-1:], block[:1]
+
+    def moved(value, step_dp, step_expert):
+        pairs = []
+        for d in range(slabs):
+            for e in range(experts):
+                dd, ee = d + step_dp, e + step_expert
+                if 0 <= dd < slabs and 0 <= ee < experts:
+                    pairs.append((d * experts + e, dd * experts + ee))
+        return lax.ppermute(value, ("dp", "expert"), pairs)
+
+    lower = [moved(last, 1, 1), moved(block, 1, 0), moved(first, 1, -1)]
+    middle = [moved(last, 0, 1), block, moved(first, 0, -1)]
+    upper = [moved(last, -1, 1), moved(block, -1, 0), moved(first, -1, -1)]
+    planes = [jnp.concatenate(side, axis=0) for side in (lower, middle, upper)]
+    return jnp.stack(planes, axis=0)
+
+
 def conv_block(grid, kernel, flip):
-    padded = extended(grid, (("dp", 0), ("expert", 1)), 1)
+    padded = halo(grid)
     padded = jnp.pad(padded, ((0, 0), (0, 0), (1, 1), (0, 0)))
     depth_cells = grid.shape[2]
     shifted = jnp.stack(
@@ -97,7 +118,7 @@
 
 
 def expert_kernel(
-    cols, rows_ref, first_ref, second_ref, back_ref, part_ref, result_acc, input_acc
+    cols, rows_ref, first_ref, second_ref, prior_ref, back_ref, part_ref, result_acc, input_acc
 ):
     step = pl.program_id(0)
 
@@ -120,10 +141,10 @@
     input_acc[...] += lax.dot_general(
         gate_grad, first, (((1,), (1,)), ((), ())), preferred_element_type=jnp.float32
     )
-    part_ref[:, :cols] = lax.dot_general(
+    part_ref[:, :cols] = prior_ref[:, :cols] + lax.dot_general(
         gate_grad, rows, (((0,), (0,)), ((), ())), preferred_element_type=jnp.float32
     )
-    part_ref[:, cols:] = lax.dot_general(
+    part_ref[:, cols:] = prior_ref[:, cols:] + lax.dot_general(
         activation, grads, (((0,), (0,)), ((), ())), preferred_element_type=jnp.float32
     )
 
@@ -134,7 +155,7 @@
         back_ref[:, width:] = input_acc[...].astype(back_ref.dtype)
 
 
-def expert(inbound, weight_one, weight_two, chunk):
+def expert(inbound, weight_one, weight_two, prior, chunk):
     slots, both = inbound.shape
     cols, hidden = weight_one.shape
     channels = weight_two.shape[1]
@@ -146,6 +167,7 @@
             pl.BlockSpec((slots, both), lambda h: (0, 0)),
             pl.BlockSpec((cols, chunk), lambda h: (0, h)),
             pl.BlockSpec((chunk, channels), lambda h: (h, 0)),
+            pl.BlockSpec((chunk, both), lambda h: (h, 0)),
         ],
         out_specs=[
             pl.BlockSpec((slots, both), lambda h: (0, 0)),
@@ -159,15 +181,16 @@
             pltpu.VMEM((slots, channels), jnp.float32),
             pltpu.VMEM((slots, cols), jnp.float32),
         ],
+        input_output_aliases={3: 1},
         compiler_params=pltpu.CompilerParams(
             dimension_semantics=("arbitrary",), vmem_limit_bytes=56 * 1024 * 1024
         ),
         cost_estimate=pl.CostEstimate(
             flops=flops,
             transcendentals=slots * hidden,
-            bytes_accessed=2 * (2 * slots * both + hidden * (cols + channels)) + 4 * hidden * both,
+            bytes_accessed=2 * (2 * slots * both + hidden * (cols + channels)) + 8 * hidden * both,
         ),
-    )(inbound, weight_one, weight_two)
+    )(inbound, weight_one, weight_two, prior)
 
 
 def per_device(feats, labels, w_first, w_second, kernel, cotangent):
@@ -195,24 +218,35 @@
 
     flat_feats = feats.reshape(patch_count, feat_width)
     outbound = jnp.dot(route, flat_feats, preferred_element_type=jnp.float32).astype(jnp.bfloat16)
-    received = lax.all_to_all(
-        outbound.reshape(experts, capacity, feat_width), "expert", split_axis=0, concat_axis=0, tiled=True
-    )
+    outbound = outbound.reshape(experts, capacity, feat_width)
     field_rows = conv_block(cotangent, kernel, True)
     grad_outbound = jnp.dot(route, field_rows, preferred_element_type=jnp.float32).astype(
         jnp.bfloat16
     )
-    grad_inbound = lax.all_to_all(
-        grad_outbound.reshape(experts, capacity, channels), "expert", split_axis=0, concat_axis=0, tiled=True
-    )
+    grad_outbound = grad_outbound.reshape(experts, capacity, channels)
     both = feat_width + channels
-    inbound = jnp.concatenate(
-        [received.reshape(slots, feat_width), grad_inbound.reshape(slots, channels)], axis=1
-    )
-    back, part = expert(inbound, w_first[0], w_second[0], 512)
-    returned = lax.all_to_all(
-        back.reshape(experts, capacity, both), "expert", split_axis=0, concat_axis=0, tiled=True
-    )
+    half = capacity // 2
+    part = jnp.zeros((hidden, both), jnp.float32)
+    backs = []
+    for piece in range(2):
+        window = slice(piece * half, (piece + 1) * half)
+        received = lax.all_to_all(
+            outbound[:, window], "expert", split_axis=0, concat_axis=0, tiled=True
+        )
+        grad_inbound = lax.all_to_all(
+            grad_outbound[:, window], "expert", split_axis=0, concat_axis=0, tiled=True
+        )
+        inbound = jnp.concatenate(
+            [received.reshape(slots // 2, feat_width), grad_inbound.reshape(slots // 2, channels)],
+            axis=1,
+        )
+        back, part = expert(inbound, w_first[0], w_second[0], part, 512)
+        backs.append(
+            lax.all_to_all(
+                back.reshape(experts, half, both), "expert", split_axis=0, concat_axis=0, tiled=True
+            )
+        )
+    returned = jnp.concatenate(backs, axis=1)
     mixed = lax.dot_general(
         route,
         returned.reshape(slots, both),

time: 208 us -> 262 us (1.26)
  blocking collectives: 0 us -> 41.7 us
  starting transfers between devices: 67.4 us -> 108 us
  waiting for transfers between devices: 81 us -> 43.9 us
  Pallas kernels: 25.8 us -> 31.4 us
  local copies, waits for them, and re-layouts: 17.4 us -> 21.1 us
  matrix products: 6.63 us -> 3.44 us
    ppermute x8 -> x16, starting transfers between devices: 27.6 us -> 70.9 us  [moved(): return lax.ppermute(value, ('dp', 'expert'), pairs)]
    all_to_all x0 -> x2, blocking collectives: none -> 41.7 us  [the longest x1 22.1 us: per_device(): lax.all_to_all(outbound[:, window], 'expert', split_axis=0, concat_axis=0...]
    ppermute x8 -> x16, waiting for transfers between devices: 32.4 us -> 2.08 us  [moved(): return lax.ppermute(value, ('dp', 'expert'), pairs)]
    ppermute x4, waiting for transfers between devices: 27.6 us -> 10.6 us  [tree_scatter(): got = lax.ppermute(send.astype(jnp.bfloat16), 'dp', pairs)]
    all_to_all x3 -> x4, waiting for transfers between devices: 21.1 us -> 31.3 us  [the longest x2 16.8 us: per_device(): lax.all_to_all(back.reshape(experts, half, both), 'expert', split_axis=0,...]
    ppermute x4, starting transfers between devices: 15.1 us -> 8.35 us  [tree_scatter(): got = lax.ppermute(send.astype(jnp.bfloat16), 'dp', pairs)]
    pallas_call x1 -> x2, Pallas kernels: 17.1 us -> 22.7 us  [expert(): pl.pallas_call(functools.partial(expert_kernel, cols), grid=(hidden // ch...]
    all_to_all x3 -> x4, starting transfers between devices: 24.7 us -> 29.1 us  [the longest x2 16.5 us: per_device(): lax.all_to_all(back.reshape(experts, half, both), 'expert', split_axis=0,...]
  transfers between devices with their start and end apart: 15 -> 24, of which waited for: 11 -> 6; matrix products, arithmetic and copies ran while one was open for 10% -> 9% of each run, Pallas kernels for 0% -> 2%
where the time goes in v5:
time: 262 us; the launch traced here: 260 us
  starting transfers between devices  108 us (41%)
  waiting for transfers between devices  43.9 us (17%)
  blocking collectives  41.7 us (16%)
  Pallas kernels  31.4 us (12%)
  local copies, waits for them, and re-layouts  21.1 us (8%)
  other arithmetic  8.45 us (3%)
  matrix products  3.44 us (1%)
    ppermute x16, starting transfers between devices, moved(): return lax.ppermute(value, ('dp', 'expert'), pairs)  70.9 us
    pallas_call x2, Pallas kernels, expert(): pl.pallas_call(functools.partial(expert_kernel, cols), grid=(hidden // ch...  22.7 us
    all_to_all x1, blocking collectives, per_device(): lax.all_to_all(outbound[:, window], 'expert', split_axis=0, concat_axis=0...  22.1 us
    all_to_all x1, blocking collectives, per_device(): lax.all_to_all(grad_outbound[:, window], 'expert', split_axis=0, concat_a...  19.6 us
    all_to_all x2, waiting for transfers between devices, per_device(): lax.all_to_all(back.reshape(experts, half, both), 'expert', split_axis=0,...  16.8 us
    all_to_all x2, starting transfers between devices, per_device(): lax.all_to_all(back.reshape(experts, half, both), 'expert', split_axis=0,...  16.5 us
    ppermute x4, waiting for transfers between devices, tree_scatter(): got = lax.ppermute(send.astype(jnp.bfloat16), 'dp', pairs)  10.6 us
    pallas_call x2, Pallas kernels, conv_block(): pl.pallas_call(functools.partial(conv_kernel, flip), out_shape=jax.ShapeD...  8.77 us
  transfers between devices with their start and end apart: 24, of which 6 were waited for; matrix products, arithmetic and copies ran while one was open for 9% of the time, Pallas kernels for 2%

profile of v5, /device:TPU:95, one launch (start us, length us, event | category | flops | bytes accessed | tf_op | source)
XLA Modules:
  0.0 259.6 jit_solution(1435883093418881534)
XLA Ops:
  1.6 3.0 %collective-permute-start.7 = (bf16[1,128,256]{2,1,0:T(8,128)(2,1)S(1)}, bf16[1,128,256]{2,1,0:T(8,128)(2,1)S(1)}, u32[]{:S(2)}, u32[]{:S(2)}) collective-permute-start(bf16[1,128,256]{2,1,0:T(8,128)(2,1)S(1)} %get-tuple-element.31), channel_id=1, source_target_pairs={{17,0},{18,1},{19,2},{20,3},{21,4},{22,5},{23,6},{24,7},{25,8},{26... | collective-permute-start | bytes 196616 | tf_op jit(solution)/shard_map/ppermute | solution.py:87
  4.6 2.2 collective-permute-start.4
  6.8 2.2 collective-permute-start.6
  9.0 5.5 %collective-permute-start.1 = (bf16[4,128,256]{2,1,0:T(8,128)(2,1)}, bf16[4,128,256]{2,1,0:T(8,128)(2,1)S(1)}, u32[]{:S(2)}, u32[]{:S(2)}) collective-permute-start(bf16[4,128,256]{2,1,0:T(8,128)(2,1)} %bitcast.95), channel_id=1, source_target_pairs={{0,16},{1,17},{2,18},{3,19},{4,20},{5,21},{6,22},{7,23},{8,24},{9,... | collective-permute-start | bytes 786440 | tf_op jit(solution)/shard_map/ppermute | solution.py:87
  14.5 7.3 %collective-permute-start.3 = (bf16[1,128,256]{2,1,0:T(8,128)(2,1)S(1)}, bf16[1,128,256]{2,1,0:T(8,128)(2,1)S(1)}, u32[]{:S(2)}, u32[]{:S(2)}) collective-permute-start(bf16[1,128,256]{2,1,0:T(8,128)(2,1)S(1)} %get-tuple-element.30), channel_id=1, source_target_pairs={{0,1},{1,2},{2,3},{3,4},{4,5},{5,6},{6,7},{7,8},{8,9},{9,10},{10,1... | collective-permute-start | bytes 196616 | tf_op jit(solution)/shard_map/ppermute | solution.py:87
  25.5 6.7 %collective-permute-start.2 = (bf16[1,128,256]{2,1,0:T(8,128)(2,1)S(1)}, bf16[1,128,256]{2,1,0:T(8,128)(2,1)S(1)}, u32[]{:S(2)}, u32[]{:S(2)}) collective-permute-start(bf16[1,128,256]{2,1,0:T(8,128)(2,1)S(1)} %get-tuple-element.31), channel_id=1, source_target_pairs={{1,16},{2,17},{3,18},{4,19},{5,20},{6,21},{7,22},{8,23},{9,24},{10... | collective-permute-start | bytes 196616 | tf_op jit(solution)/shard_map/ppermute | solution.py:87
  33.1 4.0 %collective-permute-start = (bf16[1,128,256]{2,1,0:T(8,128)(2,1)S(1)}, bf16[1,128,256]{2,1,0:T(8,128)(2,1)S(1)}, u32[]{:S(2)}, u32[]{:S(2)}) collective-permute-start(bf16[1,128,256]{2,1,0:T(8,128)(2,1)S(1)} %get-tuple-element.30), channel_id=1, source_target_pairs={{0,17},{1,18},{2,19},{3,20},{4,21},{5,22},{6,23},{7,24},{8,25},{9,... | collective-permute-start | bytes 196616 | tf_op jit(solution)/shard_map/ppermute | solution.py:87
  40.0 4.0 %shard_map.93 = bf16[512,256]{1,0:T(8,128)(2,1)S(1)} custom-call(bf16[1,3,3,6,128,256]{5,4,3,2,1,0:T(8,128)(2,1)S(1)} %maximum_bitcast_fusion.shifted_ref, bf16[27,256,256]{2,1,0:T(8,128)(2,1)} %taps_ref.3), custom_call_target="tpu_custom_call" | custom-call | flops 1811939328 | bytes 7340032 | tf_op jit(solution)/shard_map/pallas_call | solution.py:105
  45.3 19.6 %all_to_all.30 = bf16[16,32,256]{2,1,0:T(8,128)(2,1)S(1)} all-to-all(bf16[16,32,256]{2,1,0:T(8,128)(2,1)S(1)} %get-tuple-element.29), channel_id=1, replica_groups=mesh['dp'=16,'expert'=16] {'expert'}, dimensions={0} | all-to-all | bytes 524288 | tf_op jit(solution)/shard_map/all_to_all | solution.py:236
  64.9 6.3 %all-to-all-start.1 = ((bf16[16,32,256]{2,1,0:T(8,128)(2,1)}), bf16[16,32,256]{2,1,0:T(8,128)(2,1)S(1)}, u32[]{:S(2)}, u32[]{:S(2)}) async-start(bf16[16,32,256]{2,1,0:T(8,128)(2,1)} %get-tuple-element.28), calls=%async_computation.1 | async-start | bytes 524288 | tf_op jit(solution)/shard_map/all_to_all | solution.py:236
  72.8 6.4 %all-to-all-done.1 = bf16[16,32,256]{2,1,0:T(8,128)(2,1)S(1)} async-done(((bf16[16,32,256]{2,1,0:T(8,128)(2,1)}), bf16[16,32,256]{2,1,0:T(8,128)(2,1)S(1)}, u32[]{:S(2)}, u32[]{:S(2)}) %all-to-all-start.1) | async-done | bytes 262176 | tf_op jit(solution)/shard_map/all_to_all | solution.py:236
  79.2 22.1 %all_to_all.31 = bf16[16,32,512]{2,1,0:T(8,128)(2,1)S(1)} all-to-all(bf16[16,32,512]{2,1,0:T(8,128)(2,1)S(1)} %get-tuple-element.25), channel_id=1, replica_groups=mesh['dp'=16,'expert'=16] {'expert'}, dimensions={0} | all-to-all | bytes 1048576 | tf_op jit(solution)/shard_map/all_to_all | solution.py:233
  101.3 6.3 %all-to-all-start = ((bf16[16,32,512]{2,1,0:T(8,128)(2,1)}), bf16[16,32,512]{2,1,0:T(8,128)(2,1)S(1)}, u32[]{:S(2)}, u32[]{:S(2)}) async-start(bf16[16,32,512]{2,1,0:T(8,128)(2,1)} %get-tuple-element.24), calls=%async_computation | async-start | bytes 1048576 | tf_op jit(solution)/shard_map/all_to_all | solution.py:233
  108.6 8.0 %all-to-all-done = bf16[16,32,512]{2,1,0:T(8,128)(2,1)S(1)} async-done(((bf16[16,32,512]{2,1,0:T(8,128)(2,1)}), bf16[16,32,512]{2,1,0:T(8,128)(2,1)S(1)}, u32[]{:S(2)}, u32[]{:S(2)}) %all-to-all-start) | async-done | bytes 524320 | tf_op jit(solution)/shard_map/all_to_all | solution.py:233
  117.6 3.0 %broadcast_in_dim.21.prior_ref = f32[2048,768]{1,0:T(8,128)} broadcast(f32[]{:T(128)} %constant.42.clone.1), dimensions={} | broadcast | bytes 6291460 | tf_op jit(solution)/shard_map/broadcast_in_dim | solution.py:229
  120.7 11.3 %shard_map.94 = (bf16[512,768]{1,0:T(8,128)(2,1)}, f32[2048,768]{1,0:T(8,128)}) custom-call(bf16[512,768]{1,0:T(8,128)(2,1)} %pad_maximum_fusion.3.rows_ref, bf16[512,2048]{1,0:T(8,128)(2,1)} %bitcast.102, bf16[2048,256]{1,0:T(8,128)(2,1)} %bitcast.104, f32[2048,768]{1,0:T(8,128)} %broadcast_in_dim.21.prior_ref), custom_call_target="tpu_custom_call", output_to_operand_aliasing={{1}: (3, {})} | custom-call | flops 4831838208 | bytes 17301504 | tf_op jit(solution)/shard_map/pallas_call | solution.py:163
  132.0 11.4 %shard_map.95 = (bf16[512,768]{1,0:T(8,128)(2,1)}, f32[2048,768]{1,0:T(8,128)}) custom-call(bf16[512,768]{1,0:T(8,128)(2,1)} %pad_maximum_fusion.4.rows_ref, bf16[512,2048]{1,0:T(8,128)(2,1)} %bitcast.103, bf16[2048,256]{1,0:T(8,128)(2,1)} %bitcast.105, f32[2048,768]{1,0:T(8,128)} %get-tuple-element.9.prior_ref), custom_call_target="tpu_custom_call", output_to_operand_aliasing={{1}: (3, {})} | custom-call | flops 4831838208 | bytes 17301504 | tf_op jit(solution)/shard_map/pallas_call | solution.py:163
  143.3 8.9 %all-to-all-start.5 = ((bf16[16,32,768]{2,1,0:T(8,128)(2,1)}), bf16[16,32,768]{2,1,0:T(8,128)(2,1)S(1)}, u32[]{:S(2)}, u32[]{:S(2)}) async-start(bf16[16,32,768]{2,1,0:T(8,128)(2,1)} %bitcast.93), calls=%async_computation.5 | async-start | bytes 1572864 | tf_op jit(solution)/shard_map/all_to_all | solution.py:245
  152.2 16.8 %all-to-all-done.5 = bf16[16,32,768]{2,1,0:T(8,128)(2,1)S(1)} async-done(((bf16[16,32,768]{2,1,0:T(8,128)(2,1)}), bf16[16,32,768]{2,1,0:T(8,128)(2,1)S(1)}, u32[]{:S(2)}, u32[]{:S(2)}) %all-to-all-start.5) | async-done | bytes 786464 | tf_op jit(solution)/shard_map/all_to_all | solution.py:245
  169.0 7.6 %all-to-all-start.2 = ((bf16[16,32,768]{2,1,0:T(8,128)(2,1)}), bf16[16,32,768]{2,1,0:T(8,128)(2,1)}, u32[]{:S(2)}, u32[]{:S(2)}) async-start(bf16[16,32,768]{2,1,0:T(8,128)(2,1)} %bitcast.18), calls=%async_computation.2 | async-start | bytes 1572864 | tf_op jit(solution)/shard_map/all_to_all | solution.py:245
  180.3 2.5 collective-permute-start.16
  182.8 3.8 %constant_dynamic-slice_fusion.1 = f32[2,2,2,1,128,768]{5,4,3,2,1,0:T(8,128)} fusion(f32[2,2,2,2,128,768]{5,4,3,2,1,0:T(8,128)} %bitcast.82, s32[]{:T(128)S(6)} %select_n.28), kind=kLoop, calls=%fused_computation.51 | loop fusion | bytes 6291460 | tf_op jit(solution)/shard_map/jit(dynamic_index_in_dim)/dynamic_slice | solution.py:41
  186.6 3.5 %copy.14 = f32[2,2,2,1,128,768]{4,5,0,1,2,3:T(8,128)} copy(f32[2,2,2,1,128,768]{5,4,3,2,1,0:T(8,128)} %constant_dynamic-slice_fusion.1) | data formatting | bytes 6291456 | tf_op jit(solution)/shard_map/jit(dynamic_index_in_dim)/dynamic_slice | solution.py:41
  192.7 5.7 %collective-permute-start.17 = (bf16[2,2,128,768]{2,3,0,1:T(8,128)(2,1)S(1)}, bf16[2,2,128,768]{2,3,0,1:T(8,128)(2,1)S(1)}, u32[]{:S(2)}, u32[]{:S(2)}) collective-permute-start(bf16[2,2,128,768]{2,3,0,1:T(8,128)(2,1)S(1)} %fusion.10), channel_id=1, source_target_pairs={{0,32},{16,48},{32,0},{48,16},{64,96},{80,112},{96,64},{112,80},{1... | collective-permute-start | bytes 2359304 | tf_op jit(solution)/shard_map/ppermute | solution.py:44
  199.7 4.7 %collective-permute-start.14 = (bf16[4,128,256]{2,1,0:T(8,128)(2,1)S(1)}, bf16[4,128,256]{2,1,0:T(8,128)(2,1)S(1)}, u32[]{:S(2)}, u32[]{:S(2)}) collective-permute-start(bf16[4,128,256]{2,1,0:T(8,128)(2,1)S(1)} %bitcast.87), channel_id=1, source_target_pairs={{16,0},{17,1},{18,2},{19,3},{20,4},{21,5},{22,6},{23,7},{24,8},{25... | collective-permute-start | bytes 786440 | tf_op jit(solution)/shard_map/ppermute | solution.py:87
  204.4 2.7 %collective-permute-start.12 = (bf16[1,128,256]{2,1,0:T(8,128)(2,1)S(1)}, bf16[1,128,256]{2,1,0:T(8,128)(2,1)S(1)}, u32[]{:S(2)}, u32[]{:S(2)}) collective-permute-start(bf16[1,128,256]{2,1,0:T(8,128)(2,1)S(1)} %get-tuple-element.27), channel_id=1, source_target_pairs={{1,0},{2,1},{3,2},{4,3},{5,4},{6,5},{7,6},{8,7},{9,8},{10,9},{11,1... | collective-permute-start | bytes 196616 | tf_op jit(solution)/shard_map/ppermute | solution.py:87
  207.1 6.8 %collective-permute-start.11 = (bf16[1,128,256]{2,1,0:T(8,128)(2,1)S(1)}, bf16[1,128,256]{2,1,0:T(8,128)(2,1)S(1)}, u32[]{:S(2)}, u32[]{:S(2)}) collective-permute-start(bf16[1,128,256]{2,1,0:T(8,128)(2,1)S(1)} %get-tuple-element.26), channel_id=1, source_target_pairs={{0,1},{1,2},{2,3},{3,4},{4,5},{5,6},{6,7},{7,8},{8,9},{9,10},{10,1... | collective-permute-start | bytes 196616 | tf_op jit(solution)/shard_map/ppermute | solution.py:87
  216.7 7.4 %collective-permute-start.13 = (bf16[1,128,256]{2,1,0:T(8,128)(2,1)S(1)}, bf16[1,128,256]{2,1,0:T(8,128)(2,1)S(1)}, u32[]{:S(2)}, u32[]{:S(2)}) collective-permute-start(bf16[1,128,256]{2,1,0:T(8,128)(2,1)S(1)} %get-tuple-element.26), channel_id=1, source_target_pairs={{16,1},{17,2},{18,3},{19,4},{20,5},{21,6},{22,7},{23,8},{24,9},{25... | collective-permute-start | bytes 196616 | tf_op jit(solution)/shard_map/ppermute | solution.py:87
  226.8 4.6 %collective-permute-start.9 = (bf16[4,128,256]{2,1,0:T(8,128)(2,1)S(1)}, bf16[4,128,256]{2,1,0:T(8,128)(2,1)S(1)}, u32[]{:S(2)}, u32[]{:S(2)}) collective-permute-start(bf16[4,128,256]{2,1,0:T(8,128)(2,1)S(1)} %bitcast.89), channel_id=1, source_target_pairs={{0,16},{1,17},{2,18},{3,19},{4,20},{5,21},{6,22},{7,23},{8,24},{9,... | collective-permute-start | bytes 786440 | tf_op jit(solution)/shard_map/ppermute | solution.py:87
  231.3 8.0 %collective-permute-start.8 = (bf16[1,128,256]{2,1,0:T(8,128)(2,1)S(1)}, bf16[1,128,256]{2,1,0:T(8,128)(2,1)S(1)}, u32[]{:S(2)}, u32[]{:S(2)}) collective-permute-start(bf16[1,128,256]{2,1,0:T(8,128)(2,1)S(1)} %get-tuple-element.26), channel_id=1, source_target_pairs={{0,17},{1,18},{2,19},{3,20},{4,21},{5,22},{6,23},{7,24},{8,25},{9,... | collective-permute-start | bytes 196616 | tf_op jit(solution)/shard_map/ppermute | solution.py:87
  242.1 10.6 %collective-permute-done.18 = bf16[2,128,768]{1,2,0:T(8,128)(2,1)S(1)} collective-permute-done((bf16[2,128,768]{1,2,0:T(8,128)(2,1)S(1)}, bf16[2,128,768]{1,2,0:T(8,128)(2,1)S(1)}, u32[]{:S(2)}, u32[]{:S(2)}) %collective-permute-start.18) | collective-permute-done | bytes 393248 | tf_op jit(solution)/shard_map/ppermute | solution.py:44
  253.3 4.8 %shard_map.96 = bf16[512,256]{1,0:T(8,128)(2,1)} custom-call(bf16[1,3,3,6,128,256]{5,4,3,2,1,0:T(8,128)(2,1)S(1)} %maximum_bitcast_fusion.1.shifted_ref, bf16[27,256,256]{2,1,0:T(8,128)(2,1)} %taps_ref.3), custom_call_target="tpu_custom_call" | custom-call | flops 1811939328 | bytes 7340032 | tf_op jit(solution)/shard_map/pallas_call | solution.py:105
  (71 shorter events, 30.6 us)
Async XLA Ops:
  0.6 70.6 %copy-start = (bf16[1,4,128,512]{3,2,1,0:T(8,128)(2,1)S(1)}, bf16[1,4,128,512]{3,2,1,0:T(8,128)(2,1)}, u32[]{:S(2)}) copy-start(bf16[1,4,128,512]{3,2,1,0:T(8,128)(2,1)} %param.6) | copy-start | bytes 1572868
  1.6 31.6 %collective-permute-start.7 = (bf16[1,128,256]{2,1,0:T(8,128)(2,1)S(1)}, bf16[1,128,256]{2,1,0:T(8,128)(2,1)S(1)}, u32[]{:S(2)}, u32[]{:S(2)}) collective-permute-start(bf16[1,128,256]{2,1,0:T(8,128)(2,1)S(1)} %get-tuple-element.31), channel_id=1, source_target_pairs={{17,0},{18,1},{19,2},{20,3},{21,4},{22,5},{23,6},{24,7},{25,8},{26... | collective-permute-start | bytes 196616 | tf_op jit(solution)/shard_map/ppermute | solution.py:87
  4.6 18.9 %collective-permute-start.4 = (bf16[1,128,256]{2,1,0:T(8,128)(2,1)S(1)}, bf16[1,128,256]{2,1,0:T(8,128)(2,1)S(1)}, u32[]{:S(2)}, u32[]{:S(2)}) collective-permute-start(bf16[1,128,256]{2,1,0:T(8,128)(2,1)S(1)} %get-tuple-element.31), channel_id=1, source_target_pairs={{1,0},{2,1},{3,2},{4,3},{5,4},{6,5},{7,6},{8,7},{9,8},{10,9},{11,1... | collective-permute-start | bytes 196616 | tf_op jit(solution)/shard_map/ppermute | solution.py:87
  6.8 30.4 %collective-permute-start.6 = (bf16[4,128,256]{2,1,0:T(8,128)(2,1)}, bf16[4,128,256]{2,1,0:T(8,128)(2,1)S(1)}, u32[]{:S(2)}, u32[]{:S(2)}) collective-permute-start(bf16[4,128,256]{2,1,0:T(8,128)(2,1)} %bitcast.94), channel_id=1, source_target_pairs={{16,0},{17,1},{18,2},{19,3},{20,4},{21,5},{22,6},{23,7},{24,8},{25... | collective-permute-start | bytes 786440 | tf_op jit(solution)/shard_map/ppermute | solution.py:87
  9.0 29.7 %collective-permute-start.1 = (bf16[4,128,256]{2,1,0:T(8,128)(2,1)}, bf16[4,128,256]{2,1,0:T(8,128)(2,1)S(1)}, u32[]{:S(2)}, u32[]{:S(2)}) collective-permute-start(bf16[4,128,256]{2,1,0:T(8,128)(2,1)} %bitcast.95), channel_id=1, source_target_pairs={{0,16},{1,17},{2,18},{3,19},{4,20},{5,21},{6,22},{7,23},{8,24},{9,... | collective-permute-start | bytes 786440 | tf_op jit(solution)/shard_map/ppermute | solution.py:87
  14.5 11.0 %collective-permute-start.3 = (bf16[1,128,256]{2,1,0:T(8,128)(2,1)S(1)}, bf16[1,128,256]{2,1,0:T(8,128)(2,1)S(1)}, u32[]{:S(2)}, u32[]{:S(2)}) collective-permute-start(bf16[1,128,256]{2,1,0:T(8,128)(2,1)S(1)} %get-tuple-element.30), channel_id=1, source_target_pairs={{0,1},{1,2},{2,3},{3,4},{4,5},{5,6},{6,7},{7,8},{8,9},{9,10},{10,1... | collective-permute-start | bytes 196616 | tf_op jit(solution)/shard_map/ppermute | solution.py:87
  23.5 13.7 %collective-permute-start.5 = (bf16[1,128,256]{2,1,0:T(8,128)(2,1)S(1)}, bf16[1,128,256]{2,1,0:T(8,128)(2,1)S(1)}, u32[]{:S(2)}, u32[]{:S(2)}) collective-permute-start(bf16[1,128,256]{2,1,0:T(8,128)(2,1)S(1)} %get-tuple-element.30), channel_id=1, source_target_pairs={{16,1},{17,2},{18,3},{19,4},{20,5},{21,6},{22,7},{23,8},{24,9},{25... | collective-permute-start | bytes 196616 | tf_op jit(solution)/shard_map/ppermute | solution.py:87
  25.5 11.8 %collective-permute-start.2 = (bf16[1,128,256]{2,1,0:T(8,128)(2,1)S(1)}, bf16[1,128,256]{2,1,0:T(8,128)(2,1)S(1)}, u32[]{:S(2)}, u32[]{:S(2)}) collective-permute-start(bf16[1,128,256]{2,1,0:T(8,128)(2,1)S(1)} %get-tuple-element.31), channel_id=1, source_target_pairs={{1,16},{2,17},{3,18},{4,19},{5,20},{6,21},{7,22},{8,23},{9,24},{10... | collective-permute-start | bytes 196616 | tf_op jit(solution)/shard_map/ppermute | solution.py:87
  33.1 5.6 %collective-permute-start = (bf16[1,128,256]{2,1,0:T(8,128)(2,1)S(1)}, bf16[1,128,256]{2,1,0:T(8,128)(2,1)S(1)}, u32[]{:S(2)}, u32[]{:S(2)}) collective-permute-start(bf16[1,128,256]{2,1,0:T(8,128)(2,1)S(1)} %get-tuple-element.30), channel_id=1, source_target_pairs={{0,17},{1,18},{2,19},{3,20},{4,21},{5,22},{6,23},{7,24},{8,25},{9,... | collective-permute-start | bytes 196616 | tf_op jit(solution)/shard_map/ppermute | solution.py:87
  64.9 14.3 %all-to-all-start.1 = ((bf16[16,32,256]{2,1,0:T(8,128)(2,1)}), bf16[16,32,256]{2,1,0:T(8,128)(2,1)S(1)}, u32[]{:S(2)}, u32[]{:S(2)}) async-start(bf16[16,32,256]{2,1,0:T(8,128)(2,1)} %get-tuple-element.28), calls=%async_computation.1 | async-start | bytes 524288 | tf_op jit(solution)/shard_map/all_to_all | solution.py:236
  101.3 15.3 %all-to-all-start = ((bf16[16,32,512]{2,1,0:T(8,128)(2,1)}), bf16[16,32,512]{2,1,0:T(8,128)(2,1)S(1)}, u32[]{:S(2)}, u32[]{:S(2)}) async-start(bf16[16,32,512]{2,1,0:T(8,128)(2,1)} %get-tuple-element.24), calls=%async_computation | async-start | bytes 1048576 | tf_op jit(solution)/shard_map/all_to_all | solution.py:233
  143.3 25.7 %all-to-all-start.5 = ((bf16[16,32,768]{2,1,0:T(8,128)(2,1)}), bf16[16,32,768]{2,1,0:T(8,128)(2,1)S(1)}, u32[]{:S(2)}, u32[]{:S(2)}) async-start(bf16[16,32,768]{2,1,0:T(8,128)(2,1)} %bitcast.93), calls=%async_computation.5 | async-start | bytes 1572864 | tf_op jit(solution)/shard_map/all_to_all | solution.py:245
  169.0 21.1 %all-to-all-start.2 = ((bf16[16,32,768]{2,1,0:T(8,128)(2,1)}), bf16[16,32,768]{2,1,0:T(8,128)(2,1)}, u32[]{:S(2)}, u32[]{:S(2)}) async-start(bf16[16,32,768]{2,1,0:T(8,128)(2,1)} %bitcast.18), calls=%async_computation.2 | async-start | bytes 1572864 | tf_op jit(solution)/shard_map/all_to_all | solution.py:245
  180.3 11.2 %collective-permute-start.16 = (bf16[2,2,2,128,768]{3,4,0,1,2:T(8,128)(2,1)}, bf16[2,2,2,128,768]{3,4,0,1,2:T(8,128)(2,1)S(1)}, u32[]{:S(2)}, u32[]{:S(2)}) collective-permute-start(bf16[2,2,2,128,768]{3,4,0,1,2:T(8,128)(2,1)} %bitcast.85), channel_id=1, source_target_pairs={{0,16},{16,0},{32,48},{48,32},{64,80},{80,64},{96,112},{112,96},{1... | collective-permute-start | bytes 4718600 | tf_op jit(solution)/shard_map/ppermute | solution.py:44
  190.1 2.1 copy-start.2
  192.6 7.1 %copy-start.3 = (f32[2,2,2,128,768]{3,4,0,1,2:T(8,128)}, f32[2,2,2,128,768]{3,4,0,1,2:T(8,128)S(1)}, u32[]{:S(2)}) copy-start(f32[2,2,2,128,768]{3,4,0,1,2:T(8,128)S(1)} %bitcast_add_fusion) | copy-start | bytes 9437188
  192.7 46.8 %collective-permute-start.17 = (bf16[2,2,128,768]{2,3,0,1:T(8,128)(2,1)S(1)}, bf16[2,2,128,768]{2,3,0,1:T(8,128)(2,1)S(1)}, u32[]{:S(2)}, u32[]{:S(2)}) collective-permute-start(bf16[2,2,128,768]{2,3,0,1:T(8,128)(2,1)S(1)} %fusion.10), channel_id=1, source_target_pairs={{0,32},{16,48},{32,0},{48,16},{64,96},{80,112},{96,64},{112,80},{1... | collective-permute-start | bytes 2359304 | tf_op jit(solution)/shard_map/ppermute | solution.py:44
  199.7 39.7 %collective-permute-start.14 = (bf16[4,128,256]{2,1,0:T(8,128)(2,1)S(1)}, bf16[4,128,256]{2,1,0:T(8,128)(2,1)S(1)}, u32[]{:S(2)}, u32[]{:S(2)}) collective-permute-start(bf16[4,128,256]{2,1,0:T(8,128)(2,1)S(1)} %bitcast.87), channel_id=1, source_target_pairs={{16,0},{17,1},{18,2},{19,3},{20,4},{21,5},{22,6},{23,7},{24,8},{25... | collective-permute-start | bytes 786440 | tf_op jit(solution)/shard_map/ppermute | solution.py:87
  204.4 12.3 %collective-permute-start.12 = (bf16[1,128,256]{2,1,0:T(8,128)(2,1)S(1)}, bf16[1,128,256]{2,1,0:T(8,128)(2,1)S(1)}, u32[]{:S(2)}, u32[]{:S(2)}) collective-permute-start(bf16[1,128,256]{2,1,0:T(8,128)(2,1)S(1)} %get-tuple-element.27), channel_id=1, source_target_pairs={{1,0},{2,1},{3,2},{4,3},{5,4},{6,5},{7,6},{8,7},{9,8},{10,9},{11,1... | collective-permute-start | bytes 196616 | tf_op jit(solution)/shard_map/ppermute | solution.py:87
  207.1 17.0 %collective-permute-start.11 = (bf16[1,128,256]{2,1,0:T(8,128)(2,1)S(1)}, bf16[1,128,256]{2,1,0:T(8,128)(2,1)S(1)}, u32[]{:S(2)}, u32[]{:S(2)}) collective-permute-start(bf16[1,128,256]{2,1,0:T(8,128)(2,1)S(1)} %get-tuple-element.26), channel_id=1, source_target_pairs={{0,1},{1,2},{2,3},{3,4},{4,5},{5,6},{6,7},{7,8},{8,9},{9,10},{10,1... | collective-permute-start | bytes 196616 | tf_op jit(solution)/shard_map/ppermute | solution.py:87
  213.9 12.8 %collective-permute-start.15 = (bf16[1,128,256]{2,1,0:T(8,128)(2,1)S(1)}, bf16[1,128,256]{2,1,0:T(8,128)(2,1)S(1)}, u32[]{:S(2)}, u32[]{:S(2)}) collective-permute-start(bf16[1,128,256]{2,1,0:T(8,128)(2,1)S(1)} %get-tuple-element.27), channel_id=1, source_target_pairs={{17,0},{18,1},{19,2},{20,3},{21,4},{22,5},{23,6},{24,7},{25,8},{26... | collective-permute-start | bytes 196616 | tf_op jit(solution)/shard_map/ppermute | solution.py:87
  216.7 14.6 %collective-permute-start.13 = (bf16[1,128,256]{2,1,0:T(8,128)(2,1)S(1)}, bf16[1,128,256]{2,1,0:T(8,128)(2,1)S(1)}, u32[]{:S(2)}, u32[]{:S(2)}) collective-permute-start(bf16[1,128,256]{2,1,0:T(8,128)(2,1)S(1)} %get-tuple-element.26), channel_id=1, source_target_pairs={{16,1},{17,2},{18,3},{19,4},{20,5},{21,6},{22,7},{23,8},{24,9},{25... | collective-permute-start | bytes 196616 | tf_op jit(solution)/shard_map/ppermute | solution.py:87
  224.2 17.0 %collective-permute-start.10 = (bf16[1,128,256]{2,1,0:T(8,128)(2,1)S(1)}, bf16[1,128,256]{2,1,0:T(8,128)(2,1)S(1)}, u32[]{:S(2)}, u32[]{:S(2)}) collective-permute-start(bf16[1,128,256]{2,1,0:T(8,128)(2,1)S(1)} %get-tuple-element.27), channel_id=1, source_target_pairs={{1,16},{2,17},{3,18},{4,19},{5,20},{6,21},{7,22},{8,23},{9,24},{10... | collective-permute-start | bytes 196616 | tf_op jit(solution)/shard_map/ppermute | solution.py:87
  226.8 14.4 %collective-permute-start.9 = (bf16[4,128,256]{2,1,0:T(8,128)(2,1)S(1)}, bf16[4,128,256]{2,1,0:T(8,128)(2,1)S(1)}, u32[]{:S(2)}, u32[]{:S(2)}) collective-permute-start(bf16[4,128,256]{2,1,0:T(8,128)(2,1)S(1)} %bitcast.89), channel_id=1, source_target_pairs={{0,16},{1,17},{2,18},{3,19},{4,20},{5,21},{6,22},{7,23},{8,24},{9,... | collective-permute-start | bytes 786440 | tf_op jit(solution)/shard_map/ppermute | solution.py:87
  231.3 9.9 %collective-permute-start.8 = (bf16[1,128,256]{2,1,0:T(8,128)(2,1)S(1)}, bf16[1,128,256]{2,1,0:T(8,128)(2,1)S(1)}, u32[]{:S(2)}, u32[]{:S(2)}) collective-permute-start(bf16[1,128,256]{2,1,0:T(8,128)(2,1)S(1)} %get-tuple-element.26), channel_id=1, source_target_pairs={{0,17},{1,18},{2,19},{3,20},{4,21},{5,22},{6,23},{7,24},{8,25},{9,... | collective-permute-start | bytes 196616 | tf_op jit(solution)/shard_map/ppermute | solution.py:87
  241.1 11.6 %collective-permute-start.18 = (bf16[2,128,768]{1,2,0:T(8,128)(2,1)S(1)}, bf16[2,128,768]{1,2,0:T(8,128)(2,1)S(1)}, u32[]{:S(2)}, u32[]{:S(2)}) collective-permute-start(bf16[2,128,768]{1,2,0:T(8,128)(2,1)S(1)} %fusion.11), channel_id=1, source_target_pairs={{0,64},{16,80},{32,96},{48,112},{64,0},{80,16},{96,32},{112,48},{1... | collective-permute-start | bytes 1179656 | tf_op jit(solution)/shard_map/ppermute | solution.py:44
  252.8 5.3 %collective-permute-start.19 = (bf16[128,768]{0,1:T(8,128)(2,1)S(1)}, bf16[128,768]{0,1:T(8,128)(2,1)S(1)}, u32[]{:S(2)}, u32[]{:S(2)}) collective-permute-start(bf16[128,768]{0,1:T(8,128)(2,1)S(1)} %fusion.12), channel_id=1, source_target_pairs={{0,128},{16,144},{32,160},{48,176},{64,192},{80,208},{96,224},{112... | collective-permute-start | bytes 589832 | tf_op jit(solution)/shard_map/ppermute | solution.py:44
  253.3 6.3 %copy-start.1 = (bf16[1,4,128,512]{3,2,1,0:T(8,128)(2,1)S(1)}, bf16[1,4,128,512]{3,2,1,0:T(8,128)(2,1)}, u32[]{:S(2)}) copy-start(bf16[1,4,128,512]{3,2,1,0:T(8,128)(2,1)} %param.6) | copy-start | bytes 1572868

commit v6 on v4

--- a/solution.py
+++ b/solution.py
@@ -213,6 +213,7 @@
     returned = lax.all_to_all(
         back.reshape(experts, capacity, both), "expert", split_axis=0, concat_axis=0, tiled=True
     )
+    returned, part = lax.optimization_barrier((returned, part))
     mixed = lax.dot_general(
         route,
         returned.reshape(slots, both),

time: 208 us -> 216 us (1.038)
  the two profiles are of different devices: /device:TPU:95 before, /device:TPU:72 now
where the time goes in v6:
time: 216 us; the launch traced here: 215 us
  waiting for transfers between devices  79.2 us (37%)
  starting transfers between devices  49.1 us (23%)
  blocking collectives  29.9 us (14%)
  Pallas kernels  25.8 us (12%)
  local copies, waits for them, and re-layouts  19.3 us (9%)
  other arithmetic  6.76 us (3%)
  matrix products  4.25 us (2%)
    all_to_all x1, waiting for transfers between devices, per_device(): lax.all_to_all(back.reshape(experts, capacity, both), 'expert', split_axi...  33.5 us
    all_to_all x1, blocking collectives, per_device(): lax.all_to_all(outbound.reshape(experts, capacity, feat_width), 'expert',...  29.9 us
    ppermute x4, starting transfers between devices, extended(): after = lax.ppermute(first, axis, down)  18.7 us
    pallas_call x1, Pallas kernels, expert(): pl.pallas_call(functools.partial(expert_kernel, cols), grid=(hidden // ch...  17.1 us
    ppermute x4, waiting for transfers between devices, extended(): before = lax.ppermute(last, axis, up)  17 us
    all_to_all x1, waiting for transfers between devices, per_device(): lax.all_to_all(grad_outbound.reshape(experts, capacity, channels), 'exper...  14.5 us
    all_to_all x1, starting transfers between devices, per_device(): lax.all_to_all(grad_outbound.reshape(experts, capacity, channels), 'exper...  12.3 us
    ppermute x4, starting transfers between devices, extended(): before = lax.ppermute(last, axis, up)  10.4 us
  transfers between devices with their start and end apart: 14, of which 9 were waited for; matrix products, arithmetic and copies ran while one was open for 7% of the time, Pallas kernels for 2%

profile of v6, /device:TPU:72, one launch (start us, length us, event | category | flops | bytes accessed | tf_op | source)
XLA Modules:
  0.0 215.2 jit_solution(336906864473720706)
XLA Ops:
  0.7 2.1 collective-permute-start
  2.7 3.6 %collective-permute-start.1 = (bf16[1,4,128,256]{3,2,1,0:T(8,128)(2,1)}, bf16[1,4,128,256]{3,2,1,0:T(8,128)(2,1)S(1)}, u32[]{:S(2)}, u32[]{:S(2)}) collective-permute-start(bf16[1,4,128,256]{3,2,1,0:T(8,128)(2,1)} %param.11), channel_id=1, source_target_pairs={{16,0},{32,16},{48,32},{64,48},{80,64},{96,80},{112,96},{128,112},... | collective-permute-start | bytes 786440 | tf_op jit(solution)/shard_map/ppermute | solution.py:19
  7.4 1.3 collective-permute-done
  10.6 3.4 %collective-permute-start.2 = (bf16[3,1,128,256]{3,2,1,0:T(8,128)(2,1)S(1)}, bf16[3,1,128,256]{3,2,1,0:T(8,128)(2,1)S(1)}, u32[]{:S(2)}, u32[]{:S(2)}) collective-permute-start(bf16[3,1,128,256]{3,2,1,0:T(8,128)(2,1)S(1)} %get-tuple-element.24), channel_id=1, source_target_pairs={{0,1},{1,2},{2,3},{3,4},{4,5},{5,6},{6,7},{7,8},{8,9},{9,10},{10,1... | collective-permute-start | bytes 589832 | tf_op jit(solution)/shard_map/ppermute | solution.py:18
  14.0 5.5 %collective-permute-start.3 = (bf16[3,1,128,256]{3,2,1,0:T(8,128)(2,1)S(1)}, bf16[3,1,128,256]{3,2,1,0:T(8,128)(2,1)S(1)}, u32[]{:S(2)}, u32[]{:S(2)}) collective-permute-start(bf16[3,1,128,256]{3,2,1,0:T(8,128)(2,1)S(1)} %get-tuple-element.25), channel_id=1, source_target_pairs={{1,0},{2,1},{3,2},{4,3},{5,4},{6,5},{7,6},{8,7},{9,8},{10,9},{11,1... | collective-permute-start | bytes 589832 | tf_op jit(solution)/shard_map/ppermute | solution.py:19
  19.5 3.1 %collective-permute-done.2 = bf16[3,1,128,256]{3,2,1,0:T(8,128)(2,1)S(1)} collective-permute-done((bf16[3,1,128,256]{3,2,1,0:T(8,128)(2,1)S(1)}, bf16[3,1,128,256]{3,2,1,0:T(8,128)(2,1)S(1)}, u32[]{:S(2)}, u32[]{:S(2)}) %collective-permute-start.2) | collective-permute-done | bytes 196640 | tf_op jit(solution)/shard_map/ppermute | solution.py:18
  22.6 5.9 %collective-permute-done.3 = bf16[3,1,128,256]{3,2,1,0:T(8,128)(2,1)S(1)} collective-permute-done((bf16[3,1,128,256]{3,2,1,0:T(8,128)(2,1)S(1)}, bf16[3,1,128,256]{3,2,1,0:T(8,128)(2,1)S(1)}, u32[]{:S(2)}, u32[]{:S(2)}) %collective-permute-start.3) | collective-permute-done | bytes 196640 | tf_op jit(solution)/shard_map/ppermute | solution.py:19
  29.8 4.0 %shard_map.93 = bf16[512,256]{1,0:T(8,128)(2,1)S(1)} custom-call(bf16[1,3,3,6,128,256]{5,4,3,2,1,0:T(8,128)(2,1)S(1)} %maximum_bitcast_fusion.shifted_ref, bf16[27,256,256]{2,1,0:T(8,128)(2,1)} %taps_ref.3), custom_call_target="tpu_custom_call" | custom-call | flops 1811939328 | bytes 7340032 | tf_op jit(solution)/shard_map/pallas_call | solution.py:84
  33.8 1.3 fusion.5
  35.1 12.3 %all-to-all-start.1 = ((bf16[16,64,256]{2,1,0:T(8,128)(2,1)}), bf16[16,64,256]{2,1,0:T(8,128)(2,1)S(1)}, u32[]{:S(2)}, u32[]{:S(2)}) async-start(bf16[16,64,256]{2,1,0:T(8,128)(2,1)} %bitcast.8), calls=%async_computation.1 | async-start | bytes 1048576 | tf_op jit(solution)/shard_map/all_to_all | solution.py:205
  48.1 14.5 %all-to-all-done.1 = bf16[16,64,256]{2,1,0:T(8,128)(2,1)S(1)} async-done(((bf16[16,64,256]{2,1,0:T(8,128)(2,1)}), bf16[16,64,256]{2,1,0:T(8,128)(2,1)S(1)}, u32[]{:S(2)}, u32[]{:S(2)}) %all-to-all-start.1) | async-done | bytes 524320 | tf_op jit(solution)/shard_map/all_to_all | solution.py:205
  62.6 29.9 %all_to_all.15 = bf16[16,64,512]{2,1,0:T(8,128)(2,1)S(1)} all-to-all(bf16[16,64,512]{2,1,0:T(8,128)(2,1)S(1)} %bitcast.69), channel_id=1, replica_groups=mesh['dp'=16,'expert'=16] {'expert'}, dimensions={0} | all-to-all | bytes 2097152 | tf_op jit(solution)/shard_map/all_to_all | solution.py:198
  92.6 1.2 pad_maximum_fusion.rows_ref
  93.8 17.1 %shard_map.94 = (bf16[1024,768]{1,0:T(8,128)(2,1)}, f32[2048,768]{1,0:T(8,128)}) custom-call(bf16[1024,768]{1,0:T(8,128)(2,1)} %pad_maximum_fusion.rows_ref, bf16[512,2048]{1,0:T(8,128)(2,1)} %bitcast.74, bf16[2048,256]{1,0:T(8,128)(2,1)} %bitcast.75), custom_call_target="tpu_custom_call" | custom-call | flops 9663676416 | bytes 12582912 | tf_op jit(solution)/shard_map/pallas_call | solution.py:142
  110.9 5.9 %all-to-all-start.2 = ((bf16[16,64,768]{2,1,0:T(8,128)(2,1)}), bf16[16,64,768]{2,1,0:T(8,128)(2,1)S(1)}, u32[]{:S(2)}, u32[]{:S(2)}) async-start(bf16[16,64,768]{2,1,0:T(8,128)(2,1)} %bitcast.67), calls=%async_computation.2 | async-start | bytes 3145728 | tf_op jit(solution)/shard_map/all_to_all | solution.py:213
  116.8 33.5 %all-to-all-done.2 = bf16[16,64,768]{2,1,0:T(8,128)(2,1)S(1)} async-done(((bf16[16,64,768]{2,1,0:T(8,128)(2,1)}), bf16[16,64,768]{2,1,0:T(8,128)(2,1)S(1)}, u32[]{:S(2)}, u32[]{:S(2)}) %all-to-all-start.2) | async-done | bytes 1572896 | tf_op jit(solution)/shard_map/all_to_all | solution.py:213
  151.5 2.1 constant_dynamic-slice_fusion
  153.6 1.6 copy.15
  155.2 3.8 %constant_dynamic-slice_fusion.1 = f32[2,2,2,1,128,768]{5,4,3,2,1,0:T(8,128)} fusion(f32[2,2,2,2,128,768]{5,4,3,2,1,0:T(8,128)} %bitcast.64, s32[]{:T(128)S(6)} %select_n.28), kind=kLoop, calls=%fused_computation.45 | loop fusion | bytes 6291460 | tf_op jit(solution)/shard_map/jit(dynamic_index_in_dim)/dynamic_slice | solution.py:41
  159.0 3.5 %copy.12 = f32[2,2,2,1,128,768]{4,5,0,1,2,3:T(8,128)} copy(f32[2,2,2,1,128,768]{5,4,3,2,1,0:T(8,128)} %constant_dynamic-slice_fusion.1) | data formatting | bytes 6291456 | tf_op jit(solution)/shard_map/jit(dynamic_index_in_dim)/dynamic_slice | solution.py:41
  162.5 2.1 bitcast_add_fusion
  164.9 2.3 %copy-done.3 = bf16[16,64,768]{2,1,0:T(8,128)(2,1)S(1)} copy-done((bf16[16,64,768]{2,1,0:T(8,128)(2,1)S(1)}, bf16[16,64,768]{2,1,0:T(8,128)(2,1)}, u32[]{:S(2)}) %copy-start.3) | copy-done | bytes 1572888
  167.2 1.2 fusion.4
  168.5 2.6 %collective-permute-start.4 = (bf16[1,4,128,256]{3,2,1,0:T(8,128)(2,1)S(1)}, bf16[1,4,128,256]{3,2,1,0:T(8,128)(2,1)S(1)}, u32[]{:S(2)}, u32[]{:S(2)}) collective-permute-start(bf16[1,4,128,256]{3,2,1,0:T(8,128)(2,1)S(1)} %bitcast.58), channel_id=1, source_target_pairs={{0,16},{16,32},{32,48},{48,64},{64,80},{80,96},{96,112},{112,128},... | collective-permute-start | bytes 786440 | tf_op jit(solution)/shard_map/ppermute | solution.py:18
  171.1 3.1 %collective-permute-start.5 = (bf16[1,4,128,256]{3,2,1,0:T(8,128)(2,1)S(1)}, bf16[1,4,128,256]{3,2,1,0:T(8,128)(2,1)S(1)}, u32[]{:S(2)}, u32[]{:S(2)}) collective-permute-start(bf16[1,4,128,256]{3,2,1,0:T(8,128)(2,1)S(1)} %bitcast.59), channel_id=1, source_target_pairs={{16,0},{32,16},{48,32},{64,48},{80,64},{96,80},{112,96},{128,112},... | collective-permute-start | bytes 786440 | tf_op jit(solution)/shard_map/ppermute | solution.py:19
  175.1 12.6 %collective-permute-done.4 = bf16[1,4,128,256]{3,2,1,0:T(8,128)(2,1)S(1)} collective-permute-done((bf16[1,4,128,256]{3,2,1,0:T(8,128)(2,1)S(1)}, bf16[1,4,128,256]{3,2,1,0:T(8,128)(2,1)S(1)}, u32[]{:S(2)}, u32[]{:S(2)}) %collective-permute-start.4) | collective-permute-done | bytes 262176 | tf_op jit(solution)/shard_map/ppermute | solution.py:18
  187.7 2.4 %collective-permute-start.6 = (bf16[3,1,128,256]{3,2,1,0:T(8,128)(2,1)S(1)}, bf16[3,1,128,256]{3,2,1,0:T(8,128)(2,1)S(1)}, u32[]{:S(2)}, u32[]{:S(2)}) collective-permute-start(bf16[3,1,128,256]{3,2,1,0:T(8,128)(2,1)S(1)} %get-tuple-element.22), channel_id=1, source_target_pairs={{0,1},{1,2},{2,3},{3,4},{4,5},{5,6},{6,7},{7,8},{8,9},{9,10},{10,1... | collective-permute-start | bytes 589832 | tf_op jit(solution)/shard_map/ppermute | solution.py:18
  190.1 6.5 %collective-permute-start.7 = (bf16[3,1,128,256]{3,2,1,0:T(8,128)(2,1)S(1)}, bf16[3,1,128,256]{3,2,1,0:T(8,128)(2,1)S(1)}, u32[]{:S(2)}, u32[]{:S(2)}) collective-permute-start(bf16[3,1,128,256]{3,2,1,0:T(8,128)(2,1)S(1)} %get-tuple-element.23), channel_id=1, source_target_pairs={{1,0},{2,1},{3,2},{4,3},{5,4},{6,5},{7,6},{8,7},{9,8},{10,9},{11,1... | collective-permute-start | bytes 589832 | tf_op jit(solution)/shard_map/ppermute | solution.py:19
  196.6 1.8 bitcast_add_fusion.1
  198.4 1.5 collective-permute-start.10
  200.9 6.9 %collective-permute-done.10 = bf16[2,128,768]{1,2,0:T(8,128)(2,1)S(1)} collective-permute-done((bf16[2,128,768]{1,2,0:T(8,128)(2,1)S(1)}, bf16[2,128,768]{1,2,0:T(8,128)(2,1)S(1)}, u32[]{:S(2)}, u32[]{:S(2)}) %collective-permute-start.10) | collective-permute-done | bytes 393248 | tf_op jit(solution)/shard_map/ppermute | solution.py:44
  208.5 4.7 %shard_map.95 = bf16[512,256]{1,0:T(8,128)(2,1)} custom-call(bf16[1,3,3,6,128,256]{5,4,3,2,1,0:T(8,128)(2,1)S(1)} %maximum_bitcast_fusion.1.shifted_ref, bf16[27,256,256]{2,1,0:T(8,128)(2,1)} %taps_ref.3), custom_call_target="tpu_custom_call" | custom-call | flops 1811939328 | bytes 7340032 | tf_op jit(solution)/shard_map/pallas_call | solution.py:84
  (44 shorter events, 10.9 us)
Async XLA Ops:
  0.6 46.8 %copy-start = (bf16[1,4,128,512]{3,2,1,0:T(8,128)(2,1)S(1)}, bf16[1,4,128,512]{3,2,1,0:T(8,128)(2,1)}, u32[]{:S(2)}) copy-start(bf16[1,4,128,512]{3,2,1,0:T(8,128)(2,1)} %param.6) | copy-start | bytes 1572868
  0.6 18.8 %copy-start.4 = (s32[1,4,128,1]{2,3,1,0:T(1,128)S(1)}, s32[1,4,128,1]{2,3,1,0:T(1,128)}, u32[]{:S(2)}) copy-start(s32[1,4,128,1]{2,3,1,0:T(1,128)} %param.7) | copy-start | bytes 6148
  0.7 8.0 %collective-permute-start = (bf16[1,4,128,256]{3,2,1,0:T(8,128)(2,1)}, bf16[1,4,128,256]{3,2,1,0:T(8,128)(2,1)S(1)}, u32[]{:S(2)}, u32[]{:S(2)}) collective-permute-start(bf16[1,4,128,256]{3,2,1,0:T(8,128)(2,1)} %param.11), channel_id=1, source_target_pairs={{0,16},{16,32},{32,48},{48,64},{64,80},{80,96},{96,112},{112,128},... | collective-permute-start | bytes 786440 | tf_op jit(solution)/shard_map/ppermute | solution.py:18
  2.7 7.8 %collective-permute-start.1 = (bf16[1,4,128,256]{3,2,1,0:T(8,128)(2,1)}, bf16[1,4,128,256]{3,2,1,0:T(8,128)(2,1)S(1)}, u32[]{:S(2)}, u32[]{:S(2)}) collective-permute-start(bf16[1,4,128,256]{3,2,1,0:T(8,128)(2,1)} %param.11), channel_id=1, source_target_pairs={{16,0},{32,16},{48,32},{64,48},{80,64},{96,80},{112,96},{128,112},... | collective-permute-start | bytes 786440 | tf_op jit(solution)/shard_map/ppermute | solution.py:19
  10.6 12.0 %collective-permute-start.2 = (bf16[3,1,128,256]{3,2,1,0:T(8,128)(2,1)S(1)}, bf16[3,1,128,256]{3,2,1,0:T(8,128)(2,1)S(1)}, u32[]{:S(2)}, u32[]{:S(2)}) collective-permute-start(bf16[3,1,128,256]{3,2,1,0:T(8,128)(2,1)S(1)} %get-tuple-element.24), channel_id=1, source_target_pairs={{0,1},{1,2},{2,3},{3,4},{4,5},{5,6},{6,7},{7,8},{8,9},{9,10},{10,1... | collective-permute-start | bytes 589832 | tf_op jit(solution)/shard_map/ppermute | solution.py:18
  14.0 14.5 %collective-permute-start.3 = (bf16[3,1,128,256]{3,2,1,0:T(8,128)(2,1)S(1)}, bf16[3,1,128,256]{3,2,1,0:T(8,128)(2,1)S(1)}, u32[]{:S(2)}, u32[]{:S(2)}) collective-permute-start(bf16[3,1,128,256]{3,2,1,0:T(8,128)(2,1)S(1)} %get-tuple-element.25), channel_id=1, source_target_pairs={{1,0},{2,1},{3,2},{4,3},{5,4},{6,5},{7,6},{8,7},{9,8},{10,9},{11,1... | collective-permute-start | bytes 589832 | tf_op jit(solution)/shard_map/ppermute | solution.py:19
  35.1 27.6 %all-to-all-start.1 = ((bf16[16,64,256]{2,1,0:T(8,128)(2,1)}), bf16[16,64,256]{2,1,0:T(8,128)(2,1)S(1)}, u32[]{:S(2)}, u32[]{:S(2)}) async-start(bf16[16,64,256]{2,1,0:T(8,128)(2,1)} %bitcast.8), calls=%async_computation.1 | async-start | bytes 1048576 | tf_op jit(solution)/shard_map/all_to_all | solution.py:205
  110.9 39.4 %all-to-all-start.2 = ((bf16[16,64,768]{2,1,0:T(8,128)(2,1)}), bf16[16,64,768]{2,1,0:T(8,128)(2,1)S(1)}, u32[]{:S(2)}, u32[]{:S(2)}) async-start(bf16[16,64,768]{2,1,0:T(8,128)(2,1)} %bitcast.67), calls=%async_computation.2 | async-start | bytes 3145728 | tf_op jit(solution)/shard_map/all_to_all | solution.py:213
  150.4 1.1 copy-start.2
  155.2 7.4 %collective-permute-start.8 = (bf16[2,2,2,128,768]{3,4,0,1,2:T(8,128)(2,1)}, bf16[2,2,2,128,768]{3,4,0,1,2:T(8,128)(2,1)S(1)}, u32[]{:S(2)}, u32[]{:S(2)}) collective-permute-start(bf16[2,2,2,128,768]{3,4,0,1,2:T(8,128)(2,1)} %bitcast.68), channel_id=1, source_target_pairs={{0,16},{16,0},{32,48},{48,32},{64,80},{80,64},{96,112},{112,96},{1... | collective-permute-start | bytes 4718600 | tf_op jit(solution)/shard_map/ppermute | solution.py:44
  164.7 3.8 %copy-start.1 = (f32[2,2,2,128,768]{3,4,0,1,2:T(8,128)}, f32[2,2,2,128,768]{3,4,0,1,2:T(8,128)S(1)}, u32[]{:S(2)}) copy-start(f32[2,2,2,128,768]{3,4,0,1,2:T(8,128)S(1)} %bitcast_add_fusion) | copy-start | bytes 9437188
  164.7 2.5 %copy-start.3 = (bf16[16,64,768]{2,1,0:T(8,128)(2,1)S(1)}, bf16[16,64,768]{2,1,0:T(8,128)(2,1)}, u32[]{:S(2)}) copy-start(bf16[16,64,768]{2,1,0:T(8,128)(2,1)} %copy-done.2) | copy-start | bytes 4718596
  164.8 31.8 %collective-permute-start.9 = (bf16[2,2,128,768]{2,3,0,1:T(8,128)(2,1)S(1)}, bf16[2,2,128,768]{2,3,0,1:T(8,128)(2,1)}, u32[]{:S(2)}, u32[]{:S(2)}) collective-permute-start(bf16[2,2,128,768]{2,3,0,1:T(8,128)(2,1)S(1)} %fusion.10), channel_id=1, source_target_pairs={{0,32},{16,48},{32,0},{48,16},{64,96},{80,112},{96,64},{112,80},{1... | collective-permute-start | bytes 2359304 | tf_op jit(solution)/shard_map/ppermute | solution.py:44
  168.5 19.2 %collective-permute-start.4 = (bf16[1,4,128,256]{3,2,1,0:T(8,128)(2,1)S(1)}, bf16[1,4,128,256]{3,2,1,0:T(8,128)(2,1)S(1)}, u32[]{:S(2)}, u32[]{:S(2)}) collective-permute-start(bf16[1,4,128,256]{3,2,1,0:T(8,128)(2,1)S(1)} %bitcast.58), channel_id=1, source_target_pairs={{0,16},{16,32},{32,48},{48,64},{64,80},{80,96},{96,112},{112,128},... | collective-permute-start | bytes 786440 | tf_op jit(solution)/shard_map/ppermute | solution.py:18
  171.1 16.5 %collective-permute-start.5 = (bf16[1,4,128,256]{3,2,1,0:T(8,128)(2,1)S(1)}, bf16[1,4,128,256]{3,2,1,0:T(8,128)(2,1)S(1)}, u32[]{:S(2)}, u32[]{:S(2)}) collective-permute-start(bf16[1,4,128,256]{3,2,1,0:T(8,128)(2,1)S(1)} %bitcast.59), channel_id=1, source_target_pairs={{16,0},{32,16},{48,32},{64,48},{80,64},{96,80},{112,96},{128,112},... | collective-permute-start | bytes 786440 | tf_op jit(solution)/shard_map/ppermute | solution.py:19
  187.7 12.3 %collective-permute-start.6 = (bf16[3,1,128,256]{3,2,1,0:T(8,128)(2,1)S(1)}, bf16[3,1,128,256]{3,2,1,0:T(8,128)(2,1)S(1)}, u32[]{:S(2)}, u32[]{:S(2)}) collective-permute-start(bf16[3,1,128,256]{3,2,1,0:T(8,128)(2,1)S(1)} %get-tuple-element.22), channel_id=1, source_target_pairs={{0,1},{1,2},{2,3},{3,4},{4,5},{5,6},{6,7},{7,8},{8,9},{9,10},{10,1... | collective-permute-start | bytes 589832 | tf_op jit(solution)/shard_map/ppermute | solution.py:18
  190.1 9.9 %collective-permute-start.7 = (bf16[3,1,128,256]{3,2,1,0:T(8,128)(2,1)S(1)}, bf16[3,1,128,256]{3,2,1,0:T(8,128)(2,1)S(1)}, u32[]{:S(2)}, u32[]{:S(2)}) collective-permute-start(bf16[3,1,128,256]{3,2,1,0:T(8,128)(2,1)S(1)} %get-tuple-element.23), channel_id=1, source_target_pairs={{1,0},{2,1},{3,2},{4,3},{5,4},{6,5},{7,6},{8,7},{9,8},{10,9},{11,1... | collective-permute-start | bytes 589832 | tf_op jit(solution)/shard_map/ppermute | solution.py:19
  198.4 9.4 %collective-permute-start.10 = (bf16[2,128,768]{1,2,0:T(8,128)(2,1)S(1)}, bf16[2,128,768]{1,2,0:T(8,128)(2,1)S(1)}, u32[]{:S(2)}, u32[]{:S(2)}) collective-permute-start(bf16[2,128,768]{1,2,0:T(8,128)(2,1)S(1)} %fusion.11), channel_id=1, source_target_pairs={{0,64},{16,80},{32,96},{48,112},{64,0},{80,16},{96,32},{112,48},{1... | collective-permute-start | bytes 1179656 | tf_op jit(solution)/shard_map/ppermute | solution.py:44
  207.9 5.8 %collective-permute-start.11 = (bf16[128,768]{0,1:T(8,128)(2,1)S(1)}, bf16[128,768]{0,1:T(8,128)(2,1)S(1)}, u32[]{:S(2)}, u32[]{:S(2)}) collective-permute-start(bf16[128,768]{0,1:T(8,128)(2,1)S(1)} %fusion.12), channel_id=1, source_target_pairs={{0,128},{16,144},{32,160},{48,176},{64,192},{80,208},{96,224},{112... | collective-permute-start | bytes 589832 | tf_op jit(solution)/shard_map/ppermute | solution.py:44

commit v7 on v4

--- a/solution.py
+++ b/solution.py
@@ -72,8 +72,10 @@
     out_ref[...] = acc_ref[...].astype(out_ref.dtype)
 
 
-def conv_block(grid, kernel, flip):
+def conv_block(grid, kernel, flip, after=None):
     padded = extended(grid, (("dp", 0), ("expert", 1)), 1)
+    if after is not None:
+        after, padded = lax.optimization_barrier((after, padded))
     padded = jnp.pad(padded, ((0, 0), (0, 0), (1, 1), (0, 0)))
     depth_cells = grid.shape[2]
     shifted = jnp.stack(
@@ -81,7 +83,7 @@
     )[None]
     count = grid.shape[1] * depth_cells
     width = kernel.shape[2]
-    return pl.pallas_call(
+    result = pl.pallas_call(
         functools.partial(conv_kernel, flip),
         out_shape=jax.ShapeDtypeStruct((count, width), jnp.bfloat16),
         in_specs=[pl.BlockSpec(memory_space=pltpu.VMEM)] * 2,
@@ -94,6 +96,9 @@
             bytes_accessed=2 * (shifted.size + kernel.size + count * width),
         ),
     )(shifted, kernel)
+    if after is not None:
+        return result, after
+    return result
 
 
 def expert_kernel(
@@ -198,7 +203,7 @@
     received = lax.all_to_all(
         outbound.reshape(experts, capacity, feat_width), "expert", split_axis=0, concat_axis=0, tiled=True
     )
-    field_rows = conv_block(cotangent, kernel, True)
+    field_rows, received = conv_block(cotangent, kernel, True, received)
     grad_outbound = jnp.dot(route, field_rows, preferred_element_type=jnp.float32).astype(
         jnp.bfloat16
     )

time: 208 us -> 208 us (level)
  starting transfers between devices: 67.4 us -> 52.5 us
  waiting for transfers between devices: 81 us -> 95.9 us
    ppermute x4, waiting for transfers between devices: 3.74 us -> 28.2 us  [extended(): before = lax.ppermute(last, axis, up)]
    ppermute x4, starting transfers between devices: 15.1 us -> 0.46 us  [tree_scatter(): got = lax.ppermute(send.astype(jnp.bfloat16), 'dp', pairs)]
    all_to_all x1, waiting for transfers between devices: 12 us -> 0.01 us  [per_device(): lax.all_to_all(outbound.reshape(experts, capacity, feat_width), 'expert',...]
    ppermute x4, waiting for transfers between devices: 28.6 us -> 31.1 us  [extended(): after = lax.ppermute(first, axis, down)]
  transfers between devices with their start and end apart: 15 -> 15, of which waited for: 11 -> 9; matrix products, arithmetic and copies ran while one was open for 10% -> 8% of each run, Pallas kernels for 0% -> 0%
where the time goes in v7:
time: 208 us; the launch traced here: 205 us
  waiting for transfers between devices  95.9 us (46%)
  starting transfers between devices  52.5 us (25%)
  Pallas kernels  25.8 us (12%)
  local copies, waits for them, and re-layouts  16.5 us (8%)
  other arithmetic  7.15 us (3%)
  matrix products  6.63 us (3%)
    ppermute x4, waiting for transfers between devices, extended(): after = lax.ppermute(first, axis, down)  31.1 us
    ppermute x4, waiting for transfers between devices, tree_scatter(): got = lax.ppermute(send.astype(jnp.bfloat16), 'dp', pairs)  28.7 us
    ppermute x4, waiting for transfers between devices, extended(): before = lax.ppermute(last, axis, up)  28.2 us
    ppermute x4, starting transfers between devices, extended(): before = lax.ppermute(last, axis, up)  20.8 us
    pallas_call x1, Pallas kernels, expert(): pl.pallas_call(functools.partial(expert_kernel, cols), grid=(hidden // ch...  17.1 us
    all_to_all x1, starting transfers between devices, per_device(): lax.all_to_all(outbound.reshape(experts, capacity, feat_width), 'expert',...  10.1 us
    pallas_call x2, Pallas kernels, conv_block(): pl.pallas_call(functools.partial(conv_kernel, flip), out_shape=jax.ShapeD...  8.72 us
    all_to_all x1, waiting for transfers between devices, per_device(): lax.all_to_all(grad_outbound.reshape(experts, capacity, channels), 'exper...  7.96 us
  transfers between devices with their start and end apart: 15, of which 9 were waited for; matrix products, arithmetic and copies ran while one was open for 8% of the time, Pallas kernels for 0%

profile of v7, /device:TPU:95, one launch (start us, length us, event | category | flops | bytes accessed | tf_op | source)
XLA Modules:
  0.0 205.4 jit_solution(12340565154210936842)
XLA Ops:
  2.4 1.7 fusion.3
  4.1 10.1 %all-to-all-start = ((bf16[16,64,512]{2,1,0:T(8,128)(2,1)}), bf16[16,64,512]{2,1,0:T(8,128)(2,1)S(1)}, u32[]{:S(2)}, u32[]{:S(2)}) async-start(bf16[16,64,512]{2,1,0:T(8,128)(2,1)} %bitcast.2), calls=%async_computation | async-start | bytes 2097152 | tf_op jit(solution)/shard_map/all_to_all | solution.py:203
  14.2 3.4 %collective-permute-start = (bf16[1,4,128,256]{3,2,1,0:T(8,128)(2,1)S(1)}, bf16[1,4,128,256]{3,2,1,0:T(8,128)(2,1)S(1)}, u32[]{:S(2)}, u32[]{:S(2)}) collective-permute-start(bf16[1,4,128,256]{3,2,1,0:T(8,128)(2,1)S(1)} %copy-done.2), channel_id=1, source_target_pairs={{0,16},{16,32},{32,48},{48,64},{64,80},{80,96},{96,112},{112,128},... | collective-permute-start | bytes 786440 | tf_op jit(solution)/shard_map/ppermute | solution.py:18
  17.6 1.9 collective-permute-start.1
  19.5 26.3 %collective-permute-done = bf16[1,4,128,256]{3,2,1,0:T(8,128)(2,1)S(1)} collective-permute-done((bf16[1,4,128,256]{3,2,1,0:T(8,128)(2,1)S(1)}, bf16[1,4,128,256]{3,2,1,0:T(8,128)(2,1)S(1)}, u32[]{:S(2)}, u32[]{:S(2)}) %collective-permute-start) | collective-permute-done | bytes 262176 | tf_op jit(solution)/shard_map/ppermute | solution.py:18
  46.0 6.6 %collective-permute-start.2 = (bf16[3,1,128,256]{3,2,1,0:T(8,128)(2,1)S(1)}, bf16[3,1,128,256]{3,2,1,0:T(8,128)(2,1)S(1)}, u32[]{:S(2)}, u32[]{:S(2)}) collective-permute-start(bf16[3,1,128,256]{3,2,1,0:T(8,128)(2,1)S(1)} %get-tuple-element.22), channel_id=1, source_target_pairs={{0,1},{1,2},{2,3},{3,4},{4,5},{5,6},{6,7},{7,8},{8,9},{9,10},{10,1... | collective-permute-start | bytes 589832 | tf_op jit(solution)/shard_map/ppermute | solution.py:18
  52.6 1.9 collective-permute-start.3
  55.2 17.4 %collective-permute-done.3 = bf16[3,1,128,256]{3,2,1,0:T(8,128)(2,1)S(1)} collective-permute-done((bf16[3,1,128,256]{3,2,1,0:T(8,128)(2,1)S(1)}, bf16[3,1,128,256]{3,2,1,0:T(8,128)(2,1)S(1)}, u32[]{:S(2)}, u32[]{:S(2)}) %collective-permute-start.3) | collective-permute-done | bytes 196640 | tf_op jit(solution)/shard_map/ppermute | solution.py:19
  73.8 4.0 %shard_map.93 = bf16[512,256]{1,0:T(8,128)(2,1)S(1)} custom-call(bf16[1,3,3,6,128,256]{5,4,3,2,1,0:T(8,128)(2,1)S(1)} %maximum_bitcast_fusion.shifted_ref, bf16[27,256,256]{2,1,0:T(8,128)(2,1)} %taps_ref.3), custom_call_target="tpu_custom_call" | custom-call | flops 1811939328 | bytes 7340032 | tf_op jit(solution)/shard_map/pallas_call | solution.py:86
  77.8 1.3 fusion.5
  79.1 5.8 %all-to-all-start.1 = ((bf16[16,64,256]{2,1,0:T(8,128)(2,1)}), bf16[16,64,256]{2,1,0:T(8,128)(2,1)S(1)}, u32[]{:S(2)}, u32[]{:S(2)}) async-start(bf16[16,64,256]{2,1,0:T(8,128)(2,1)} %bitcast.8), calls=%async_computation.1 | async-start | bytes 1048576 | tf_op jit(solution)/shard_map/all_to_all | solution.py:210
  84.9 8.0 %all-to-all-done.1 = bf16[16,64,256]{2,1,0:T(8,128)(2,1)S(1)} async-done(((bf16[16,64,256]{2,1,0:T(8,128)(2,1)}), bf16[16,64,256]{2,1,0:T(8,128)(2,1)S(1)}, u32[]{:S(2)}, u32[]{:S(2)}) %all-to-all-start.1) | async-done | bytes 524320 | tf_op jit(solution)/shard_map/all_to_all | solution.py:210
  92.8 1.2 pad_maximum_fusion.rows_ref
  94.1 17.1 %shard_map.94 = (bf16[1024,768]{1,0:T(8,128)(2,1)}, f32[2048,768]{1,0:T(8,128)}) custom-call(bf16[1024,768]{1,0:T(8,128)(2,1)} %pad_maximum_fusion.rows_ref, bf16[512,2048]{1,0:T(8,128)(2,1)} %bitcast.72, bf16[2048,256]{1,0:T(8,128)(2,1)} %bitcast.73), custom_call_target="tpu_custom_call" | custom-call | flops 9663676416 | bytes 12582912 | tf_op jit(solution)/shard_map/pallas_call | solution.py:147
  111.1 2.1 %constant_dynamic-slice_fusion = bf16[2,2,2,1,128,768]{5,4,3,2,1,0:T(8,128)(2,1)S(1)} fusion(f32[2,2,2,2,128,768]{5,4,3,2,1,0:T(8,128)} %bitcast.63, s32[]{:T(128)S(6)} %select_n.29), kind=kLoop, calls=%fused_computation.44 | loop fusion | bytes 3145732 | tf_op jit(solution)/shard_map/jit(dynamic_index_in_dim)/dynamic_slice | solution.py:42
  113.2 1.6 copy.15
  114.8 7.7 %all-to-all-start.2 = ((bf16[16,64,768]{2,1,0:T(8,128)(2,1)}), bf16[16,64,768]{2,1,0:T(8,128)(2,1)}, u32[]{:S(2)}, u32[]{:S(2)}) async-start(bf16[16,64,768]{2,1,0:T(8,128)(2,1)} %bitcast.66), calls=%async_computation.2 | async-start | bytes 3145728 | tf_op jit(solution)/shard_map/all_to_all | solution.py:218
  122.5 3.8 %constant_dynamic-slice_fusion.1 = f32[2,2,2,1,128,768]{5,4,3,2,1,0:T(8,128)} fusion(f32[2,2,2,2,128,768]{5,4,3,2,1,0:T(8,128)} %bitcast.64, s32[]{:T(128)S(6)} %select_n.28), kind=kLoop, calls=%fused_computation.45 | loop fusion | bytes 6291460 | tf_op jit(solution)/shard_map/jit(dynamic_index_in_dim)/dynamic_slice | solution.py:41
  126.3 3.5 %copy.12 = f32[2,2,2,1,128,768]{4,5,0,1,2,3:T(8,128)} copy(f32[2,2,2,1,128,768]{5,4,3,2,1,0:T(8,128)} %constant_dynamic-slice_fusion.1) | data formatting | bytes 6291456 | tf_op jit(solution)/shard_map/jit(dynamic_index_in_dim)/dynamic_slice | solution.py:41
  129.8 2.1 %bitcast_add_fusion = f32[2,2,2,128,768]{3,4,0,1,2:T(8,128)S(1)} fusion(f32[2,2,2,1,128,768]{4,5,0,1,2,3:T(8,128)} %copy.12, bf16[2,2,2,128,768]{3,4,0,1,2:T(8,128)(2,1)S(1)} %collective-permute-done.8), kind=kLoop, calls=%fused_computation.2 | loop fusion | flops 1572864 | bytes 7864320 | tf_op jit(solution)/shard_map/add | solution.py:45
  132.0 1.6 copy-done.1
  133.8 18.3 %collective-permute-done.9 = bf16[2,2,128,768]{2,3,0,1:T(8,128)(2,1)S(1)} collective-permute-done((bf16[2,2,128,768]{2,3,0,1:T(8,128)(2,1)S(1)}, bf16[2,2,128,768]{2,3,0,1:T(8,128)(2,1)S(1)}, u32[]{:S(2)}, u32[]{:S(2)}) %collective-permute-start.9) | collective-permute-done | bytes 786464 | tf_op jit(solution)/shard_map/ppermute | solution.py:44
  152.1 1.5 bitcast_add_fusion.1
  153.8 10.4 %collective-permute-done.10 = bf16[2,128,768]{1,2,0:T(8,128)(2,1)S(1)} collective-permute-done((bf16[2,128,768]{1,2,0:T(8,128)(2,1)S(1)}, bf16[2,128,768]{1,2,0:T(8,128)(2,1)S(1)}, u32[]{:S(2)}, u32[]{:S(2)}) %collective-permute-start.10) | collective-permute-done | bytes 393248 | tf_op jit(solution)/shard_map/ppermute | solution.py:44
  164.6 2.6 %fusion.4 = bf16[512,768]{1,0:T(8,128)(2,1)S(1)} fusion(bf16[1024,768]{1,0:T(8,128)(2,1)} %bitcast.13, s32[512]{0:T(512)S(1)} %add_add_fusion), kind=kOutput, calls=%fused_computation.12 | convolution fusion | flops 806223872 | bytes 2361344 | tf_op jit(solution)/shard_map/dot_general | solution.py:221
  167.3 5.6 %collective-permute-start.4 = (bf16[1,4,128,256]{3,2,1,0:T(8,128)(2,1)S(1)}, bf16[1,4,128,256]{3,2,1,0:T(8,128)(2,1)S(1)}, u32[]{:S(2)}, u32[]{:S(2)}) collective-permute-start(bf16[1,4,128,256]{3,2,1,0:T(8,128)(2,1)S(1)} %bitcast.58), channel_id=1, source_target_pairs={{0,16},{16,32},{32,48},{48,64},{64,80},{80,96},{96,112},{112,128},... | collective-permute-start | bytes 786440 | tf_op jit(solution)/shard_map/ppermute | solution.py:18
  172.9 1.9 collective-permute-start.5
  176.5 6.2 %collective-permute-done.5 = bf16[1,4,128,256]{3,2,1,0:T(8,128)(2,1)S(1)} collective-permute-done((bf16[1,4,128,256]{3,2,1,0:T(8,128)(2,1)S(1)}, bf16[1,4,128,256]{3,2,1,0:T(8,128)(2,1)S(1)}, u32[]{:S(2)}, u32[]{:S(2)}) %collective-permute-start.5) | collective-permute-done | bytes 262176 | tf_op jit(solution)/shard_map/ppermute | solution.py:19
  182.7 5.2 %collective-permute-start.6 = (bf16[3,1,128,256]{3,2,1,0:T(8,128)(2,1)S(1)}, bf16[3,1,128,256]{3,2,1,0:T(8,128)(2,1)S(1)}, u32[]{:S(2)}, u32[]{:S(2)}) collective-permute-start(bf16[3,1,128,256]{3,2,1,0:T(8,128)(2,1)S(1)} %get-tuple-element.20), channel_id=1, source_target_pairs={{0,1},{1,2},{2,3},{3,4},{4,5},{5,6},{6,7},{7,8},{8,9},{9,10},{10,1... | collective-permute-start | bytes 589832 | tf_op jit(solution)/shard_map/ppermute | solution.py:18
  187.9 1.9 collective-permute-start.7
  191.8 7.5 %collective-permute-done.7 = bf16[3,1,128,256]{3,2,1,0:T(8,128)(2,1)S(1)} collective-permute-done((bf16[3,1,128,256]{3,2,1,0:T(8,128)(2,1)S(1)}, bf16[3,1,128,256]{3,2,1,0:T(8,128)(2,1)S(1)}, u32[]{:S(2)}, u32[]{:S(2)}) %collective-permute-start.7) | collective-permute-done | bytes 196640 | tf_op jit(solution)/shard_map/ppermute | solution.py:19
  200.7 4.7 %shard_map.95 = bf16[512,256]{1,0:T(8,128)(2,1)} custom-call(bf16[1,3,3,6,128,256]{5,4,3,2,1,0:T(8,128)(2,1)S(1)} %maximum_bitcast_fusion.1.shifted_ref, bf16[27,256,256]{2,1,0:T(8,128)(2,1)} %taps_ref.3), custom_call_target="tpu_custom_call" | custom-call | flops 1811939328 | bytes 7340032 | tf_op jit(solution)/shard_map/pallas_call | solution.py:86
  (41 shorter events, 9.4 us)
Async XLA Ops:
  0.6 1.7 copy-start
  4.1 10.1 %copy-start.2 = (bf16[1,4,128,256]{3,2,1,0:T(8,128)(2,1)S(1)}, bf16[1,4,128,256]{3,2,1,0:T(8,128)(2,1)}, u32[]{:S(2)}) copy-start(bf16[1,4,128,256]{3,2,1,0:T(8,128)(2,1)} %param.11) | copy-start | bytes 786436
  4.1 68.7 %all-to-all-start = ((bf16[16,64,512]{2,1,0:T(8,128)(2,1)}), bf16[16,64,512]{2,1,0:T(8,128)(2,1)S(1)}, u32[]{:S(2)}, u32[]{:S(2)}) async-start(bf16[16,64,512]{2,1,0:T(8,128)(2,1)} %bitcast.2), calls=%async_computation | async-start | bytes 2097152 | tf_op jit(solution)/shard_map/all_to_all | solution.py:203
  14.2 31.7 %collective-permute-start = (bf16[1,4,128,256]{3,2,1,0:T(8,128)(2,1)S(1)}, bf16[1,4,128,256]{3,2,1,0:T(8,128)(2,1)S(1)}, u32[]{:S(2)}, u32[]{:S(2)}) collective-permute-start(bf16[1,4,128,256]{3,2,1,0:T(8,128)(2,1)S(1)} %copy-done.2), channel_id=1, source_target_pairs={{0,16},{16,32},{32,48},{48,64},{64,80},{80,96},{96,112},{112,128},... | collective-permute-start | bytes 786440 | tf_op jit(solution)/shard_map/ppermute | solution.py:18
  17.6 28.3 %collective-permute-start.1 = (bf16[1,4,128,256]{3,2,1,0:T(8,128)(2,1)S(1)}, bf16[1,4,128,256]{3,2,1,0:T(8,128)(2,1)S(1)}, u32[]{:S(2)}, u32[]{:S(2)}) collective-permute-start(bf16[1,4,128,256]{3,2,1,0:T(8,128)(2,1)S(1)} %copy-done.2), channel_id=1, source_target_pairs={{16,0},{32,16},{48,32},{64,48},{80,64},{96,80},{112,96},{128,112},... | collective-permute-start | bytes 786440 | tf_op jit(solution)/shard_map/ppermute | solution.py:19
  46.0 9.2 %collective-permute-start.2 = (bf16[3,1,128,256]{3,2,1,0:T(8,128)(2,1)S(1)}, bf16[3,1,128,256]{3,2,1,0:T(8,128)(2,1)S(1)}, u32[]{:S(2)}, u32[]{:S(2)}) collective-permute-start(bf16[3,1,128,256]{3,2,1,0:T(8,128)(2,1)S(1)} %get-tuple-element.22), channel_id=1, source_target_pairs={{0,1},{1,2},{2,3},{3,4},{4,5},{5,6},{6,7},{7,8},{8,9},{9,10},{10,1... | collective-permute-start | bytes 589832 | tf_op jit(solution)/shard_map/ppermute | solution.py:18
  52.6 20.0 %collective-permute-start.3 = (bf16[3,1,128,256]{3,2,1,0:T(8,128)(2,1)S(1)}, bf16[3,1,128,256]{3,2,1,0:T(8,128)(2,1)S(1)}, u32[]{:S(2)}, u32[]{:S(2)}) collective-permute-start(bf16[3,1,128,256]{3,2,1,0:T(8,128)(2,1)S(1)} %get-tuple-element.23), channel_id=1, source_target_pairs={{1,0},{2,1},{3,2},{4,3},{5,4},{6,5},{7,6},{8,7},{9,8},{10,9},{11,1... | collective-permute-start | bytes 589832 | tf_op jit(solution)/shard_map/ppermute | solution.py:19
  79.1 13.7 %all-to-all-start.1 = ((bf16[16,64,256]{2,1,0:T(8,128)(2,1)}), bf16[16,64,256]{2,1,0:T(8,128)(2,1)S(1)}, u32[]{:S(2)}, u32[]{:S(2)}) async-start(bf16[16,64,256]{2,1,0:T(8,128)(2,1)} %bitcast.8), calls=%async_computation.1 | async-start | bytes 1048576 | tf_op jit(solution)/shard_map/all_to_all | solution.py:210
  114.8 15.0 %collective-permute-start.8 = (bf16[2,2,2,128,768]{3,4,0,1,2:T(8,128)(2,1)}, bf16[2,2,2,128,768]{3,4,0,1,2:T(8,128)(2,1)S(1)}, u32[]{:S(2)}, u32[]{:S(2)}) collective-permute-start(bf16[2,2,2,128,768]{3,4,0,1,2:T(8,128)(2,1)} %bitcast.67), channel_id=1, source_target_pairs={{0,16},{16,0},{32,48},{48,32},{64,80},{80,64},{96,112},{112,96},{1... | collective-permute-start | bytes 4718600 | tf_op jit(solution)/shard_map/ppermute | solution.py:44
  114.8 49.8 %all-to-all-start.2 = ((bf16[16,64,768]{2,1,0:T(8,128)(2,1)}), bf16[16,64,768]{2,1,0:T(8,128)(2,1)}, u32[]{:S(2)}, u32[]{:S(2)}) async-start(bf16[16,64,768]{2,1,0:T(8,128)(2,1)} %bitcast.66), calls=%async_computation.2 | async-start | bytes 3145728 | tf_op jit(solution)/shard_map/all_to_all | solution.py:218
  132.0 1.6 copy-start.1
  133.7 18.4 %collective-permute-start.9 = (bf16[2,2,128,768]{2,3,0,1:T(8,128)(2,1)S(1)}, bf16[2,2,128,768]{2,3,0,1:T(8,128)(2,1)S(1)}, u32[]{:S(2)}, u32[]{:S(2)}) collective-permute-start(bf16[2,2,128,768]{2,3,0,1:T(8,128)(2,1)S(1)} %fusion.10), channel_id=1, source_target_pairs={{0,32},{16,48},{32,0},{48,16},{64,96},{80,112},{96,64},{112,80},{1... | collective-permute-start | bytes 2359304 | tf_op jit(solution)/shard_map/ppermute | solution.py:44
  153.7 10.5 %collective-permute-start.10 = (bf16[2,128,768]{1,2,0:T(8,128)(2,1)S(1)}, bf16[2,128,768]{1,2,0:T(8,128)(2,1)S(1)}, u32[]{:S(2)}, u32[]{:S(2)}) collective-permute-start(bf16[2,128,768]{1,2,0:T(8,128)(2,1)S(1)} %fusion.11), channel_id=1, source_target_pairs={{0,64},{16,80},{32,96},{48,112},{64,0},{80,16},{96,32},{112,48},{1... | collective-permute-start | bytes 1179656 | tf_op jit(solution)/shard_map/ppermute | solution.py:44
  164.3 10.5 %collective-permute-start.11 = (bf16[128,768]{0,1:T(8,128)(2,1)S(1)}, bf16[128,768]{0,1:T(8,128)(2,1)S(1)}, u32[]{:S(2)}, u32[]{:S(2)}) collective-permute-start(bf16[128,768]{0,1:T(8,128)(2,1)S(1)} %fusion.12), channel_id=1, source_target_pairs={{0,128},{16,144},{32,160},{48,176},{64,192},{80,208},{96,224},{112... | collective-permute-start | bytes 589832 | tf_op jit(solution)/shard_map/ppermute | solution.py:44
  167.3 9.2 %collective-permute-start.4 = (bf16[1,4,128,256]{3,2,1,0:T(8,128)(2,1)S(1)}, bf16[1,4,128,256]{3,2,1,0:T(8,128)(2,1)S(1)}, u32[]{:S(2)}, u32[]{:S(2)}) collective-permute-start(bf16[1,4,128,256]{3,2,1,0:T(8,128)(2,1)S(1)} %bitcast.58), channel_id=1, source_target_pairs={{0,16},{16,32},{32,48},{48,64},{64,80},{80,96},{96,112},{112,128},... | collective-permute-start | bytes 786440 | tf_op jit(solution)/shard_map/ppermute | solution.py:18
  172.9 9.8 %collective-permute-start.5 = (bf16[1,4,128,256]{3,2,1,0:T(8,128)(2,1)S(1)}, bf16[1,4,128,256]{3,2,1,0:T(8,128)(2,1)S(1)}, u32[]{:S(2)}, u32[]{:S(2)}) collective-permute-start(bf16[1,4,128,256]{3,2,1,0:T(8,128)(2,1)S(1)} %bitcast.59), channel_id=1, source_target_pairs={{16,0},{32,16},{48,32},{64,48},{80,64},{96,80},{112,96},{128,112},... | collective-permute-start | bytes 786440 | tf_op jit(solution)/shard_map/ppermute | solution.py:19
  182.7 9.1 %collective-permute-start.6 = (bf16[3,1,128,256]{3,2,1,0:T(8,128)(2,1)S(1)}, bf16[3,1,128,256]{3,2,1,0:T(8,128)(2,1)S(1)}, u32[]{:S(2)}, u32[]{:S(2)}) collective-permute-start(bf16[3,1,128,256]{3,2,1,0:T(8,128)(2,1)S(1)} %get-tuple-element.20), channel_id=1, source_target_pairs={{0,1},{1,2},{2,3},{3,4},{4,5},{5,6},{6,7},{7,8},{8,9},{9,10},{10,1... | collective-permute-start | bytes 589832 | tf_op jit(solution)/shard_map/ppermute | solution.py:18
  187.9 11.3 %collective-permute-start.7 = (bf16[3,1,128,256]{3,2,1,0:T(8,128)(2,1)S(1)}, bf16[3,1,128,256]{3,2,1,0:T(8,128)(2,1)S(1)}, u32[]{:S(2)}, u32[]{:S(2)}) collective-permute-start(bf16[3,1,128,256]{3,2,1,0:T(8,128)(2,1)S(1)} %get-tuple-element.21), channel_id=1, source_target_pairs={{1,0},{2,1},{3,2},{4,3},{5,4},{6,5},{7,6},{8,7},{9,8},{10,9},{11,1... | collective-permute-start | bytes 589832 | tf_op jit(solution)/shard_map/ppermute | solution.py:19

commit v8 on v7

--- a/solution.py
+++ b/solution.py
@@ -228,7 +228,9 @@
     imitated = conv_block(patch_grid, kernel, False).reshape(1, rows_y, depth_cells, channels)
     feat_grad = mixed[:, channels:].reshape(1, rows_y, depth_cells, feat_width)
 
-    grads = tree_scatter(part.reshape(slabs, hidden // slabs, both), (0, 1, 2, 3))
+    grads = lax.psum_scatter(
+        part.astype(jnp.bfloat16), "dp", scatter_dimension=0, tiled=True
+    ).astype(jnp.float32)
     grad_one = grads[:, :feat_width].T
     grad_two = grads[:, feat_width:]
     return (imitated, feat_grad, grad_one[None], grad_two[None])

time: 208 us -> 209 us (level)
  the two profiles are of different devices: /device:TPU:95 before, /device:TPU:64 now
where the time goes in v8:
time: 209 us; the launch traced here: 208 us
  blocking collectives  63 us (30%)
  waiting for transfers between devices  47.9 us (23%)
  starting transfers between devices  38.5 us (18%)
  Pallas kernels  25.8 us (12%)
  between operations  14.3 us (7%)
  other arithmetic  9.11 us (4%)
  local copies, waits for them, and re-layouts  5.06 us (2%)
  matrix products  4.44 us (2%)
    all_to_all x1, blocking collectives, per_device(): lax.all_to_all(back.reshape(experts, capacity, both), 'expert', split_axi...  40.8 us
    reduce_scatter x1, waiting for transfers between devices, per_device(): lax.psum_scatter(part.astype(jnp.bfloat16), 'dp', scatter_dimension=0, ti...  26 us
    all_to_all x1, blocking collectives, per_device(): lax.all_to_all(grad_outbound.reshape(experts, capacity, channels), 'exper...  22.2 us
    ppermute x4, waiting for transfers between devices, extended(): before = lax.ppermute(last, axis, up)  18 us
    pallas_call x1, Pallas kernels, expert(): pl.pallas_call(functools.partial(expert_kernel, cols), grid=(hidden // ch...  17.1 us
    ppermute x4, starting transfers between devices, extended(): after = lax.ppermute(first, axis, down)  16.4 us
    ppermute x4, starting transfers between devices, extended(): before = lax.ppermute(last, axis, up)  11.4 us
    all_to_all x1, starting transfers between devices, per_device(): lax.all_to_all(outbound.reshape(experts, capacity, feat_width), 'expert',...  10.7 us
  transfers between devices with their start and end apart: 10, of which 5 were waited for; matrix products, arithmetic and copies ran while one was open for 2% of the time, Pallas kernels for 2%

profile of v8, /device:TPU:64, one launch (start us, length us, event | category | flops | bytes accessed | tf_op | source)
XLA Modules:
  0.0 208.2 jit_solution(1681362906065630758)
XLA Ops:
  7.2 1.0 fusion.6
  8.2 0.7 add_add_fusion
  8.9 1.7 fusion.3
  10.6 10.7 %all-to-all-start = ((bf16[16,64,512]{2,1,0:T(8,128)(2,1)}), bf16[16,64,512]{2,1,0:T(8,128)(2,1)S(1)}, u32[]{:S(2)}, u32[]{:S(2)}) async-start(bf16[16,64,512]{2,1,0:T(8,128)(2,1)} %bitcast.2), calls=%async_computation | async-start | bytes 2097152 | tf_op jit(solution)/shard_map/all_to_all | solution.py:203
  21.4 1.3 collective-permute-start
  22.7 1.3 collective-permute-start.1
  24.0 3.9 %collective-permute-done.1 = bf16[1,4,128,256]{3,2,1,0:T(8,128)(2,1)S(1)} collective-permute-done((bf16[1,4,128,256]{3,2,1,0:T(8,128)(2,1)S(1)}, bf16[1,4,128,256]{3,2,1,0:T(8,128)(2,1)S(1)}, u32[]{:S(2)}, u32[]{:S(2)}) %collective-permute-start.1) | collective-permute-done | bytes 262176 | tf_op jit(solution)/shard_map/ppermute | solution.py:19
  28.0 3.4 %collective-permute-start.2 = (bf16[3,1,128,256]{3,2,1,0:T(8,128)(2,1)S(1)}, bf16[3,1,128,256]{3,2,1,0:T(8,128)(2,1)S(1)}, u32[]{:S(2)}, u32[]{:S(2)}) collective-permute-start(bf16[3,1,128,256]{3,2,1,0:T(8,128)(2,1)S(1)} %get-tuple-element.22), channel_id=1, source_target_pairs={{0,1},{1,2},{2,3},{3,4},{4,5},{5,6},{6,7},{7,8},{8,9},{9,10},{10,1... | collective-permute-start | bytes 589832 | tf_op jit(solution)/shard_map/ppermute | solution.py:18
  31.3 5.5 %collective-permute-start.3 = (bf16[3,1,128,256]{3,2,1,0:T(8,128)(2,1)S(1)}, bf16[3,1,128,256]{3,2,1,0:T(8,128)(2,1)S(1)}, u32[]{:S(2)}, u32[]{:S(2)}) collective-permute-start(bf16[3,1,128,256]{3,2,1,0:T(8,128)(2,1)S(1)} %get-tuple-element.23), channel_id=1, source_target_pairs={{1,0},{2,1},{3,2},{4,3},{5,4},{6,5},{7,6},{8,7},{9,8},{10,9},{11,1... | collective-permute-start | bytes 589832 | tf_op jit(solution)/shard_map/ppermute | solution.py:19
  36.8 14.3 %collective-permute-done.2 = bf16[3,1,128,256]{3,2,1,0:T(8,128)(2,1)S(1)} collective-permute-done((bf16[3,1,128,256]{3,2,1,0:T(8,128)(2,1)S(1)}, bf16[3,1,128,256]{3,2,1,0:T(8,128)(2,1)S(1)}, u32[]{:S(2)}, u32[]{:S(2)}) %collective-permute-start.2) | collective-permute-done | bytes 196640 | tf_op jit(solution)/shard_map/ppermute | solution.py:18
  51.3 0.6 slice_bitcast_fusion.3
  52.3 4.0 %shard_map.93 = bf16[512,256]{1,0:T(8,128)(2,1)S(1)} custom-call(bf16[1,3,3,6,128,256]{5,4,3,2,1,0:T(8,128)(2,1)S(1)} %maximum_bitcast_fusion.shifted_ref, bf16[27,256,256]{2,1,0:T(8,128)(2,1)} %taps_ref.3), custom_call_target="tpu_custom_call" | custom-call | flops 1811939328 | bytes 7340032 | tf_op jit(solution)/shard_map/pallas_call | solution.py:86
  56.9 22.2 %all_to_all.15 = bf16[16,64,256]{2,1,0:T(8,128)(2,1)S(1)} all-to-all(bf16[16,64,256]{2,1,0:T(8,128)(2,1)S(1)} %bitcast.49), channel_id=1, replica_groups=mesh['dp'=16,'expert'=16] {'expert'}, dimensions={0} | all-to-all | bytes 1048576 | tf_op jit(solution)/shard_map/all_to_all | solution.py:210
  79.1 1.3 pad_maximum_fusion.rows_ref
  80.3 17.1 %shard_map.94 = (bf16[1024,768]{1,0:T(8,128)(2,1)}, f32[2048,768]{1,0:T(8,128)}) custom-call(bf16[1024,768]{1,0:T(8,128)(2,1)} %pad_maximum_fusion.rows_ref, bf16[512,2048]{1,0:T(8,128)(2,1)} %bitcast.53, bf16[2048,256]{1,0:T(8,128)(2,1)} %bitcast.54), custom_call_target="tpu_custom_call" | custom-call | flops 9663676416 | bytes 12582912 | tf_op jit(solution)/shard_map/pallas_call | solution.py:147
  97.4 4.8 %convert_element_type.39 = bf16[2048,768]{1,0:T(8,128)(2,1)} convert(f32[2048,768]{1,0:T(8,128)} %get-tuple-element.11) | non-fusion elementwise | flops 1572864 | bytes 9437184 | tf_op jit(solution)/shard_map/convert_element_type | solution.py:232
  102.2 1.4 copy-done.1
  103.6 40.8 %all_to_all.16 = bf16[16,64,768]{2,1,0:T(8,128)(2,1)S(1)} all-to-all(bf16[16,64,768]{2,1,0:T(8,128)(2,1)S(1)} %bitcast.46), channel_id=1, replica_groups=mesh['dp'=16,'expert'=16] {'expert'}, dimensions={0} | all-to-all | bytes 3145728 | tf_op jit(solution)/shard_map/all_to_all | solution.py:218
  144.4 1.2 fusion.4
  145.7 1.3 collective-permute-start.5
  147.0 3.0 %collective-permute-start.4 = (bf16[1,4,128,256]{3,2,1,0:T(8,128)(2,1)S(1)}, bf16[1,4,128,256]{3,2,1,0:T(8,128)(2,1)S(1)}, u32[]{:S(2)}, u32[]{:S(2)}) collective-permute-start(bf16[1,4,128,256]{3,2,1,0:T(8,128)(2,1)S(1)} %bitcast.41), channel_id=1, source_target_pairs={{0,16},{16,32},{32,48},{48,64},{64,80},{80,96},{96,112},{112,128},... | collective-permute-start | bytes 786440 | tf_op jit(solution)/shard_map/ppermute | solution.py:18
  150.1 1.1 collective-permute-done.4
  151.2 3.6 %collective-permute-start.6 = (bf16[3,1,128,256]{3,2,1,0:T(8,128)(2,1)S(1)}, bf16[3,1,128,256]{3,2,1,0:T(8,128)(2,1)S(1)}, u32[]{:S(2)}, u32[]{:S(2)}) collective-permute-start(bf16[3,1,128,256]{3,2,1,0:T(8,128)(2,1)S(1)} %get-tuple-element.20), channel_id=1, source_target_pairs={{0,1},{1,2},{2,3},{3,4},{4,5},{5,6},{6,7},{7,8},{8,9},{9,10},{10,1... | collective-permute-start | bytes 589832 | tf_op jit(solution)/shard_map/ppermute | solution.py:18
  154.9 8.3 %collective-permute-start.7 = (bf16[3,1,128,256]{3,2,1,0:T(8,128)(2,1)S(1)}, bf16[3,1,128,256]{3,2,1,0:T(8,128)(2,1)S(1)}, u32[]{:S(2)}, u32[]{:S(2)}) collective-permute-start(bf16[3,1,128,256]{3,2,1,0:T(8,128)(2,1)S(1)} %get-tuple-element.21), channel_id=1, source_target_pairs={{1,0},{2,1},{3,2},{4,3},{5,4},{6,5},{7,6},{8,7},{9,8},{10,9},{11,1... | collective-permute-start | bytes 589832 | tf_op jit(solution)/shard_map/ppermute | solution.py:19
  163.2 0.8 slice.53
  164.0 2.6 %collective-permute-done.6 = bf16[3,1,128,256]{3,2,1,0:T(8,128)(2,1)S(1)} collective-permute-done((bf16[3,1,128,256]{3,2,1,0:T(8,128)(2,1)S(1)}, bf16[3,1,128,256]{3,2,1,0:T(8,128)(2,1)S(1)}, u32[]{:S(2)}, u32[]{:S(2)}) %collective-permute-start.6) | collective-permute-done | bytes 196640 | tf_op jit(solution)/shard_map/ppermute | solution.py:18
  167.0 0.6 slice_bitcast_fusion.1
  168.1 4.7 %shard_map.95 = bf16[512,256]{1,0:T(8,128)(2,1)} custom-call(bf16[1,3,3,6,128,256]{5,4,3,2,1,0:T(8,128)(2,1)S(1)} %maximum_bitcast_fusion.1.shifted_ref, bf16[27,256,256]{2,1,0:T(8,128)(2,1)} %taps_ref.3), custom_call_target="tpu_custom_call" | custom-call | flops 1811939328 | bytes 7340032 | tf_op jit(solution)/shard_map/pallas_call | solution.py:86
  172.8 26.0 %reduce-scatter.2.cloned.1.call-done = bf16[128,768]{1,0:T(8,128)(2,1)} async-done(((bf16[2048,768]{1,0:T(8,128)(2,1)}), bf16[128,768]{1,0:T(8,128)(2,1)}) %reduce-scatter.2.cloned.1.call-update) | async-done | bytes 196624 | tf_op jit(solution)/shard_map/reduce_scatter | solution.py:231
  198.8 1.0 convert_element_type.40
  199.8 0.7 slice_bitcast_fusion.5
  200.5 0.8 copy.10
  (25 shorter events, 2.1 us)
Async XLA Ops:
  7.2 1.7 copy-start
  10.6 10.8 %copy-start.2 = (bf16[1,4,128,256]{3,2,1,0:T(8,128)(2,1)S(1)}, bf16[1,4,128,256]{3,2,1,0:T(8,128)(2,1)}, u32[]{:S(2)}) copy-start(bf16[1,4,128,256]{3,2,1,0:T(8,128)(2,1)} %param.11) | copy-start | bytes 786436
  10.6 40.7 %all-to-all-start = ((bf16[16,64,512]{2,1,0:T(8,128)(2,1)}), bf16[16,64,512]{2,1,0:T(8,128)(2,1)S(1)}, u32[]{:S(2)}, u32[]{:S(2)}) async-start(bf16[16,64,512]{2,1,0:T(8,128)(2,1)} %bitcast.2), calls=%async_computation | async-start | bytes 2097152 | tf_op jit(solution)/shard_map/all_to_all | solution.py:203
  21.3 177.5 %reduce-scatter.2.cloned.1.call-start = ((), (), s32[]{:S(2)}) async-start(), calls=%async_computation.4 | async-start | bytes 3342336 | tf_op jit(solution)/shard_map/reduce_scatter | solution.py:231
  21.4 2.6 %collective-permute-start = (bf16[1,4,128,256]{3,2,1,0:T(8,128)(2,1)S(1)}, bf16[1,4,128,256]{3,2,1,0:T(8,128)(2,1)S(1)}, u32[]{:S(2)}, u32[]{:S(2)}) collective-permute-start(bf16[1,4,128,256]{3,2,1,0:T(8,128)(2,1)S(1)} %copy-done.2), channel_id=1, source_target_pairs={{0,16},{16,32},{32,48},{48,64},{64,80},{80,96},{96,112},{112,128},... | collective-permute-start | bytes 786440 | tf_op jit(solution)/shard_map/ppermute | solution.py:18
  22.7 5.2 %collective-permute-start.1 = (bf16[1,4,128,256]{3,2,1,0:T(8,128)(2,1)S(1)}, bf16[1,4,128,256]{3,2,1,0:T(8,128)(2,1)S(1)}, u32[]{:S(2)}, u32[]{:S(2)}) collective-permute-start(bf16[1,4,128,256]{3,2,1,0:T(8,128)(2,1)S(1)} %copy-done.2), channel_id=1, source_target_pairs={{16,0},{32,16},{48,32},{64,48},{80,64},{96,80},{112,96},{128,112},... | collective-permute-start | bytes 786440 | tf_op jit(solution)/shard_map/ppermute | solution.py:19
  28.0 23.2 %collective-permute-start.2 = (bf16[3,1,128,256]{3,2,1,0:T(8,128)(2,1)S(1)}, bf16[3,1,128,256]{3,2,1,0:T(8,128)(2,1)S(1)}, u32[]{:S(2)}, u32[]{:S(2)}) collective-permute-start(bf16[3,1,128,256]{3,2,1,0:T(8,128)(2,1)S(1)} %get-tuple-element.22), channel_id=1, source_target_pairs={{0,1},{1,2},{2,3},{3,4},{4,5},{5,6},{6,7},{7,8},{8,9},{9,10},{10,1... | collective-permute-start | bytes 589832 | tf_op jit(solution)/shard_map/ppermute | solution.py:18
  31.3 19.8 %collective-permute-start.3 = (bf16[3,1,128,256]{3,2,1,0:T(8,128)(2,1)S(1)}, bf16[3,1,128,256]{3,2,1,0:T(8,128)(2,1)S(1)}, u32[]{:S(2)}, u32[]{:S(2)}) collective-permute-start(bf16[3,1,128,256]{3,2,1,0:T(8,128)(2,1)S(1)} %get-tuple-element.23), channel_id=1, source_target_pairs={{1,0},{2,1},{3,2},{4,3},{5,4},{6,5},{7,6},{8,7},{9,8},{10,9},{11,1... | collective-permute-start | bytes 589832 | tf_op jit(solution)/shard_map/ppermute | solution.py:19
  102.2 1.4 copy-start.1
  145.7 4.4 %collective-permute-start.5 = (bf16[1,4,128,256]{3,2,1,0:T(8,128)(2,1)S(1)}, bf16[1,4,128,256]{3,2,1,0:T(8,128)(2,1)S(1)}, u32[]{:S(2)}, u32[]{:S(2)}) collective-permute-start(bf16[1,4,128,256]{3,2,1,0:T(8,128)(2,1)S(1)} %bitcast.40), channel_id=1, source_target_pairs={{16,0},{32,16},{48,32},{64,48},{80,64},{96,80},{112,96},{128,112},... | collective-permute-start | bytes 786440 | tf_op jit(solution)/shard_map/ppermute | solution.py:19
  147.0 4.2 %collective-permute-start.4 = (bf16[1,4,128,256]{3,2,1,0:T(8,128)(2,1)S(1)}, bf16[1,4,128,256]{3,2,1,0:T(8,128)(2,1)S(1)}, u32[]{:S(2)}, u32[]{:S(2)}) collective-permute-start(bf16[1,4,128,256]{3,2,1,0:T(8,128)(2,1)S(1)} %bitcast.41), channel_id=1, source_target_pairs={{0,16},{16,32},{32,48},{48,64},{64,80},{80,96},{96,112},{112,128},... | collective-permute-start | bytes 786440 | tf_op jit(solution)/shard_map/ppermute | solution.py:18
  151.2 15.4 %collective-permute-start.6 = (bf16[3,1,128,256]{3,2,1,0:T(8,128)(2,1)S(1)}, bf16[3,1,128,256]{3,2,1,0:T(8,128)(2,1)S(1)}, u32[]{:S(2)}, u32[]{:S(2)}) collective-permute-start(bf16[3,1,128,256]{3,2,1,0:T(8,128)(2,1)S(1)} %get-tuple-element.20), channel_id=1, source_target_pairs={{0,1},{1,2},{2,3},{3,4},{4,5},{5,6},{6,7},{7,8},{8,9},{9,10},{10,1... | collective-permute-start | bytes 589832 | tf_op jit(solution)/shard_map/ppermute | solution.py:18
  154.9 11.8 %collective-permute-start.7 = (bf16[3,1,128,256]{3,2,1,0:T(8,128)(2,1)S(1)}, bf16[3,1,128,256]{3,2,1,0:T(8,128)(2,1)S(1)}, u32[]{:S(2)}, u32[]{:S(2)}) collective-permute-start(bf16[3,1,128,256]{3,2,1,0:T(8,128)(2,1)S(1)} %get-tuple-element.21), channel_id=1, source_target_pairs={{1,0},{2,1},{3,2},{4,3},{5,4},{6,5},{7,6},{8,7},{9,8},{10,9},{11,1... | collective-permute-start | bytes 589832 | tf_op jit(solution)/shard_map/ppermute | solution.py:19
Sparse Core Ops, SparseCore 0:
  102.3 96.4 reduce-scatter.1

commit v9 on v7

--- a/solution.py
+++ b/solution.py
@@ -199,21 +199,13 @@
     route = (target[None, :] == jnp.arange(slots, dtype=jnp.int32)[:, None]).astype(jnp.bfloat16)
 
     flat_feats = feats.reshape(patch_count, feat_width)
-    outbound = jnp.dot(route, flat_feats, preferred_element_type=jnp.float32).astype(jnp.bfloat16)
-    received = lax.all_to_all(
-        outbound.reshape(experts, capacity, feat_width), "expert", split_axis=0, concat_axis=0, tiled=True
-    )
-    field_rows, received = conv_block(cotangent, kernel, True, received)
-    grad_outbound = jnp.dot(route, field_rows, preferred_element_type=jnp.float32).astype(
-        jnp.bfloat16
-    )
-    grad_inbound = lax.all_to_all(
-        grad_outbound.reshape(experts, capacity, channels), "expert", split_axis=0, concat_axis=0, tiled=True
-    )
+    field_rows = conv_block(cotangent, kernel, True)
+    local = jnp.concatenate([flat_feats, field_rows], axis=1)
+    outbound = jnp.dot(route, local, preferred_element_type=jnp.float32).astype(jnp.bfloat16)
     both = feat_width + channels
-    inbound = jnp.concatenate(
-        [received.reshape(slots, feat_width), grad_inbound.reshape(slots, channels)], axis=1
-    )
+    inbound = lax.all_to_all(
+        outbound.reshape(experts, capacity, both), "expert", split_axis=0, concat_axis=0, tiled=True
+    ).reshape(slots, both)
     back, part = expert(inbound, w_first[0], w_second[0], 512)
     returned = lax.all_to_all(
         back.reshape(experts, capacity, both), "expert", split_axis=0, concat_axis=0, tiled=True

time: 208 us -> 202 us (0.971)
  waiting for transfers between devices: 95.9 us -> 90.5 us
    ppermute x4, waiting for transfers between devices: 28.2 us -> 3.65 us  [extended(): before = lax.ppermute(last, axis, up)]
    all_to_all x2 -> x1, waiting for transfers between devices: 7.96 us -> 30.8 us  [per_device(): lax.all_to_all(outbound.reshape(experts, capacity, both), 'expert', split...]
    ppermute x4, starting transfers between devices: 0.46 us -> 12.5 us  [tree_scatter(): got = lax.ppermute(send.astype(jnp.bfloat16), 'dp', pairs)]
    all_to_all x2 -> x1, starting transfers between devices: 15.8 us -> 5.77 us  [per_device(): lax.all_to_all(outbound.reshape(experts, capacity, both), 'expert', split...]
    dynamic_slice x2, local copies, waits for them, and re-layouts: 7.35 us -> 4.55 us  [tree_scatter(): keep = lax.dynamic_index_in_dim(x, mine, axis=axis, keepdims=False)]
    ppermute x4, waiting for transfers between devices: 31.1 us -> 28.7 us  [extended(): after = lax.ppermute(first, axis, down)]
    unnamed x10 -> x12, local copies, waits for them, and re-layouts: 4.03 us -> 5.71 us
  transfers between devices with their start and end apart: 15 -> 14, of which waited for: 9 -> 10; matrix products, arithmetic and copies ran while one was open for 8% -> 9% of each run, Pallas kernels for 0% -> 0%
where the time goes in v9:
time: 202 us; the launch traced here: 200 us
  waiting for transfers between devices  90.5 us (45%)
  starting transfers between devices  53.6 us (27%)
  Pallas kernels  25.8 us (13%)
  local copies, waits for them, and re-layouts  16.3 us (8%)
  other arithmetic  6.58 us (3%)
  matrix products  5.85 us (3%)
    all_to_all x1, waiting for transfers between devices, per_device(): lax.all_to_all(outbound.reshape(experts, capacity, both), 'expert', split...  30.8 us
    ppermute x4, waiting for transfers between devices, extended(): after = lax.ppermute(first, axis, down)  28.7 us
    ppermute x4, waiting for transfers between devices, tree_scatter(): got = lax.ppermute(send.astype(jnp.bfloat16), 'dp', pairs)  27.3 us
    ppermute x4, starting transfers between devices, extended(): before = lax.ppermute(last, axis, up)  20 us
    pallas_call x1, Pallas kernels, expert(): pl.pallas_call(functools.partial(expert_kernel, cols), grid=(hidden // ch...  17 us
    ppermute x4, starting transfers between devices, tree_scatter(): got = lax.ppermute(send.astype(jnp.bfloat16), 'dp', pairs)  12.5 us
    pallas_call x2, Pallas kernels, conv_block(): pl.pallas_call(functools.partial(conv_kernel, flip), out_shape=jax.ShapeD...  8.77 us
    ppermute x4, starting transfers between devices, extended(): after = lax.ppermute(first, axis, down)  7.68 us
  transfers between devices with their start and end apart: 14, of which 10 were waited for; matrix products, arithmetic and copies ran while one was open for 9% of the time, Pallas kernels for 0%

profile of v9, /device:TPU:95, one launch (start us, length us, event | category | flops | bytes accessed | tf_op | source)
XLA Modules:
  0.0 199.5 jit_solution(6698912819326930705)
XLA Ops:
  0.6 3.8 %collective-permute-start = (bf16[1,4,128,256]{3,2,1,0:T(8,128)(2,1)}, bf16[1,4,128,256]{3,2,1,0:T(8,128)(2,1)S(1)}, u32[]{:S(2)}, u32[]{:S(2)}) collective-permute-start(bf16[1,4,128,256]{3,2,1,0:T(8,128)(2,1)} %param.11), channel_id=1, source_target_pairs={{0,16},{16,32},{32,48},{48,64},{64,80},{80,96},{96,112},{112,128},... | collective-permute-start | bytes 786440 | tf_op jit(solution)/shard_map/ppermute | solution.py:18
  4.4 1.9 collective-permute-start.1
  9.0 5.4 %collective-permute-done.1 = bf16[1,4,128,256]{3,2,1,0:T(8,128)(2,1)S(1)} collective-permute-done((bf16[1,4,128,256]{3,2,1,0:T(8,128)(2,1)}, bf16[1,4,128,256]{3,2,1,0:T(8,128)(2,1)S(1)}, u32[]{:S(2)}, u32[]{:S(2)}) %collective-permute-start.1) | collective-permute-done | bytes 262176 | tf_op jit(solution)/shard_map/ppermute | solution.py:19
  14.5 5.1 %collective-permute-start.2 = (bf16[3,1,128,256]{3,2,1,0:T(8,128)(2,1)S(1)}, bf16[3,1,128,256]{3,2,1,0:T(8,128)(2,1)S(1)}, u32[]{:S(2)}, u32[]{:S(2)}) collective-permute-start(bf16[3,1,128,256]{3,2,1,0:T(8,128)(2,1)S(1)} %get-tuple-element.20), channel_id=1, source_target_pairs={{0,1},{1,2},{2,3},{3,4},{4,5},{5,6},{6,7},{7,8},{8,9},{9,10},{10,1... | collective-permute-start | bytes 589832 | tf_op jit(solution)/shard_map/ppermute | solution.py:18
  19.6 1.9 collective-permute-start.3
  21.6 2.8 %collective-permute-done.2 = bf16[3,1,128,256]{3,2,1,0:T(8,128)(2,1)S(1)} collective-permute-done((bf16[3,1,128,256]{3,2,1,0:T(8,128)(2,1)S(1)}, bf16[3,1,128,256]{3,2,1,0:T(8,128)(2,1)S(1)}, u32[]{:S(2)}, u32[]{:S(2)}) %collective-permute-start.2) | collective-permute-done | bytes 196640 | tf_op jit(solution)/shard_map/ppermute | solution.py:18
  24.3 8.3 %collective-permute-done.3 = bf16[3,1,128,256]{3,2,1,0:T(8,128)(2,1)S(1)} collective-permute-done((bf16[3,1,128,256]{3,2,1,0:T(8,128)(2,1)S(1)}, bf16[3,1,128,256]{3,2,1,0:T(8,128)(2,1)S(1)}, u32[]{:S(2)}, u32[]{:S(2)}) %collective-permute-start.3) | collective-permute-done | bytes 196640 | tf_op jit(solution)/shard_map/ppermute | solution.py:19
  33.9 4.1 %shard_map.93 = bf16[512,256]{1,0:T(8,128)(2,1)S(1)} custom-call(bf16[1,3,3,6,128,256]{5,4,3,2,1,0:T(8,128)(2,1)S(1)} %maximum_bitcast_fusion.shifted_ref, bf16[27,256,256]{2,1,0:T(8,128)(2,1)} %taps_ref.3), custom_call_target="tpu_custom_call" | custom-call | flops 1811939328 | bytes 7340032 | tf_op jit(solution)/shard_map/pallas_call | solution.py:86
  38.0 2.2 %fusion.2 = bf16[1024,768]{1,0:T(8,128)(2,1)} fusion(s32[512]{0:T(512)S(1)} %add_add_fusion, bf16[512,256]{1,0:T(8,128)(2,1)S(1)} %shard_map.93, bf16[512,512]{1,0:T(8,128)(2,1)S(1)} %bitcast.66), kind=kOutput, calls=%fused_computation.6 | convolution fusion | flops 808189952 | bytes 2361344 | tf_op jit(solution)/shard_map/dot_general | solution.py:204
  40.2 5.8 %all-to-all-start = ((bf16[16,64,768]{2,1,0:T(8,128)(2,1)}), bf16[16,64,768]{2,1,0:T(8,128)(2,1)S(1)}, u32[]{:S(2)}, u32[]{:S(2)}) async-start(bf16[16,64,768]{2,1,0:T(8,128)(2,1)} %bitcast.6), calls=%async_computation | async-start | bytes 3145728 | tf_op jit(solution)/shard_map/all_to_all | solution.py:206
  45.9 30.8 %all-to-all-done = bf16[16,64,768]{2,1,0:T(8,128)(2,1)S(1)} async-done(((bf16[16,64,768]{2,1,0:T(8,128)(2,1)}), bf16[16,64,768]{2,1,0:T(8,128)(2,1)S(1)}, u32[]{:S(2)}, u32[]{:S(2)}) %all-to-all-start) | async-done | bytes 1572896 | tf_op jit(solution)/shard_map/all_to_all | solution.py:206
  78.0 17.0 %shard_map.94 = (bf16[1024,768]{1,0:T(8,128)(2,1)}, f32[2048,768]{1,0:T(8,128)}) custom-call(bf16[1024,768]{1,0:T(8,128)(2,1)} %bitcast.59, bf16[512,2048]{1,0:T(8,128)(2,1)} %bitcast.64, bf16[2048,256]{1,0:T(8,128)(2,1)} %bitcast.65), custom_call_target="tpu_custom_call" | custom-call | flops 9663676416 | bytes 12582912 | tf_op jit(solution)/shard_map/pallas_call | solution.py:147
  95.0 2.1 %constant_dynamic-slice_fusion = bf16[2,2,2,1,128,768]{5,4,3,2,1,0:T(8,128)(2,1)S(1)} fusion(f32[2,2,2,2,128,768]{5,4,3,2,1,0:T(8,128)} %bitcast.57, s32[]{:T(128)S(6)} %select_n.29), kind=kLoop, calls=%fused_computation.43 | loop fusion | bytes 3145732 | tf_op jit(solution)/shard_map/jit(dynamic_index_in_dim)/dynamic_slice | solution.py:42
  97.1 1.6 copy.15
  98.7 2.2 %collective-permute-start.8 = (bf16[2,2,2,128,768]{3,4,0,1,2:T(8,128)(2,1)}, bf16[2,2,2,128,768]{3,4,0,1,2:T(8,128)(2,1)}, u32[]{:S(2)}, u32[]{:S(2)}) collective-permute-start(bf16[2,2,2,128,768]{3,4,0,1,2:T(8,128)(2,1)} %bitcast.49), channel_id=1, source_target_pairs={{0,16},{16,0},{32,48},{48,32},{64,80},{80,64},{96,112},{112,96},{1... | collective-permute-start | bytes 4718600 | tf_op jit(solution)/shard_map/ppermute | solution.py:44
  100.9 7.7 %all-to-all-start.1 = ((bf16[16,64,768]{2,1,0:T(8,128)(2,1)}), bf16[16,64,768]{2,1,0:T(8,128)(2,1)}, u32[]{:S(2)}, u32[]{:S(2)}) async-start(bf16[16,64,768]{2,1,0:T(8,128)(2,1)} %bitcast.10), calls=%async_computation.1 | async-start | bytes 3145728 | tf_op jit(solution)/shard_map/all_to_all | solution.py:210
  108.6 2.2 %constant_dynamic-slice_fusion.1 = f32[2,2,2,1,128,768]{5,4,3,2,1,0:T(8,128)S(1)} fusion(f32[2,2,2,2,128,768]{5,4,3,2,1,0:T(8,128)} %bitcast.58, s32[]{:T(128)S(6)} %select_n.28), kind=kLoop, calls=%fused_computation.44 | loop fusion | bytes 6291460 | tf_op jit(solution)/shard_map/jit(dynamic_index_in_dim)/dynamic_slice | solution.py:41
  110.8 2.3 %copy.12 = f32[2,2,2,1,128,768]{4,5,0,1,2,3:T(8,128)} copy(f32[2,2,2,1,128,768]{5,4,3,2,1,0:T(8,128)S(1)} %constant_dynamic-slice_fusion.1) | data formatting | bytes 6291456 | tf_op jit(solution)/shard_map/jit(dynamic_index_in_dim)/dynamic_slice | solution.py:41
  113.1 2.6 %bitcast_add_fusion = f32[2,2,2,128,768]{3,4,0,1,2:T(8,128)S(1)} fusion(f32[2,2,2,1,128,768]{4,5,0,1,2,3:T(8,128)} %copy.12, bf16[2,2,2,128,768]{3,4,0,1,2:T(8,128)(2,1)} %collective-permute-done.8), kind=kLoop, calls=%fused_computation.2 | loop fusion | flops 1572864 | bytes 7864320 | tf_op jit(solution)/shard_map/add | solution.py:45
  116.8 8.3 %collective-permute-start.9 = (bf16[2,2,128,768]{2,3,0,1:T(8,128)(2,1)}, bf16[2,2,128,768]{2,3,0,1:T(8,128)(2,1)}, u32[]{:S(2)}, u32[]{:S(2)}) collective-permute-start(bf16[2,2,128,768]{2,3,0,1:T(8,128)(2,1)} %fusion.7), channel_id=1, source_target_pairs={{0,32},{16,48},{32,0},{48,16},{64,96},{80,112},{96,64},{112,80},{1... | collective-permute-start | bytes 2359304 | tf_op jit(solution)/shard_map/ppermute | solution.py:44
  125.0 17.8 %collective-permute-done.9 = bf16[2,2,128,768]{2,3,0,1:T(8,128)(2,1)} collective-permute-done((bf16[2,2,128,768]{2,3,0,1:T(8,128)(2,1)}, bf16[2,2,128,768]{2,3,0,1:T(8,128)(2,1)}, u32[]{:S(2)}, u32[]{:S(2)}) %collective-permute-start.9) | collective-permute-done | bytes 786464 | tf_op jit(solution)/shard_map/ppermute | solution.py:44
  142.8 1.3 bitcast_add_fusion.1
  145.3 1.7 collective-permute-start.10
  147.1 9.5 %collective-permute-done.10 = bf16[2,128,768]{1,2,0:T(8,128)(2,1)S(1)} collective-permute-done((bf16[2,128,768]{1,2,0:T(8,128)(2,1)S(1)}, bf16[2,128,768]{1,2,0:T(8,128)(2,1)S(1)}, u32[]{:S(2)}, u32[]{:S(2)}) %collective-permute-start.10) | collective-permute-done | bytes 393248 | tf_op jit(solution)/shard_map/ppermute | solution.py:44
  158.1 2.6 %fusion.3 = bf16[512,768]{1,0:T(8,128)(2,1)S(1)} fusion(bf16[1024,768]{1,0:T(8,128)(2,1)} %bitcast.11, s32[512]{0:T(512)S(1)} %add_add_fusion), kind=kOutput, calls=%fused_computation.10 | convolution fusion | flops 806223872 | bytes 2361344 | tf_op jit(solution)/shard_map/dot_general | solution.py:213
  160.7 5.9 %collective-permute-start.4 = (bf16[1,4,128,256]{3,2,1,0:T(8,128)(2,1)S(1)}, bf16[1,4,128,256]{3,2,1,0:T(8,128)(2,1)S(1)}, u32[]{:S(2)}, u32[]{:S(2)}) collective-permute-start(bf16[1,4,128,256]{3,2,1,0:T(8,128)(2,1)S(1)} %bitcast.52), channel_id=1, source_target_pairs={{0,16},{16,32},{32,48},{48,64},{64,80},{80,96},{96,112},{112,128},... | collective-permute-start | bytes 786440 | tf_op jit(solution)/shard_map/ppermute | solution.py:18
  166.7 1.9 collective-permute-start.5
  170.3 6.2 %collective-permute-done.5 = bf16[1,4,128,256]{3,2,1,0:T(8,128)(2,1)S(1)} collective-permute-done((bf16[1,4,128,256]{3,2,1,0:T(8,128)(2,1)S(1)}, bf16[1,4,128,256]{3,2,1,0:T(8,128)(2,1)S(1)}, u32[]{:S(2)}, u32[]{:S(2)}) %collective-permute-start.5) | collective-permute-done | bytes 262176 | tf_op jit(solution)/shard_map/ppermute | solution.py:19
  176.5 5.2 %collective-permute-start.6 = (bf16[3,1,128,256]{3,2,1,0:T(8,128)(2,1)S(1)}, bf16[3,1,128,256]{3,2,1,0:T(8,128)(2,1)S(1)}, u32[]{:S(2)}, u32[]{:S(2)}) collective-permute-start(bf16[3,1,128,256]{3,2,1,0:T(8,128)(2,1)S(1)} %get-tuple-element.18), channel_id=1, source_target_pairs={{0,1},{1,2},{2,3},{3,4},{4,5},{5,6},{6,7},{7,8},{8,9},{9,10},{10,1... | collective-permute-start | bytes 589832 | tf_op jit(solution)/shard_map/ppermute | solution.py:18
  181.7 1.9 collective-permute-start.7
  184.6 8.8 %collective-permute-done.7 = bf16[3,1,128,256]{3,2,1,0:T(8,128)(2,1)S(1)} collective-permute-done((bf16[3,1,128,256]{3,2,1,0:T(8,128)(2,1)S(1)}, bf16[3,1,128,256]{3,2,1,0:T(8,128)(2,1)S(1)}, u32[]{:S(2)}, u32[]{:S(2)}) %collective-permute-start.7) | collective-permute-done | bytes 196640 | tf_op jit(solution)/shard_map/ppermute | solution.py:19
  194.8 4.7 %shard_map.95 = bf16[512,256]{1,0:T(8,128)(2,1)} custom-call(bf16[1,3,3,6,128,256]{5,4,3,2,1,0:T(8,128)(2,1)S(1)} %maximum_bitcast_fusion.1.shifted_ref, bf16[27,256,256]{2,1,0:T(8,128)(2,1)} %taps_ref.3), custom_call_target="tpu_custom_call" | custom-call | flops 1811939328 | bytes 7340032 | tf_op jit(solution)/shard_map/pallas_call | solution.py:86
  (39 shorter events, 13.0 us)
Async XLA Ops:
  0.6 20.9 %copy-start.2 = (s32[1,4,128,1]{2,3,1,0:T(1,128)S(1)}, s32[1,4,128,1]{2,3,1,0:T(1,128)}, u32[]{:S(2)}) copy-start(s32[1,4,128,1]{2,3,1,0:T(1,128)} %param.7) | copy-start | bytes 6148
  0.6 7.4 %collective-permute-start = (bf16[1,4,128,256]{3,2,1,0:T(8,128)(2,1)}, bf16[1,4,128,256]{3,2,1,0:T(8,128)(2,1)S(1)}, u32[]{:S(2)}, u32[]{:S(2)}) collective-permute-start(bf16[1,4,128,256]{3,2,1,0:T(8,128)(2,1)} %param.11), channel_id=1, source_target_pairs={{0,16},{16,32},{32,48},{48,64},{64,80},{80,96},{96,112},{112,128},... | collective-permute-start | bytes 786440 | tf_op jit(solution)/shard_map/ppermute | solution.py:18
  4.4 10.0 %collective-permute-start.1 = (bf16[1,4,128,256]{3,2,1,0:T(8,128)(2,1)}, bf16[1,4,128,256]{3,2,1,0:T(8,128)(2,1)S(1)}, u32[]{:S(2)}, u32[]{:S(2)}) collective-permute-start(bf16[1,4,128,256]{3,2,1,0:T(8,128)(2,1)} %param.11), channel_id=1, source_target_pairs={{16,0},{32,16},{48,32},{64,48},{80,64},{96,80},{112,96},{128,112},... | collective-permute-start | bytes 786440 | tf_op jit(solution)/shard_map/ppermute | solution.py:19
  14.5 9.9 %collective-permute-start.2 = (bf16[3,1,128,256]{3,2,1,0:T(8,128)(2,1)S(1)}, bf16[3,1,128,256]{3,2,1,0:T(8,128)(2,1)S(1)}, u32[]{:S(2)}, u32[]{:S(2)}) collective-permute-start(bf16[3,1,128,256]{3,2,1,0:T(8,128)(2,1)S(1)} %get-tuple-element.20), channel_id=1, source_target_pairs={{0,1},{1,2},{2,3},{3,4},{4,5},{5,6},{6,7},{7,8},{8,9},{9,10},{10,1... | collective-permute-start | bytes 589832 | tf_op jit(solution)/shard_map/ppermute | solution.py:18
  19.6 13.0 %collective-permute-start.3 = (bf16[3,1,128,256]{3,2,1,0:T(8,128)(2,1)S(1)}, bf16[3,1,128,256]{3,2,1,0:T(8,128)(2,1)S(1)}, u32[]{:S(2)}, u32[]{:S(2)}) collective-permute-start(bf16[3,1,128,256]{3,2,1,0:T(8,128)(2,1)S(1)} %get-tuple-element.21), channel_id=1, source_target_pairs={{1,0},{2,1},{3,2},{4,3},{5,4},{6,5},{7,6},{8,7},{9,8},{10,9},{11,1... | collective-permute-start | bytes 589832 | tf_op jit(solution)/shard_map/ppermute | solution.py:19
  33.9 4.1 %copy-start.3 = (bf16[1,4,128,512]{3,2,1,0:T(8,128)(2,1)S(1)}, bf16[1,4,128,512]{3,2,1,0:T(8,128)(2,1)}, u32[]{:S(2)}) copy-start(bf16[1,4,128,512]{3,2,1,0:T(8,128)(2,1)} %param.6) | copy-start | bytes 1572868
  40.2 36.6 %all-to-all-start = ((bf16[16,64,768]{2,1,0:T(8,128)(2,1)}), bf16[16,64,768]{2,1,0:T(8,128)(2,1)S(1)}, u32[]{:S(2)}, u32[]{:S(2)}) async-start(bf16[16,64,768]{2,1,0:T(8,128)(2,1)} %bitcast.6), calls=%async_computation | async-start | bytes 3145728 | tf_op jit(solution)/shard_map/all_to_all | solution.py:206
  76.8 1.2 copy-start.1
  98.7 14.5 %collective-permute-start.8 = (bf16[2,2,2,128,768]{3,4,0,1,2:T(8,128)(2,1)}, bf16[2,2,2,128,768]{3,4,0,1,2:T(8,128)(2,1)}, u32[]{:S(2)}, u32[]{:S(2)}) collective-permute-start(bf16[2,2,2,128,768]{3,4,0,1,2:T(8,128)(2,1)} %bitcast.49), channel_id=1, source_target_pairs={{0,16},{16,0},{32,48},{48,32},{64,80},{80,64},{96,112},{112,96},{1... | collective-permute-start | bytes 4718600 | tf_op jit(solution)/shard_map/ppermute | solution.py:44
  100.9 57.2 %all-to-all-start.1 = ((bf16[16,64,768]{2,1,0:T(8,128)(2,1)}), bf16[16,64,768]{2,1,0:T(8,128)(2,1)}, u32[]{:S(2)}, u32[]{:S(2)}) async-start(bf16[16,64,768]{2,1,0:T(8,128)(2,1)} %bitcast.10), calls=%async_computation.1 | async-start | bytes 3145728 | tf_op jit(solution)/shard_map/all_to_all | solution.py:210
  116.8 26.1 %collective-permute-start.9 = (bf16[2,2,128,768]{2,3,0,1:T(8,128)(2,1)}, bf16[2,2,128,768]{2,3,0,1:T(8,128)(2,1)}, u32[]{:S(2)}, u32[]{:S(2)}) collective-permute-start(bf16[2,2,128,768]{2,3,0,1:T(8,128)(2,1)} %fusion.7), channel_id=1, source_target_pairs={{0,32},{16,48},{32,0},{48,16},{64,96},{80,112},{96,64},{112,80},{1... | collective-permute-start | bytes 2359304 | tf_op jit(solution)/shard_map/ppermute | solution.py:44
  144.1 1.2 copy-start
  145.3 11.2 %collective-permute-start.10 = (bf16[2,128,768]{1,2,0:T(8,128)(2,1)S(1)}, bf16[2,128,768]{1,2,0:T(8,128)(2,1)S(1)}, u32[]{:S(2)}, u32[]{:S(2)}) collective-permute-start(bf16[2,128,768]{1,2,0:T(8,128)(2,1)S(1)} %fusion.11), channel_id=1, source_target_pairs={{0,64},{16,80},{32,96},{48,112},{64,0},{80,16},{96,32},{112,48},{1... | collective-permute-start | bytes 1179656 | tf_op jit(solution)/shard_map/ppermute | solution.py:44
  157.8 10.8 %collective-permute-start.11 = (bf16[128,768]{0,1:T(8,128)(2,1)S(1)}, bf16[128,768]{0,1:T(8,128)(2,1)S(1)}, u32[]{:S(2)}, u32[]{:S(2)}) collective-permute-start(bf16[128,768]{0,1:T(8,128)(2,1)S(1)} %fusion.12), channel_id=1, source_target_pairs={{0,128},{16,144},{32,160},{48,176},{64,192},{80,208},{96,224},{112... | collective-permute-start | bytes 589832 | tf_op jit(solution)/shard_map/ppermute | solution.py:44
  160.7 9.5 %collective-permute-start.4 = (bf16[1,4,128,256]{3,2,1,0:T(8,128)(2,1)S(1)}, bf16[1,4,128,256]{3,2,1,0:T(8,128)(2,1)S(1)}, u32[]{:S(2)}, u32[]{:S(2)}) collective-permute-start(bf16[1,4,128,256]{3,2,1,0:T(8,128)(2,1)S(1)} %bitcast.52), channel_id=1, source_target_pairs={{0,16},{16,32},{32,48},{48,64},{64,80},{80,96},{96,112},{112,128},... | collective-permute-start | bytes 786440 | tf_op jit(solution)/shard_map/ppermute | solution.py:18
  166.7 9.8 %collective-permute-start.5 = (bf16[1,4,128,256]{3,2,1,0:T(8,128)(2,1)S(1)}, bf16[1,4,128,256]{3,2,1,0:T(8,128)(2,1)S(1)}, u32[]{:S(2)}, u32[]{:S(2)}) collective-permute-start(bf16[1,4,128,256]{3,2,1,0:T(8,128)(2,1)S(1)} %bitcast.53), channel_id=1, source_target_pairs={{16,0},{32,16},{48,32},{64,48},{80,64},{96,80},{112,96},{128,112},... | collective-permute-start | bytes 786440 | tf_op jit(solution)/shard_map/ppermute | solution.py:19
  176.5 8.1 %collective-permute-start.6 = (bf16[3,1,128,256]{3,2,1,0:T(8,128)(2,1)S(1)}, bf16[3,1,128,256]{3,2,1,0:T(8,128)(2,1)S(1)}, u32[]{:S(2)}, u32[]{:S(2)}) collective-permute-start(bf16[3,1,128,256]{3,2,1,0:T(8,128)(2,1)S(1)} %get-tuple-element.18), channel_id=1, source_target_pairs={{0,1},{1,2},{2,3},{3,4},{4,5},{5,6},{6,7},{7,8},{8,9},{9,10},{10,1... | collective-permute-start | bytes 589832 | tf_op jit(solution)/shard_map/ppermute | solution.py:18
  181.7 11.6 %collective-permute-start.7 = (bf16[3,1,128,256]{3,2,1,0:T(8,128)(2,1)S(1)}, bf16[3,1,128,256]{3,2,1,0:T(8,128)(2,1)S(1)}, u32[]{:S(2)}, u32[]{:S(2)}) collective-permute-start(bf16[3,1,128,256]{3,2,1,0:T(8,128)(2,1)S(1)} %get-tuple-element.19), channel_id=1, source_target_pairs={{1,0},{2,1},{3,2},{4,3},{5,4},{6,5},{7,6},{8,7},{9,8},{10,9},{11,1... | collective-permute-start | bytes 589832 | tf_op jit(solution)/shard_map/ppermute | solution.py:19

commit v10 on v9

--- a/solution.py
+++ b/solution.py
@@ -206,7 +206,7 @@
     inbound = lax.all_to_all(
         outbound.reshape(experts, capacity, both), "expert", split_axis=0, concat_axis=0, tiled=True
     ).reshape(slots, both)
-    back, part = expert(inbound, w_first[0], w_second[0], 512)
+    back, part = expert(inbound, w_first[0], w_second[0], 1024)
     returned = lax.all_to_all(
         back.reshape(experts, capacity, both), "expert", split_axis=0, concat_axis=0, tiled=True
     )

time: 202 us -> 201 us (level)
  no operation moved by 1% of the time
where the time goes in v10:
time: 201 us; the launch traced here: 199 us
  waiting for transfers between devices  90.4 us (45%)
  starting transfers between devices  53.5 us (27%)
  Pallas kernels  25.7 us (13%)
  local copies, waits for them, and re-layouts  16.3 us (8%)
  other arithmetic  6.58 us (3%)
  matrix products  5.84 us (3%)
    all_to_all x1, waiting for transfers between devices, per_device(): lax.all_to_all(outbound.reshape(experts, capacity, both), 'expert', split...  30.8 us
    ppermute x4, waiting for transfers between devices, extended(): after = lax.ppermute(first, axis, down)  28.7 us
    ppermute x4, waiting for transfers between devices, tree_scatter(): got = lax.ppermute(send.astype(jnp.bfloat16), 'dp', pairs)  27.3 us
    ppermute x4, starting transfers between devices, extended(): before = lax.ppermute(last, axis, up)  20 us
    pallas_call x1, Pallas kernels, expert(): pl.pallas_call(functools.partial(expert_kernel, cols), grid=(hidden // ch...  17 us
    ppermute x4, starting transfers between devices, tree_scatter(): got = lax.ppermute(send.astype(jnp.bfloat16), 'dp', pairs)  12.3 us
    pallas_call x2, Pallas kernels, conv_block(): pl.pallas_call(functools.partial(conv_kernel, flip), out_shape=jax.ShapeD...  8.77 us
    ppermute x4, starting transfers between devices, extended(): after = lax.ppermute(first, axis, down)  7.68 us
  transfers between devices with their start and end apart: 14, of which 10 were waited for; matrix products, arithmetic and copies ran while one was open for 9% of the time, Pallas kernels for 0%

profile of v10, /device:TPU:95, one launch (start us, length us, event | category | flops | bytes accessed | tf_op | source)
XLA Modules:
  0.0 199.2 jit_solution(15884523472706041021)
XLA Ops:
  0.6 3.8 %collective-permute-start = (bf16[1,4,128,256]{3,2,1,0:T(8,128)(2,1)}, bf16[1,4,128,256]{3,2,1,0:T(8,128)(2,1)S(1)}, u32[]{:S(2)}, u32[]{:S(2)}) collective-permute-start(bf16[1,4,128,256]{3,2,1,0:T(8,128)(2,1)} %param.11), channel_id=1, source_target_pairs={{0,16},{16,32},{32,48},{48,64},{64,80},{80,96},{96,112},{112,128},... | collective-permute-start | bytes 786440 | tf_op jit(solution)/shard_map/ppermute | solution.py:18
  4.4 1.9 collective-permute-start.1
  9.0 5.4 %collective-permute-done.1 = bf16[1,4,128,256]{3,2,1,0:T(8,128)(2,1)S(1)} collective-permute-done((bf16[1,4,128,256]{3,2,1,0:T(8,128)(2,1)}, bf16[1,4,128,256]{3,2,1,0:T(8,128)(2,1)S(1)}, u32[]{:S(2)}, u32[]{:S(2)}) %collective-permute-start.1) | collective-permute-done | bytes 262176 | tf_op jit(solution)/shard_map/ppermute | solution.py:19
  14.5 5.1 %collective-permute-start.2 = (bf16[3,1,128,256]{3,2,1,0:T(8,128)(2,1)S(1)}, bf16[3,1,128,256]{3,2,1,0:T(8,128)(2,1)S(1)}, u32[]{:S(2)}, u32[]{:S(2)}) collective-permute-start(bf16[3,1,128,256]{3,2,1,0:T(8,128)(2,1)S(1)} %get-tuple-element.20), channel_id=1, source_target_pairs={{0,1},{1,2},{2,3},{3,4},{4,5},{5,6},{6,7},{7,8},{8,9},{9,10},{10,1... | collective-permute-start | bytes 589832 | tf_op jit(solution)/shard_map/ppermute | solution.py:18
  19.6 1.9 collective-permute-start.3
  21.6 2.8 %collective-permute-done.2 = bf16[3,1,128,256]{3,2,1,0:T(8,128)(2,1)S(1)} collective-permute-done((bf16[3,1,128,256]{3,2,1,0:T(8,128)(2,1)S(1)}, bf16[3,1,128,256]{3,2,1,0:T(8,128)(2,1)S(1)}, u32[]{:S(2)}, u32[]{:S(2)}) %collective-permute-start.2) | collective-permute-done | bytes 196640 | tf_op jit(solution)/shard_map/ppermute | solution.py:18
  24.3 8.3 %collective-permute-done.3 = bf16[3,1,128,256]{3,2,1,0:T(8,128)(2,1)S(1)} collective-permute-done((bf16[3,1,128,256]{3,2,1,0:T(8,128)(2,1)S(1)}, bf16[3,1,128,256]{3,2,1,0:T(8,128)(2,1)S(1)}, u32[]{:S(2)}, u32[]{:S(2)}) %collective-permute-start.3) | collective-permute-done | bytes 196640 | tf_op jit(solution)/shard_map/ppermute | solution.py:19
  33.9 4.1 %shard_map.93 = bf16[512,256]{1,0:T(8,128)(2,1)S(1)} custom-call(bf16[1,3,3,6,128,256]{5,4,3,2,1,0:T(8,128)(2,1)S(1)} %maximum_bitcast_fusion.shifted_ref, bf16[27,256,256]{2,1,0:T(8,128)(2,1)} %taps_ref.3), custom_call_target="tpu_custom_call" | custom-call | flops 1811939328 | bytes 7340032 | tf_op jit(solution)/shard_map/pallas_call | solution.py:86
  38.0 2.2 %fusion.2 = bf16[1024,768]{1,0:T(8,128)(2,1)} fusion(s32[512]{0:T(512)S(1)} %add_add_fusion, bf16[512,256]{1,0:T(8,128)(2,1)S(1)} %shard_map.93, bf16[512,512]{1,0:T(8,128)(2,1)S(1)} %bitcast.66), kind=kOutput, calls=%fused_computation.6 | convolution fusion | flops 808189952 | bytes 2361344 | tf_op jit(solution)/shard_map/dot_general | solution.py:204
  40.2 5.8 %all-to-all-start = ((bf16[16,64,768]{2,1,0:T(8,128)(2,1)}), bf16[16,64,768]{2,1,0:T(8,128)(2,1)S(1)}, u32[]{:S(2)}, u32[]{:S(2)}) async-start(bf16[16,64,768]{2,1,0:T(8,128)(2,1)} %bitcast.6), calls=%async_computation | async-start | bytes 3145728 | tf_op jit(solution)/shard_map/all_to_all | solution.py:206
  45.9 30.8 %all-to-all-done = bf16[16,64,768]{2,1,0:T(8,128)(2,1)S(1)} async-done(((bf16[16,64,768]{2,1,0:T(8,128)(2,1)}), bf16[16,64,768]{2,1,0:T(8,128)(2,1)S(1)}, u32[]{:S(2)}, u32[]{:S(2)}) %all-to-all-start) | async-done | bytes 1572896 | tf_op jit(solution)/shard_map/all_to_all | solution.py:206
  78.0 17.0 %shard_map.94 = (bf16[1024,768]{1,0:T(8,128)(2,1)}, f32[2048,768]{1,0:T(8,128)}) custom-call(bf16[1024,768]{1,0:T(8,128)(2,1)} %bitcast.59, bf16[512,2048]{1,0:T(8,128)(2,1)} %bitcast.64, bf16[2048,256]{1,0:T(8,128)(2,1)} %bitcast.65), custom_call_target="tpu_custom_call" | custom-call | flops 9663676416 | bytes 12582912 | tf_op jit(solution)/shard_map/pallas_call | solution.py:147
  95.0 2.1 %constant_dynamic-slice_fusion = bf16[2,2,2,1,128,768]{5,4,3,2,1,0:T(8,128)(2,1)S(1)} fusion(f32[2,2,2,2,128,768]{5,4,3,2,1,0:T(8,128)} %bitcast.57, s32[]{:T(128)S(6)} %select_n.29), kind=kLoop, calls=%fused_computation.43 | loop fusion | bytes 3145732 | tf_op jit(solution)/shard_map/jit(dynamic_index_in_dim)/dynamic_slice | solution.py:42
  97.0 1.6 copy.15
  98.6 2.2 %collective-permute-start.8 = (bf16[2,2,2,128,768]{3,4,0,1,2:T(8,128)(2,1)}, bf16[2,2,2,128,768]{3,4,0,1,2:T(8,128)(2,1)}, u32[]{:S(2)}, u32[]{:S(2)}) collective-permute-start(bf16[2,2,2,128,768]{3,4,0,1,2:T(8,128)(2,1)} %bitcast.49), channel_id=1, source_target_pairs={{0,16},{16,0},{32,48},{48,32},{64,80},{80,64},{96,112},{112,96},{1... | collective-permute-start | bytes 4718600 | tf_op jit(solution)/shard_map/ppermute | solution.py:44
  100.8 7.7 %all-to-all-start.1 = ((bf16[16,64,768]{2,1,0:T(8,128)(2,1)}), bf16[16,64,768]{2,1,0:T(8,128)(2,1)}, u32[]{:S(2)}, u32[]{:S(2)}) async-start(bf16[16,64,768]{2,1,0:T(8,128)(2,1)} %bitcast.10), calls=%async_computation.1 | async-start | bytes 3145728 | tf_op jit(solution)/shard_map/all_to_all | solution.py:210
  108.5 2.2 %constant_dynamic-slice_fusion.1 = f32[2,2,2,1,128,768]{5,4,3,2,1,0:T(8,128)S(1)} fusion(f32[2,2,2,2,128,768]{5,4,3,2,1,0:T(8,128)} %bitcast.58, s32[]{:T(128)S(6)} %select_n.28), kind=kLoop, calls=%fused_computation.44 | loop fusion | bytes 6291460 | tf_op jit(solution)/shard_map/jit(dynamic_index_in_dim)/dynamic_slice | solution.py:41
  110.7 2.3 %copy.12 = f32[2,2,2,1,128,768]{4,5,0,1,2,3:T(8,128)} copy(f32[2,2,2,1,128,768]{5,4,3,2,1,0:T(8,128)S(1)} %constant_dynamic-slice_fusion.1) | data formatting | bytes 6291456 | tf_op jit(solution)/shard_map/jit(dynamic_index_in_dim)/dynamic_slice | solution.py:41
  113.1 2.6 %bitcast_add_fusion = f32[2,2,2,128,768]{3,4,0,1,2:T(8,128)S(1)} fusion(f32[2,2,2,1,128,768]{4,5,0,1,2,3:T(8,128)} %copy.12, bf16[2,2,2,128,768]{3,4,0,1,2:T(8,128)(2,1)} %collective-permute-done.8), kind=kLoop, calls=%fused_computation.2 | loop fusion | flops 1572864 | bytes 7864320 | tf_op jit(solution)/shard_map/add | solution.py:45
  116.7 8.3 %collective-permute-start.9 = (bf16[2,2,128,768]{2,3,0,1:T(8,128)(2,1)}, bf16[2,2,128,768]{2,3,0,1:T(8,128)(2,1)}, u32[]{:S(2)}, u32[]{:S(2)}) collective-permute-start(bf16[2,2,128,768]{2,3,0,1:T(8,128)(2,1)} %fusion.7), channel_id=1, source_target_pairs={{0,32},{16,48},{32,0},{48,16},{64,96},{80,112},{96,64},{112,80},{1... | collective-permute-start | bytes 2359304 | tf_op jit(solution)/shard_map/ppermute | solution.py:44
  125.0 17.8 %collective-permute-done.9 = bf16[2,2,128,768]{2,3,0,1:T(8,128)(2,1)} collective-permute-done((bf16[2,2,128,768]{2,3,0,1:T(8,128)(2,1)}, bf16[2,2,128,768]{2,3,0,1:T(8,128)(2,1)}, u32[]{:S(2)}, u32[]{:S(2)}) %collective-permute-start.9) | collective-permute-done | bytes 786464 | tf_op jit(solution)/shard_map/ppermute | solution.py:44
  142.8 1.3 bitcast_add_fusion.1
  145.3 1.7 collective-permute-start.10
  147.0 9.5 %collective-permute-done.10 = bf16[2,128,768]{1,2,0:T(8,128)(2,1)S(1)} collective-permute-done((bf16[2,128,768]{1,2,0:T(8,128)(2,1)S(1)}, bf16[2,128,768]{1,2,0:T(8,128)(2,1)S(1)}, u32[]{:S(2)}, u32[]{:S(2)}) %collective-permute-start.10) | collective-permute-done | bytes 393248 | tf_op jit(solution)/shard_map/ppermute | solution.py:44
  157.8 2.6 %fusion.3 = bf16[512,768]{1,0:T(8,128)(2,1)S(1)} fusion(bf16[1024,768]{1,0:T(8,128)(2,1)} %bitcast.11, s32[512]{0:T(512)S(1)} %add_add_fusion), kind=kOutput, calls=%fused_computation.10 | convolution fusion | flops 806223872 | bytes 2361344 | tf_op jit(solution)/shard_map/dot_general | solution.py:213
  160.5 5.9 %collective-permute-start.4 = (bf16[1,4,128,256]{3,2,1,0:T(8,128)(2,1)S(1)}, bf16[1,4,128,256]{3,2,1,0:T(8,128)(2,1)S(1)}, u32[]{:S(2)}, u32[]{:S(2)}) collective-permute-start(bf16[1,4,128,256]{3,2,1,0:T(8,128)(2,1)S(1)} %bitcast.52), channel_id=1, source_target_pairs={{0,16},{16,32},{32,48},{48,64},{64,80},{80,96},{96,112},{112,128},... | collective-permute-start | bytes 786440 | tf_op jit(solution)/shard_map/ppermute | solution.py:18
  166.4 1.9 collective-permute-start.5
  170.0 6.2 %collective-permute-done.5 = bf16[1,4,128,256]{3,2,1,0:T(8,128)(2,1)S(1)} collective-permute-done((bf16[1,4,128,256]{3,2,1,0:T(8,128)(2,1)S(1)}, bf16[1,4,128,256]{3,2,1,0:T(8,128)(2,1)S(1)}, u32[]{:S(2)}, u32[]{:S(2)}) %collective-permute-start.5) | collective-permute-done | bytes 262176 | tf_op jit(solution)/shard_map/ppermute | solution.py:19
  176.3 5.2 %collective-permute-start.6 = (bf16[3,1,128,256]{3,2,1,0:T(8,128)(2,1)S(1)}, bf16[3,1,128,256]{3,2,1,0:T(8,128)(2,1)S(1)}, u32[]{:S(2)}, u32[]{:S(2)}) collective-permute-start(bf16[3,1,128,256]{3,2,1,0:T(8,128)(2,1)S(1)} %get-tuple-element.18), channel_id=1, source_target_pairs={{0,1},{1,2},{2,3},{3,4},{4,5},{5,6},{6,7},{7,8},{8,9},{9,10},{10,1... | collective-permute-start | bytes 589832 | tf_op jit(solution)/shard_map/ppermute | solution.py:18
  181.5 1.9 collective-permute-start.7
  184.4 8.7 %collective-permute-done.7 = bf16[3,1,128,256]{3,2,1,0:T(8,128)(2,1)S(1)} collective-permute-done((bf16[3,1,128,256]{3,2,1,0:T(8,128)(2,1)S(1)}, bf16[3,1,128,256]{3,2,1,0:T(8,128)(2,1)S(1)}, u32[]{:S(2)}, u32[]{:S(2)}) %collective-permute-start.7) | collective-permute-done | bytes 196640 | tf_op jit(solution)/shard_map/ppermute | solution.py:19
  194.5 4.7 %shard_map.95 = bf16[512,256]{1,0:T(8,128)(2,1)} custom-call(bf16[1,3,3,6,128,256]{5,4,3,2,1,0:T(8,128)(2,1)S(1)} %maximum_bitcast_fusion.1.shifted_ref, bf16[27,256,256]{2,1,0:T(8,128)(2,1)} %taps_ref.3), custom_call_target="tpu_custom_call" | custom-call | flops 1811939328 | bytes 7340032 | tf_op jit(solution)/shard_map/pallas_call | solution.py:86
  (39 shorter events, 12.8 us)
Async XLA Ops:
  0.6 20.9 %copy-start.2 = (s32[1,4,128,1]{2,3,1,0:T(1,128)S(1)}, s32[1,4,128,1]{2,3,1,0:T(1,128)}, u32[]{:S(2)}) copy-start(s32[1,4,128,1]{2,3,1,0:T(1,128)} %param.7) | copy-start | bytes 6148
  0.6 7.4 %collective-permute-start = (bf16[1,4,128,256]{3,2,1,0:T(8,128)(2,1)}, bf16[1,4,128,256]{3,2,1,0:T(8,128)(2,1)S(1)}, u32[]{:S(2)}, u32[]{:S(2)}) collective-permute-start(bf16[1,4,128,256]{3,2,1,0:T(8,128)(2,1)} %param.11), channel_id=1, source_target_pairs={{0,16},{16,32},{32,48},{48,64},{64,80},{80,96},{96,112},{112,128},... | collective-permute-start | bytes 786440 | tf_op jit(solution)/shard_map/ppermute | solution.py:18
  4.4 10.0 %collective-permute-start.1 = (bf16[1,4,128,256]{3,2,1,0:T(8,128)(2,1)}, bf16[1,4,128,256]{3,2,1,0:T(8,128)(2,1)S(1)}, u32[]{:S(2)}, u32[]{:S(2)}) collective-permute-start(bf16[1,4,128,256]{3,2,1,0:T(8,128)(2,1)} %param.11), channel_id=1, source_target_pairs={{16,0},{32,16},{48,32},{64,48},{80,64},{96,80},{112,96},{128,112},... | collective-permute-start | bytes 786440 | tf_op jit(solution)/shard_map/ppermute | solution.py:19
  14.5 9.9 %collective-permute-start.2 = (bf16[3,1,128,256]{3,2,1,0:T(8,128)(2,1)S(1)}, bf16[3,1,128,256]{3,2,1,0:T(8,128)(2,1)S(1)}, u32[]{:S(2)}, u32[]{:S(2)}) collective-permute-start(bf16[3,1,128,256]{3,2,1,0:T(8,128)(2,1)S(1)} %get-tuple-element.20), channel_id=1, source_target_pairs={{0,1},{1,2},{2,3},{3,4},{4,5},{5,6},{6,7},{7,8},{8,9},{9,10},{10,1... | collective-permute-start | bytes 589832 | tf_op jit(solution)/shard_map/ppermute | solution.py:18
  19.6 13.0 %collective-permute-start.3 = (bf16[3,1,128,256]{3,2,1,0:T(8,128)(2,1)S(1)}, bf16[3,1,128,256]{3,2,1,0:T(8,128)(2,1)S(1)}, u32[]{:S(2)}, u32[]{:S(2)}) collective-permute-start(bf16[3,1,128,256]{3,2,1,0:T(8,128)(2,1)S(1)} %get-tuple-element.21), channel_id=1, source_target_pairs={{1,0},{2,1},{3,2},{4,3},{5,4},{6,5},{7,6},{8,7},{9,8},{10,9},{11,1... | collective-permute-start | bytes 589832 | tf_op jit(solution)/shard_map/ppermute | solution.py:19
  33.9 4.1 %copy-start.3 = (bf16[1,4,128,512]{3,2,1,0:T(8,128)(2,1)S(1)}, bf16[1,4,128,512]{3,2,1,0:T(8,128)(2,1)}, u32[]{:S(2)}) copy-start(bf16[1,4,128,512]{3,2,1,0:T(8,128)(2,1)} %param.6) | copy-start | bytes 1572868
  40.2 36.6 %all-to-all-start = ((bf16[16,64,768]{2,1,0:T(8,128)(2,1)}), bf16[16,64,768]{2,1,0:T(8,128)(2,1)S(1)}, u32[]{:S(2)}, u32[]{:S(2)}) async-start(bf16[16,64,768]{2,1,0:T(8,128)(2,1)} %bitcast.6), calls=%async_computation | async-start | bytes 3145728 | tf_op jit(solution)/shard_map/all_to_all | solution.py:206
  76.8 1.2 copy-start.1
  98.6 14.5 %collective-permute-start.8 = (bf16[2,2,2,128,768]{3,4,0,1,2:T(8,128)(2,1)}, bf16[2,2,2,128,768]{3,4,0,1,2:T(8,128)(2,1)}, u32[]{:S(2)}, u32[]{:S(2)}) collective-permute-start(bf16[2,2,2,128,768]{3,4,0,1,2:T(8,128)(2,1)} %bitcast.49), channel_id=1, source_target_pairs={{0,16},{16,0},{32,48},{48,32},{64,80},{80,64},{96,112},{112,96},{1... | collective-permute-start | bytes 4718600 | tf_op jit(solution)/shard_map/ppermute | solution.py:44
  100.8 57.0 %all-to-all-start.1 = ((bf16[16,64,768]{2,1,0:T(8,128)(2,1)}), bf16[16,64,768]{2,1,0:T(8,128)(2,1)}, u32[]{:S(2)}, u32[]{:S(2)}) async-start(bf16[16,64,768]{2,1,0:T(8,128)(2,1)} %bitcast.10), calls=%async_computation.1 | async-start | bytes 3145728 | tf_op jit(solution)/shard_map/all_to_all | solution.py:210
  116.7 26.1 %collective-permute-start.9 = (bf16[2,2,128,768]{2,3,0,1:T(8,128)(2,1)}, bf16[2,2,128,768]{2,3,0,1:T(8,128)(2,1)}, u32[]{:S(2)}, u32[]{:S(2)}) collective-permute-start(bf16[2,2,128,768]{2,3,0,1:T(8,128)(2,1)} %fusion.7), channel_id=1, source_target_pairs={{0,32},{16,48},{32,0},{48,16},{64,96},{80,112},{96,64},{112,80},{1... | collective-permute-start | bytes 2359304 | tf_op jit(solution)/shard_map/ppermute | solution.py:44
  144.0 1.2 copy-start
  145.3 11.2 %collective-permute-start.10 = (bf16[2,128,768]{1,2,0:T(8,128)(2,1)S(1)}, bf16[2,128,768]{1,2,0:T(8,128)(2,1)S(1)}, u32[]{:S(2)}, u32[]{:S(2)}) collective-permute-start(bf16[2,128,768]{1,2,0:T(8,128)(2,1)S(1)} %fusion.11), channel_id=1, source_target_pairs={{0,64},{16,80},{32,96},{48,112},{64,0},{80,16},{96,32},{112,48},{1... | collective-permute-start | bytes 1179656 | tf_op jit(solution)/shard_map/ppermute | solution.py:44
  157.7 10.6 %collective-permute-start.11 = (bf16[128,768]{0,1:T(8,128)(2,1)S(1)}, bf16[128,768]{0,1:T(8,128)(2,1)S(1)}, u32[]{:S(2)}, u32[]{:S(2)}) collective-permute-start(bf16[128,768]{0,1:T(8,128)(2,1)S(1)} %fusion.12), channel_id=1, source_target_pairs={{0,128},{16,144},{32,160},{48,176},{64,192},{80,208},{96,224},{112... | collective-permute-start | bytes 589832 | tf_op jit(solution)/shard_map/ppermute | solution.py:44
  160.5 9.5 %collective-permute-start.4 = (bf16[1,4,128,256]{3,2,1,0:T(8,128)(2,1)S(1)}, bf16[1,4,128,256]{3,2,1,0:T(8,128)(2,1)S(1)}, u32[]{:S(2)}, u32[]{:S(2)}) collective-permute-start(bf16[1,4,128,256]{3,2,1,0:T(8,128)(2,1)S(1)} %bitcast.52), channel_id=1, source_target_pairs={{0,16},{16,32},{32,48},{48,64},{64,80},{80,96},{96,112},{112,128},... | collective-permute-start | bytes 786440 | tf_op jit(solution)/shard_map/ppermute | solution.py:18
  166.4 9.8 %collective-permute-start.5 = (bf16[1,4,128,256]{3,2,1,0:T(8,128)(2,1)S(1)}, bf16[1,4,128,256]{3,2,1,0:T(8,128)(2,1)S(1)}, u32[]{:S(2)}, u32[]{:S(2)}) collective-permute-start(bf16[1,4,128,256]{3,2,1,0:T(8,128)(2,1)S(1)} %bitcast.53), channel_id=1, source_target_pairs={{16,0},{32,16},{48,32},{64,48},{80,64},{96,80},{112,96},{128,112},... | collective-permute-start | bytes 786440 | tf_op jit(solution)/shard_map/ppermute | solution.py:19
  176.3 8.1 %collective-permute-start.6 = (bf16[3,1,128,256]{3,2,1,0:T(8,128)(2,1)S(1)}, bf16[3,1,128,256]{3,2,1,0:T(8,128)(2,1)S(1)}, u32[]{:S(2)}, u32[]{:S(2)}) collective-permute-start(bf16[3,1,128,256]{3,2,1,0:T(8,128)(2,1)S(1)} %get-tuple-element.18), channel_id=1, source_target_pairs={{0,1},{1,2},{2,3},{3,4},{4,5},{5,6},{6,7},{7,8},{8,9},{9,10},{10,1... | collective-permute-start | bytes 589832 | tf_op jit(solution)/shard_map/ppermute | solution.py:18
  181.5 11.6 %collective-permute-start.7 = (bf16[3,1,128,256]{3,2,1,0:T(8,128)(2,1)S(1)}, bf16[3,1,128,256]{3,2,1,0:T(8,128)(2,1)S(1)}, u32[]{:S(2)}, u32[]{:S(2)}) collective-permute-start(bf16[3,1,128,256]{3,2,1,0:T(8,128)(2,1)S(1)} %get-tuple-element.19), channel_id=1, source_target_pairs={{1,0},{2,1},{3,2},{4,3},{5,4},{6,5},{7,6},{8,7},{9,8},{10,9},{11,1... | collective-permute-start | bytes 589832 | tf_op jit(solution)/shard_map/ppermute | solution.py:19

commit v11 on v10

--- a/solution.py
+++ b/solution.py
@@ -38,7 +38,7 @@
     for bit in order:
         axis = remaining.index(bit)
         mine = (me >> bit) & 1
-        keep = lax.dynamic_index_in_dim(x, mine, axis=axis, keepdims=False)
+        keep = lax.dynamic_index_in_dim(x, mine, axis=axis, keepdims=False).astype(jnp.float32)
         send = lax.dynamic_index_in_dim(x, 1 - mine, axis=axis, keepdims=False)
         pairs = [(i, i ^ (1 << bit)) for i in range(count)]
         got = lax.ppermute(send.astype(jnp.bfloat16), "dp", pairs)
@@ -127,10 +127,10 @@
     )
     part_ref[:, :cols] = lax.dot_general(
         gate_grad, rows, (((0,), (0,)), ((), ())), preferred_element_type=jnp.float32
-    )
+    ).astype(part_ref.dtype)
     part_ref[:, cols:] = lax.dot_general(
         activation, grads, (((0,), (0,)), ((), ())), preferred_element_type=jnp.float32
-    )
+    ).astype(part_ref.dtype)
 
     @pl.when(step == pl.num_programs(0) - 1)
     def _():
@@ -158,7 +158,7 @@
         ],
         out_shape=[
             jax.ShapeDtypeStruct((slots, both), jnp.bfloat16),
-            jax.ShapeDtypeStruct((hidden, both), jnp.float32),
+            jax.ShapeDtypeStruct((hidden, both), jnp.bfloat16),
         ],
         scratch_shapes=[
             pltpu.VMEM((slots, channels), jnp.float32),
@@ -170,7 +170,7 @@
         cost_estimate=pl.CostEstimate(
             flops=flops,
             transcendentals=slots * hidden,
-            bytes_accessed=2 * (2 * slots * both + hidden * (cols + channels)) + 4 * hidden * both,
+            bytes_accessed=2 * (2 * slots * both + hidden * (cols + channels)) + 2 * hidden * both,
         ),
     )(inbound, weight_one, weight_two)
 

time: 201 us -> 197 us (0.980)
  local copies, waits for them, and re-layouts: 16.3 us -> 13.3 us
    dynamic_slice x2 -> x1, local copies, waits for them, and re-layouts: 4.56 us -> 2.09 us  [tree_scatter(): lax.dynamic_index_in_dim(x, mine, axis=axis, keepdims=False)]
  transfers between devices with their start and end apart: 14 -> 14, of which waited for: 10 -> 10; matrix products, arithmetic and copies ran while one was open for 9% -> 7% of each run, Pallas kernels for 0% -> 0%
where the time goes in v11:
time: 197 us; the launch traced here: 195 us
  waiting for transfers between devices  90.4 us (46%)
  starting transfers between devices  53.5 us (27%)
  Pallas kernels  25.2 us (13%)
  local copies, waits for them, and re-layouts  13.3 us (7%)
  other arithmetic  6.15 us (3%)
  matrix products  5.84 us (3%)
    all_to_all x1, waiting for transfers between devices, per_device(): lax.all_to_all(outbound.reshape(experts, capacity, both), 'expert', split...  30.8 us
    ppermute x4, waiting for transfers between devices, extended(): after = lax.ppermute(first, axis, down)  28.7 us
    ppermute x4, waiting for transfers between devices, tree_scatter(): got = lax.ppermute(send.astype(jnp.bfloat16), 'dp', pairs)  27.3 us
    ppermute x4, starting transfers between devices, extended(): before = lax.ppermute(last, axis, up)  20.1 us
    pallas_call x1, Pallas kernels, expert(): pl.pallas_call(functools.partial(expert_kernel, cols), grid=(hidden // ch...  16.5 us
    ppermute x4, starting transfers between devices, tree_scatter(): got = lax.ppermute(send.astype(jnp.bfloat16), 'dp', pairs)  12.3 us
    pallas_call x2, Pallas kernels, conv_block(): pl.pallas_call(functools.partial(conv_kernel, flip), out_shape=jax.ShapeD...  8.77 us
    ppermute x4, starting transfers between devices, extended(): after = lax.ppermute(first, axis, down)  7.68 us
  transfers between devices with their start and end apart: 14, of which 10 were waited for; matrix products, arithmetic and copies ran while one was open for 7% of the time, Pallas kernels for 0%

profile of v11, /device:TPU:95, one launch (start us, length us, event | category | flops | bytes accessed | tf_op | source)
XLA Modules:
  0.0 195.3 jit_solution(12166635851413962824)
XLA Ops:
  0.6 3.8 %collective-permute-start = (bf16[1,4,128,256]{3,2,1,0:T(8,128)(2,1)}, bf16[1,4,128,256]{3,2,1,0:T(8,128)(2,1)S(1)}, u32[]{:S(2)}, u32[]{:S(2)}) collective-permute-start(bf16[1,4,128,256]{3,2,1,0:T(8,128)(2,1)} %param.11), channel_id=1, source_target_pairs={{0,16},{16,32},{32,48},{48,64},{64,80},{80,96},{96,112},{112,128},... | collective-permute-start | bytes 786440 | tf_op jit(solution)/shard_map/ppermute | solution.py:18
  4.4 1.9 collective-permute-start.1
  9.0 5.4 %collective-permute-done.1 = bf16[1,4,128,256]{3,2,1,0:T(8,128)(2,1)S(1)} collective-permute-done((bf16[1,4,128,256]{3,2,1,0:T(8,128)(2,1)}, bf16[1,4,128,256]{3,2,1,0:T(8,128)(2,1)S(1)}, u32[]{:S(2)}, u32[]{:S(2)}) %collective-permute-start.1) | collective-permute-done | bytes 262176 | tf_op jit(solution)/shard_map/ppermute | solution.py:19
  14.5 5.1 %collective-permute-start.2 = (bf16[3,1,128,256]{3,2,1,0:T(8,128)(2,1)S(1)}, bf16[3,1,128,256]{3,2,1,0:T(8,128)(2,1)S(1)}, u32[]{:S(2)}, u32[]{:S(2)}) collective-permute-start(bf16[3,1,128,256]{3,2,1,0:T(8,128)(2,1)S(1)} %get-tuple-element.22), channel_id=1, source_target_pairs={{0,1},{1,2},{2,3},{3,4},{4,5},{5,6},{6,7},{7,8},{8,9},{9,10},{10,1... | collective-permute-start | bytes 589832 | tf_op jit(solution)/shard_map/ppermute | solution.py:18
  19.6 1.9 collective-permute-start.3
  21.6 2.8 %collective-permute-done.2 = bf16[3,1,128,256]{3,2,1,0:T(8,128)(2,1)S(1)} collective-permute-done((bf16[3,1,128,256]{3,2,1,0:T(8,128)(2,1)S(1)}, bf16[3,1,128,256]{3,2,1,0:T(8,128)(2,1)S(1)}, u32[]{:S(2)}, u32[]{:S(2)}) %collective-permute-start.2) | collective-permute-done | bytes 196640 | tf_op jit(solution)/shard_map/ppermute | solution.py:18
  24.3 8.3 %collective-permute-done.3 = bf16[3,1,128,256]{3,2,1,0:T(8,128)(2,1)S(1)} collective-permute-done((bf16[3,1,128,256]{3,2,1,0:T(8,128)(2,1)S(1)}, bf16[3,1,128,256]{3,2,1,0:T(8,128)(2,1)S(1)}, u32[]{:S(2)}, u32[]{:S(2)}) %collective-permute-start.3) | collective-permute-done | bytes 196640 | tf_op jit(solution)/shard_map/ppermute | solution.py:19
  33.9 4.1 %shard_map.93 = bf16[512,256]{1,0:T(8,128)(2,1)S(1)} custom-call(bf16[1,3,3,6,128,256]{5,4,3,2,1,0:T(8,128)(2,1)S(1)} %maximum_bitcast_fusion.shifted_ref, bf16[27,256,256]{2,1,0:T(8,128)(2,1)} %taps_ref.3), custom_call_target="tpu_custom_call" | custom-call | flops 1811939328 | bytes 7340032 | tf_op jit(solution)/shard_map/pallas_call | solution.py:86
  38.0 2.2 %fusion.2 = bf16[1024,768]{1,0:T(8,128)(2,1)} fusion(s32[512]{0:T(512)S(1)} %add_add_fusion, bf16[512,256]{1,0:T(8,128)(2,1)S(1)} %shard_map.93, bf16[512,512]{1,0:T(8,128)(2,1)S(1)} %bitcast.66), kind=kOutput, calls=%fused_computation.6 | convolution fusion | flops 808189952 | bytes 2361344 | tf_op jit(solution)/shard_map/dot_general | solution.py:204
  40.2 5.8 %all-to-all-start = ((bf16[16,64,768]{2,1,0:T(8,128)(2,1)}), bf16[16,64,768]{2,1,0:T(8,128)(2,1)S(1)}, u32[]{:S(2)}, u32[]{:S(2)}) async-start(bf16[16,64,768]{2,1,0:T(8,128)(2,1)} %bitcast.6), calls=%async_computation | async-start | bytes 3145728 | tf_op jit(solution)/shard_map/all_to_all | solution.py:206
  45.9 30.8 %all-to-all-done = bf16[16,64,768]{2,1,0:T(8,128)(2,1)S(1)} async-done(((bf16[16,64,768]{2,1,0:T(8,128)(2,1)}), bf16[16,64,768]{2,1,0:T(8,128)(2,1)S(1)}, u32[]{:S(2)}, u32[]{:S(2)}) %all-to-all-start) | async-done | bytes 1572896 | tf_op jit(solution)/shard_map/all_to_all | solution.py:206
  77.9 16.5 %shard_map.94 = (bf16[1024,768]{1,0:T(8,128)(2,1)}, bf16[2048,768]{1,0:T(8,128)(2,1)}) custom-call(bf16[1024,768]{1,0:T(8,128)(2,1)} %bitcast.58, bf16[512,2048]{1,0:T(8,128)(2,1)} %bitcast.64, bf16[2048,256]{1,0:T(8,128)(2,1)} %bitcast.65), custom_call_target="tpu_custom_call" | custom-call | flops 9663676416 | bytes 9437184 | tf_op jit(solution)/shard_map/pallas_call | solution.py:147
  94.4 2.1 %constant_dynamic-slice_fusion.1 = (bf16[2,2,2,1,128,768]{5,4,3,2,1,0:T(8,128)(2,1)S(1)}, bf16[2,2,2,1,128,768]{5,4,3,2,1,0:T(8,128)(2,1)S(1)}) fusion(bf16[2,2,2,2,128,768]{5,4,3,2,1,0:T(8,128)(2,1)} %bitcast.56, s32[]{:T(128)S(6)} %select_n.28, s32[]{:T(128)S(6)} %select_n.29), kind=kLoop, calls=%fused_computation.43 | loop fusion | bytes 6291464 | tf_op jit(solution)/shard_map/jit(dynamic_index_in_dim)/dynamic_slice | solution.py:41
  96.5 1.6 copy.13
  98.1 2.2 %collective-permute-start.8 = (bf16[2,2,2,128,768]{3,4,0,1,2:T(8,128)(2,1)}, bf16[2,2,2,128,768]{3,4,0,1,2:T(8,128)(2,1)}, u32[]{:S(2)}, u32[]{:S(2)}) collective-permute-start(bf16[2,2,2,128,768]{3,4,0,1,2:T(8,128)(2,1)} %bitcast.59), channel_id=1, source_target_pairs={{0,16},{16,0},{32,48},{48,32},{64,80},{80,64},{96,112},{112,96},{1... | collective-permute-start | bytes 4718600 | tf_op jit(solution)/shard_map/ppermute | solution.py:44
  100.3 7.7 %all-to-all-start.1 = ((bf16[16,64,768]{2,1,0:T(8,128)(2,1)}), bf16[16,64,768]{2,1,0:T(8,128)(2,1)}, u32[]{:S(2)}, u32[]{:S(2)}) async-start(bf16[16,64,768]{2,1,0:T(8,128)(2,1)} %bitcast.57), calls=%async_computation.1 | async-start | bytes 3145728 | tf_op jit(solution)/shard_map/all_to_all | solution.py:210
  108.0 1.6 copy.15
  109.6 2.2 %convert_add_fusion = f32[2,2,2,128,768]{3,4,0,1,2:T(8,128)S(1)} fusion(bf16[2,2,2,128,768]{3,4,0,1,2:T(8,128)(2,1)} %collective-permute-done.8, bf16[2,2,2,1,128,768]{4,5,0,1,2,3:T(8,128)(2,1)} %copy.15), kind=kLoop, calls=%fused_computation.2 | loop fusion | flops 2359296 | bytes 6291456 | tf_op jit(solution)/shard_map/add | solution.py:45
  112.8 8.3 %collective-permute-start.9 = (bf16[2,2,128,768]{2,3,0,1:T(8,128)(2,1)}, bf16[2,2,128,768]{2,3,0,1:T(8,128)(2,1)}, u32[]{:S(2)}, u32[]{:S(2)}) collective-permute-start(bf16[2,2,128,768]{2,3,0,1:T(8,128)(2,1)} %fusion.7), channel_id=1, source_target_pairs={{0,32},{16,48},{32,0},{48,16},{64,96},{80,112},{96,64},{112,80},{1... | collective-permute-start | bytes 2359304 | tf_op jit(solution)/shard_map/ppermute | solution.py:44
  121.0 17.8 %collective-permute-done.9 = bf16[2,2,128,768]{2,3,0,1:T(8,128)(2,1)} collective-permute-done((bf16[2,2,128,768]{2,3,0,1:T(8,128)(2,1)}, bf16[2,2,128,768]{2,3,0,1:T(8,128)(2,1)}, u32[]{:S(2)}, u32[]{:S(2)}) %collective-permute-start.9) | collective-permute-done | bytes 786464 | tf_op jit(solution)/shard_map/ppermute | solution.py:44
  138.8 1.3 bitcast_add_fusion
  141.3 1.7 collective-permute-start.10
  143.0 9.5 %collective-permute-done.10 = bf16[2,128,768]{1,2,0:T(8,128)(2,1)S(1)} collective-permute-done((bf16[2,128,768]{1,2,0:T(8,128)(2,1)S(1)}, bf16[2,128,768]{1,2,0:T(8,128)(2,1)S(1)}, u32[]{:S(2)}, u32[]{:S(2)}) %collective-permute-start.10) | collective-permute-done | bytes 393248 | tf_op jit(solution)/shard_map/ppermute | solution.py:44
  152.5 1.2 bitcast_add_fusion.1
  153.9 2.6 %fusion.3 = bf16[512,768]{1,0:T(8,128)(2,1)S(1)} fusion(bf16[1024,768]{1,0:T(8,128)(2,1)} %bitcast.11, s32[512]{0:T(512)S(1)} %add_add_fusion), kind=kOutput, calls=%fused_computation.9 | convolution fusion | flops 806223872 | bytes 2361344 | tf_op jit(solution)/shard_map/dot_general | solution.py:213
  156.5 5.9 %collective-permute-start.4 = (bf16[1,4,128,256]{3,2,1,0:T(8,128)(2,1)S(1)}, bf16[1,4,128,256]{3,2,1,0:T(8,128)(2,1)S(1)}, u32[]{:S(2)}, u32[]{:S(2)}) collective-permute-start(bf16[1,4,128,256]{3,2,1,0:T(8,128)(2,1)S(1)} %bitcast.51), channel_id=1, source_target_pairs={{0,16},{16,32},{32,48},{48,64},{64,80},{80,96},{96,112},{112,128},... | collective-permute-start | bytes 786440 | tf_op jit(solution)/shard_map/ppermute | solution.py:18
  162.5 1.9 collective-permute-start.5
  166.1 6.2 %collective-permute-done.5 = bf16[1,4,128,256]{3,2,1,0:T(8,128)(2,1)S(1)} collective-permute-done((bf16[1,4,128,256]{3,2,1,0:T(8,128)(2,1)S(1)}, bf16[1,4,128,256]{3,2,1,0:T(8,128)(2,1)S(1)}, u32[]{:S(2)}, u32[]{:S(2)}) %collective-permute-start.5) | collective-permute-done | bytes 262176 | tf_op jit(solution)/shard_map/ppermute | solution.py:19
  172.3 5.2 %collective-permute-start.6 = (bf16[3,1,128,256]{3,2,1,0:T(8,128)(2,1)S(1)}, bf16[3,1,128,256]{3,2,1,0:T(8,128)(2,1)S(1)}, u32[]{:S(2)}, u32[]{:S(2)}) collective-permute-start(bf16[3,1,128,256]{3,2,1,0:T(8,128)(2,1)S(1)} %get-tuple-element.20), channel_id=1, source_target_pairs={{0,1},{1,2},{2,3},{3,4},{4,5},{5,6},{6,7},{7,8},{8,9},{9,10},{10,1... | collective-permute-start | bytes 589832 | tf_op jit(solution)/shard_map/ppermute | solution.py:18
  177.5 1.9 collective-permute-start.7
  180.4 8.8 %collective-permute-done.7 = bf16[3,1,128,256]{3,2,1,0:T(8,128)(2,1)S(1)} collective-permute-done((bf16[3,1,128,256]{3,2,1,0:T(8,128)(2,1)S(1)}, bf16[3,1,128,256]{3,2,1,0:T(8,128)(2,1)S(1)}, u32[]{:S(2)}, u32[]{:S(2)}) %collective-permute-start.7) | collective-permute-done | bytes 196640 | tf_op jit(solution)/shard_map/ppermute | solution.py:19
  190.6 4.7 %shard_map.95 = bf16[512,256]{1,0:T(8,128)(2,1)} custom-call(bf16[1,3,3,6,128,256]{5,4,3,2,1,0:T(8,128)(2,1)S(1)} %maximum_bitcast_fusion.1.shifted_ref, bf16[27,256,256]{2,1,0:T(8,128)(2,1)} %taps_ref.3), custom_call_target="tpu_custom_call" | custom-call | flops 1811939328 | bytes 7340032 | tf_op jit(solution)/shard_map/pallas_call | solution.py:86
  (38 shorter events, 11.5 us)
Async XLA Ops:
  0.6 20.9 %copy-start.2 = (s32[1,4,128,1]{2,3,1,0:T(1,128)S(1)}, s32[1,4,128,1]{2,3,1,0:T(1,128)}, u32[]{:S(2)}) copy-start(s32[1,4,128,1]{2,3,1,0:T(1,128)} %param.7) | copy-start | bytes 6148
  0.6 7.4 %collective-permute-start = (bf16[1,4,128,256]{3,2,1,0:T(8,128)(2,1)}, bf16[1,4,128,256]{3,2,1,0:T(8,128)(2,1)S(1)}, u32[]{:S(2)}, u32[]{:S(2)}) collective-permute-start(bf16[1,4,128,256]{3,2,1,0:T(8,128)(2,1)} %param.11), channel_id=1, source_target_pairs={{0,16},{16,32},{32,48},{48,64},{64,80},{80,96},{96,112},{112,128},... | collective-permute-start | bytes 786440 | tf_op jit(solution)/shard_map/ppermute | solution.py:18
  4.4 10.0 %collective-permute-start.1 = (bf16[1,4,128,256]{3,2,1,0:T(8,128)(2,1)}, bf16[1,4,128,256]{3,2,1,0:T(8,128)(2,1)S(1)}, u32[]{:S(2)}, u32[]{:S(2)}) collective-permute-start(bf16[1,4,128,256]{3,2,1,0:T(8,128)(2,1)} %param.11), channel_id=1, source_target_pairs={{16,0},{32,16},{48,32},{64,48},{80,64},{96,80},{112,96},{128,112},... | collective-permute-start | bytes 786440 | tf_op jit(solution)/shard_map/ppermute | solution.py:19
  14.5 9.9 %collective-permute-start.2 = (bf16[3,1,128,256]{3,2,1,0:T(8,128)(2,1)S(1)}, bf16[3,1,128,256]{3,2,1,0:T(8,128)(2,1)S(1)}, u32[]{:S(2)}, u32[]{:S(2)}) collective-permute-start(bf16[3,1,128,256]{3,2,1,0:T(8,128)(2,1)S(1)} %get-tuple-element.22), channel_id=1, source_target_pairs={{0,1},{1,2},{2,3},{3,4},{4,5},{5,6},{6,7},{7,8},{8,9},{9,10},{10,1... | collective-permute-start | bytes 589832 | tf_op jit(solution)/shard_map/ppermute | solution.py:18
  19.6 13.0 %collective-permute-start.3 = (bf16[3,1,128,256]{3,2,1,0:T(8,128)(2,1)S(1)}, bf16[3,1,128,256]{3,2,1,0:T(8,128)(2,1)S(1)}, u32[]{:S(2)}, u32[]{:S(2)}) collective-permute-start(bf16[3,1,128,256]{3,2,1,0:T(8,128)(2,1)S(1)} %get-tuple-element.23), channel_id=1, source_target_pairs={{1,0},{2,1},{3,2},{4,3},{5,4},{6,5},{7,6},{8,7},{9,8},{10,9},{11,1... | collective-permute-start | bytes 589832 | tf_op jit(solution)/shard_map/ppermute | solution.py:19
  33.9 4.1 %copy-start.3 = (bf16[1,4,128,512]{3,2,1,0:T(8,128)(2,1)S(1)}, bf16[1,4,128,512]{3,2,1,0:T(8,128)(2,1)}, u32[]{:S(2)}) copy-start(bf16[1,4,128,512]{3,2,1,0:T(8,128)(2,1)} %param.6) | copy-start | bytes 1572868
  40.2 36.6 %all-to-all-start = ((bf16[16,64,768]{2,1,0:T(8,128)(2,1)}), bf16[16,64,768]{2,1,0:T(8,128)(2,1)S(1)}, u32[]{:S(2)}, u32[]{:S(2)}) async-start(bf16[16,64,768]{2,1,0:T(8,128)(2,1)} %bitcast.6), calls=%async_computation | async-start | bytes 3145728 | tf_op jit(solution)/shard_map/all_to_all | solution.py:206
  76.8 1.2 copy-start.1
  98.1 11.5 %collective-permute-start.8 = (bf16[2,2,2,128,768]{3,4,0,1,2:T(8,128)(2,1)}, bf16[2,2,2,128,768]{3,4,0,1,2:T(8,128)(2,1)}, u32[]{:S(2)}, u32[]{:S(2)}) collective-permute-start(bf16[2,2,2,128,768]{3,4,0,1,2:T(8,128)(2,1)} %bitcast.59), channel_id=1, source_target_pairs={{0,16},{16,0},{32,48},{48,32},{64,80},{80,64},{96,112},{112,96},{1... | collective-permute-start | bytes 4718600 | tf_op jit(solution)/shard_map/ppermute | solution.py:44
  100.3 53.5 %all-to-all-start.1 = ((bf16[16,64,768]{2,1,0:T(8,128)(2,1)}), bf16[16,64,768]{2,1,0:T(8,128)(2,1)}, u32[]{:S(2)}, u32[]{:S(2)}) async-start(bf16[16,64,768]{2,1,0:T(8,128)(2,1)} %bitcast.57), calls=%async_computation.1 | async-start | bytes 3145728 | tf_op jit(solution)/shard_map/all_to_all | solution.py:210
  112.8 26.1 %collective-permute-start.9 = (bf16[2,2,128,768]{2,3,0,1:T(8,128)(2,1)}, bf16[2,2,128,768]{2,3,0,1:T(8,128)(2,1)}, u32[]{:S(2)}, u32[]{:S(2)}) collective-permute-start(bf16[2,2,128,768]{2,3,0,1:T(8,128)(2,1)} %fusion.7), channel_id=1, source_target_pairs={{0,32},{16,48},{32,0},{48,16},{64,96},{80,112},{96,64},{112,80},{1... | collective-permute-start | bytes 2359304 | tf_op jit(solution)/shard_map/ppermute | solution.py:44
  140.1 1.1 copy-start
  141.3 11.2 %collective-permute-start.10 = (bf16[2,128,768]{1,2,0:T(8,128)(2,1)S(1)}, bf16[2,128,768]{1,2,0:T(8,128)(2,1)S(1)}, u32[]{:S(2)}, u32[]{:S(2)}) collective-permute-start(bf16[2,128,768]{1,2,0:T(8,128)(2,1)S(1)} %fusion.11), channel_id=1, source_target_pairs={{0,64},{16,80},{32,96},{48,112},{64,0},{80,16},{96,32},{112,48},{1... | collective-permute-start | bytes 1179656 | tf_op jit(solution)/shard_map/ppermute | solution.py:44
  153.7 10.7 %collective-permute-start.11 = (bf16[128,768]{0,1:T(8,128)(2,1)S(1)}, bf16[128,768]{0,1:T(8,128)(2,1)S(1)}, u32[]{:S(2)}, u32[]{:S(2)}) collective-permute-start(bf16[128,768]{0,1:T(8,128)(2,1)S(1)} %fusion.12), channel_id=1, source_target_pairs={{0,128},{16,144},{32,160},{48,176},{64,192},{80,208},{96,224},{112... | collective-permute-start | bytes 589832 | tf_op jit(solution)/shard_map/ppermute | solution.py:44
  156.5 9.5 %collective-permute-start.4 = (bf16[1,4,128,256]{3,2,1,0:T(8,128)(2,1)S(1)}, bf16[1,4,128,256]{3,2,1,0:T(8,128)(2,1)S(1)}, u32[]{:S(2)}, u32[]{:S(2)}) collective-permute-start(bf16[1,4,128,256]{3,2,1,0:T(8,128)(2,1)S(1)} %bitcast.51), channel_id=1, source_target_pairs={{0,16},{16,32},{32,48},{48,64},{64,80},{80,96},{96,112},{112,128},... | collective-permute-start | bytes 786440 | tf_op jit(solution)/shard_map/ppermute | solution.py:18
  162.5 9.8 %collective-permute-start.5 = (bf16[1,4,128,256]{3,2,1,0:T(8,128)(2,1)S(1)}, bf16[1,4,128,256]{3,2,1,0:T(8,128)(2,1)S(1)}, u32[]{:S(2)}, u32[]{:S(2)}) collective-permute-start(bf16[1,4,128,256]{3,2,1,0:T(8,128)(2,1)S(1)} %bitcast.52), channel_id=1, source_target_pairs={{16,0},{32,16},{48,32},{64,48},{80,64},{96,80},{112,96},{128,112},... | collective-permute-start | bytes 786440 | tf_op jit(solution)/shard_map/ppermute | solution.py:19
  172.3 8.1 %collective-permute-start.6 = (bf16[3,1,128,256]{3,2,1,0:T(8,128)(2,1)S(1)}, bf16[3,1,128,256]{3,2,1,0:T(8,128)(2,1)S(1)}, u32[]{:S(2)}, u32[]{:S(2)}) collective-permute-start(bf16[3,1,128,256]{3,2,1,0:T(8,128)(2,1)S(1)} %get-tuple-element.20), channel_id=1, source_target_pairs={{0,1},{1,2},{2,3},{3,4},{4,5},{5,6},{6,7},{7,8},{8,9},{9,10},{10,1... | collective-permute-start | bytes 589832 | tf_op jit(solution)/shard_map/ppermute | solution.py:18
  177.5 11.6 %collective-permute-start.7 = (bf16[3,1,128,256]{3,2,1,0:T(8,128)(2,1)S(1)}, bf16[3,1,128,256]{3,2,1,0:T(8,128)(2,1)S(1)}, u32[]{:S(2)}, u32[]{:S(2)}) collective-permute-start(bf16[3,1,128,256]{3,2,1,0:T(8,128)(2,1)S(1)} %get-tuple-element.21), channel_id=1, source_target_pairs={{1,0},{2,1},{3,2},{4,3},{5,4},{6,5},{7,6},{8,7},{9,8},{10,9},{11,1... | collective-permute-start | bytes 589832 | tf_op jit(solution)/shard_map/ppermute | solution.py:19

commit v12 on v11

--- a/solution.py
+++ b/solution.py
@@ -102,7 +102,7 @@
 
 
 def expert_kernel(
-    cols, rows_ref, first_ref, second_ref, back_ref, part_ref, result_acc, input_acc
+    cols, rows_ref, first_ref, second_ref, back_ref, part_ref, result_acc, input_acc, across_ref
 ):
     step = pl.program_id(0)
 
@@ -110,6 +110,7 @@
     def _():
         result_acc[...] = jnp.zeros_like(result_acc)
         input_acc[...] = jnp.zeros_like(input_acc)
+        across_ref[...] = rows_ref[...].T
 
     rows = rows_ref[:, :cols]
     grads = rows_ref[:, cols:]
@@ -125,12 +126,13 @@
     input_acc[...] += lax.dot_general(
         gate_grad, first, (((1,), (1,)), ((), ())), preferred_element_type=jnp.float32
     )
-    part_ref[:, :cols] = lax.dot_general(
-        gate_grad, rows, (((0,), (0,)), ((), ())), preferred_element_type=jnp.float32
-    ).astype(part_ref.dtype)
-    part_ref[:, cols:] = lax.dot_general(
-        activation, grads, (((0,), (0,)), ((), ())), preferred_element_type=jnp.float32
-    ).astype(part_ref.dtype)
+    part_one = jnp.dot(across_ref[:cols, :], gate_grad, preferred_element_type=jnp.float32)
+    part_two = jnp.dot(across_ref[cols:, :], activation, preferred_element_type=jnp.float32)
+    lanes = part_ref.shape[2]
+    for block in range(part_ref.shape[0]):
+        window = slice(block * lanes, (block + 1) * lanes)
+        part_ref[block, :cols, :] = part_one[:, window].astype(part_ref.dtype)
+        part_ref[block, cols:, :] = part_two[:, window].astype(part_ref.dtype)
 
     @pl.when(step == pl.num_programs(0) - 1)
     def _():
@@ -139,10 +141,12 @@
         back_ref[:, width:] = input_acc[...].astype(back_ref.dtype)
 
 
-def expert(inbound, weight_one, weight_two, chunk):
+def expert(inbound, weight_one, weight_two, chunk, blocks):
     slots, both = inbound.shape
     cols, hidden = weight_one.shape
     channels = weight_two.shape[1]
+    lanes = hidden // blocks
+    per_step = chunk // lanes
     flops = 2 * slots * hidden * (3 * cols + 3 * channels)
     return pl.pallas_call(
         functools.partial(expert_kernel, cols),
@@ -154,15 +158,16 @@
         ],
         out_specs=[
             pl.BlockSpec((slots, both), lambda h: (0, 0)),
-            pl.BlockSpec((chunk, both), lambda h: (h, 0)),
+            pl.BlockSpec((per_step, both, lanes), lambda h: (h, 0, 0)),
         ],
         out_shape=[
             jax.ShapeDtypeStruct((slots, both), jnp.bfloat16),
-            jax.ShapeDtypeStruct((hidden, both), jnp.bfloat16),
+            jax.ShapeDtypeStruct((blocks, both, lanes), jnp.bfloat16),
         ],
         scratch_shapes=[
             pltpu.VMEM((slots, channels), jnp.float32),
             pltpu.VMEM((slots, cols), jnp.float32),
+            pltpu.VMEM((both, slots), jnp.bfloat16),
         ],
         compiler_params=pltpu.CompilerParams(
             dimension_semantics=("arbitrary",), vmem_limit_bytes=56 * 1024 * 1024
@@ -206,7 +211,7 @@
     inbound = lax.all_to_all(
         outbound.reshape(experts, capacity, both), "expert", split_axis=0, concat_axis=0, tiled=True
     ).reshape(slots, both)
-    back, part = expert(inbound, w_first[0], w_second[0], 1024)
+    back, part = expert(inbound, w_first[0], w_second[0], 1024, slabs)
     returned = lax.all_to_all(
         back.reshape(experts, capacity, both), "expert", split_axis=0, concat_axis=0, tiled=True
     )
@@ -220,9 +225,9 @@
     imitated = conv_block(patch_grid, kernel, False).reshape(1, rows_y, depth_cells, channels)
     feat_grad = mixed[:, channels:].reshape(1, rows_y, depth_cells, feat_width)
 
-    grads = tree_scatter(part.reshape(slabs, hidden // slabs, both), (0, 1, 2, 3))
-    grad_one = grads[:, :feat_width].T
-    grad_two = grads[:, feat_width:]
+    grads = tree_scatter(part, (0, 1, 2, 3))
+    grad_one = grads[:feat_width]
+    grad_two = grads[feat_width:].T
     return (imitated, feat_grad, grad_one[None], grad_two[None])
 
 

time: 197 us -> 197 us (level)
    unnamed x12 -> x13, local copies, waits for them, and re-layouts: 5.64 us -> 5.22 us
where the time goes in v12:
time: 197 us; the launch traced here: 195 us
  waiting for transfers between devices  90.3 us (46%)
  starting transfers between devices  53.6 us (27%)
  Pallas kernels  25.5 us (13%)
  local copies, waits for them, and re-layouts  12.6 us (6%)
  other arithmetic  6.15 us (3%)
  matrix products  5.85 us (3%)
    all_to_all x1, waiting for transfers between devices, per_device(): lax.all_to_all(outbound.reshape(experts, capacity, both), 'expert', split...  30.8 us
    ppermute x4, waiting for transfers between devices, extended(): after = lax.ppermute(first, axis, down)  28.7 us
    ppermute x4, waiting for transfers between devices, tree_scatter(): got = lax.ppermute(send.astype(jnp.bfloat16), 'dp', pairs)  27.2 us
    ppermute x4, starting transfers between devices, extended(): before = lax.ppermute(last, axis, up)  20.1 us
    pallas_call x1, Pallas kernels, expert(): pl.pallas_call(functools.partial(expert_kernel, cols), grid=(hidden // ch...  16.7 us
    ppermute x4, starting transfers between devices, tree_scatter(): got = lax.ppermute(send.astype(jnp.bfloat16), 'dp', pairs)  12.4 us
    pallas_call x2, Pallas kernels, conv_block(): pl.pallas_call(functools.partial(conv_kernel, flip), out_shape=jax.ShapeD...  8.77 us
    ppermute x4, starting transfers between devices, extended(): after = lax.ppermute(first, axis, down)  7.68 us
  transfers between devices with their start and end apart: 14, of which 10 were waited for; matrix products, arithmetic and copies ran while one was open for 7% of the time, Pallas kernels for 0%

profile of v12, /device:TPU:95, one launch (start us, length us, event | category | flops | bytes accessed | tf_op | source)
XLA Modules:
  0.0 195.0 jit_solution(8964109444520811964)
XLA Ops:
  0.6 3.8 %collective-permute-start = (bf16[1,4,128,256]{3,2,1,0:T(8,128)(2,1)}, bf16[1,4,128,256]{3,2,1,0:T(8,128)(2,1)S(1)}, u32[]{:S(2)}, u32[]{:S(2)}) collective-permute-start(bf16[1,4,128,256]{3,2,1,0:T(8,128)(2,1)} %param.11), channel_id=1, source_target_pairs={{0,16},{16,32},{32,48},{48,64},{64,80},{80,96},{96,112},{112,128},... | collective-permute-start | bytes 786440 | tf_op jit(solution)/shard_map/ppermute | solution.py:18
  4.4 1.9 collective-permute-start.1
  9.0 5.4 %collective-permute-done.1 = bf16[1,4,128,256]{3,2,1,0:T(8,128)(2,1)S(1)} collective-permute-done((bf16[1,4,128,256]{3,2,1,0:T(8,128)(2,1)}, bf16[1,4,128,256]{3,2,1,0:T(8,128)(2,1)S(1)}, u32[]{:S(2)}, u32[]{:S(2)}) %collective-permute-start.1) | collective-permute-done | bytes 262176 | tf_op jit(solution)/shard_map/ppermute | solution.py:19
  14.5 5.1 %collective-permute-start.2 = (bf16[3,1,128,256]{3,2,1,0:T(8,128)(2,1)S(1)}, bf16[3,1,128,256]{3,2,1,0:T(8,128)(2,1)S(1)}, u32[]{:S(2)}, u32[]{:S(2)}) collective-permute-start(bf16[3,1,128,256]{3,2,1,0:T(8,128)(2,1)S(1)} %get-tuple-element.22), channel_id=1, source_target_pairs={{0,1},{1,2},{2,3},{3,4},{4,5},{5,6},{6,7},{7,8},{8,9},{9,10},{10,1... | collective-permute-start | bytes 589832 | tf_op jit(solution)/shard_map/ppermute | solution.py:18
  19.6 1.9 collective-permute-start.3
  21.6 2.8 %collective-permute-done.2 = bf16[3,1,128,256]{3,2,1,0:T(8,128)(2,1)S(1)} collective-permute-done((bf16[3,1,128,256]{3,2,1,0:T(8,128)(2,1)S(1)}, bf16[3,1,128,256]{3,2,1,0:T(8,128)(2,1)S(1)}, u32[]{:S(2)}, u32[]{:S(2)}) %collective-permute-start.2) | collective-permute-done | bytes 196640 | tf_op jit(solution)/shard_map/ppermute | solution.py:18
  24.3 8.3 %collective-permute-done.3 = bf16[3,1,128,256]{3,2,1,0:T(8,128)(2,1)S(1)} collective-permute-done((bf16[3,1,128,256]{3,2,1,0:T(8,128)(2,1)S(1)}, bf16[3,1,128,256]{3,2,1,0:T(8,128)(2,1)S(1)}, u32[]{:S(2)}, u32[]{:S(2)}) %collective-permute-start.3) | collective-permute-done | bytes 196640 | tf_op jit(solution)/shard_map/ppermute | solution.py:19
  33.9 4.1 %shard_map.93 = bf16[512,256]{1,0:T(8,128)(2,1)S(1)} custom-call(bf16[1,3,3,6,128,256]{5,4,3,2,1,0:T(8,128)(2,1)S(1)} %maximum_bitcast_fusion.shifted_ref, bf16[27,256,256]{2,1,0:T(8,128)(2,1)} %taps_ref.3), custom_call_target="tpu_custom_call" | custom-call | flops 1811939328 | bytes 7340032 | tf_op jit(solution)/shard_map/pallas_call | solution.py:86
  38.0 2.2 %fusion.2 = bf16[1024,768]{1,0:T(8,128)(2,1)} fusion(s32[512]{0:T(512)S(1)} %add_add_fusion, bf16[512,256]{1,0:T(8,128)(2,1)S(1)} %shard_map.93, bf16[512,512]{1,0:T(8,128)(2,1)S(1)} %bitcast.69), kind=kOutput, calls=%fused_computation.6 | convolution fusion | flops 808189952 | bytes 2361344 | tf_op jit(solution)/shard_map/dot_general | solution.py:209
  40.2 5.8 %all-to-all-start = ((bf16[16,64,768]{2,1,0:T(8,128)(2,1)}), bf16[16,64,768]{2,1,0:T(8,128)(2,1)S(1)}, u32[]{:S(2)}, u32[]{:S(2)}) async-start(bf16[16,64,768]{2,1,0:T(8,128)(2,1)} %bitcast.6), calls=%async_computation | async-start | bytes 3145728 | tf_op jit(solution)/shard_map/all_to_all | solution.py:211
  45.9 30.8 %all-to-all-done = bf16[16,64,768]{2,1,0:T(8,128)(2,1)S(1)} async-done(((bf16[16,64,768]{2,1,0:T(8,128)(2,1)}), bf16[16,64,768]{2,1,0:T(8,128)(2,1)S(1)}, u32[]{:S(2)}, u32[]{:S(2)}) %all-to-all-start) | async-done | bytes 1572896 | tf_op jit(solution)/shard_map/all_to_all | solution.py:211
  76.8 1.2 copy-done.1
  78.0 16.7 %shard_map.94 = (bf16[1024,768]{1,0:T(8,128)(2,1)}, bf16[16,768,128]{2,1,0:T(8,128)(2,1)}) custom-call(bf16[1024,768]{1,0:T(8,128)(2,1)} %bitcast.61, bf16[512,2048]{1,0:T(8,128)(2,1)} %bitcast.67, bf16[2048,256]{1,0:T(8,128)(2,1)} %bitcast.68), custom_call_target="tpu_custom_call" | custom-call | flops 9663676416 | bytes 9437184 | tf_op jit(solution)/shard_map/pallas_call | solution.py:151
  94.7 3.4 %constant_dynamic-slice_fusion.1 = (bf16[2,2,2,1,768,128]{5,4,3,2,1,0:T(8,128)(2,1)}, bf16[2,2,2,1,768,128]{5,4,3,2,1,0:T(8,128)(2,1)S(1)}) fusion(bf16[2,2,2,2,768,128]{5,4,3,2,1,0:T(8,128)(2,1)} %bitcast.60, s32[]{:T(128)S(6)} %select_n.28, s32[]{:T(128)S(6)} %select_n.29), kind=kLoop, calls=%fused_computation.45 | loop fusion | bytes 6291464 | tf_op jit(solution)/shard_map/jit(dynamic_index_in_dim)/dynamic_slice | solution.py:41
  98.2 2.3 %collective-permute-start.8 = (bf16[2,2,2,768,128]{4,3,0,1,2:T(8,128)(2,1)S(1)}, bf16[2,2,2,768,128]{4,3,0,1,2:T(8,128)(2,1)S(1)}, u32[]{:S(2)}, u32[]{:S(2)}) collective-permute-start(bf16[2,2,2,768,128]{4,3,0,1,2:T(8,128)(2,1)S(1)} %bitcast.62), channel_id=1, source_target_pairs={{0,16},{16,0},{32,48},{48,32},{64,80},{80,64},{96,112},{112,96},{1... | collective-permute-start | bytes 4718600 | tf_op jit(solution)/shard_map/ppermute | solution.py:44
  100.5 7.7 %all-to-all-start.1 = ((bf16[16,64,768]{2,1,0:T(8,128)(2,1)}), bf16[16,64,768]{2,1,0:T(8,128)(2,1)}, u32[]{:S(2)}, u32[]{:S(2)}) async-start(bf16[16,64,768]{2,1,0:T(8,128)(2,1)} %bitcast.10), calls=%async_computation.1 | async-start | bytes 3145728 | tf_op jit(solution)/shard_map/all_to_all | solution.py:215
  108.2 1.1 copy-done.2
  109.3 2.2 %convert_add_fusion = f32[2,2,2,768,128]{4,3,0,1,2:T(8,128)S(1)} fusion(bf16[2,2,2,768,128]{4,3,0,1,2:T(8,128)(2,1)} %copy-done.2, bf16[2,2,2,1,768,128]{5,4,3,2,1,0:T(8,128)(2,1)} %get-tuple-element.12), kind=kLoop, calls=%fused_computation.2 | loop fusion | flops 2359296 | bytes 6291456 | tf_op jit(solution)/shard_map/add | solution.py:45
  112.5 8.3 %collective-permute-start.9 = (bf16[2,2,768,128]{3,2,0,1:T(8,128)(2,1)}, bf16[2,2,768,128]{3,2,0,1:T(8,128)(2,1)}, u32[]{:S(2)}, u32[]{:S(2)}) collective-permute-start(bf16[2,2,768,128]{3,2,0,1:T(8,128)(2,1)} %fusion.7), channel_id=1, source_target_pairs={{0,32},{16,48},{32,0},{48,16},{64,96},{80,112},{96,64},{112,80},{1... | collective-permute-start | bytes 2359304 | tf_op jit(solution)/shard_map/ppermute | solution.py:44
  120.8 17.8 %collective-permute-done.9 = bf16[2,2,768,128]{3,2,0,1:T(8,128)(2,1)} collective-permute-done((bf16[2,2,768,128]{3,2,0,1:T(8,128)(2,1)}, bf16[2,2,768,128]{3,2,0,1:T(8,128)(2,1)}, u32[]{:S(2)}, u32[]{:S(2)}) %collective-permute-start.9) | collective-permute-done | bytes 786464 | tf_op jit(solution)/shard_map/ppermute | solution.py:44
  138.5 1.3 bitcast_add_fusion
  141.0 1.7 collective-permute-start.10
  142.8 9.4 %collective-permute-done.10 = bf16[2,768,128]{2,1,0:T(8,128)(2,1)S(1)} collective-permute-done((bf16[2,768,128]{2,1,0:T(8,128)(2,1)S(1)}, bf16[2,768,128]{2,1,0:T(8,128)(2,1)S(1)}, u32[]{:S(2)}, u32[]{:S(2)}) %collective-permute-start.10) | collective-permute-done | bytes 393248 | tf_op jit(solution)/shard_map/ppermute | solution.py:44
  152.2 1.2 bitcast_add_fusion.1
  153.5 2.6 %fusion.3 = bf16[512,768]{1,0:T(8,128)(2,1)S(1)} fusion(bf16[1024,768]{1,0:T(8,128)(2,1)} %bitcast.11, s32[512]{0:T(512)S(1)} %add_add_fusion), kind=kOutput, calls=%fused_computation.11 | convolution fusion | flops 806223872 | bytes 2361344 | tf_op jit(solution)/shard_map/dot_general | solution.py:218
  156.2 6.0 %collective-permute-start.4 = (bf16[1,4,128,256]{3,2,1,0:T(8,128)(2,1)S(1)}, bf16[1,4,128,256]{3,2,1,0:T(8,128)(2,1)S(1)}, u32[]{:S(2)}, u32[]{:S(2)}) collective-permute-start(bf16[1,4,128,256]{3,2,1,0:T(8,128)(2,1)S(1)} %bitcast.55), channel_id=1, source_target_pairs={{0,16},{16,32},{32,48},{48,64},{64,80},{80,96},{96,112},{112,128},... | collective-permute-start | bytes 786440 | tf_op jit(solution)/shard_map/ppermute | solution.py:18
  162.2 1.9 collective-permute-start.5
  165.8 6.2 %collective-permute-done.5 = bf16[1,4,128,256]{3,2,1,0:T(8,128)(2,1)S(1)} collective-permute-done((bf16[1,4,128,256]{3,2,1,0:T(8,128)(2,1)S(1)}, bf16[1,4,128,256]{3,2,1,0:T(8,128)(2,1)S(1)}, u32[]{:S(2)}, u32[]{:S(2)}) %collective-permute-start.5) | collective-permute-done | bytes 262176 | tf_op jit(solution)/shard_map/ppermute | solution.py:19
  172.0 5.2 %collective-permute-start.6 = (bf16[3,1,128,256]{3,2,1,0:T(8,128)(2,1)S(1)}, bf16[3,1,128,256]{3,2,1,0:T(8,128)(2,1)S(1)}, u32[]{:S(2)}, u32[]{:S(2)}) collective-permute-start(bf16[3,1,128,256]{3,2,1,0:T(8,128)(2,1)S(1)} %get-tuple-element.20), channel_id=1, source_target_pairs={{0,1},{1,2},{2,3},{3,4},{4,5},{5,6},{6,7},{7,8},{8,9},{9,10},{10,1... | collective-permute-start | bytes 589832 | tf_op jit(solution)/shard_map/ppermute | solution.py:18
  177.3 1.9 collective-permute-start.7
  180.1 8.8 %collective-permute-done.7 = bf16[3,1,128,256]{3,2,1,0:T(8,128)(2,1)S(1)} collective-permute-done((bf16[3,1,128,256]{3,2,1,0:T(8,128)(2,1)S(1)}, bf16[3,1,128,256]{3,2,1,0:T(8,128)(2,1)S(1)}, u32[]{:S(2)}, u32[]{:S(2)}) %collective-permute-start.7) | collective-permute-done | bytes 196640 | tf_op jit(solution)/shard_map/ppermute | solution.py:19
  190.3 4.7 %shard_map.95 = bf16[512,256]{1,0:T(8,128)(2,1)} custom-call(bf16[1,3,3,6,128,256]{5,4,3,2,1,0:T(8,128)(2,1)S(1)} %maximum_bitcast_fusion.1.shifted_ref, bf16[27,256,256]{2,1,0:T(8,128)(2,1)} %taps_ref.3), custom_call_target="tpu_custom_call" | custom-call | flops 1811939328 | bytes 7340032 | tf_op jit(solution)/shard_map/pallas_call | solution.py:86
  (39 shorter events, 10.4 us)
Async XLA Ops:
  0.6 20.9 %copy-start.3 = (s32[1,4,128,1]{2,3,1,0:T(1,128)S(1)}, s32[1,4,128,1]{2,3,1,0:T(1,128)}, u32[]{:S(2)}) copy-start(s32[1,4,128,1]{2,3,1,0:T(1,128)} %param.7) | copy-start | bytes 6148
  0.6 7.4 %collective-permute-start = (bf16[1,4,128,256]{3,2,1,0:T(8,128)(2,1)}, bf16[1,4,128,256]{3,2,1,0:T(8,128)(2,1)S(1)}, u32[]{:S(2)}, u32[]{:S(2)}) collective-permute-start(bf16[1,4,128,256]{3,2,1,0:T(8,128)(2,1)} %param.11), channel_id=1, source_target_pairs={{0,16},{16,32},{32,48},{48,64},{64,80},{80,96},{96,112},{112,128},... | collective-permute-start | bytes 786440 | tf_op jit(solution)/shard_map/ppermute | solution.py:18
  4.4 10.0 %collective-permute-start.1 = (bf16[1,4,128,256]{3,2,1,0:T(8,128)(2,1)}, bf16[1,4,128,256]{3,2,1,0:T(8,128)(2,1)S(1)}, u32[]{:S(2)}, u32[]{:S(2)}) collective-permute-start(bf16[1,4,128,256]{3,2,1,0:T(8,128)(2,1)} %param.11), channel_id=1, source_target_pairs={{16,0},{32,16},{48,32},{64,48},{80,64},{96,80},{112,96},{128,112},... | collective-permute-start | bytes 786440 | tf_op jit(solution)/shard_map/ppermute | solution.py:19
  14.5 9.9 %collective-permute-start.2 = (bf16[3,1,128,256]{3,2,1,0:T(8,128)(2,1)S(1)}, bf16[3,1,128,256]{3,2,1,0:T(8,128)(2,1)S(1)}, u32[]{:S(2)}, u32[]{:S(2)}) collective-permute-start(bf16[3,1,128,256]{3,2,1,0:T(8,128)(2,1)S(1)} %get-tuple-element.22), channel_id=1, source_target_pairs={{0,1},{1,2},{2,3},{3,4},{4,5},{5,6},{6,7},{7,8},{8,9},{9,10},{10,1... | collective-permute-start | bytes 589832 | tf_op jit(solution)/shard_map/ppermute | solution.py:18
  19.6 13.0 %collective-permute-start.3 = (bf16[3,1,128,256]{3,2,1,0:T(8,128)(2,1)S(1)}, bf16[3,1,128,256]{3,2,1,0:T(8,128)(2,1)S(1)}, u32[]{:S(2)}, u32[]{:S(2)}) collective-permute-start(bf16[3,1,128,256]{3,2,1,0:T(8,128)(2,1)S(1)} %get-tuple-element.23), channel_id=1, source_target_pairs={{1,0},{2,1},{3,2},{4,3},{5,4},{6,5},{7,6},{8,7},{9,8},{10,9},{11,1... | collective-permute-start | bytes 589832 | tf_op jit(solution)/shard_map/ppermute | solution.py:19
  33.9 4.1 %copy-start.4 = (bf16[1,4,128,512]{3,2,1,0:T(8,128)(2,1)S(1)}, bf16[1,4,128,512]{3,2,1,0:T(8,128)(2,1)}, u32[]{:S(2)}) copy-start(bf16[1,4,128,512]{3,2,1,0:T(8,128)(2,1)} %param.6) | copy-start | bytes 1572868
  40.2 36.6 %all-to-all-start = ((bf16[16,64,768]{2,1,0:T(8,128)(2,1)}), bf16[16,64,768]{2,1,0:T(8,128)(2,1)S(1)}, u32[]{:S(2)}, u32[]{:S(2)}) async-start(bf16[16,64,768]{2,1,0:T(8,128)(2,1)} %bitcast.6), calls=%async_computation | async-start | bytes 3145728 | tf_op jit(solution)/shard_map/all_to_all | solution.py:211
  76.8 1.2 copy-start.1
  98.2 10.0 %collective-permute-start.8 = (bf16[2,2,2,768,128]{4,3,0,1,2:T(8,128)(2,1)S(1)}, bf16[2,2,2,768,128]{4,3,0,1,2:T(8,128)(2,1)S(1)}, u32[]{:S(2)}, u32[]{:S(2)}) collective-permute-start(bf16[2,2,2,768,128]{4,3,0,1,2:T(8,128)(2,1)S(1)} %bitcast.62), channel_id=1, source_target_pairs={{0,16},{16,0},{32,48},{48,32},{64,80},{80,64},{96,112},{112,96},{1... | collective-permute-start | bytes 4718600 | tf_op jit(solution)/shard_map/ppermute | solution.py:44
  100.5 53.0 %all-to-all-start.1 = ((bf16[16,64,768]{2,1,0:T(8,128)(2,1)}), bf16[16,64,768]{2,1,0:T(8,128)(2,1)}, u32[]{:S(2)}, u32[]{:S(2)}) async-start(bf16[16,64,768]{2,1,0:T(8,128)(2,1)} %bitcast.10), calls=%async_computation.1 | async-start | bytes 3145728 | tf_op jit(solution)/shard_map/all_to_all | solution.py:215
  108.2 1.1 copy-start.2
  112.5 26.0 %collective-permute-start.9 = (bf16[2,2,768,128]{3,2,0,1:T(8,128)(2,1)}, bf16[2,2,768,128]{3,2,0,1:T(8,128)(2,1)}, u32[]{:S(2)}, u32[]{:S(2)}) collective-permute-start(bf16[2,2,768,128]{3,2,0,1:T(8,128)(2,1)} %fusion.7), channel_id=1, source_target_pairs={{0,32},{16,48},{32,0},{48,16},{64,96},{80,112},{96,64},{112,80},{1... | collective-permute-start | bytes 2359304 | tf_op jit(solution)/shard_map/ppermute | solution.py:44
  139.8 1.1 copy-start
  141.0 11.2 %collective-permute-start.10 = (bf16[2,768,128]{2,1,0:T(8,128)(2,1)S(1)}, bf16[2,768,128]{2,1,0:T(8,128)(2,1)S(1)}, u32[]{:S(2)}, u32[]{:S(2)}) collective-permute-start(bf16[2,768,128]{2,1,0:T(8,128)(2,1)S(1)} %fusion.11), channel_id=1, source_target_pairs={{0,64},{16,80},{32,96},{48,112},{64,0},{80,16},{96,32},{112,48},{1... | collective-permute-start | bytes 1179656 | tf_op jit(solution)/shard_map/ppermute | solution.py:44
  153.4 10.7 %collective-permute-start.11 = (bf16[768,128]{1,0:T(8,128)(2,1)S(1)}, bf16[768,128]{1,0:T(8,128)(2,1)S(1)}, u32[]{:S(2)}, u32[]{:S(2)}) collective-permute-start(bf16[768,128]{1,0:T(8,128)(2,1)S(1)} %fusion.12), channel_id=1, source_target_pairs={{0,128},{16,144},{32,160},{48,176},{64,192},{80,208},{96,224},{112... | collective-permute-start | bytes 589832 | tf_op jit(solution)/shard_map/ppermute | solution.py:44
  156.2 9.6 %collective-permute-start.4 = (bf16[1,4,128,256]{3,2,1,0:T(8,128)(2,1)S(1)}, bf16[1,4,128,256]{3,2,1,0:T(8,128)(2,1)S(1)}, u32[]{:S(2)}, u32[]{:S(2)}) collective-permute-start(bf16[1,4,128,256]{3,2,1,0:T(8,128)(2,1)S(1)} %bitcast.55), channel_id=1, source_target_pairs={{0,16},{16,32},{32,48},{48,64},{64,80},{80,96},{96,112},{112,128},... | collective-permute-start | bytes 786440 | tf_op jit(solution)/shard_map/ppermute | solution.py:18
  162.2 9.8 %collective-permute-start.5 = (bf16[1,4,128,256]{3,2,1,0:T(8,128)(2,1)S(1)}, bf16[1,4,128,256]{3,2,1,0:T(8,128)(2,1)S(1)}, u32[]{:S(2)}, u32[]{:S(2)}) collective-permute-start(bf16[1,4,128,256]{3,2,1,0:T(8,128)(2,1)S(1)} %bitcast.56), channel_id=1, source_target_pairs={{16,0},{32,16},{48,32},{64,48},{80,64},{96,80},{112,96},{128,112},... | collective-permute-start | bytes 786440 | tf_op jit(solution)/shard_map/ppermute | solution.py:19
  172.0 8.1 %collective-permute-start.6 = (bf16[3,1,128,256]{3,2,1,0:T(8,128)(2,1)S(1)}, bf16[3,1,128,256]{3,2,1,0:T(8,128)(2,1)S(1)}, u32[]{:S(2)}, u32[]{:S(2)}) collective-permute-start(bf16[3,1,128,256]{3,2,1,0:T(8,128)(2,1)S(1)} %get-tuple-element.20), channel_id=1, source_target_pairs={{0,1},{1,2},{2,3},{3,4},{4,5},{5,6},{6,7},{7,8},{8,9},{9,10},{10,1... | collective-permute-start | bytes 589832 | tf_op jit(solution)/shard_map/ppermute | solution.py:18
  177.3 11.6 %collective-permute-start.7 = (bf16[3,1,128,256]{3,2,1,0:T(8,128)(2,1)S(1)}, bf16[3,1,128,256]{3,2,1,0:T(8,128)(2,1)S(1)}, u32[]{:S(2)}, u32[]{:S(2)}) collective-permute-start(bf16[3,1,128,256]{3,2,1,0:T(8,128)(2,1)S(1)} %get-tuple-element.21), channel_id=1, source_target_pairs={{1,0},{2,1},{3,2},{4,3},{5,4},{6,5},{7,6},{8,7},{9,8},{10,9},{11,1... | collective-permute-start | bytes 589832 | tf_op jit(solution)/shard_map/ppermute | solution.py:19

commit v13 on v12

--- a/solution.py
+++ b/solution.py
@@ -34,7 +34,7 @@
     me = lax.axis_index("dp")
     bits = count.bit_length() - 1
     x = blocks.reshape((2,) * bits + blocks.shape[1:])
-    remaining = list(range(bits - 1, -1, -1))
+    remaining = list(range(bits))
     for bit in order:
         axis = remaining.index(bit)
         mine = (me >> bit) & 1
@@ -129,10 +129,14 @@
     part_one = jnp.dot(across_ref[:cols, :], gate_grad, preferred_element_type=jnp.float32)
     part_two = jnp.dot(across_ref[cols:, :], activation, preferred_element_type=jnp.float32)
     lanes = part_ref.shape[2]
-    for block in range(part_ref.shape[0]):
+    bits = part_ref.shape[0].bit_length() - 1
+    per_step = part_one.shape[1] // lanes
+    for block in range(per_step):
         window = slice(block * lanes, (block + 1) * lanes)
-        part_ref[block, :cols, :] = part_one[:, window].astype(part_ref.dtype)
-        part_ref[block, cols:, :] = part_two[:, window].astype(part_ref.dtype)
+        owner = step * per_step + block
+        place = sum(((owner >> bit) & 1) << (bits - 1 - bit) for bit in range(bits))
+        part_ref[place, :cols, :] = part_one[:, window].astype(part_ref.dtype)
+        part_ref[place, cols:, :] = part_two[:, window].astype(part_ref.dtype)
 
     @pl.when(step == pl.num_programs(0) - 1)
     def _():
@@ -146,7 +150,6 @@
     cols, hidden = weight_one.shape
     channels = weight_two.shape[1]
     lanes = hidden // blocks
-    per_step = chunk // lanes
     flops = 2 * slots * hidden * (3 * cols + 3 * channels)
     return pl.pallas_call(
         functools.partial(expert_kernel, cols),
@@ -158,7 +161,7 @@
         ],
         out_specs=[
             pl.BlockSpec((slots, both), lambda h: (0, 0)),
-            pl.BlockSpec((per_step, both, lanes), lambda h: (h, 0, 0)),
+            pl.BlockSpec((blocks, both, lanes), lambda h: (0, 0, 0)),
         ],
         out_shape=[
             jax.ShapeDtypeStruct((slots, both), jnp.bfloat16),

time: 197 us -> 195 us (0.990)
  local copies, waits for them, and re-layouts: 12.6 us -> 9.54 us
    dynamic_slice x2 -> x0, local copies, waits for them, and re-layouts: 3.47 us -> none  [the longest x1 3.36 us: tree_scatter(): lax.dynamic_index_in_dim(x, mine, axis=axis, keepdims=False)]
    unnamed x13 -> x11, local copies, waits for them, and re-layouts: 5.22 us -> 4.09 us
where the time goes in v13:
time: 195 us; the launch traced here: 193 us
  waiting for transfers between devices  90.3 us (46%)
  starting transfers between devices  53.6 us (27%)
  Pallas kernels  26.2 us (13%)
  local copies, waits for them, and re-layouts  9.54 us (5%)
  other arithmetic  6.15 us (3%)
  matrix products  5.85 us (3%)
    all_to_all x1, waiting for transfers between devices, per_device(): lax.all_to_all(outbound.reshape(experts, capacity, both), 'expert', split...  30.8 us
    ppermute x4, waiting for transfers between devices, extended(): after = lax.ppermute(first, axis, down)  28.7 us
    ppermute x4, waiting for transfers between devices, tree_scatter(): got = lax.ppermute(send.astype(jnp.bfloat16), 'dp', pairs)  27.2 us
    ppermute x4, starting transfers between devices, extended(): before = lax.ppermute(last, axis, up)  20.1 us
    pallas_call x1, Pallas kernels, expert(): pl.pallas_call(functools.partial(expert_kernel, cols), grid=(hidden // ch...  17.5 us
    ppermute x4, starting transfers between devices, tree_scatter(): got = lax.ppermute(send.astype(jnp.bfloat16), 'dp', pairs)  12.4 us
    pallas_call x2, Pallas kernels, conv_block(): pl.pallas_call(functools.partial(conv_kernel, flip), out_shape=jax.ShapeD...  8.77 us
    all_to_all x1, starting transfers between devices, per_device(): lax.all_to_all(back.reshape(experts, capacity, both), 'expert', split_axi...  7.69 us
  transfers between devices with their start and end apart: 14, of which 10 were waited for; matrix products, arithmetic and copies ran while one was open for 7% of the time, Pallas kernels for 0%

profile of v13, /device:TPU:95, one launch (start us, length us, event | category | flops | bytes accessed | tf_op | source)
XLA Modules:
  0.0 192.7 jit_solution(10166859583343991267)
XLA Ops:
  0.6 3.8 %collective-permute-start = (bf16[1,4,128,256]{3,2,1,0:T(8,128)(2,1)}, bf16[1,4,128,256]{3,2,1,0:T(8,128)(2,1)S(1)}, u32[]{:S(2)}, u32[]{:S(2)}) collective-permute-start(bf16[1,4,128,256]{3,2,1,0:T(8,128)(2,1)} %param.11), channel_id=1, source_target_pairs={{0,16},{16,32},{32,48},{48,64},{64,80},{80,96},{96,112},{112,128},... | collective-permute-start | bytes 786440 | tf_op jit(solution)/shard_map/ppermute | solution.py:18
  4.4 1.9 collective-permute-start.1
  9.0 5.4 %collective-permute-done.1 = bf16[1,4,128,256]{3,2,1,0:T(8,128)(2,1)S(1)} collective-permute-done((bf16[1,4,128,256]{3,2,1,0:T(8,128)(2,1)}, bf16[1,4,128,256]{3,2,1,0:T(8,128)(2,1)S(1)}, u32[]{:S(2)}, u32[]{:S(2)}) %collective-permute-start.1) | collective-permute-done | bytes 262176 | tf_op jit(solution)/shard_map/ppermute | solution.py:19
  14.5 5.1 %collective-permute-start.2 = (bf16[3,1,128,256]{3,2,1,0:T(8,128)(2,1)S(1)}, bf16[3,1,128,256]{3,2,1,0:T(8,128)(2,1)S(1)}, u32[]{:S(2)}, u32[]{:S(2)}) collective-permute-start(bf16[3,1,128,256]{3,2,1,0:T(8,128)(2,1)S(1)} %get-tuple-element.20), channel_id=1, source_target_pairs={{0,1},{1,2},{2,3},{3,4},{4,5},{5,6},{6,7},{7,8},{8,9},{9,10},{10,1... | collective-permute-start | bytes 589832 | tf_op jit(solution)/shard_map/ppermute | solution.py:18
  19.6 1.9 collective-permute-start.3
  21.6 2.8 %collective-permute-done.2 = bf16[3,1,128,256]{3,2,1,0:T(8,128)(2,1)S(1)} collective-permute-done((bf16[3,1,128,256]{3,2,1,0:T(8,128)(2,1)S(1)}, bf16[3,1,128,256]{3,2,1,0:T(8,128)(2,1)S(1)}, u32[]{:S(2)}, u32[]{:S(2)}) %collective-permute-start.2) | collective-permute-done | bytes 196640 | tf_op jit(solution)/shard_map/ppermute | solution.py:18
  24.3 8.3 %collective-permute-done.3 = bf16[3,1,128,256]{3,2,1,0:T(8,128)(2,1)S(1)} collective-permute-done((bf16[3,1,128,256]{3,2,1,0:T(8,128)(2,1)S(1)}, bf16[3,1,128,256]{3,2,1,0:T(8,128)(2,1)S(1)}, u32[]{:S(2)}, u32[]{:S(2)}) %collective-permute-start.3) | collective-permute-done | bytes 196640 | tf_op jit(solution)/shard_map/ppermute | solution.py:19
  33.9 4.1 %shard_map.93 = bf16[512,256]{1,0:T(8,128)(2,1)S(1)} custom-call(bf16[1,3,3,6,128,256]{5,4,3,2,1,0:T(8,128)(2,1)S(1)} %maximum_bitcast_fusion.shifted_ref, bf16[27,256,256]{2,1,0:T(8,128)(2,1)} %taps_ref.3), custom_call_target="tpu_custom_call" | custom-call | flops 1811939328 | bytes 7340032 | tf_op jit(solution)/shard_map/pallas_call | solution.py:86
  38.0 2.2 %fusion.2 = bf16[1024,768]{1,0:T(8,128)(2,1)} fusion(s32[512]{0:T(512)S(1)} %add_add_fusion, bf16[512,256]{1,0:T(8,128)(2,1)S(1)} %shard_map.93, bf16[512,512]{1,0:T(8,128)(2,1)S(1)} %bitcast.66), kind=kOutput, calls=%fused_computation.6 | convolution fusion | flops 808189952 | bytes 2361344 | tf_op jit(solution)/shard_map/dot_general | solution.py:212
  40.2 5.8 %all-to-all-start = ((bf16[16,64,768]{2,1,0:T(8,128)(2,1)}), bf16[16,64,768]{2,1,0:T(8,128)(2,1)S(1)}, u32[]{:S(2)}, u32[]{:S(2)}) async-start(bf16[16,64,768]{2,1,0:T(8,128)(2,1)} %bitcast.6), calls=%async_computation | async-start | bytes 3145728 | tf_op jit(solution)/shard_map/all_to_all | solution.py:214
  45.9 30.8 %all-to-all-done = bf16[16,64,768]{2,1,0:T(8,128)(2,1)S(1)} async-done(((bf16[16,64,768]{2,1,0:T(8,128)(2,1)}), bf16[16,64,768]{2,1,0:T(8,128)(2,1)S(1)}, u32[]{:S(2)}, u32[]{:S(2)}) %all-to-all-start) | async-done | bytes 1572896 | tf_op jit(solution)/shard_map/all_to_all | solution.py:214
  76.8 1.2 copy-done.1
  78.0 17.5 %shard_map.94 = (bf16[1024,768]{1,0:T(8,128)(2,1)}, bf16[16,768,128]{2,1,0:T(8,128)(2,1)}) custom-call(bf16[1024,768]{1,0:T(8,128)(2,1)} %bitcast.59, bf16[512,2048]{1,0:T(8,128)(2,1)} %bitcast.64, bf16[2048,256]{1,0:T(8,128)(2,1)} %bitcast.65), custom_call_target="tpu_custom_call" | custom-call | flops 9663676416 | bytes 9437184 | tf_op jit(solution)/shard_map/pallas_call | solution.py:154
  95.4 1.5 dynamic-slice_bitcast_fusion
  96.9 2.3 %collective-permute-start.8 = (bf16[2,2,2,768,128]{4,3,2,1,0:T(8,128)(2,1)S(1)}, bf16[2,2,2,768,128]{4,3,2,1,0:T(8,128)(2,1)}, u32[]{:S(2)}, u32[]{:S(2)}) collective-permute-start(bf16[2,2,2,768,128]{4,3,2,1,0:T(8,128)(2,1)S(1)} %dynamic-slice_bitcast_fusion), channel_id=1, source_target_pairs={{0,16},{16,0},{32,48},{48,32},{64,80},{80,64},{96,112},{112,96},{1... | collective-permute-start | bytes 4718600 | tf_op jit(solution)/shard_map/ppermute | solution.py:44
  99.2 7.7 %all-to-all-start.1 = ((bf16[16,64,768]{2,1,0:T(8,128)(2,1)}), bf16[16,64,768]{2,1,0:T(8,128)(2,1)}, u32[]{:S(2)}, u32[]{:S(2)}) async-start(bf16[16,64,768]{2,1,0:T(8,128)(2,1)} %bitcast.10), calls=%async_computation.1 | async-start | bytes 3145728 | tf_op jit(solution)/shard_map/all_to_all | solution.py:218
  106.9 2.2 %convert_add_fusion = f32[2,2,2,768,128]{4,3,2,1,0:T(8,128)S(1)} fusion(bf16[2,2,2,768,128]{4,3,2,1,0:T(8,128)(2,1)} %collective-permute-done.8, bf16[2,2,2,2,768,128]{5,4,3,2,1,0:T(8,128)(2,1)} %bitcast.58, s32[]{:T(128)S(6)} %select_n.28), kind=kLoop, calls=%fused_computation.2 | loop fusion | flops 2359296 | bytes 6291460 | tf_op jit(solution)/shard_map/add | solution.py:45
  110.1 8.3 %collective-permute-start.9 = (bf16[2,2,768,128]{3,2,1,0:T(8,128)(2,1)}, bf16[2,2,768,128]{3,2,1,0:T(8,128)(2,1)}, u32[]{:S(2)}, u32[]{:S(2)}) collective-permute-start(bf16[2,2,768,128]{3,2,1,0:T(8,128)(2,1)} %fusion.7), channel_id=1, source_target_pairs={{0,32},{16,48},{32,0},{48,16},{64,96},{80,112},{96,64},{112,80},{1... | collective-permute-start | bytes 2359304 | tf_op jit(solution)/shard_map/ppermute | solution.py:44
  118.4 17.8 %collective-permute-done.9 = bf16[2,2,768,128]{3,2,1,0:T(8,128)(2,1)} collective-permute-done((bf16[2,2,768,128]{3,2,1,0:T(8,128)(2,1)}, bf16[2,2,768,128]{3,2,1,0:T(8,128)(2,1)}, u32[]{:S(2)}, u32[]{:S(2)}) %collective-permute-start.9) | collective-permute-done | bytes 786464 | tf_op jit(solution)/shard_map/ppermute | solution.py:44
  136.2 1.3 bitcast_add_fusion
  137.4 1.2 copy-done
  138.7 1.7 collective-permute-start.10
  140.4 9.4 %collective-permute-done.10 = bf16[2,768,128]{2,1,0:T(8,128)(2,1)S(1)} collective-permute-done((bf16[2,768,128]{2,1,0:T(8,128)(2,1)S(1)}, bf16[2,768,128]{2,1,0:T(8,128)(2,1)S(1)}, u32[]{:S(2)}, u32[]{:S(2)}) %collective-permute-start.10) | collective-permute-done | bytes 393248 | tf_op jit(solution)/shard_map/ppermute | solution.py:44
  149.8 1.2 bitcast_add_fusion.1
  151.2 2.6 %fusion.3 = bf16[512,768]{1,0:T(8,128)(2,1)S(1)} fusion(bf16[1024,768]{1,0:T(8,128)(2,1)} %bitcast.11, s32[512]{0:T(512)S(1)} %add_add_fusion), kind=kOutput, calls=%fused_computation.10 | convolution fusion | flops 806223872 | bytes 2361344 | tf_op jit(solution)/shard_map/dot_general | solution.py:221
  153.8 6.0 %collective-permute-start.4 = (bf16[1,4,128,256]{3,2,1,0:T(8,128)(2,1)S(1)}, bf16[1,4,128,256]{3,2,1,0:T(8,128)(2,1)S(1)}, u32[]{:S(2)}, u32[]{:S(2)}) collective-permute-start(bf16[1,4,128,256]{3,2,1,0:T(8,128)(2,1)S(1)} %bitcast.52), channel_id=1, source_target_pairs={{0,16},{16,32},{32,48},{48,64},{64,80},{80,96},{96,112},{112,128},... | collective-permute-start | bytes 786440 | tf_op jit(solution)/shard_map/ppermute | solution.py:18
  159.8 1.9 collective-permute-start.5
  163.4 6.2 %collective-permute-done.5 = bf16[1,4,128,256]{3,2,1,0:T(8,128)(2,1)S(1)} collective-permute-done((bf16[1,4,128,256]{3,2,1,0:T(8,128)(2,1)S(1)}, bf16[1,4,128,256]{3,2,1,0:T(8,128)(2,1)S(1)}, u32[]{:S(2)}, u32[]{:S(2)}) %collective-permute-start.5) | collective-permute-done | bytes 262176 | tf_op jit(solution)/shard_map/ppermute | solution.py:19
  169.7 5.2 %collective-permute-start.6 = (bf16[3,1,128,256]{3,2,1,0:T(8,128)(2,1)S(1)}, bf16[3,1,128,256]{3,2,1,0:T(8,128)(2,1)S(1)}, u32[]{:S(2)}, u32[]{:S(2)}) collective-permute-start(bf16[3,1,128,256]{3,2,1,0:T(8,128)(2,1)S(1)} %get-tuple-element.18), channel_id=1, source_target_pairs={{0,1},{1,2},{2,3},{3,4},{4,5},{5,6},{6,7},{7,8},{8,9},{9,10},{10,1... | collective-permute-start | bytes 589832 | tf_op jit(solution)/shard_map/ppermute | solution.py:18
  174.9 1.9 collective-permute-start.7
  177.7 8.8 %collective-permute-done.7 = bf16[3,1,128,256]{3,2,1,0:T(8,128)(2,1)S(1)} collective-permute-done((bf16[3,1,128,256]{3,2,1,0:T(8,128)(2,1)S(1)}, bf16[3,1,128,256]{3,2,1,0:T(8,128)(2,1)S(1)}, u32[]{:S(2)}, u32[]{:S(2)}) %collective-permute-start.7) | collective-permute-done | bytes 196640 | tf_op jit(solution)/shard_map/ppermute | solution.py:19
  188.0 4.7 %shard_map.95 = bf16[512,256]{1,0:T(8,128)(2,1)} custom-call(bf16[1,3,3,6,128,256]{5,4,3,2,1,0:T(8,128)(2,1)S(1)} %maximum_bitcast_fusion.1.shifted_ref, bf16[27,256,256]{2,1,0:T(8,128)(2,1)} %taps_ref.3), custom_call_target="tpu_custom_call" | custom-call | flops 1811939328 | bytes 7340032 | tf_op jit(solution)/shard_map/pallas_call | solution.py:86
  (36 shorter events, 9.2 us)
Async XLA Ops:
  0.6 20.9 %copy-start.2 = (s32[1,4,128,1]{2,3,1,0:T(1,128)S(1)}, s32[1,4,128,1]{2,3,1,0:T(1,128)}, u32[]{:S(2)}) copy-start(s32[1,4,128,1]{2,3,1,0:T(1,128)} %param.7) | copy-start | bytes 6148
  0.6 7.4 %collective-permute-start = (bf16[1,4,128,256]{3,2,1,0:T(8,128)(2,1)}, bf16[1,4,128,256]{3,2,1,0:T(8,128)(2,1)S(1)}, u32[]{:S(2)}, u32[]{:S(2)}) collective-permute-start(bf16[1,4,128,256]{3,2,1,0:T(8,128)(2,1)} %param.11), channel_id=1, source_target_pairs={{0,16},{16,32},{32,48},{48,64},{64,80},{80,96},{96,112},{112,128},... | collective-permute-start | bytes 786440 | tf_op jit(solution)/shard_map/ppermute | solution.py:18
  4.4 10.0 %collective-permute-start.1 = (bf16[1,4,128,256]{3,2,1,0:T(8,128)(2,1)}, bf16[1,4,128,256]{3,2,1,0:T(8,128)(2,1)S(1)}, u32[]{:S(2)}, u32[]{:S(2)}) collective-permute-start(bf16[1,4,128,256]{3,2,1,0:T(8,128)(2,1)} %param.11), channel_id=1, source_target_pairs={{16,0},{32,16},{48,32},{64,48},{80,64},{96,80},{112,96},{128,112},... | collective-permute-start | bytes 786440 | tf_op jit(solution)/shard_map/ppermute | solution.py:19
  14.5 9.9 %collective-permute-start.2 = (bf16[3,1,128,256]{3,2,1,0:T(8,128)(2,1)S(1)}, bf16[3,1,128,256]{3,2,1,0:T(8,128)(2,1)S(1)}, u32[]{:S(2)}, u32[]{:S(2)}) collective-permute-start(bf16[3,1,128,256]{3,2,1,0:T(8,128)(2,1)S(1)} %get-tuple-element.20), channel_id=1, source_target_pairs={{0,1},{1,2},{2,3},{3,4},{4,5},{5,6},{6,7},{7,8},{8,9},{9,10},{10,1... | collective-permute-start | bytes 589832 | tf_op jit(solution)/shard_map/ppermute | solution.py:18
  19.6 13.0 %collective-permute-start.3 = (bf16[3,1,128,256]{3,2,1,0:T(8,128)(2,1)S(1)}, bf16[3,1,128,256]{3,2,1,0:T(8,128)(2,1)S(1)}, u32[]{:S(2)}, u32[]{:S(2)}) collective-permute-start(bf16[3,1,128,256]{3,2,1,0:T(8,128)(2,1)S(1)} %get-tuple-element.21), channel_id=1, source_target_pairs={{1,0},{2,1},{3,2},{4,3},{5,4},{6,5},{7,6},{8,7},{9,8},{10,9},{11,1... | collective-permute-start | bytes 589832 | tf_op jit(solution)/shard_map/ppermute | solution.py:19
  33.9 4.1 %copy-start.3 = (bf16[1,4,128,512]{3,2,1,0:T(8,128)(2,1)S(1)}, bf16[1,4,128,512]{3,2,1,0:T(8,128)(2,1)}, u32[]{:S(2)}) copy-start(bf16[1,4,128,512]{3,2,1,0:T(8,128)(2,1)} %param.6) | copy-start | bytes 1572868
  40.2 36.6 %all-to-all-start = ((bf16[16,64,768]{2,1,0:T(8,128)(2,1)}), bf16[16,64,768]{2,1,0:T(8,128)(2,1)S(1)}, u32[]{:S(2)}, u32[]{:S(2)}) async-start(bf16[16,64,768]{2,1,0:T(8,128)(2,1)} %bitcast.6), calls=%async_computation | async-start | bytes 3145728 | tf_op jit(solution)/shard_map/all_to_all | solution.py:214
  76.8 1.2 copy-start.1
  96.9 10.0 %collective-permute-start.8 = (bf16[2,2,2,768,128]{4,3,2,1,0:T(8,128)(2,1)S(1)}, bf16[2,2,2,768,128]{4,3,2,1,0:T(8,128)(2,1)}, u32[]{:S(2)}, u32[]{:S(2)}) collective-permute-start(bf16[2,2,2,768,128]{4,3,2,1,0:T(8,128)(2,1)S(1)} %dynamic-slice_bitcast_fusion), channel_id=1, source_target_pairs={{0,16},{16,0},{32,48},{48,32},{64,80},{80,64},{96,112},{112,96},{1... | collective-permute-start | bytes 4718600 | tf_op jit(solution)/shard_map/ppermute | solution.py:44
  99.2 51.9 %all-to-all-start.1 = ((bf16[16,64,768]{2,1,0:T(8,128)(2,1)}), bf16[16,64,768]{2,1,0:T(8,128)(2,1)}, u32[]{:S(2)}, u32[]{:S(2)}) async-start(bf16[16,64,768]{2,1,0:T(8,128)(2,1)} %bitcast.10), calls=%async_computation.1 | async-start | bytes 3145728 | tf_op jit(solution)/shard_map/all_to_all | solution.py:218
  110.1 26.0 %collective-permute-start.9 = (bf16[2,2,768,128]{3,2,1,0:T(8,128)(2,1)}, bf16[2,2,768,128]{3,2,1,0:T(8,128)(2,1)}, u32[]{:S(2)}, u32[]{:S(2)}) collective-permute-start(bf16[2,2,768,128]{3,2,1,0:T(8,128)(2,1)} %fusion.7), channel_id=1, source_target_pairs={{0,32},{16,48},{32,0},{48,16},{64,96},{80,112},{96,64},{112,80},{1... | collective-permute-start | bytes 2359304 | tf_op jit(solution)/shard_map/ppermute | solution.py:44
  137.4 1.2 copy-start
  138.7 11.2 %collective-permute-start.10 = (bf16[2,768,128]{2,1,0:T(8,128)(2,1)S(1)}, bf16[2,768,128]{2,1,0:T(8,128)(2,1)S(1)}, u32[]{:S(2)}, u32[]{:S(2)}) collective-permute-start(bf16[2,768,128]{2,1,0:T(8,128)(2,1)S(1)} %fusion.11), channel_id=1, source_target_pairs={{0,64},{16,80},{32,96},{48,112},{64,0},{80,16},{96,32},{112,48},{1... | collective-permute-start | bytes 1179656 | tf_op jit(solution)/shard_map/ppermute | solution.py:44
  151.1 10.7 %collective-permute-start.11 = (bf16[768,128]{1,0:T(8,128)(2,1)S(1)}, bf16[768,128]{1,0:T(8,128)(2,1)S(1)}, u32[]{:S(2)}, u32[]{:S(2)}) collective-permute-start(bf16[768,128]{1,0:T(8,128)(2,1)S(1)} %fusion.12), channel_id=1, source_target_pairs={{0,128},{16,144},{32,160},{48,176},{64,192},{80,208},{96,224},{112... | collective-permute-start | bytes 589832 | tf_op jit(solution)/shard_map/ppermute | solution.py:44
  153.8 9.6 %collective-permute-start.4 = (bf16[1,4,128,256]{3,2,1,0:T(8,128)(2,1)S(1)}, bf16[1,4,128,256]{3,2,1,0:T(8,128)(2,1)S(1)}, u32[]{:S(2)}, u32[]{:S(2)}) collective-permute-start(bf16[1,4,128,256]{3,2,1,0:T(8,128)(2,1)S(1)} %bitcast.52), channel_id=1, source_target_pairs={{0,16},{16,32},{32,48},{48,64},{64,80},{80,96},{96,112},{112,128},... | collective-permute-start | bytes 786440 | tf_op jit(solution)/shard_map/ppermute | solution.py:18
  159.8 9.8 %collective-permute-start.5 = (bf16[1,4,128,256]{3,2,1,0:T(8,128)(2,1)S(1)}, bf16[1,4,128,256]{3,2,1,0:T(8,128)(2,1)S(1)}, u32[]{:S(2)}, u32[]{:S(2)}) collective-permute-start(bf16[1,4,128,256]{3,2,1,0:T(8,128)(2,1)S(1)} %bitcast.53), channel_id=1, source_target_pairs={{16,0},{32,16},{48,32},{64,48},{80,64},{96,80},{112,96},{128,112},... | collective-permute-start | bytes 786440 | tf_op jit(solution)/shard_map/ppermute | solution.py:19
  169.7 8.1 %collective-permute-start.6 = (bf16[3,1,128,256]{3,2,1,0:T(8,128)(2,1)S(1)}, bf16[3,1,128,256]{3,2,1,0:T(8,128)(2,1)S(1)}, u32[]{:S(2)}, u32[]{:S(2)}) collective-permute-start(bf16[3,1,128,256]{3,2,1,0:T(8,128)(2,1)S(1)} %get-tuple-element.18), channel_id=1, source_target_pairs={{0,1},{1,2},{2,3},{3,4},{4,5},{5,6},{6,7},{7,8},{8,9},{9,10},{10,1... | collective-permute-start | bytes 589832 | tf_op jit(solution)/shard_map/ppermute | solution.py:18
  174.9 11.6 %collective-permute-start.7 = (bf16[3,1,128,256]{3,2,1,0:T(8,128)(2,1)S(1)}, bf16[3,1,128,256]{3,2,1,0:T(8,128)(2,1)S(1)}, u32[]{:S(2)}, u32[]{:S(2)}) collective-permute-start(bf16[3,1,128,256]{3,2,1,0:T(8,128)(2,1)S(1)} %get-tuple-element.19), channel_id=1, source_target_pairs={{1,0},{2,1},{3,2},{4,3},{5,4},{6,5},{7,6},{8,7},{9,8},{10,9},{11,1... | collective-permute-start | bytes 589832 | tf_op jit(solution)/shard_map/ppermute | solution.py:19

commit v14 on v13

--- a/solution.py
+++ b/solution.py
@@ -73,7 +73,7 @@
 
 
 def conv_block(grid, kernel, flip, after=None):
-    padded = extended(grid, (("dp", 0), ("expert", 1)), 1)
+    padded = extended(grid, (("expert", 1), ("dp", 0)), 1)
     if after is not None:
         after, padded = lax.optimization_barrier((after, padded))
     padded = jnp.pad(padded, ((0, 0), (0, 0), (1, 1), (0, 0)))

time: 195 us -> 191 us (0.979)
  starting transfers between devices: 53.6 us -> 50.7 us
    ppermute x4, starting transfers between devices: 12.4 us -> 7.36 us  [tree_scatter(): got = lax.ppermute(send.astype(jnp.bfloat16), 'dp', pairs)]
    ppermute x4, waiting for transfers between devices: 28.7 us -> 26.3 us  [extended(): after = lax.ppermute(first, axis, down)]
    all_to_all x1, waiting for transfers between devices: 30.8 us -> 32.9 us  [per_device(): lax.all_to_all(outbound.reshape(experts, capacity, both), 'expert', split...]
    ppermute x4, starting transfers between devices: 20.1 us -> 22.1 us  [extended(): before = lax.ppermute(last, axis, up)]
    unnamed x11 -> x9, local copies, waits for them, and re-layouts: 4.09 us -> 4.08 us
where the time goes in v14:
time: 191 us
  waiting for transfers between devices  89.6 us (47%)
  starting transfers between devices  50.7 us (27%)
  Pallas kernels  26.3 us (14%)
  local copies, waits for them, and re-layouts  10.4 us (5%)
  other arithmetic  6.77 us (4%)
  matrix products  5.85 us (3%)
    all_to_all x1, waiting for transfers between devices, per_device(): lax.all_to_all(outbound.reshape(experts, capacity, both), 'expert', split...  32.9 us
    ppermute x4, waiting for transfers between devices, tree_scatter(): got = lax.ppermute(send.astype(jnp.bfloat16), 'dp', pairs)  28.4 us
    ppermute x4, waiting for transfers between devices, extended(): after = lax.ppermute(first, axis, down)  26.3 us
    ppermute x4, starting transfers between devices, extended(): before = lax.ppermute(last, axis, up)  22.1 us
    pallas_call x1, Pallas kernels, expert(): pl.pallas_call(functools.partial(expert_kernel, cols), grid=(hidden // ch...  17.5 us
    pallas_call x2, Pallas kernels, conv_block(): pl.pallas_call(functools.partial(conv_kernel, flip), out_shape=jax.ShapeD...  8.77 us
    ppermute x4, starting transfers between devices, extended(): after = lax.ppermute(first, axis, down)  8.05 us
    all_to_all x1, starting transfers between devices, per_device(): lax.all_to_all(back.reshape(experts, capacity, both), 'expert', split_axi...  7.47 us
  transfers between devices with their start and end apart: 14, of which 10 were waited for; matrix products, arithmetic and copies ran while one was open for 7% of the time, Pallas kernels for 0%

profile of v14, /device:TPU:95, one launch (start us, length us, event | category | flops | bytes accessed | tf_op | source)
XLA Modules:
  0.0 190.5 jit_solution(4762731949637745371)
XLA Ops:
  1.5 6.0 %collective-permute-start = (bf16[1,1,128,256]{3,2,1,0:T(8,128)(2,1)S(1)}, bf16[1,1,128,256]{3,2,1,0:T(8,128)(2,1)S(1)}, u32[]{:S(2)}, u32[]{:S(2)}) collective-permute-start(bf16[1,1,128,256]{3,2,1,0:T(8,128)(2,1)S(1)} %get-tuple-element.21), channel_id=1, source_target_pairs={{0,1},{1,2},{2,3},{3,4},{4,5},{5,6},{6,7},{7,8},{8,9},{9,10},{10,1... | collective-permute-start | bytes 196616 | tf_op jit(solution)/shard_map/ppermute | solution.py:18
  7.5 1.9 %collective-permute-start.1 = (bf16[1,1,128,256]{3,2,1,0:T(8,128)(2,1)S(1)}, bf16[1,1,128,256]{3,2,1,0:T(8,128)(2,1)S(1)}, u32[]{:S(2)}, u32[]{:S(2)}) collective-permute-start(bf16[1,1,128,256]{3,2,1,0:T(8,128)(2,1)S(1)} %get-tuple-element.20), channel_id=1, source_target_pairs={{1,0},{2,1},{3,2},{4,3},{5,4},{6,5},{7,6},{8,7},{9,8},{10,9},{11,1... | collective-permute-start | bytes 196616 | tf_op jit(solution)/shard_map/ppermute | solution.py:19
  10.6 6.7 %collective-permute-done.1 = bf16[1,1,128,256]{3,2,1,0:T(8,128)(2,1)S(1)} collective-permute-done((bf16[1,1,128,256]{3,2,1,0:T(8,128)(2,1)S(1)}, bf16[1,1,128,256]{3,2,1,0:T(8,128)(2,1)S(1)}, u32[]{:S(2)}, u32[]{:S(2)}) %collective-permute-start.1) | collective-permute-done | bytes 65568 | tf_op jit(solution)/shard_map/ppermute | solution.py:19
  17.4 3.8 %collective-permute-start.2 = (bf16[1,6,128,256]{3,2,1,0:T(8,128)(2,1)S(1)}, bf16[1,6,128,256]{3,2,1,0:T(8,128)(2,1)S(1)}, u32[]{:S(2)}, u32[]{:S(2)}) collective-permute-start(bf16[1,6,128,256]{3,2,1,0:T(8,128)(2,1)S(1)} %constant_dynamic-update-slice_fusion), channel_id=1, source_target_pairs={{0,16},{16,32},{32,48},{48,64},{64,80},{80,96},{96,112},{112,128},... | collective-permute-start | bytes 1179656 | tf_op jit(solution)/shard_map/ppermute | solution.py:18
  21.2 2.3 %collective-permute-start.3 = (bf16[1,6,128,256]{3,2,1,0:T(8,128)(2,1)S(1)}, bf16[1,6,128,256]{3,2,1,0:T(8,128)(2,1)S(1)}, u32[]{:S(2)}, u32[]{:S(2)}) collective-permute-start(bf16[1,6,128,256]{3,2,1,0:T(8,128)(2,1)S(1)} %constant_dynamic-update-slice_fusion), channel_id=1, source_target_pairs={{16,0},{32,16},{48,32},{64,48},{80,64},{96,80},{112,96},{128,112},... | collective-permute-start | bytes 1179656 | tf_op jit(solution)/shard_map/ppermute | solution.py:19
  23.5 1.0 fusion.4
  25.9 6.5 %collective-permute-done.3 = bf16[1,6,128,256]{3,2,1,0:T(8,128)(2,1)S(1)} collective-permute-done((bf16[1,6,128,256]{3,2,1,0:T(8,128)(2,1)S(1)}, bf16[1,6,128,256]{3,2,1,0:T(8,128)(2,1)S(1)}, u32[]{:S(2)}, u32[]{:S(2)}) %collective-permute-start.3) | collective-permute-done | bytes 393248 | tf_op jit(solution)/shard_map/ppermute | solution.py:19
  33.7 4.1 %shard_map.93 = bf16[512,256]{1,0:T(8,128)(2,1)S(1)} custom-call(bf16[1,3,3,6,128,256]{5,4,3,2,1,0:T(8,128)(2,1)S(1)} %maximum_bitcast_fusion.shifted_ref, bf16[27,256,256]{2,1,0:T(8,128)(2,1)} %taps_ref.3), custom_call_target="tpu_custom_call" | custom-call | flops 1811939328 | bytes 7340032 | tf_op jit(solution)/shard_map/pallas_call | solution.py:86
  37.8 2.2 %fusion.2 = bf16[1024,768]{1,0:T(8,128)(2,1)} fusion(s32[512]{0:T(512)S(1)} %add_add_fusion, bf16[512,256]{1,0:T(8,128)(2,1)S(1)} %shard_map.93, bf16[512,512]{1,0:T(8,128)(2,1)S(1)} %bitcast.65), kind=kOutput, calls=%fused_computation.6 | convolution fusion | flops 808189952 | bytes 2361344 | tf_op jit(solution)/shard_map/dot_general | solution.py:212
  40.0 5.8 %all-to-all-start = ((bf16[16,64,768]{2,1,0:T(8,128)(2,1)}), bf16[16,64,768]{2,1,0:T(8,128)(2,1)S(1)}, u32[]{:S(2)}, u32[]{:S(2)}) async-start(bf16[16,64,768]{2,1,0:T(8,128)(2,1)} %bitcast.6), calls=%async_computation | async-start | bytes 3145728 | tf_op jit(solution)/shard_map/all_to_all | solution.py:214
  45.7 32.9 %all-to-all-done = bf16[16,64,768]{2,1,0:T(8,128)(2,1)S(1)} async-done(((bf16[16,64,768]{2,1,0:T(8,128)(2,1)}), bf16[16,64,768]{2,1,0:T(8,128)(2,1)S(1)}, u32[]{:S(2)}, u32[]{:S(2)}) %all-to-all-start) | async-done | bytes 1572896 | tf_op jit(solution)/shard_map/all_to_all | solution.py:214
  78.6 1.2 copy-done.1
  79.8 17.5 %shard_map.94 = (bf16[1024,768]{1,0:T(8,128)(2,1)}, bf16[16,768,128]{2,1,0:T(8,128)(2,1)}) custom-call(bf16[1024,768]{1,0:T(8,128)(2,1)} %bitcast.58, bf16[512,2048]{1,0:T(8,128)(2,1)} %bitcast.63, bf16[2048,256]{1,0:T(8,128)(2,1)} %bitcast.64), custom_call_target="tpu_custom_call" | custom-call | flops 9663676416 | bytes 9437184 | tf_op jit(solution)/shard_map/pallas_call | solution.py:154
  97.3 1.5 dynamic-slice_bitcast_fusion
  99.5 7.5 %all-to-all-start.1 = ((bf16[16,64,768]{2,1,0:T(8,128)(2,1)}), bf16[16,64,768]{2,1,0:T(8,128)(2,1)}, u32[]{:S(2)}, u32[]{:S(2)}) async-start(bf16[16,64,768]{2,1,0:T(8,128)(2,1)} %bitcast.10), calls=%async_computation.1 | async-start | bytes 3145728 | tf_op jit(solution)/shard_map/all_to_all | solution.py:218
  107.0 2.2 %convert_add_fusion = f32[2,2,2,768,128]{4,3,2,1,0:T(8,128)S(1)} fusion(bf16[2,2,2,768,128]{4,3,2,1,0:T(8,128)(2,1)} %collective-permute-done.8, bf16[2,2,2,2,768,128]{5,4,3,2,1,0:T(8,128)(2,1)} %bitcast.57, s32[]{:T(128)S(6)} %select_n.28), kind=kLoop, calls=%fused_computation.2 | loop fusion | flops 2359296 | bytes 6291460 | tf_op jit(solution)/shard_map/add | solution.py:45
  109.2 1.0 fusion.7
  110.2 5.8 %collective-permute-start.9 = (bf16[2,2,768,128]{3,2,1,0:T(8,128)(2,1)}, bf16[2,2,768,128]{3,2,1,0:T(8,128)(2,1)}, u32[]{:S(2)}, u32[]{:S(2)}) collective-permute-start(bf16[2,2,768,128]{3,2,1,0:T(8,128)(2,1)} %fusion.7), channel_id=1, source_target_pairs={{0,32},{16,48},{32,0},{48,16},{64,96},{80,112},{96,64},{112,80},{1... | collective-permute-start | bytes 2359304 | tf_op jit(solution)/shard_map/ppermute | solution.py:44
  116.0 17.9 %collective-permute-done.9 = bf16[2,2,768,128]{3,2,1,0:T(8,128)(2,1)} collective-permute-done((bf16[2,2,768,128]{3,2,1,0:T(8,128)(2,1)}, bf16[2,2,768,128]{3,2,1,0:T(8,128)(2,1)}, u32[]{:S(2)}, u32[]{:S(2)}) %collective-permute-start.9) | collective-permute-done | bytes 786464 | tf_op jit(solution)/shard_map/ppermute | solution.py:44
  133.9 1.3 bitcast_add_fusion
  135.1 1.2 copy-done
  137.1 10.5 %collective-permute-done.10 = bf16[2,768,128]{2,1,0:T(8,128)(2,1)S(1)} collective-permute-done((bf16[2,768,128]{2,1,0:T(8,128)(2,1)S(1)}, bf16[2,768,128]{2,1,0:T(8,128)(2,1)S(1)}, u32[]{:S(2)}, u32[]{:S(2)}) %collective-permute-start.10) | collective-permute-done | bytes 393248 | tf_op jit(solution)/shard_map/ppermute | solution.py:44
  147.6 1.2 bitcast_add_fusion.1
  149.0 2.6 %fusion.3 = bf16[512,768]{1,0:T(8,128)(2,1)S(1)} fusion(bf16[1024,768]{1,0:T(8,128)(2,1)} %bitcast.11, s32[512]{0:T(512)S(1)} %add_add_fusion), kind=kOutput, calls=%fused_computation.10 | convolution fusion | flops 806223872 | bytes 2361344 | tf_op jit(solution)/shard_map/dot_general | solution.py:221
  151.6 5.2 %collective-permute-start.4 = (bf16[1,1,128,256]{3,2,1,0:T(8,128)(2,1)S(1)}, bf16[1,1,128,256]{3,2,1,0:T(8,128)(2,1)S(1)}, u32[]{:S(2)}, u32[]{:S(2)}) collective-permute-start(bf16[1,1,128,256]{3,2,1,0:T(8,128)(2,1)S(1)} %get-tuple-element.18), channel_id=1, source_target_pairs={{0,1},{1,2},{2,3},{3,4},{4,5},{5,6},{6,7},{7,8},{8,9},{9,10},{10,1... | collective-permute-start | bytes 196616 | tf_op jit(solution)/shard_map/ppermute | solution.py:18
  156.8 1.9 %collective-permute-start.5 = (bf16[1,1,128,256]{3,2,1,0:T(8,128)(2,1)S(1)}, bf16[1,1,128,256]{3,2,1,0:T(8,128)(2,1)S(1)}, u32[]{:S(2)}, u32[]{:S(2)}) collective-permute-start(bf16[1,1,128,256]{3,2,1,0:T(8,128)(2,1)S(1)} %get-tuple-element.19), channel_id=1, source_target_pairs={{1,0},{2,1},{3,2},{4,3},{5,4},{6,5},{7,6},{8,7},{9,8},{10,9},{11,1... | collective-permute-start | bytes 196616 | tf_op jit(solution)/shard_map/ppermute | solution.py:19
  159.7 6.5 %collective-permute-done.5 = bf16[1,1,128,256]{3,2,1,0:T(8,128)(2,1)S(1)} collective-permute-done((bf16[1,1,128,256]{3,2,1,0:T(8,128)(2,1)S(1)}, bf16[1,1,128,256]{3,2,1,0:T(8,128)(2,1)S(1)}, u32[]{:S(2)}, u32[]{:S(2)}) %collective-permute-start.5) | collective-permute-done | bytes 65568 | tf_op jit(solution)/shard_map/ppermute | solution.py:19
  166.2 7.0 %collective-permute-start.6 = (bf16[1,6,128,256]{3,2,1,0:T(8,128)(2,1)S(1)}, bf16[1,6,128,256]{3,2,1,0:T(8,128)(2,1)S(1)}, u32[]{:S(2)}, u32[]{:S(2)}) collective-permute-start(bf16[1,6,128,256]{3,2,1,0:T(8,128)(2,1)S(1)} %pad_maximum_fusion.2), channel_id=1, source_target_pairs={{0,16},{16,32},{32,48},{48,64},{64,80},{80,96},{96,112},{112,128},... | collective-permute-start | bytes 1179656 | tf_op jit(solution)/shard_map/ppermute | solution.py:18
  173.2 1.9 %collective-permute-start.7 = (bf16[1,6,128,256]{3,2,1,0:T(8,128)(2,1)S(1)}, bf16[1,6,128,256]{3,2,1,0:T(8,128)(2,1)S(1)}, u32[]{:S(2)}, u32[]{:S(2)}) collective-permute-start(bf16[1,6,128,256]{3,2,1,0:T(8,128)(2,1)S(1)} %pad_maximum_fusion.2), channel_id=1, source_target_pairs={{16,0},{32,16},{48,32},{64,48},{80,64},{96,80},{112,96},{128,112},... | collective-permute-start | bytes 1179656 | tf_op jit(solution)/shard_map/ppermute | solution.py:19
  176.7 1.3 collective-permute-done.6
  177.9 6.5 %collective-permute-done.7 = bf16[1,6,128,256]{3,2,1,0:T(8,128)(2,1)S(1)} collective-permute-done((bf16[1,6,128,256]{3,2,1,0:T(8,128)(2,1)S(1)}, bf16[1,6,128,256]{3,2,1,0:T(8,128)(2,1)S(1)}, u32[]{:S(2)}, u32[]{:S(2)}) %collective-permute-start.7) | collective-permute-done | bytes 393248 | tf_op jit(solution)/shard_map/ppermute | solution.py:19
  185.8 4.7 %shard_map.95 = bf16[512,256]{1,0:T(8,128)(2,1)} custom-call(bf16[1,3,3,6,128,256]{5,4,3,2,1,0:T(8,128)(2,1)S(1)} %maximum_bitcast_fusion.1.shifted_ref, bf16[27,256,256]{2,1,0:T(8,128)(2,1)} %taps_ref.3), custom_call_target="tpu_custom_call" | custom-call | flops 1811939328 | bytes 7340032 | tf_op jit(solution)/shard_map/pallas_call | solution.py:86
  (35 shorter events, 10.0 us)
Async XLA Ops:
  1.5 8.1 %collective-permute-start = (bf16[1,1,128,256]{3,2,1,0:T(8,128)(2,1)S(1)}, bf16[1,1,128,256]{3,2,1,0:T(8,128)(2,1)S(1)}, u32[]{:S(2)}, u32[]{:S(2)}) collective-permute-start(bf16[1,1,128,256]{3,2,1,0:T(8,128)(2,1)S(1)} %get-tuple-element.21), channel_id=1, source_target_pairs={{0,1},{1,2},{2,3},{3,4},{4,5},{5,6},{6,7},{7,8},{8,9},{9,10},{10,1... | collective-permute-start | bytes 196616 | tf_op jit(solution)/shard_map/ppermute | solution.py:18
  7.5 9.8 %collective-permute-start.1 = (bf16[1,1,128,256]{3,2,1,0:T(8,128)(2,1)S(1)}, bf16[1,1,128,256]{3,2,1,0:T(8,128)(2,1)S(1)}, u32[]{:S(2)}, u32[]{:S(2)}) collective-permute-start(bf16[1,1,128,256]{3,2,1,0:T(8,128)(2,1)S(1)} %get-tuple-element.20), channel_id=1, source_target_pairs={{1,0},{2,1},{3,2},{4,3},{5,4},{6,5},{7,6},{8,7},{9,8},{10,9},{11,1... | collective-permute-start | bytes 196616 | tf_op jit(solution)/shard_map/ppermute | solution.py:19
  17.4 8.5 %collective-permute-start.2 = (bf16[1,6,128,256]{3,2,1,0:T(8,128)(2,1)S(1)}, bf16[1,6,128,256]{3,2,1,0:T(8,128)(2,1)S(1)}, u32[]{:S(2)}, u32[]{:S(2)}) collective-permute-start(bf16[1,6,128,256]{3,2,1,0:T(8,128)(2,1)S(1)} %constant_dynamic-update-slice_fusion), channel_id=1, source_target_pairs={{0,16},{16,32},{32,48},{48,64},{64,80},{80,96},{96,112},{112,128},... | collective-permute-start | bytes 1179656 | tf_op jit(solution)/shard_map/ppermute | solution.py:18
  21.2 11.2 %collective-permute-start.3 = (bf16[1,6,128,256]{3,2,1,0:T(8,128)(2,1)S(1)}, bf16[1,6,128,256]{3,2,1,0:T(8,128)(2,1)S(1)}, u32[]{:S(2)}, u32[]{:S(2)}) collective-permute-start(bf16[1,6,128,256]{3,2,1,0:T(8,128)(2,1)S(1)} %constant_dynamic-update-slice_fusion), channel_id=1, source_target_pairs={{16,0},{32,16},{48,32},{64,48},{80,64},{96,80},{112,96},{128,112},... | collective-permute-start | bytes 1179656 | tf_op jit(solution)/shard_map/ppermute | solution.py:19
  33.7 4.1 %copy-start.2 = (bf16[1,4,128,512]{3,2,1,0:T(8,128)(2,1)S(1)}, bf16[1,4,128,512]{3,2,1,0:T(8,128)(2,1)}, u32[]{:S(2)}) copy-start(bf16[1,4,128,512]{3,2,1,0:T(8,128)(2,1)} %param.6) | copy-start | bytes 1572868
  40.0 38.6 %all-to-all-start = ((bf16[16,64,768]{2,1,0:T(8,128)(2,1)}), bf16[16,64,768]{2,1,0:T(8,128)(2,1)S(1)}, u32[]{:S(2)}, u32[]{:S(2)}) async-start(bf16[16,64,768]{2,1,0:T(8,128)(2,1)} %bitcast.6), calls=%async_computation | async-start | bytes 3145728 | tf_op jit(solution)/shard_map/all_to_all | solution.py:214
  78.6 1.2 copy-start.1
  98.8 8.2 %collective-permute-start.8 = (bf16[2,2,2,768,128]{4,3,2,1,0:T(8,128)(2,1)S(1)}, bf16[2,2,2,768,128]{4,3,2,1,0:T(8,128)(2,1)}, u32[]{:S(2)}, u32[]{:S(2)}) collective-permute-start(bf16[2,2,2,768,128]{4,3,2,1,0:T(8,128)(2,1)S(1)} %dynamic-slice_bitcast_fusion), channel_id=1, source_target_pairs={{0,16},{16,0},{32,48},{48,32},{64,80},{80,64},{96,112},{112,96},{1... | collective-permute-start | bytes 4718600 | tf_op jit(solution)/shard_map/ppermute | solution.py:44
  99.5 49.5 %all-to-all-start.1 = ((bf16[16,64,768]{2,1,0:T(8,128)(2,1)}), bf16[16,64,768]{2,1,0:T(8,128)(2,1)}, u32[]{:S(2)}, u32[]{:S(2)}) async-start(bf16[16,64,768]{2,1,0:T(8,128)(2,1)} %bitcast.10), calls=%async_computation.1 | async-start | bytes 3145728 | tf_op jit(solution)/shard_map/all_to_all | solution.py:218
  110.2 23.7 %collective-permute-start.9 = (bf16[2,2,768,128]{3,2,1,0:T(8,128)(2,1)}, bf16[2,2,768,128]{3,2,1,0:T(8,128)(2,1)}, u32[]{:S(2)}, u32[]{:S(2)}) collective-permute-start(bf16[2,2,768,128]{3,2,1,0:T(8,128)(2,1)} %fusion.7), channel_id=1, source_target_pairs={{0,32},{16,48},{32,0},{48,16},{64,96},{80,112},{96,64},{112,80},{1... | collective-permute-start | bytes 2359304 | tf_op jit(solution)/shard_map/ppermute | solution.py:44
  135.1 1.2 copy-start
  136.3 11.3 %collective-permute-start.10 = (bf16[2,768,128]{2,1,0:T(8,128)(2,1)S(1)}, bf16[2,768,128]{2,1,0:T(8,128)(2,1)S(1)}, u32[]{:S(2)}, u32[]{:S(2)}) collective-permute-start(bf16[2,768,128]{2,1,0:T(8,128)(2,1)S(1)} %fusion.11), channel_id=1, source_target_pairs={{0,64},{16,80},{32,96},{48,112},{64,0},{80,16},{96,32},{112,48},{1... | collective-permute-start | bytes 1179656 | tf_op jit(solution)/shard_map/ppermute | solution.py:44
  148.8 9.9 %collective-permute-start.11 = (bf16[768,128]{1,0:T(8,128)(2,1)S(1)}, bf16[768,128]{1,0:T(8,128)(2,1)S(1)}, u32[]{:S(2)}, u32[]{:S(2)}) collective-permute-start(bf16[768,128]{1,0:T(8,128)(2,1)S(1)} %fusion.12), channel_id=1, source_target_pairs={{0,128},{16,144},{32,160},{48,176},{64,192},{80,208},{96,224},{112... | collective-permute-start | bytes 589832 | tf_op jit(solution)/shard_map/ppermute | solution.py:44
  151.6 8.0 %collective-permute-start.4 = (bf16[1,1,128,256]{3,2,1,0:T(8,128)(2,1)S(1)}, bf16[1,1,128,256]{3,2,1,0:T(8,128)(2,1)S(1)}, u32[]{:S(2)}, u32[]{:S(2)}) collective-permute-start(bf16[1,1,128,256]{3,2,1,0:T(8,128)(2,1)S(1)} %get-tuple-element.18), channel_id=1, source_target_pairs={{0,1},{1,2},{2,3},{3,4},{4,5},{5,6},{6,7},{7,8},{8,9},{9,10},{10,1... | collective-permute-start | bytes 196616 | tf_op jit(solution)/shard_map/ppermute | solution.py:18
  156.8 9.3 %collective-permute-start.5 = (bf16[1,1,128,256]{3,2,1,0:T(8,128)(2,1)S(1)}, bf16[1,1,128,256]{3,2,1,0:T(8,128)(2,1)S(1)}, u32[]{:S(2)}, u32[]{:S(2)}) collective-permute-start(bf16[1,1,128,256]{3,2,1,0:T(8,128)(2,1)S(1)} %get-tuple-element.19), channel_id=1, source_target_pairs={{1,0},{2,1},{3,2},{4,3},{5,4},{6,5},{7,6},{8,7},{9,8},{10,9},{11,1... | collective-permute-start | bytes 196616 | tf_op jit(solution)/shard_map/ppermute | solution.py:19
  166.2 11.7 %collective-permute-start.6 = (bf16[1,6,128,256]{3,2,1,0:T(8,128)(2,1)S(1)}, bf16[1,6,128,256]{3,2,1,0:T(8,128)(2,1)S(1)}, u32[]{:S(2)}, u32[]{:S(2)}) collective-permute-start(bf16[1,6,128,256]{3,2,1,0:T(8,128)(2,1)S(1)} %pad_maximum_fusion.2), channel_id=1, source_target_pairs={{0,16},{16,32},{32,48},{48,64},{64,80},{80,96},{96,112},{112,128},... | collective-permute-start | bytes 1179656 | tf_op jit(solution)/shard_map/ppermute | solution.py:18
  173.2 11.2 %collective-permute-start.7 = (bf16[1,6,128,256]{3,2,1,0:T(8,128)(2,1)S(1)}, bf16[1,6,128,256]{3,2,1,0:T(8,128)(2,1)S(1)}, u32[]{:S(2)}, u32[]{:S(2)}) collective-permute-start(bf16[1,6,128,256]{3,2,1,0:T(8,128)(2,1)S(1)} %pad_maximum_fusion.2), channel_id=1, source_target_pairs={{16,0},{32,16},{48,32},{64,48},{80,64},{96,80},{112,96},{128,112},... | collective-permute-start | bytes 1179656 | tf_op jit(solution)/shard_map/ppermute | solution.py:19

commit v15 on v14

--- a/solution.py
+++ b/solution.py
@@ -218,15 +218,16 @@
     returned = lax.all_to_all(
         back.reshape(experts, capacity, both), "expert", split_axis=0, concat_axis=0, tiled=True
     )
-    mixed = lax.dot_general(
-        route,
-        returned.reshape(slots, both),
-        (((0,), (0,)), ((), ())),
-        preferred_element_type=jnp.float32,
+    returned = returned.reshape(slots, both)
+    mixed_out = lax.dot_general(
+        route, returned[:, :channels], (((0,), (0,)), ((), ())), preferred_element_type=jnp.float32
     ).astype(jnp.bfloat16)
-    patch_grid = mixed[:, :channels].reshape(1, rows_y, depth_cells, channels)
+    patch_grid = mixed_out.reshape(1, rows_y, depth_cells, channels)
     imitated = conv_block(patch_grid, kernel, False).reshape(1, rows_y, depth_cells, channels)
-    feat_grad = mixed[:, channels:].reshape(1, rows_y, depth_cells, feat_width)
+    feat_grad = lax.dot_general(
+        route, returned[:, channels:], (((0,), (0,)), ((), ())), preferred_element_type=jnp.float32
+    ).astype(jnp.bfloat16)
+    feat_grad = feat_grad.reshape(1, rows_y, depth_cells, feat_width)
 
     grads = tree_scatter(part, (0, 1, 2, 3))
     grad_one = grads[:feat_width]

time: 191 us -> 190 us (level)
  matrix products: 5.85 us -> 7.81 us
    dot_general x1 -> x2, matrix products: 2.63 us -> 4.59 us  [the longest x1 2.78 us: per_device(): lax.dot_general(route, returned[:, channels:], (((0,), (0,)), ((), ())),...]
  transfers between devices with their start and end apart: 14 -> 14, of which waited for: 10 -> 9; matrix products, arithmetic and copies ran while one was open for 7% -> 8% of each run, Pallas kernels for 0% -> 0%
where the time goes in v15:
time: 190 us
  waiting for transfers between devices  87.7 us (46%)
  starting transfers between devices  50.7 us (27%)
  Pallas kernels  26.3 us (14%)
  local copies, waits for them, and re-layouts  9.54 us (5%)
  matrix products  7.81 us (4%)
  other arithmetic  6.77 us (4%)
    all_to_all x1, waiting for transfers between devices, per_device(): lax.all_to_all(outbound.reshape(experts, capacity, both), 'expert', split...  32.9 us
    ppermute x4, waiting for transfers between devices, tree_scatter(): got = lax.ppermute(send.astype(jnp.bfloat16), 'dp', pairs)  28.4 us
    ppermute x4, waiting for transfers between devices, extended(): after = lax.ppermute(first, axis, down)  25.6 us
    ppermute x4, starting transfers between devices, extended(): before = lax.ppermute(last, axis, up)  22.1 us
    pallas_call x1, Pallas kernels, expert(): pl.pallas_call(functools.partial(expert_kernel, cols), grid=(hidden // ch...  17.5 us
    pallas_call x2, Pallas kernels, conv_block(): pl.pallas_call(functools.partial(conv_kernel, flip), out_shape=jax.ShapeD...  8.77 us
    ppermute x4, starting transfers between devices, extended(): after = lax.ppermute(first, axis, down)  8.05 us
    all_to_all x1, starting transfers between devices, per_device(): lax.all_to_all(back.reshape(experts, capacity, both), 'expert', split_axi...  7.47 us
  transfers between devices with their start and end apart: 14, of which 9 were waited for; matrix products, arithmetic and copies ran while one was open for 8% of the time, Pallas kernels for 0%

profile of v15, /device:TPU:95, one launch (start us, length us, event | category | flops | bytes accessed | tf_op | source)
XLA Modules:
  0.0 189.7 jit_solution(8456246003325145846)
XLA Ops:
  1.5 6.0 %collective-permute-start = (bf16[1,1,128,256]{3,2,1,0:T(8,128)(2,1)S(1)}, bf16[1,1,128,256]{3,2,1,0:T(8,128)(2,1)S(1)}, u32[]{:S(2)}, u32[]{:S(2)}) collective-permute-start(bf16[1,1,128,256]{3,2,1,0:T(8,128)(2,1)S(1)} %get-tuple-element.21), channel_id=1, source_target_pairs={{0,1},{1,2},{2,3},{3,4},{4,5},{5,6},{6,7},{7,8},{8,9},{9,10},{10,1... | collective-permute-start | bytes 196616 | tf_op jit(solution)/shard_map/ppermute | solution.py:18
  7.5 1.9 %collective-permute-start.1 = (bf16[1,1,128,256]{3,2,1,0:T(8,128)(2,1)S(1)}, bf16[1,1,128,256]{3,2,1,0:T(8,128)(2,1)S(1)}, u32[]{:S(2)}, u32[]{:S(2)}) collective-permute-start(bf16[1,1,128,256]{3,2,1,0:T(8,128)(2,1)S(1)} %get-tuple-element.20), channel_id=1, source_target_pairs={{1,0},{2,1},{3,2},{4,3},{5,4},{6,5},{7,6},{8,7},{9,8},{10,9},{11,1... | collective-permute-start | bytes 196616 | tf_op jit(solution)/shard_map/ppermute | solution.py:19
  10.6 6.7 %collective-permute-done.1 = bf16[1,1,128,256]{3,2,1,0:T(8,128)(2,1)S(1)} collective-permute-done((bf16[1,1,128,256]{3,2,1,0:T(8,128)(2,1)S(1)}, bf16[1,1,128,256]{3,2,1,0:T(8,128)(2,1)S(1)}, u32[]{:S(2)}, u32[]{:S(2)}) %collective-permute-start.1) | collective-permute-done | bytes 65568 | tf_op jit(solution)/shard_map/ppermute | solution.py:19
  17.4 3.8 %collective-permute-start.2 = (bf16[1,6,128,256]{3,2,1,0:T(8,128)(2,1)S(1)}, bf16[1,6,128,256]{3,2,1,0:T(8,128)(2,1)S(1)}, u32[]{:S(2)}, u32[]{:S(2)}) collective-permute-start(bf16[1,6,128,256]{3,2,1,0:T(8,128)(2,1)S(1)} %constant_dynamic-update-slice_fusion), channel_id=1, source_target_pairs={{0,16},{16,32},{32,48},{48,64},{64,80},{80,96},{96,112},{112,128},... | collective-permute-start | bytes 1179656 | tf_op jit(solution)/shard_map/ppermute | solution.py:18
  21.2 2.3 %collective-permute-start.3 = (bf16[1,6,128,256]{3,2,1,0:T(8,128)(2,1)S(1)}, bf16[1,6,128,256]{3,2,1,0:T(8,128)(2,1)S(1)}, u32[]{:S(2)}, u32[]{:S(2)}) collective-permute-start(bf16[1,6,128,256]{3,2,1,0:T(8,128)(2,1)S(1)} %constant_dynamic-update-slice_fusion), channel_id=1, source_target_pairs={{16,0},{32,16},{48,32},{64,48},{80,64},{96,80},{112,96},{128,112},... | collective-permute-start | bytes 1179656 | tf_op jit(solution)/shard_map/ppermute | solution.py:19
  23.5 1.0 fusion.6
  25.9 6.5 %collective-permute-done.3 = bf16[1,6,128,256]{3,2,1,0:T(8,128)(2,1)S(1)} collective-permute-done((bf16[1,6,128,256]{3,2,1,0:T(8,128)(2,1)S(1)}, bf16[1,6,128,256]{3,2,1,0:T(8,128)(2,1)S(1)}, u32[]{:S(2)}, u32[]{:S(2)}) %collective-permute-start.3) | collective-permute-done | bytes 393248 | tf_op jit(solution)/shard_map/ppermute | solution.py:19
  33.7 4.1 %shard_map.93 = bf16[512,256]{1,0:T(8,128)(2,1)S(1)} custom-call(bf16[1,3,3,6,128,256]{5,4,3,2,1,0:T(8,128)(2,1)S(1)} %maximum_bitcast_fusion.shifted_ref, bf16[27,256,256]{2,1,0:T(8,128)(2,1)} %taps_ref.3), custom_call_target="tpu_custom_call" | custom-call | flops 1811939328 | bytes 7340032 | tf_op jit(solution)/shard_map/pallas_call | solution.py:86
  37.8 2.2 %fusion.3 = bf16[1024,768]{1,0:T(8,128)(2,1)} fusion(s32[512]{0:T(512)S(1)} %add_add_fusion, bf16[512,256]{1,0:T(8,128)(2,1)S(1)} %shard_map.93, bf16[512,512]{1,0:T(8,128)(2,1)S(1)} %bitcast.63), kind=kOutput, calls=%fused_computation.7 | convolution fusion | flops 808189952 | bytes 2361344 | tf_op jit(solution)/shard_map/dot_general | solution.py:212
  40.0 5.8 %all-to-all-start = ((bf16[16,64,768]{2,1,0:T(8,128)(2,1)}), bf16[16,64,768]{2,1,0:T(8,128)(2,1)S(1)}, u32[]{:S(2)}, u32[]{:S(2)}) async-start(bf16[16,64,768]{2,1,0:T(8,128)(2,1)} %bitcast.6), calls=%async_computation | async-start | bytes 3145728 | tf_op jit(solution)/shard_map/all_to_all | solution.py:214
  45.7 32.9 %all-to-all-done = bf16[16,64,768]{2,1,0:T(8,128)(2,1)S(1)} async-done(((bf16[16,64,768]{2,1,0:T(8,128)(2,1)}), bf16[16,64,768]{2,1,0:T(8,128)(2,1)S(1)}, u32[]{:S(2)}, u32[]{:S(2)}) %all-to-all-start) | async-done | bytes 1572896 | tf_op jit(solution)/shard_map/all_to_all | solution.py:214
  78.6 1.2 copy-done.1
  79.8 17.5 %shard_map.94 = (bf16[1024,768]{1,0:T(8,128)(2,1)}, bf16[16,768,128]{2,1,0:T(8,128)(2,1)}) custom-call(bf16[1024,768]{1,0:T(8,128)(2,1)} %bitcast.57, bf16[512,2048]{1,0:T(8,128)(2,1)} %bitcast.61, bf16[2048,256]{1,0:T(8,128)(2,1)} %bitcast.62), custom_call_target="tpu_custom_call" | custom-call | flops 9663676416 | bytes 9437184 | tf_op jit(solution)/shard_map/pallas_call | solution.py:154
  97.3 1.5 dynamic-slice_bitcast_fusion
  99.5 7.5 %all-to-all-start.1 = ((bf16[16,64,768]{2,1,0:T(8,128)(2,1)}), bf16[16,64,768]{2,1,0:T(8,128)(2,1)}, u32[]{:S(2)}, u32[]{:S(2)}) async-start(bf16[16,64,768]{2,1,0:T(8,128)(2,1)} %bitcast.10), calls=%async_computation.1 | async-start | bytes 3145728 | tf_op jit(solution)/shard_map/all_to_all | solution.py:218
  107.0 2.2 %convert_add_fusion = f32[2,2,2,768,128]{4,3,2,1,0:T(8,128)S(1)} fusion(bf16[2,2,2,768,128]{4,3,2,1,0:T(8,128)(2,1)} %collective-permute-done.8, bf16[2,2,2,2,768,128]{5,4,3,2,1,0:T(8,128)(2,1)} %bitcast.56, s32[]{:T(128)S(6)} %select_n.28), kind=kLoop, calls=%fused_computation.2 | loop fusion | flops 2359296 | bytes 6291460 | tf_op jit(solution)/shard_map/add | solution.py:45
  109.2 1.0 fusion.11
  110.2 5.8 %collective-permute-start.9 = (bf16[2,2,768,128]{3,2,1,0:T(8,128)(2,1)}, bf16[2,2,768,128]{3,2,1,0:T(8,128)(2,1)}, u32[]{:S(2)}, u32[]{:S(2)}) collective-permute-start(bf16[2,2,768,128]{3,2,1,0:T(8,128)(2,1)} %fusion.11), channel_id=1, source_target_pairs={{0,32},{16,48},{32,0},{48,16},{64,96},{80,112},{96,64},{112,80},{1... | collective-permute-start | bytes 2359304 | tf_op jit(solution)/shard_map/ppermute | solution.py:44
  116.0 17.9 %collective-permute-done.9 = bf16[2,2,768,128]{3,2,1,0:T(8,128)(2,1)} collective-permute-done((bf16[2,2,768,128]{3,2,1,0:T(8,128)(2,1)}, bf16[2,2,768,128]{3,2,1,0:T(8,128)(2,1)}, u32[]{:S(2)}, u32[]{:S(2)}) %collective-permute-start.9) | collective-permute-done | bytes 786464 | tf_op jit(solution)/shard_map/ppermute | solution.py:44
  133.9 1.3 bitcast_add_fusion
  135.1 1.2 copy-done
  137.1 10.5 %collective-permute-done.10 = bf16[2,768,128]{2,1,0:T(8,128)(2,1)S(1)} collective-permute-done((bf16[2,768,128]{2,1,0:T(8,128)(2,1)S(1)}, bf16[2,768,128]{2,1,0:T(8,128)(2,1)S(1)}, u32[]{:S(2)}, u32[]{:S(2)}) %collective-permute-start.10) | collective-permute-done | bytes 393248 | tf_op jit(solution)/shard_map/ppermute | solution.py:44
  147.6 1.2 bitcast_add_fusion.1
  149.0 1.8 fusion.5
  150.8 5.2 %collective-permute-start.4 = (bf16[1,1,128,256]{3,2,1,0:T(8,128)(2,1)S(1)}, bf16[1,1,128,256]{3,2,1,0:T(8,128)(2,1)S(1)}, u32[]{:S(2)}, u32[]{:S(2)}) collective-permute-start(bf16[1,1,128,256]{3,2,1,0:T(8,128)(2,1)S(1)} %get-tuple-element.18), channel_id=1, source_target_pairs={{0,1},{1,2},{2,3},{3,4},{4,5},{5,6},{6,7},{7,8},{8,9},{9,10},{10,1... | collective-permute-start | bytes 196616 | tf_op jit(solution)/shard_map/ppermute | solution.py:18
  156.0 1.9 %collective-permute-start.5 = (bf16[1,1,128,256]{3,2,1,0:T(8,128)(2,1)S(1)}, bf16[1,1,128,256]{3,2,1,0:T(8,128)(2,1)S(1)}, u32[]{:S(2)}, u32[]{:S(2)}) collective-permute-start(bf16[1,1,128,256]{3,2,1,0:T(8,128)(2,1)S(1)} %get-tuple-element.19), channel_id=1, source_target_pairs={{1,0},{2,1},{3,2},{4,3},{5,4},{6,5},{7,6},{8,7},{9,8},{10,9},{11,1... | collective-permute-start | bytes 196616 | tf_op jit(solution)/shard_map/ppermute | solution.py:19
  158.8 6.6 %collective-permute-done.5 = bf16[1,1,128,256]{3,2,1,0:T(8,128)(2,1)S(1)} collective-permute-done((bf16[1,1,128,256]{3,2,1,0:T(8,128)(2,1)S(1)}, bf16[1,1,128,256]{3,2,1,0:T(8,128)(2,1)S(1)}, u32[]{:S(2)}, u32[]{:S(2)}) %collective-permute-start.5) | collective-permute-done | bytes 65568 | tf_op jit(solution)/shard_map/ppermute | solution.py:19
  165.4 7.0 %collective-permute-start.6 = (bf16[1,6,128,256]{3,2,1,0:T(8,128)(2,1)S(1)}, bf16[1,6,128,256]{3,2,1,0:T(8,128)(2,1)S(1)}, u32[]{:S(2)}, u32[]{:S(2)}) collective-permute-start(bf16[1,6,128,256]{3,2,1,0:T(8,128)(2,1)S(1)} %pad_maximum_fusion.2), channel_id=1, source_target_pairs={{0,16},{16,32},{32,48},{48,64},{64,80},{80,96},{96,112},{112,128},... | collective-permute-start | bytes 1179656 | tf_op jit(solution)/shard_map/ppermute | solution.py:18
  172.4 1.9 %collective-permute-start.7 = (bf16[1,6,128,256]{3,2,1,0:T(8,128)(2,1)S(1)}, bf16[1,6,128,256]{3,2,1,0:T(8,128)(2,1)S(1)}, u32[]{:S(2)}, u32[]{:S(2)}) collective-permute-start(bf16[1,6,128,256]{3,2,1,0:T(8,128)(2,1)S(1)} %pad_maximum_fusion.2), channel_id=1, source_target_pairs={{16,0},{32,16},{48,32},{64,48},{80,64},{96,80},{112,96},{128,112},... | collective-permute-start | bytes 1179656 | tf_op jit(solution)/shard_map/ppermute | solution.py:19
  175.1 2.8 %fusion.4 = bf16[512,512]{1,0:T(8,128)(2,1)} fusion(bf16[1024,768]{1,0:T(8,128)(2,1)} %bitcast.11, s32[512]{0:T(512)S(1)} %add_add_fusion), kind=kOutput, calls=%fused_computation.11 | convolution fusion | flops 537657344 | bytes 1574912 | tf_op jit(solution)/shard_map/dot_general | solution.py:227
  177.8 5.8 %collective-permute-done.7 = bf16[1,6,128,256]{3,2,1,0:T(8,128)(2,1)S(1)} collective-permute-done((bf16[1,6,128,256]{3,2,1,0:T(8,128)(2,1)S(1)}, bf16[1,6,128,256]{3,2,1,0:T(8,128)(2,1)S(1)}, u32[]{:S(2)}, u32[]{:S(2)}) %collective-permute-start.7) | collective-permute-done | bytes 393248 | tf_op jit(solution)/shard_map/ppermute | solution.py:19
  185.0 4.7 %shard_map.95 = bf16[512,256]{1,0:T(8,128)(2,1)} custom-call(bf16[1,3,3,6,128,256]{5,4,3,2,1,0:T(8,128)(2,1)S(1)} %maximum_bitcast_fusion.1.shifted_ref, bf16[27,256,256]{2,1,0:T(8,128)(2,1)} %taps_ref.3), custom_call_target="tpu_custom_call" | custom-call | flops 1811939328 | bytes 7340032 | tf_op jit(solution)/shard_map/pallas_call | solution.py:86
  (34 shorter events, 9.2 us)
Async XLA Ops:
  1.5 8.1 %collective-permute-start = (bf16[1,1,128,256]{3,2,1,0:T(8,128)(2,1)S(1)}, bf16[1,1,128,256]{3,2,1,0:T(8,128)(2,1)S(1)}, u32[]{:S(2)}, u32[]{:S(2)}) collective-permute-start(bf16[1,1,128,256]{3,2,1,0:T(8,128)(2,1)S(1)} %get-tuple-element.21), channel_id=1, source_target_pairs={{0,1},{1,2},{2,3},{3,4},{4,5},{5,6},{6,7},{7,8},{8,9},{9,10},{10,1... | collective-permute-start | bytes 196616 | tf_op jit(solution)/shard_map/ppermute | solution.py:18
  7.5 9.8 %collective-permute-start.1 = (bf16[1,1,128,256]{3,2,1,0:T(8,128)(2,1)S(1)}, bf16[1,1,128,256]{3,2,1,0:T(8,128)(2,1)S(1)}, u32[]{:S(2)}, u32[]{:S(2)}) collective-permute-start(bf16[1,1,128,256]{3,2,1,0:T(8,128)(2,1)S(1)} %get-tuple-element.20), channel_id=1, source_target_pairs={{1,0},{2,1},{3,2},{4,3},{5,4},{6,5},{7,6},{8,7},{9,8},{10,9},{11,1... | collective-permute-start | bytes 196616 | tf_op jit(solution)/shard_map/ppermute | solution.py:19
  17.4 8.5 %collective-permute-start.2 = (bf16[1,6,128,256]{3,2,1,0:T(8,128)(2,1)S(1)}, bf16[1,6,128,256]{3,2,1,0:T(8,128)(2,1)S(1)}, u32[]{:S(2)}, u32[]{:S(2)}) collective-permute-start(bf16[1,6,128,256]{3,2,1,0:T(8,128)(2,1)S(1)} %constant_dynamic-update-slice_fusion), channel_id=1, source_target_pairs={{0,16},{16,32},{32,48},{48,64},{64,80},{80,96},{96,112},{112,128},... | collective-permute-start | bytes 1179656 | tf_op jit(solution)/shard_map/ppermute | solution.py:18
  21.2 11.2 %collective-permute-start.3 = (bf16[1,6,128,256]{3,2,1,0:T(8,128)(2,1)S(1)}, bf16[1,6,128,256]{3,2,1,0:T(8,128)(2,1)S(1)}, u32[]{:S(2)}, u32[]{:S(2)}) collective-permute-start(bf16[1,6,128,256]{3,2,1,0:T(8,128)(2,1)S(1)} %constant_dynamic-update-slice_fusion), channel_id=1, source_target_pairs={{16,0},{32,16},{48,32},{64,48},{80,64},{96,80},{112,96},{128,112},... | collective-permute-start | bytes 1179656 | tf_op jit(solution)/shard_map/ppermute | solution.py:19
  33.7 4.1 %copy-start.2 = (bf16[1,4,128,512]{3,2,1,0:T(8,128)(2,1)S(1)}, bf16[1,4,128,512]{3,2,1,0:T(8,128)(2,1)}, u32[]{:S(2)}) copy-start(bf16[1,4,128,512]{3,2,1,0:T(8,128)(2,1)} %param.6) | copy-start | bytes 1572868
  40.0 38.6 %all-to-all-start = ((bf16[16,64,768]{2,1,0:T(8,128)(2,1)}), bf16[16,64,768]{2,1,0:T(8,128)(2,1)S(1)}, u32[]{:S(2)}, u32[]{:S(2)}) async-start(bf16[16,64,768]{2,1,0:T(8,128)(2,1)} %bitcast.6), calls=%async_computation | async-start | bytes 3145728 | tf_op jit(solution)/shard_map/all_to_all | solution.py:214
  78.6 1.2 copy-start.1
  98.8 8.2 %collective-permute-start.8 = (bf16[2,2,2,768,128]{4,3,2,1,0:T(8,128)(2,1)S(1)}, bf16[2,2,2,768,128]{4,3,2,1,0:T(8,128)(2,1)}, u32[]{:S(2)}, u32[]{:S(2)}) collective-permute-start(bf16[2,2,2,768,128]{4,3,2,1,0:T(8,128)(2,1)S(1)} %dynamic-slice_bitcast_fusion), channel_id=1, source_target_pairs={{0,16},{16,0},{32,48},{48,32},{64,80},{80,64},{96,112},{112,96},{1... | collective-permute-start | bytes 4718600 | tf_op jit(solution)/shard_map/ppermute | solution.py:44
  99.5 49.5 %all-to-all-start.1 = ((bf16[16,64,768]{2,1,0:T(8,128)(2,1)}), bf16[16,64,768]{2,1,0:T(8,128)(2,1)}, u32[]{:S(2)}, u32[]{:S(2)}) async-start(bf16[16,64,768]{2,1,0:T(8,128)(2,1)} %bitcast.10), calls=%async_computation.1 | async-start | bytes 3145728 | tf_op jit(solution)/shard_map/all_to_all | solution.py:218
  110.2 23.7 %collective-permute-start.9 = (bf16[2,2,768,128]{3,2,1,0:T(8,128)(2,1)}, bf16[2,2,768,128]{3,2,1,0:T(8,128)(2,1)}, u32[]{:S(2)}, u32[]{:S(2)}) collective-permute-start(bf16[2,2,768,128]{3,2,1,0:T(8,128)(2,1)} %fusion.11), channel_id=1, source_target_pairs={{0,32},{16,48},{32,0},{48,16},{64,96},{80,112},{96,64},{112,80},{1... | collective-permute-start | bytes 2359304 | tf_op jit(solution)/shard_map/ppermute | solution.py:44
  135.1 1.2 copy-start
  136.3 11.3 %collective-permute-start.10 = (bf16[2,768,128]{2,1,0:T(8,128)(2,1)S(1)}, bf16[2,768,128]{2,1,0:T(8,128)(2,1)S(1)}, u32[]{:S(2)}, u32[]{:S(2)}) collective-permute-start(bf16[2,768,128]{2,1,0:T(8,128)(2,1)S(1)} %fusion.16), channel_id=1, source_target_pairs={{0,64},{16,80},{32,96},{48,112},{64,0},{80,16},{96,32},{112,48},{1... | collective-permute-start | bytes 1179656 | tf_op jit(solution)/shard_map/ppermute | solution.py:44
  148.8 9.1 %collective-permute-start.11 = (bf16[768,128]{1,0:T(8,128)(2,1)S(1)}, bf16[768,128]{1,0:T(8,128)(2,1)S(1)}, u32[]{:S(2)}, u32[]{:S(2)}) collective-permute-start(bf16[768,128]{1,0:T(8,128)(2,1)S(1)} %fusion.17), channel_id=1, source_target_pairs={{0,128},{16,144},{32,160},{48,176},{64,192},{80,208},{96,224},{112... | collective-permute-start | bytes 589832 | tf_op jit(solution)/shard_map/ppermute | solution.py:44
  150.8 8.0 %collective-permute-start.4 = (bf16[1,1,128,256]{3,2,1,0:T(8,128)(2,1)S(1)}, bf16[1,1,128,256]{3,2,1,0:T(8,128)(2,1)S(1)}, u32[]{:S(2)}, u32[]{:S(2)}) collective-permute-start(bf16[1,1,128,256]{3,2,1,0:T(8,128)(2,1)S(1)} %get-tuple-element.18), channel_id=1, source_target_pairs={{0,1},{1,2},{2,3},{3,4},{4,5},{5,6},{6,7},{7,8},{8,9},{9,10},{10,1... | collective-permute-start | bytes 196616 | tf_op jit(solution)/shard_map/ppermute | solution.py:18
  156.0 9.3 %collective-permute-start.5 = (bf16[1,1,128,256]{3,2,1,0:T(8,128)(2,1)S(1)}, bf16[1,1,128,256]{3,2,1,0:T(8,128)(2,1)S(1)}, u32[]{:S(2)}, u32[]{:S(2)}) collective-permute-start(bf16[1,1,128,256]{3,2,1,0:T(8,128)(2,1)S(1)} %get-tuple-element.19), channel_id=1, source_target_pairs={{1,0},{2,1},{3,2},{4,3},{5,4},{6,5},{7,6},{8,7},{9,8},{10,9},{11,1... | collective-permute-start | bytes 196616 | tf_op jit(solution)/shard_map/ppermute | solution.py:19
  165.4 12.4 %collective-permute-start.6 = (bf16[1,6,128,256]{3,2,1,0:T(8,128)(2,1)S(1)}, bf16[1,6,128,256]{3,2,1,0:T(8,128)(2,1)S(1)}, u32[]{:S(2)}, u32[]{:S(2)}) collective-permute-start(bf16[1,6,128,256]{3,2,1,0:T(8,128)(2,1)S(1)} %pad_maximum_fusion.2), channel_id=1, source_target_pairs={{0,16},{16,32},{32,48},{48,64},{64,80},{80,96},{96,112},{112,128},... | collective-permute-start | bytes 1179656 | tf_op jit(solution)/shard_map/ppermute | solution.py:18
  172.4 11.2 %collective-permute-start.7 = (bf16[1,6,128,256]{3,2,1,0:T(8,128)(2,1)S(1)}, bf16[1,6,128,256]{3,2,1,0:T(8,128)(2,1)S(1)}, u32[]{:S(2)}, u32[]{:S(2)}) collective-permute-start(bf16[1,6,128,256]{3,2,1,0:T(8,128)(2,1)S(1)} %pad_maximum_fusion.2), channel_id=1, source_target_pairs={{16,0},{32,16},{48,32},{64,48},{80,64},{96,80},{112,96},{128,112},... | collective-permute-start | bytes 1179656 | tf_op jit(solution)/shard_map/ppermute | solution.py:19

commit v16 on v15

--- a/solution.py
+++ b/solution.py
@@ -229,7 +229,7 @@
     ).astype(jnp.bfloat16)
     feat_grad = feat_grad.reshape(1, rows_y, depth_cells, feat_width)
 
-    grads = tree_scatter(part, (0, 1, 2, 3))
+    grads = tree_scatter(part, (0, 1, 3, 2))
     grad_one = grads[:feat_width]
     grad_two = grads[feat_width:].T
     return (imitated, feat_grad, grad_one[None], grad_two[None])

time: 190 us -> 199 us (1.047)
  local copies, waits for them, and re-layouts: 9.54 us -> 12.6 us
  waiting for transfers between devices: 87.7 us -> 90.6 us
  starting transfers between devices: 50.7 us -> 53.1 us
    ppermute x4, starting transfers between devices: 7.36 us -> 12.1 us  [tree_scatter(): got = lax.ppermute(send.astype(jnp.bfloat16), 'dp', pairs)]
    ppermute x4, starting transfers between devices: 22.1 us -> 18.3 us  [extended(): before = lax.ppermute(last, axis, up)]
    ppermute x4, waiting for transfers between devices: 28.4 us -> 32.1 us  [tree_scatter(): got = lax.ppermute(send.astype(jnp.bfloat16), 'dp', pairs)]
    dynamic_slice x0 -> x2, local copies, waits for them, and re-layouts: none -> 3.45 us  [the longest x1 3.35 us: tree_scatter(): lax.dynamic_index_in_dim(x, mine, axis=axis, keepdims=False)]
    unnamed x9 -> x11, local copies, waits for them, and re-layouts: 4.08 us -> 5.19 us
  transfers between devices with their start and end apart: 14 -> 14, of which waited for: 9 -> 9; matrix products, arithmetic and copies ran while one was open for 8% -> 7% of each run, Pallas kernels for 0% -> 0%
where the time goes in v16:
time: 199 us; the launch traced here: 198 us
  waiting for transfers between devices  90.6 us (46%)
  starting transfers between devices  53.1 us (27%)
  Pallas kernels  26.2 us (13%)
  local copies, waits for them, and re-layouts  12.6 us (6%)
  matrix products  7.8 us (4%)
  other arithmetic  6.76 us (3%)
    all_to_all x1, waiting for transfers between devices, per_device(): lax.all_to_all(outbound.reshape(experts, capacity, both), 'expert', split...  32.9 us
    ppermute x4, waiting for transfers between devices, tree_scatter(): got = lax.ppermute(send.astype(jnp.bfloat16), 'dp', pairs)  32.1 us
    ppermute x4, waiting for transfers between devices, extended(): after = lax.ppermute(first, axis, down)  24.7 us
    ppermute x4, starting transfers between devices, extended(): before = lax.ppermute(last, axis, up)  18.3 us
    pallas_call x1, Pallas kernels, expert(): pl.pallas_call(functools.partial(expert_kernel, cols), grid=(hidden // ch...  17.5 us
    ppermute x4, starting transfers between devices, tree_scatter(): got = lax.ppermute(send.astype(jnp.bfloat16), 'dp', pairs)  12.1 us
    ppermute x4, starting transfers between devices, extended(): after = lax.ppermute(first, axis, down)  9.49 us
    pallas_call x2, Pallas kernels, conv_block(): pl.pallas_call(functools.partial(conv_kernel, flip), out_shape=jax.ShapeD...  8.77 us
  transfers between devices with their start and end apart: 14, of which 9 were waited for; matrix products, arithmetic and copies ran while one was open for 7% of the time, Pallas kernels for 0%

profile of v16, /device:TPU:95, one launch (start us, length us, event | category | flops | bytes accessed | tf_op | source)
XLA Modules:
  0.0 198.0 jit_solution(1779931560791246125)
XLA Ops:
  1.5 6.0 %collective-permute-start = (bf16[1,1,128,256]{3,2,1,0:T(8,128)(2,1)S(1)}, bf16[1,1,128,256]{3,2,1,0:T(8,128)(2,1)S(1)}, u32[]{:S(2)}, u32[]{:S(2)}) collective-permute-start(bf16[1,1,128,256]{3,2,1,0:T(8,128)(2,1)S(1)} %get-tuple-element.23), channel_id=1, source_target_pairs={{0,1},{1,2},{2,3},{3,4},{4,5},{5,6},{6,7},{7,8},{8,9},{9,10},{10,1... | collective-permute-start | bytes 196616 | tf_op jit(solution)/shard_map/ppermute | solution.py:18
  7.5 1.9 collective-permute-start.1
  10.6 6.7 %collective-permute-done.1 = bf16[1,1,128,256]{3,2,1,0:T(8,128)(2,1)S(1)} collective-permute-done((bf16[1,1,128,256]{3,2,1,0:T(8,128)(2,1)S(1)}, bf16[1,1,128,256]{3,2,1,0:T(8,128)(2,1)S(1)}, u32[]{:S(2)}, u32[]{:S(2)}) %collective-permute-start.1) | collective-permute-done | bytes 65568 | tf_op jit(solution)/shard_map/ppermute | solution.py:19
  17.4 3.8 %collective-permute-start.2 = (bf16[1,6,128,256]{3,2,1,0:T(8,128)(2,1)S(1)}, bf16[1,6,128,256]{3,2,1,0:T(8,128)(2,1)S(1)}, u32[]{:S(2)}, u32[]{:S(2)}) collective-permute-start(bf16[1,6,128,256]{3,2,1,0:T(8,128)(2,1)S(1)} %constant_dynamic-update-slice_fusion), channel_id=1, source_target_pairs={{0,16},{16,32},{32,48},{48,64},{64,80},{80,96},{96,112},{112,128},... | collective-permute-start | bytes 1179656 | tf_op jit(solution)/shard_map/ppermute | solution.py:18
  21.2 2.3 %collective-permute-start.3 = (bf16[1,6,128,256]{3,2,1,0:T(8,128)(2,1)S(1)}, bf16[1,6,128,256]{3,2,1,0:T(8,128)(2,1)S(1)}, u32[]{:S(2)}, u32[]{:S(2)}) collective-permute-start(bf16[1,6,128,256]{3,2,1,0:T(8,128)(2,1)S(1)} %constant_dynamic-update-slice_fusion), channel_id=1, source_target_pairs={{16,0},{32,16},{48,32},{64,48},{80,64},{96,80},{112,96},{128,112},... | collective-permute-start | bytes 1179656 | tf_op jit(solution)/shard_map/ppermute | solution.py:19
  25.9 6.5 %collective-permute-done.3 = bf16[1,6,128,256]{3,2,1,0:T(8,128)(2,1)S(1)} collective-permute-done((bf16[1,6,128,256]{3,2,1,0:T(8,128)(2,1)S(1)}, bf16[1,6,128,256]{3,2,1,0:T(8,128)(2,1)S(1)}, u32[]{:S(2)}, u32[]{:S(2)}) %collective-permute-start.3) | collective-permute-done | bytes 393248 | tf_op jit(solution)/shard_map/ppermute | solution.py:19
  33.7 4.1 %shard_map.93 = bf16[512,256]{1,0:T(8,128)(2,1)S(1)} custom-call(bf16[1,3,3,6,128,256]{5,4,3,2,1,0:T(8,128)(2,1)S(1)} %maximum_bitcast_fusion.shifted_ref, bf16[27,256,256]{2,1,0:T(8,128)(2,1)} %taps_ref.3), custom_call_target="tpu_custom_call" | custom-call | flops 1811939328 | bytes 7340032 | tf_op jit(solution)/shard_map/pallas_call | solution.py:86
  37.8 2.2 %fusion.3 = bf16[1024,768]{1,0:T(8,128)(2,1)} fusion(s32[512]{0:T(512)S(1)} %add_add_fusion, bf16[512,256]{1,0:T(8,128)(2,1)S(1)} %shard_map.93, bf16[512,512]{1,0:T(8,128)(2,1)S(1)} %bitcast.66), kind=kOutput, calls=%fused_computation.7 | convolution fusion | flops 808189952 | bytes 2361344 | tf_op jit(solution)/shard_map/dot_general | solution.py:212
  40.0 5.8 %all-to-all-start = ((bf16[16,64,768]{2,1,0:T(8,128)(2,1)}), bf16[16,64,768]{2,1,0:T(8,128)(2,1)S(1)}, u32[]{:S(2)}, u32[]{:S(2)}) async-start(bf16[16,64,768]{2,1,0:T(8,128)(2,1)} %bitcast.6), calls=%async_computation | async-start | bytes 3145728 | tf_op jit(solution)/shard_map/all_to_all | solution.py:214
  45.7 32.9 %all-to-all-done = bf16[16,64,768]{2,1,0:T(8,128)(2,1)S(1)} async-done(((bf16[16,64,768]{2,1,0:T(8,128)(2,1)}), bf16[16,64,768]{2,1,0:T(8,128)(2,1)S(1)}, u32[]{:S(2)}, u32[]{:S(2)}) %all-to-all-start) | async-done | bytes 1572896 | tf_op jit(solution)/shard_map/all_to_all | solution.py:214
  78.6 1.2 copy-done.1
  79.8 17.5 %shard_map.94 = (bf16[1024,768]{1,0:T(8,128)(2,1)}, bf16[16,768,128]{2,1,0:T(8,128)(2,1)}) custom-call(bf16[1024,768]{1,0:T(8,128)(2,1)} %bitcast.59, bf16[512,2048]{1,0:T(8,128)(2,1)} %bitcast.64, bf16[2048,256]{1,0:T(8,128)(2,1)} %bitcast.65), custom_call_target="tpu_custom_call" | custom-call | flops 9663676416 | bytes 9437184 | tf_op jit(solution)/shard_map/pallas_call | solution.py:154
  97.2 3.3 %constant_dynamic-slice_fusion.1 = (bf16[1,2,2,2,768,128]{5,4,3,2,1,0:T(8,128)(2,1)}, bf16[1,2,2,2,768,128]{5,4,3,2,1,0:T(8,128)(2,1)S(1)}) fusion(bf16[2,2,2,2,768,128]{5,4,3,2,1,0:T(8,128)(2,1)} %bitcast.58, s32[]{:T(128)S(6)} %select_n.28, s32[]{:T(128)S(6)} %select_n.29), kind=kLoop, calls=%fused_computation.48 | loop fusion | bytes 6291464 | tf_op jit(solution)/shard_map/jit(dynamic_index_in_dim)/dynamic_slice | solution.py:41
  101.4 7.5 %all-to-all-start.1 = ((bf16[16,64,768]{2,1,0:T(8,128)(2,1)}), bf16[16,64,768]{2,1,0:T(8,128)(2,1)}, u32[]{:S(2)}, u32[]{:S(2)}) async-start(bf16[16,64,768]{2,1,0:T(8,128)(2,1)} %bitcast.10), calls=%async_computation.1 | async-start | bytes 3145728 | tf_op jit(solution)/shard_map/all_to_all | solution.py:218
  108.9 1.1 copy-done.2
  110.0 2.2 %convert_add_fusion = f32[2,2,2,768,128]{4,3,1,2,0:T(8,128)S(1)} fusion(bf16[2,2,2,768,128]{4,3,1,2,0:T(8,128)(2,1)} %copy-done.2, bf16[1,2,2,2,768,128]{5,4,3,2,1,0:T(8,128)(2,1)} %get-tuple-element.12), kind=kLoop, calls=%fused_computation.2 | loop fusion | flops 2359296 | bytes 6291456 | tf_op jit(solution)/shard_map/add | solution.py:45
  113.2 5.8 %collective-permute-start.9 = (bf16[2,2,768,128]{3,2,0,1:T(8,128)(2,1)}, bf16[2,2,768,128]{3,2,0,1:T(8,128)(2,1)}, u32[]{:S(2)}, u32[]{:S(2)}) collective-permute-start(bf16[2,2,768,128]{3,2,0,1:T(8,128)(2,1)} %fusion.11), channel_id=1, source_target_pairs={{0,32},{16,48},{32,0},{48,16},{64,96},{80,112},{96,64},{112,80},{1... | collective-permute-start | bytes 2359304 | tf_op jit(solution)/shard_map/ppermute | solution.py:44
  119.1 17.9 %collective-permute-done.9 = bf16[2,2,768,128]{3,2,0,1:T(8,128)(2,1)} collective-permute-done((bf16[2,2,768,128]{3,2,0,1:T(8,128)(2,1)}, bf16[2,2,768,128]{3,2,0,1:T(8,128)(2,1)}, u32[]{:S(2)}, u32[]{:S(2)}) %collective-permute-start.9) | collective-permute-done | bytes 786464 | tf_op jit(solution)/shard_map/ppermute | solution.py:44
  136.9 1.3 bitcast_add_fusion
  138.2 1.1 copy-done
  139.5 14.3 %collective-permute-done.10 = bf16[2,768,128]{2,1,0:T(8,128)(2,1)S(1)} collective-permute-done((bf16[2,768,128]{2,1,0:T(8,128)(2,1)S(1)}, bf16[2,768,128]{2,1,0:T(8,128)(2,1)S(1)}, u32[]{:S(2)}, u32[]{:S(2)}) %collective-permute-start.10) | collective-permute-done | bytes 393248 | tf_op jit(solution)/shard_map/ppermute | solution.py:44
  153.8 1.2 bitcast_add_fusion.1
  155.0 5.5 %collective-permute-start.11 = (bf16[768,128]{1,0:T(8,128)(2,1)S(1)}, bf16[768,128]{1,0:T(8,128)(2,1)S(1)}, u32[]{:S(2)}, u32[]{:S(2)}) collective-permute-start(bf16[768,128]{1,0:T(8,128)(2,1)S(1)} %fusion.17), channel_id=1, source_target_pairs={{0,64},{16,80},{32,96},{48,112},{64,0},{80,16},{96,32},{112,48},{1... | collective-permute-start | bytes 589832 | tf_op jit(solution)/shard_map/ppermute | solution.py:44
  160.5 1.8 fusion.5
  162.4 1.9 collective-permute-start.4
  164.3 3.4 %collective-permute-start.5 = (bf16[1,1,128,256]{3,2,1,0:T(8,128)(2,1)S(1)}, bf16[1,1,128,256]{3,2,1,0:T(8,128)(2,1)S(1)}, u32[]{:S(2)}, u32[]{:S(2)}) collective-permute-start(bf16[1,1,128,256]{3,2,1,0:T(8,128)(2,1)S(1)} %get-tuple-element.21), channel_id=1, source_target_pairs={{1,0},{2,1},{3,2},{4,3},{5,4},{6,5},{7,6},{8,7},{9,8},{10,9},{11,1... | collective-permute-start | bytes 196616 | tf_op jit(solution)/shard_map/ppermute | solution.py:19
  168.5 5.7 %collective-permute-done.5 = bf16[1,1,128,256]{3,2,1,0:T(8,128)(2,1)S(1)} collective-permute-done((bf16[1,1,128,256]{3,2,1,0:T(8,128)(2,1)S(1)}, bf16[1,1,128,256]{3,2,1,0:T(8,128)(2,1)S(1)}, u32[]{:S(2)}, u32[]{:S(2)}) %collective-permute-start.5) | collective-permute-done | bytes 65568 | tf_op jit(solution)/shard_map/ppermute | solution.py:19
  174.3 6.5 %collective-permute-start.6 = (bf16[1,6,128,256]{3,2,1,0:T(8,128)(2,1)S(1)}, bf16[1,6,128,256]{3,2,1,0:T(8,128)(2,1)S(1)}, u32[]{:S(2)}, u32[]{:S(2)}) collective-permute-start(bf16[1,6,128,256]{3,2,1,0:T(8,128)(2,1)S(1)} %pad_maximum_fusion.2), channel_id=1, source_target_pairs={{0,16},{16,32},{32,48},{48,64},{64,80},{80,96},{96,112},{112,128},... | collective-permute-start | bytes 1179656 | tf_op jit(solution)/shard_map/ppermute | solution.py:18
  180.8 1.9 collective-permute-start.7
  183.4 2.8 %fusion.4 = bf16[512,512]{1,0:T(8,128)(2,1)} fusion(bf16[1024,768]{1,0:T(8,128)(2,1)} %bitcast.11, s32[512]{0:T(512)S(1)} %add_add_fusion), kind=kOutput, calls=%fused_computation.12 | convolution fusion | flops 537657344 | bytes 1574912 | tf_op jit(solution)/shard_map/dot_general | solution.py:227
  186.2 5.8 %collective-permute-done.7 = bf16[1,6,128,256]{3,2,1,0:T(8,128)(2,1)S(1)} collective-permute-done((bf16[1,6,128,256]{3,2,1,0:T(8,128)(2,1)S(1)}, bf16[1,6,128,256]{3,2,1,0:T(8,128)(2,1)S(1)}, u32[]{:S(2)}, u32[]{:S(2)}) %collective-permute-start.7) | collective-permute-done | bytes 393248 | tf_op jit(solution)/shard_map/ppermute | solution.py:19
  193.4 4.7 %shard_map.95 = bf16[512,256]{1,0:T(8,128)(2,1)} custom-call(bf16[1,3,3,6,128,256]{5,4,3,2,1,0:T(8,128)(2,1)S(1)} %maximum_bitcast_fusion.1.shifted_ref, bf16[27,256,256]{2,1,0:T(8,128)(2,1)} %taps_ref.3), custom_call_target="tpu_custom_call" | custom-call | flops 1811939328 | bytes 7340032 | tf_op jit(solution)/shard_map/pallas_call | solution.py:86
  (37 shorter events, 10.6 us)
Async XLA Ops:
  1.5 8.1 %collective-permute-start = (bf16[1,1,128,256]{3,2,1,0:T(8,128)(2,1)S(1)}, bf16[1,1,128,256]{3,2,1,0:T(8,128)(2,1)S(1)}, u32[]{:S(2)}, u32[]{:S(2)}) collective-permute-start(bf16[1,1,128,256]{3,2,1,0:T(8,128)(2,1)S(1)} %get-tuple-element.23), channel_id=1, source_target_pairs={{0,1},{1,2},{2,3},{3,4},{4,5},{5,6},{6,7},{7,8},{8,9},{9,10},{10,1... | collective-permute-start | bytes 196616 | tf_op jit(solution)/shard_map/ppermute | solution.py:18
  7.5 9.8 %collective-permute-start.1 = (bf16[1,1,128,256]{3,2,1,0:T(8,128)(2,1)S(1)}, bf16[1,1,128,256]{3,2,1,0:T(8,128)(2,1)S(1)}, u32[]{:S(2)}, u32[]{:S(2)}) collective-permute-start(bf16[1,1,128,256]{3,2,1,0:T(8,128)(2,1)S(1)} %get-tuple-element.22), channel_id=1, source_target_pairs={{1,0},{2,1},{3,2},{4,3},{5,4},{6,5},{7,6},{8,7},{9,8},{10,9},{11,1... | collective-permute-start | bytes 196616 | tf_op jit(solution)/shard_map/ppermute | solution.py:19
  17.4 8.5 %collective-permute-start.2 = (bf16[1,6,128,256]{3,2,1,0:T(8,128)(2,1)S(1)}, bf16[1,6,128,256]{3,2,1,0:T(8,128)(2,1)S(1)}, u32[]{:S(2)}, u32[]{:S(2)}) collective-permute-start(bf16[1,6,128,256]{3,2,1,0:T(8,128)(2,1)S(1)} %constant_dynamic-update-slice_fusion), channel_id=1, source_target_pairs={{0,16},{16,32},{32,48},{48,64},{64,80},{80,96},{96,112},{112,128},... | collective-permute-start | bytes 1179656 | tf_op jit(solution)/shard_map/ppermute | solution.py:18
  21.2 11.2 %collective-permute-start.3 = (bf16[1,6,128,256]{3,2,1,0:T(8,128)(2,1)S(1)}, bf16[1,6,128,256]{3,2,1,0:T(8,128)(2,1)S(1)}, u32[]{:S(2)}, u32[]{:S(2)}) collective-permute-start(bf16[1,6,128,256]{3,2,1,0:T(8,128)(2,1)S(1)} %constant_dynamic-update-slice_fusion), channel_id=1, source_target_pairs={{16,0},{32,16},{48,32},{64,48},{80,64},{96,80},{112,96},{128,112},... | collective-permute-start | bytes 1179656 | tf_op jit(solution)/shard_map/ppermute | solution.py:19
  33.7 4.1 %copy-start.3 = (bf16[1,4,128,512]{3,2,1,0:T(8,128)(2,1)S(1)}, bf16[1,4,128,512]{3,2,1,0:T(8,128)(2,1)}, u32[]{:S(2)}) copy-start(bf16[1,4,128,512]{3,2,1,0:T(8,128)(2,1)} %param.6) | copy-start | bytes 1572868
  40.0 38.6 %all-to-all-start = ((bf16[16,64,768]{2,1,0:T(8,128)(2,1)}), bf16[16,64,768]{2,1,0:T(8,128)(2,1)S(1)}, u32[]{:S(2)}, u32[]{:S(2)}) async-start(bf16[16,64,768]{2,1,0:T(8,128)(2,1)} %bitcast.6), calls=%async_computation | async-start | bytes 3145728 | tf_op jit(solution)/shard_map/all_to_all | solution.py:214
  78.6 1.2 copy-start.1
  100.7 8.2 %collective-permute-start.8 = (bf16[2,2,2,768,128]{4,3,1,2,0:T(8,128)(2,1)S(1)}, bf16[2,2,2,768,128]{4,3,1,2,0:T(8,128)(2,1)S(1)}, u32[]{:S(2)}, u32[]{:S(2)}) collective-permute-start(bf16[2,2,2,768,128]{4,3,1,2,0:T(8,128)(2,1)S(1)} %bitcast.60), channel_id=1, source_target_pairs={{0,16},{16,0},{32,48},{48,32},{64,80},{80,64},{96,112},{112,96},{1... | collective-permute-start | bytes 4718600 | tf_op jit(solution)/shard_map/ppermute | solution.py:44
  101.4 59.2 %all-to-all-start.1 = ((bf16[16,64,768]{2,1,0:T(8,128)(2,1)}), bf16[16,64,768]{2,1,0:T(8,128)(2,1)}, u32[]{:S(2)}, u32[]{:S(2)}) async-start(bf16[16,64,768]{2,1,0:T(8,128)(2,1)} %bitcast.10), calls=%async_computation.1 | async-start | bytes 3145728 | tf_op jit(solution)/shard_map/all_to_all | solution.py:218
  108.9 1.1 copy-start.2
  113.2 23.7 %collective-permute-start.9 = (bf16[2,2,768,128]{3,2,0,1:T(8,128)(2,1)}, bf16[2,2,768,128]{3,2,0,1:T(8,128)(2,1)}, u32[]{:S(2)}, u32[]{:S(2)}) collective-permute-start(bf16[2,2,768,128]{3,2,0,1:T(8,128)(2,1)} %fusion.11), channel_id=1, source_target_pairs={{0,32},{16,48},{32,0},{48,16},{64,96},{80,112},{96,64},{112,80},{1... | collective-permute-start | bytes 2359304 | tf_op jit(solution)/shard_map/ppermute | solution.py:44
  138.2 1.1 copy-start
  139.4 14.4 %collective-permute-start.10 = (bf16[2,768,128]{2,1,0:T(8,128)(2,1)S(1)}, bf16[2,768,128]{2,1,0:T(8,128)(2,1)S(1)}, u32[]{:S(2)}, u32[]{:S(2)}) collective-permute-start(bf16[2,768,128]{2,1,0:T(8,128)(2,1)S(1)} %fusion.16), channel_id=1, source_target_pairs={{0,128},{16,144},{32,160},{48,176},{64,192},{80,208},{96,224},{112... | collective-permute-start | bytes 1179656 | tf_op jit(solution)/shard_map/ppermute | solution.py:44
  155.0 12.7 %collective-permute-start.11 = (bf16[768,128]{1,0:T(8,128)(2,1)S(1)}, bf16[768,128]{1,0:T(8,128)(2,1)S(1)}, u32[]{:S(2)}, u32[]{:S(2)}) collective-permute-start(bf16[768,128]{1,0:T(8,128)(2,1)S(1)} %fusion.17), channel_id=1, source_target_pairs={{0,64},{16,80},{32,96},{48,112},{64,0},{80,16},{96,32},{112,48},{1... | collective-permute-start | bytes 589832 | tf_op jit(solution)/shard_map/ppermute | solution.py:44
  162.4 6.1 %collective-permute-start.4 = (bf16[1,1,128,256]{3,2,1,0:T(8,128)(2,1)S(1)}, bf16[1,1,128,256]{3,2,1,0:T(8,128)(2,1)S(1)}, u32[]{:S(2)}, u32[]{:S(2)}) collective-permute-start(bf16[1,1,128,256]{3,2,1,0:T(8,128)(2,1)S(1)} %get-tuple-element.20), channel_id=1, source_target_pairs={{0,1},{1,2},{2,3},{3,4},{4,5},{5,6},{6,7},{7,8},{8,9},{9,10},{10,1... | collective-permute-start | bytes 196616 | tf_op jit(solution)/shard_map/ppermute | solution.py:18
  164.3 9.9 %collective-permute-start.5 = (bf16[1,1,128,256]{3,2,1,0:T(8,128)(2,1)S(1)}, bf16[1,1,128,256]{3,2,1,0:T(8,128)(2,1)S(1)}, u32[]{:S(2)}, u32[]{:S(2)}) collective-permute-start(bf16[1,1,128,256]{3,2,1,0:T(8,128)(2,1)S(1)} %get-tuple-element.21), channel_id=1, source_target_pairs={{1,0},{2,1},{3,2},{4,3},{5,4},{6,5},{7,6},{8,7},{9,8},{10,9},{11,1... | collective-permute-start | bytes 196616 | tf_op jit(solution)/shard_map/ppermute | solution.py:19
  174.3 11.9 %collective-permute-start.6 = (bf16[1,6,128,256]{3,2,1,0:T(8,128)(2,1)S(1)}, bf16[1,6,128,256]{3,2,1,0:T(8,128)(2,1)S(1)}, u32[]{:S(2)}, u32[]{:S(2)}) collective-permute-start(bf16[1,6,128,256]{3,2,1,0:T(8,128)(2,1)S(1)} %pad_maximum_fusion.2), channel_id=1, source_target_pairs={{0,16},{16,32},{32,48},{48,64},{64,80},{80,96},{96,112},{112,128},... | collective-permute-start | bytes 1179656 | tf_op jit(solution)/shard_map/ppermute | solution.py:18
  180.8 11.2 %collective-permute-start.7 = (bf16[1,6,128,256]{3,2,1,0:T(8,128)(2,1)S(1)}, bf16[1,6,128,256]{3,2,1,0:T(8,128)(2,1)S(1)}, u32[]{:S(2)}, u32[]{:S(2)}) collective-permute-start(bf16[1,6,128,256]{3,2,1,0:T(8,128)(2,1)S(1)} %pad_maximum_fusion.2), channel_id=1, source_target_pairs={{16,0},{32,16},{48,32},{64,48},{80,64},{96,80},{112,96},{128,112},... | collective-permute-start | bytes 1179656 | tf_op jit(solution)/shard_map/ppermute | solution.py:19

commit v17 on v15

--- a/solution.py
+++ b/solution.py
@@ -38,8 +38,11 @@
     for bit in order:
         axis = remaining.index(bit)
         mine = (me >> bit) & 1
-        keep = lax.dynamic_index_in_dim(x, mine, axis=axis, keepdims=False).astype(jnp.float32)
-        send = lax.dynamic_index_in_dim(x, 1 - mine, axis=axis, keepdims=False)
+        if bit == 0:
+            keep, send = x[0].astype(jnp.float32), x[1]
+        else:
+            keep = lax.dynamic_index_in_dim(x, mine, axis=axis, keepdims=False).astype(jnp.float32)
+            send = lax.dynamic_index_in_dim(x, 1 - mine, axis=axis, keepdims=False)
         pairs = [(i, i ^ (1 << bit)) for i in range(count)]
         got = lax.ppermute(send.astype(jnp.bfloat16), "dp", pairs)
         x = keep + got.astype(jnp.float32)
@@ -130,11 +133,13 @@
     part_two = jnp.dot(across_ref[cols:, :], activation, preferred_element_type=jnp.float32)
     lanes = part_ref.shape[2]
     bits = part_ref.shape[0].bit_length() - 1
+    mine = lax.axis_index("dp") & 1
     per_step = part_one.shape[1] // lanes
     for block in range(per_step):
         window = slice(block * lanes, (block + 1) * lanes)
         owner = step * per_step + block
         place = sum(((owner >> bit) & 1) << (bits - 1 - bit) for bit in range(bits))
+        place = place ^ (mine << (bits - 1))
         part_ref[place, :cols, :] = part_one[:, window].astype(part_ref.dtype)
         part_ref[place, cols:, :] = part_two[:, window].astype(part_ref.dtype)
 

time: 190 us -> 189 us (level)
  blocking collectives: 0 us -> 37.6 us
  waiting for transfers between devices: 87.7 us -> 53.3 us
  starting transfers between devices: 50.7 us -> 45.2 us
    all_to_all x0 -> x1, blocking collectives: none -> 37.6 us  [per_device(): lax.all_to_all(outbound.reshape(experts, capacity, both), 'expert', split...]
    all_to_all x1 -> x0, waiting for transfers between devices: 32.9 us -> none  [per_device(): lax.all_to_all(outbound.reshape(experts, capacity, both), 'expert', split...]
    all_to_all x1 -> x0, starting transfers between devices: 5.77 us -> none  [per_device(): lax.all_to_all(outbound.reshape(experts, capacity, both), 'expert', split...]
    slice x0 -> x1, local copies, waits for them, and re-layouts: none -> 3.34 us  [tree_scatter(): keep, send = (x[0].astype(jnp.float32), x[1])]
  transfers between devices with their start and end apart: 14 -> 13, of which waited for: 9 -> 8; matrix products, arithmetic and copies ran while one was open for 8% -> 8% of each run, Pallas kernels for 0% -> 0%
where the time goes in v17:
time: 189 us; the launch traced here: 188 us
  waiting for transfers between devices  53.3 us (28%)
  starting transfers between devices  45.2 us (24%)
  blocking collectives  37.6 us (20%)
  Pallas kernels  26.3 us (14%)
  local copies, waits for them, and re-layouts  11.2 us (6%)
  other arithmetic  6.76 us (4%)
  matrix products  6.64 us (4%)
    all_to_all x1, blocking collectives, per_device(): lax.all_to_all(outbound.reshape(experts, capacity, both), 'expert', split...  37.6 us
    ppermute x4, waiting for transfers between devices, tree_scatter(): got = lax.ppermute(send.astype(jnp.bfloat16), 'dp', pairs)  26.9 us
    ppermute x4, waiting for transfers between devices, extended(): after = lax.ppermute(first, axis, down)  25.6 us
    ppermute x4, starting transfers between devices, extended(): before = lax.ppermute(last, axis, up)  22.6 us
    pallas_call x1, Pallas kernels, expert(): pl.pallas_call(functools.partial(expert_kernel, cols), grid=(hidden // ch...  17.5 us
    pallas_call x2, Pallas kernels, conv_block(): pl.pallas_call(functools.partial(conv_kernel, flip), out_shape=jax.ShapeD...  8.77 us
    ppermute x4, starting transfers between devices, extended(): after = lax.ppermute(first, axis, down)  8.05 us
    all_to_all x1, starting transfers between devices, per_device(): lax.all_to_all(back.reshape(experts, capacity, both), 'expert', split_axi...  7.3 us
  transfers between devices with their start and end apart: 13, of which 8 were waited for; matrix products, arithmetic and copies ran while one was open for 8% of the time, Pallas kernels for 0%

profile of v17, /device:TPU:95, one launch (start us, length us, event | category | flops | bytes accessed | tf_op | source)
XLA Modules:
  0.0 187.9 jit_solution(13511106721506727055)
XLA Ops:
  1.5 6.0 %collective-permute-start = (bf16[1,1,128,256]{3,2,1,0:T(8,128)(2,1)S(1)}, bf16[1,1,128,256]{3,2,1,0:T(8,128)(2,1)S(1)}, u32[]{:S(2)}, u32[]{:S(2)}) collective-permute-start(bf16[1,1,128,256]{3,2,1,0:T(8,128)(2,1)S(1)} %get-tuple-element.23), channel_id=1, source_target_pairs={{0,1},{1,2},{2,3},{3,4},{4,5},{5,6},{6,7},{7,8},{8,9},{9,10},{10,1... | collective-permute-start | bytes 196616 | tf_op jit(solution)/shard_map/ppermute | solution.py:18
  7.5 1.9 %collective-permute-start.1 = (bf16[1,1,128,256]{3,2,1,0:T(8,128)(2,1)S(1)}, bf16[1,1,128,256]{3,2,1,0:T(8,128)(2,1)S(1)}, u32[]{:S(2)}, u32[]{:S(2)}) collective-permute-start(bf16[1,1,128,256]{3,2,1,0:T(8,128)(2,1)S(1)} %get-tuple-element.22), channel_id=1, source_target_pairs={{1,0},{2,1},{3,2},{4,3},{5,4},{6,5},{7,6},{8,7},{9,8},{10,9},{11,1... | collective-permute-start | bytes 196616 | tf_op jit(solution)/shard_map/ppermute | solution.py:19
  10.6 6.7 %collective-permute-done.1 = bf16[1,1,128,256]{3,2,1,0:T(8,128)(2,1)S(1)} collective-permute-done((bf16[1,1,128,256]{3,2,1,0:T(8,128)(2,1)S(1)}, bf16[1,1,128,256]{3,2,1,0:T(8,128)(2,1)S(1)}, u32[]{:S(2)}, u32[]{:S(2)}) %collective-permute-start.1) | collective-permute-done | bytes 65568 | tf_op jit(solution)/shard_map/ppermute | solution.py:19
  17.4 3.8 %collective-permute-start.2 = (bf16[1,6,128,256]{3,2,1,0:T(8,128)(2,1)S(1)}, bf16[1,6,128,256]{3,2,1,0:T(8,128)(2,1)S(1)}, u32[]{:S(2)}, u32[]{:S(2)}) collective-permute-start(bf16[1,6,128,256]{3,2,1,0:T(8,128)(2,1)S(1)} %constant_dynamic-update-slice_fusion), channel_id=1, source_target_pairs={{0,16},{16,32},{32,48},{48,64},{64,80},{80,96},{96,112},{112,128},... | collective-permute-start | bytes 1179656 | tf_op jit(solution)/shard_map/ppermute | solution.py:18
  21.2 2.3 %collective-permute-start.3 = (bf16[1,6,128,256]{3,2,1,0:T(8,128)(2,1)S(1)}, bf16[1,6,128,256]{3,2,1,0:T(8,128)(2,1)S(1)}, u32[]{:S(2)}, u32[]{:S(2)}) collective-permute-start(bf16[1,6,128,256]{3,2,1,0:T(8,128)(2,1)S(1)} %constant_dynamic-update-slice_fusion), channel_id=1, source_target_pairs={{16,0},{32,16},{48,32},{64,48},{80,64},{96,80},{112,96},{128,112},... | collective-permute-start | bytes 1179656 | tf_op jit(solution)/shard_map/ppermute | solution.py:19
  23.5 1.0 fusion.6
  25.9 6.5 %collective-permute-done.3 = bf16[1,6,128,256]{3,2,1,0:T(8,128)(2,1)S(1)} collective-permute-done((bf16[1,6,128,256]{3,2,1,0:T(8,128)(2,1)S(1)}, bf16[1,6,128,256]{3,2,1,0:T(8,128)(2,1)S(1)}, u32[]{:S(2)}, u32[]{:S(2)}) %collective-permute-start.3) | collective-permute-done | bytes 393248 | tf_op jit(solution)/shard_map/ppermute | solution.py:19
  33.7 4.1 %shard_map.93 = bf16[512,256]{1,0:T(8,128)(2,1)S(1)} custom-call(bf16[1,3,3,6,128,256]{5,4,3,2,1,0:T(8,128)(2,1)S(1)} %maximum_bitcast_fusion.shifted_ref, bf16[27,256,256]{2,1,0:T(8,128)(2,1)} %taps_ref.3), custom_call_target="tpu_custom_call" | custom-call | flops 1811939328 | bytes 7340032 | tf_op jit(solution)/shard_map/pallas_call | solution.py:89
  37.8 1.0 fusion.3
  38.8 37.6 %all_to_all.10 = bf16[16,64,768]{2,1,0:T(8,128)(2,1)} all-to-all(bf16[16,64,768]{2,1,0:T(8,128)(2,1)S(1)} %bitcast.54), channel_id=1, replica_groups=mesh['dp'=16,'expert'=16] {'expert'}, dimensions={0} | all-to-all | bytes 3145728 | tf_op jit(solution)/shard_map/all_to_all | solution.py:219
  76.4 17.5 %shard_map.94 = (bf16[1024,768]{1,0:T(8,128)(2,1)}, bf16[16,768,128]{2,1,0:T(8,128)(2,1)}) custom-call(bf16[1024,768]{1,0:T(8,128)(2,1)} %bitcast.53, bf16[512,2048]{1,0:T(8,128)(2,1)} %bitcast.59, bf16[2048,256]{1,0:T(8,128)(2,1)} %bitcast.60), custom_call_target="tpu_custom_call" | custom-call | flops 9663676416 | bytes 9437184 | tf_op jit(solution)/shard_map/pallas_call | solution.py:159
  93.9 3.3 %fusion.22 = (bf16[8,768,128]{2,1,0:T(8,128)(2,1)S(1)}, bf16[8,768,128]{2,1,0:T(8,128)(2,1)}) fusion(bf16[16,768,128]{2,1,0:T(8,128)(2,1)} %get-tuple-element.7), kind=kLoop, calls=%fused_computation.48 | loop fusion | bytes 6291456 | tf_op jit(solution)/shard_map/slice | solution.py:42
  97.3 7.3 %all-to-all-start.1 = ((bf16[16,64,768]{2,1,0:T(8,128)(2,1)}), bf16[16,64,768]{2,1,0:T(8,128)(2,1)}, u32[]{:S(2)}, u32[]{:S(2)}) async-start(bf16[16,64,768]{2,1,0:T(8,128)(2,1)} %bitcast.10), calls=%async_computation.1 | async-start | bytes 3145728 | tf_op jit(solution)/shard_map/all_to_all | solution.py:223
  104.6 1.1 copy-done.1
  105.7 2.2 %convert_add_fusion = f32[2,2,2,768,128]{4,3,2,1,0:T(8,128)S(1)} fusion(bf16[2,2,2,768,128]{4,3,2,1,0:T(8,128)(2,1)} %bitcast.48, bf16[2,2,2,768,128]{4,3,2,1,0:T(8,128)(2,1)} %copy-done.1), kind=kLoop, calls=%fused_computation.2 | loop fusion | flops 2359296 | bytes 6291456 | tf_op jit(solution)/shard_map/add | solution.py:48
  107.9 1.0 fusion.11
  108.9 5.4 %collective-permute-start.9 = (bf16[2,2,768,128]{3,2,1,0:T(8,128)(2,1)}, bf16[2,2,768,128]{3,2,1,0:T(8,128)(2,1)}, u32[]{:S(2)}, u32[]{:S(2)}) collective-permute-start(bf16[2,2,768,128]{3,2,1,0:T(8,128)(2,1)} %fusion.11), channel_id=1, source_target_pairs={{0,32},{16,48},{32,0},{48,16},{64,96},{80,112},{96,64},{112,80},{1... | collective-permute-start | bytes 2359304 | tf_op jit(solution)/shard_map/ppermute | solution.py:47
  114.3 17.6 %collective-permute-done.9 = bf16[2,2,768,128]{3,2,1,0:T(8,128)(2,1)} collective-permute-done((bf16[2,2,768,128]{3,2,1,0:T(8,128)(2,1)}, bf16[2,2,768,128]{3,2,1,0:T(8,128)(2,1)}, u32[]{:S(2)}, u32[]{:S(2)}) %collective-permute-start.9) | collective-permute-done | bytes 786464 | tf_op jit(solution)/shard_map/ppermute | solution.py:47
  131.9 1.3 bitcast_add_fusion
  133.2 1.1 copy-done
  134.4 1.8 collective-permute-start.10
  136.1 9.2 %collective-permute-done.10 = bf16[2,768,128]{2,1,0:T(8,128)(2,1)S(1)} collective-permute-done((bf16[2,768,128]{2,1,0:T(8,128)(2,1)S(1)}, bf16[2,768,128]{2,1,0:T(8,128)(2,1)S(1)}, u32[]{:S(2)}, u32[]{:S(2)}) %collective-permute-start.10) | collective-permute-done | bytes 393248 | tf_op jit(solution)/shard_map/ppermute | solution.py:47
  145.4 1.2 bitcast_add_fusion.1
  146.7 1.8 fusion.5
  148.6 5.2 %collective-permute-start.4 = (bf16[1,1,128,256]{3,2,1,0:T(8,128)(2,1)S(1)}, bf16[1,1,128,256]{3,2,1,0:T(8,128)(2,1)S(1)}, u32[]{:S(2)}, u32[]{:S(2)}) collective-permute-start(bf16[1,1,128,256]{3,2,1,0:T(8,128)(2,1)S(1)} %get-tuple-element.20), channel_id=1, source_target_pairs={{0,1},{1,2},{2,3},{3,4},{4,5},{5,6},{6,7},{7,8},{8,9},{9,10},{10,1... | collective-permute-start | bytes 196616 | tf_op jit(solution)/shard_map/ppermute | solution.py:18
  153.8 1.9 %collective-permute-start.5 = (bf16[1,1,128,256]{3,2,1,0:T(8,128)(2,1)S(1)}, bf16[1,1,128,256]{3,2,1,0:T(8,128)(2,1)S(1)}, u32[]{:S(2)}, u32[]{:S(2)}) collective-permute-start(bf16[1,1,128,256]{3,2,1,0:T(8,128)(2,1)S(1)} %get-tuple-element.21), channel_id=1, source_target_pairs={{1,0},{2,1},{3,2},{4,3},{5,4},{6,5},{7,6},{8,7},{9,8},{10,9},{11,1... | collective-permute-start | bytes 196616 | tf_op jit(solution)/shard_map/ppermute | solution.py:19
  156.5 6.5 %collective-permute-done.5 = bf16[1,1,128,256]{3,2,1,0:T(8,128)(2,1)S(1)} collective-permute-done((bf16[1,1,128,256]{3,2,1,0:T(8,128)(2,1)S(1)}, bf16[1,1,128,256]{3,2,1,0:T(8,128)(2,1)S(1)}, u32[]{:S(2)}, u32[]{:S(2)}) %collective-permute-start.5) | collective-permute-done | bytes 65568 | tf_op jit(solution)/shard_map/ppermute | solution.py:19
  163.1 7.5 %collective-permute-start.6 = (bf16[1,6,128,256]{3,2,1,0:T(8,128)(2,1)S(1)}, bf16[1,6,128,256]{3,2,1,0:T(8,128)(2,1)S(1)}, u32[]{:S(2)}, u32[]{:S(2)}) collective-permute-start(bf16[1,6,128,256]{3,2,1,0:T(8,128)(2,1)S(1)} %pad_maximum_fusion.2), channel_id=1, source_target_pairs={{0,16},{16,32},{32,48},{48,64},{64,80},{80,96},{96,112},{112,128},... | collective-permute-start | bytes 1179656 | tf_op jit(solution)/shard_map/ppermute | solution.py:18
  170.6 1.9 %collective-permute-start.7 = (bf16[1,6,128,256]{3,2,1,0:T(8,128)(2,1)S(1)}, bf16[1,6,128,256]{3,2,1,0:T(8,128)(2,1)S(1)}, u32[]{:S(2)}, u32[]{:S(2)}) collective-permute-start(bf16[1,6,128,256]{3,2,1,0:T(8,128)(2,1)S(1)} %pad_maximum_fusion.2), channel_id=1, source_target_pairs={{16,0},{32,16},{48,32},{64,48},{80,64},{96,80},{112,96},{128,112},... | collective-permute-start | bytes 1179656 | tf_op jit(solution)/shard_map/ppermute | solution.py:19
  173.3 2.8 %fusion.4 = bf16[512,512]{1,0:T(8,128)(2,1)} fusion(bf16[1024,768]{1,0:T(8,128)(2,1)} %bitcast.11, s32[512]{0:T(512)S(1)} %add_add_fusion), kind=kOutput, calls=%fused_computation.10 | convolution fusion | flops 537657344 | bytes 1574912 | tf_op jit(solution)/shard_map/dot_general | solution.py:232
  176.1 5.8 %collective-permute-done.7 = bf16[1,6,128,256]{3,2,1,0:T(8,128)(2,1)S(1)} collective-permute-done((bf16[1,6,128,256]{3,2,1,0:T(8,128)(2,1)S(1)}, bf16[1,6,128,256]{3,2,1,0:T(8,128)(2,1)S(1)}, u32[]{:S(2)}, u32[]{:S(2)}) %collective-permute-start.7) | collective-permute-done | bytes 393248 | tf_op jit(solution)/shard_map/ppermute | solution.py:19
  183.2 4.7 %shard_map.95 = bf16[512,256]{1,0:T(8,128)(2,1)} custom-call(bf16[1,3,3,6,128,256]{5,4,3,2,1,0:T(8,128)(2,1)S(1)} %maximum_bitcast_fusion.1.shifted_ref, bf16[27,256,256]{2,1,0:T(8,128)(2,1)} %taps_ref.3), custom_call_target="tpu_custom_call" | custom-call | flops 1811939328 | bytes 7340032 | tf_op jit(solution)/shard_map/pallas_call | solution.py:89
  (33 shorter events, 7.8 us)
Async XLA Ops:
  1.5 8.1 %collective-permute-start = (bf16[1,1,128,256]{3,2,1,0:T(8,128)(2,1)S(1)}, bf16[1,1,128,256]{3,2,1,0:T(8,128)(2,1)S(1)}, u32[]{:S(2)}, u32[]{:S(2)}) collective-permute-start(bf16[1,1,128,256]{3,2,1,0:T(8,128)(2,1)S(1)} %get-tuple-element.23), channel_id=1, source_target_pairs={{0,1},{1,2},{2,3},{3,4},{4,5},{5,6},{6,7},{7,8},{8,9},{9,10},{10,1... | collective-permute-start | bytes 196616 | tf_op jit(solution)/shard_map/ppermute | solution.py:18
  7.5 9.8 %collective-permute-start.1 = (bf16[1,1,128,256]{3,2,1,0:T(8,128)(2,1)S(1)}, bf16[1,1,128,256]{3,2,1,0:T(8,128)(2,1)S(1)}, u32[]{:S(2)}, u32[]{:S(2)}) collective-permute-start(bf16[1,1,128,256]{3,2,1,0:T(8,128)(2,1)S(1)} %get-tuple-element.22), channel_id=1, source_target_pairs={{1,0},{2,1},{3,2},{4,3},{5,4},{6,5},{7,6},{8,7},{9,8},{10,9},{11,1... | collective-permute-start | bytes 196616 | tf_op jit(solution)/shard_map/ppermute | solution.py:19
  17.4 8.5 %collective-permute-start.2 = (bf16[1,6,128,256]{3,2,1,0:T(8,128)(2,1)S(1)}, bf16[1,6,128,256]{3,2,1,0:T(8,128)(2,1)S(1)}, u32[]{:S(2)}, u32[]{:S(2)}) collective-permute-start(bf16[1,6,128,256]{3,2,1,0:T(8,128)(2,1)S(1)} %constant_dynamic-update-slice_fusion), channel_id=1, source_target_pairs={{0,16},{16,32},{32,48},{48,64},{64,80},{80,96},{96,112},{112,128},... | collective-permute-start | bytes 1179656 | tf_op jit(solution)/shard_map/ppermute | solution.py:18
  21.2 11.2 %collective-permute-start.3 = (bf16[1,6,128,256]{3,2,1,0:T(8,128)(2,1)S(1)}, bf16[1,6,128,256]{3,2,1,0:T(8,128)(2,1)S(1)}, u32[]{:S(2)}, u32[]{:S(2)}) collective-permute-start(bf16[1,6,128,256]{3,2,1,0:T(8,128)(2,1)S(1)} %constant_dynamic-update-slice_fusion), channel_id=1, source_target_pairs={{16,0},{32,16},{48,32},{64,48},{80,64},{96,80},{112,96},{128,112},... | collective-permute-start | bytes 1179656 | tf_op jit(solution)/shard_map/ppermute | solution.py:19
  33.7 4.1 %copy-start.2 = (bf16[1,4,128,512]{3,2,1,0:T(8,128)(2,1)S(1)}, bf16[1,4,128,512]{3,2,1,0:T(8,128)(2,1)}, u32[]{:S(2)}) copy-start(bf16[1,4,128,512]{3,2,1,0:T(8,128)(2,1)} %param.6) | copy-start | bytes 1572868
  97.3 7.3 %collective-permute-start.8 = (bf16[2,2,2,768,128]{4,3,2,1,0:T(8,128)(2,1)S(1)}, bf16[2,2,2,768,128]{4,3,2,1,0:T(8,128)(2,1)S(1)}, u32[]{:S(2)}, u32[]{:S(2)}) collective-permute-start(bf16[2,2,2,768,128]{4,3,2,1,0:T(8,128)(2,1)S(1)} %bitcast.55), channel_id=1, source_target_pairs={{0,16},{16,0},{32,48},{48,32},{64,80},{80,64},{96,112},{112,96},{1... | collective-permute-start | bytes 4718600 | tf_op jit(solution)/shard_map/ppermute | solution.py:47
  97.3 49.4 %all-to-all-start.1 = ((bf16[16,64,768]{2,1,0:T(8,128)(2,1)}), bf16[16,64,768]{2,1,0:T(8,128)(2,1)}, u32[]{:S(2)}, u32[]{:S(2)}) async-start(bf16[16,64,768]{2,1,0:T(8,128)(2,1)} %bitcast.10), calls=%async_computation.1 | async-start | bytes 3145728 | tf_op jit(solution)/shard_map/all_to_all | solution.py:223
  104.6 1.1 copy-start.1
  108.9 23.0 %collective-permute-start.9 = (bf16[2,2,768,128]{3,2,1,0:T(8,128)(2,1)}, bf16[2,2,768,128]{3,2,1,0:T(8,128)(2,1)}, u32[]{:S(2)}, u32[]{:S(2)}) collective-permute-start(bf16[2,2,768,128]{3,2,1,0:T(8,128)(2,1)} %fusion.11), channel_id=1, source_target_pairs={{0,32},{16,48},{32,0},{48,16},{64,96},{80,112},{96,64},{112,80},{1... | collective-permute-start | bytes 2359304 | tf_op jit(solution)/shard_map/ppermute | solution.py:47
  133.2 1.1 copy-start
  134.4 11.0 %collective-permute-start.10 = (bf16[2,768,128]{2,1,0:T(8,128)(2,1)S(1)}, bf16[2,768,128]{2,1,0:T(8,128)(2,1)S(1)}, u32[]{:S(2)}, u32[]{:S(2)}) collective-permute-start(bf16[2,768,128]{2,1,0:T(8,128)(2,1)S(1)} %fusion.16), channel_id=1, source_target_pairs={{0,64},{16,80},{32,96},{48,112},{64,0},{80,16},{96,32},{112,48},{1... | collective-permute-start | bytes 1179656 | tf_op jit(solution)/shard_map/ppermute | solution.py:47
  146.6 9.1 %collective-permute-start.11 = (bf16[768,128]{1,0:T(8,128)(2,1)S(1)}, bf16[768,128]{1,0:T(8,128)(2,1)S(1)}, u32[]{:S(2)}, u32[]{:S(2)}) collective-permute-start(bf16[768,128]{1,0:T(8,128)(2,1)S(1)} %fusion.17), channel_id=1, source_target_pairs={{0,128},{16,144},{32,160},{48,176},{64,192},{80,208},{96,224},{112... | collective-permute-start | bytes 589832 | tf_op jit(solution)/shard_map/ppermute | solution.py:47
  148.6 8.0 %collective-permute-start.4 = (bf16[1,1,128,256]{3,2,1,0:T(8,128)(2,1)S(1)}, bf16[1,1,128,256]{3,2,1,0:T(8,128)(2,1)S(1)}, u32[]{:S(2)}, u32[]{:S(2)}) collective-permute-start(bf16[1,1,128,256]{3,2,1,0:T(8,128)(2,1)S(1)} %get-tuple-element.20), channel_id=1, source_target_pairs={{0,1},{1,2},{2,3},{3,4},{4,5},{5,6},{6,7},{7,8},{8,9},{9,10},{10,1... | collective-permute-start | bytes 196616 | tf_op jit(solution)/shard_map/ppermute | solution.py:18
  153.8 9.3 %collective-permute-start.5 = (bf16[1,1,128,256]{3,2,1,0:T(8,128)(2,1)S(1)}, bf16[1,1,128,256]{3,2,1,0:T(8,128)(2,1)S(1)}, u32[]{:S(2)}, u32[]{:S(2)}) collective-permute-start(bf16[1,1,128,256]{3,2,1,0:T(8,128)(2,1)S(1)} %get-tuple-element.21), channel_id=1, source_target_pairs={{1,0},{2,1},{3,2},{4,3},{5,4},{6,5},{7,6},{8,7},{9,8},{10,9},{11,1... | collective-permute-start | bytes 196616 | tf_op jit(solution)/shard_map/ppermute | solution.py:19
  163.1 13.0 %collective-permute-start.6 = (bf16[1,6,128,256]{3,2,1,0:T(8,128)(2,1)S(1)}, bf16[1,6,128,256]{3,2,1,0:T(8,128)(2,1)S(1)}, u32[]{:S(2)}, u32[]{:S(2)}) collective-permute-start(bf16[1,6,128,256]{3,2,1,0:T(8,128)(2,1)S(1)} %pad_maximum_fusion.2), channel_id=1, source_target_pairs={{0,16},{16,32},{32,48},{48,64},{64,80},{80,96},{96,112},{112,128},... | collective-permute-start | bytes 1179656 | tf_op jit(solution)/shard_map/ppermute | solution.py:18
  170.6 11.2 %collective-permute-start.7 = (bf16[1,6,128,256]{3,2,1,0:T(8,128)(2,1)S(1)}, bf16[1,6,128,256]{3,2,1,0:T(8,128)(2,1)S(1)}, u32[]{:S(2)}, u32[]{:S(2)}) collective-permute-start(bf16[1,6,128,256]{3,2,1,0:T(8,128)(2,1)S(1)} %pad_maximum_fusion.2), channel_id=1, source_target_pairs={{16,0},{32,16},{48,32},{64,48},{80,64},{96,80},{112,96},{128,112},... | collective-permute-start | bytes 1179656 | tf_op jit(solution)/shard_map/ppermute | solution.py:19

commit v18 on v17

--- a/solution.py
+++ b/solution.py
@@ -38,7 +38,7 @@
     for bit in order:
         axis = remaining.index(bit)
         mine = (me >> bit) & 1
-        if bit == 0:
+        if axis == 0:
             keep, send = x[0].astype(jnp.float32), x[1]
         else:
             keep = lax.dynamic_index_in_dim(x, mine, axis=axis, keepdims=False).astype(jnp.float32)
@@ -133,13 +133,13 @@
     part_two = jnp.dot(across_ref[cols:, :], activation, preferred_element_type=jnp.float32)
     lanes = part_ref.shape[2]
     bits = part_ref.shape[0].bit_length() - 1
-    mine = lax.axis_index("dp") & 1
+    mine = lax.axis_index("dp")
     per_step = part_one.shape[1] // lanes
     for block in range(per_step):
         window = slice(block * lanes, (block + 1) * lanes)
         owner = step * per_step + block
-        place = sum(((owner >> bit) & 1) << (bits - 1 - bit) for bit in range(bits))
-        place = place ^ (mine << (bits - 1))
+        relative = owner ^ mine
+        place = sum(((relative >> bit) & 1) << (bits - 1 - bit) for bit in range(bits))
         part_ref[place, :cols, :] = part_one[:, window].astype(part_ref.dtype)
         part_ref[place, cols:, :] = part_two[:, window].astype(part_ref.dtype)
 

time: 189 us -> 183 us (0.968)
  local copies, waits for them, and re-layouts: 11.2 us -> 8.13 us
  other arithmetic: 6.76 us -> 4.09 us
  matrix products: 6.64 us -> 4.38 us
    add x4, other arithmetic: 4.69 us -> 2.01 us  [tree_scatter(): x = keep + got.astype(jnp.float32)]
    unnamed x9 -> x5, local copies, waits for them, and re-layouts: 3.99 us -> 1.74 us
  transfers between devices with their start and end apart: 13 -> 13, of which waited for: 8 -> 9; matrix products, arithmetic and copies ran while one was open for 8% -> 5% of each run, Pallas kernels for 0% -> 0%
where the time goes in v18:
time: 183 us; the launch traced here: 181 us
  waiting for transfers between devices  54.2 us (30%)
  starting transfers between devices  45.8 us (25%)
  blocking collectives  37.6 us (21%)
  Pallas kernels  26.2 us (14%)
  local copies, waits for them, and re-layouts  8.13 us (4%)
  matrix products  4.38 us (2%)
  other arithmetic  4.09 us (2%)
    all_to_all x1, blocking collectives, per_device(): lax.all_to_all(outbound.reshape(experts, capacity, both), 'expert', split...  37.6 us
    ppermute x4, waiting for transfers between devices, tree_scatter(): got = lax.ppermute(send.astype(jnp.bfloat16), 'dp', pairs)  26.6 us
    ppermute x4, waiting for transfers between devices, extended(): after = lax.ppermute(first, axis, down)  26.2 us
    ppermute x4, starting transfers between devices, extended(): before = lax.ppermute(last, axis, up)  23.2 us
    pallas_call x1, Pallas kernels, expert(): pl.pallas_call(functools.partial(expert_kernel, cols), grid=(hidden // ch...  17.5 us
    pallas_call x2, Pallas kernels, conv_block(): pl.pallas_call(functools.partial(conv_kernel, flip), out_shape=jax.ShapeD...  8.77 us
    ppermute x4, starting transfers between devices, extended(): after = lax.ppermute(first, axis, down)  8.05 us
    ppermute x4, starting transfers between devices, tree_scatter(): got = lax.ppermute(send.astype(jnp.bfloat16), 'dp', pairs)  7.95 us
  transfers between devices with their start and end apart: 13, of which 9 were waited for; matrix products, arithmetic and copies ran while one was open for 5% of the time, Pallas kernels for 0%

profile of v18, /device:TPU:95, one launch (start us, length us, event | category | flops | bytes accessed | tf_op | source)
XLA Modules:
  0.0 181.4 jit_solution(14234946325673478019)
XLA Ops:
  0.6 0.9 fusion.27
  1.5 6.0 %collective-permute-start = (bf16[1,1,128,256]{3,2,1,0:T(8,128)(2,1)S(1)}, bf16[1,1,128,256]{3,2,1,0:T(8,128)(2,1)S(1)}, u32[]{:S(2)}, u32[]{:S(2)}) collective-permute-start(bf16[1,1,128,256]{3,2,1,0:T(8,128)(2,1)S(1)} %get-tuple-element.23), channel_id=1, source_target_pairs={{0,1},{1,2},{2,3},{3,4},{4,5},{5,6},{6,7},{7,8},{8,9},{9,10},{10,1... | collective-permute-start | bytes 196616 | tf_op jit(solution)/shard_map/ppermute | solution.py:18
  7.5 1.9 %collective-permute-start.1 = (bf16[1,1,128,256]{3,2,1,0:T(8,128)(2,1)S(1)}, bf16[1,1,128,256]{3,2,1,0:T(8,128)(2,1)S(1)}, u32[]{:S(2)}, u32[]{:S(2)}) collective-permute-start(bf16[1,1,128,256]{3,2,1,0:T(8,128)(2,1)S(1)} %get-tuple-element.22), channel_id=1, source_target_pairs={{1,0},{2,1},{3,2},{4,3},{5,4},{6,5},{7,6},{8,7},{9,8},{10,9},{11,1... | collective-permute-start | bytes 196616 | tf_op jit(solution)/shard_map/ppermute | solution.py:19
  9.7 1.0 constant_dynamic-update-slice_fusion.1
  10.6 6.7 %collective-permute-done.1 = bf16[1,1,128,256]{3,2,1,0:T(8,128)(2,1)S(1)} collective-permute-done((bf16[1,1,128,256]{3,2,1,0:T(8,128)(2,1)S(1)}, bf16[1,1,128,256]{3,2,1,0:T(8,128)(2,1)S(1)}, u32[]{:S(2)}, u32[]{:S(2)}) %collective-permute-start.1) | collective-permute-done | bytes 65568 | tf_op jit(solution)/shard_map/ppermute | solution.py:19
  17.4 3.8 %collective-permute-start.2 = (bf16[1,6,128,256]{3,2,1,0:T(8,128)(2,1)S(1)}, bf16[1,6,128,256]{3,2,1,0:T(8,128)(2,1)S(1)}, u32[]{:S(2)}, u32[]{:S(2)}) collective-permute-start(bf16[1,6,128,256]{3,2,1,0:T(8,128)(2,1)S(1)} %constant_dynamic-update-slice_fusion), channel_id=1, source_target_pairs={{0,16},{16,32},{32,48},{48,64},{64,80},{80,96},{96,112},{112,128},... | collective-permute-start | bytes 1179656 | tf_op jit(solution)/shard_map/ppermute | solution.py:18
  21.2 2.3 %collective-permute-start.3 = (bf16[1,6,128,256]{3,2,1,0:T(8,128)(2,1)S(1)}, bf16[1,6,128,256]{3,2,1,0:T(8,128)(2,1)S(1)}, u32[]{:S(2)}, u32[]{:S(2)}) collective-permute-start(bf16[1,6,128,256]{3,2,1,0:T(8,128)(2,1)S(1)} %constant_dynamic-update-slice_fusion), channel_id=1, source_target_pairs={{16,0},{32,16},{48,32},{64,48},{80,64},{96,80},{112,96},{128,112},... | collective-permute-start | bytes 1179656 | tf_op jit(solution)/shard_map/ppermute | solution.py:19
  23.5 1.0 fusion.7
  24.5 0.7 add_add_fusion
  25.9 6.5 %collective-permute-done.3 = bf16[1,6,128,256]{3,2,1,0:T(8,128)(2,1)S(1)} collective-permute-done((bf16[1,6,128,256]{3,2,1,0:T(8,128)(2,1)S(1)}, bf16[1,6,128,256]{3,2,1,0:T(8,128)(2,1)S(1)}, u32[]{:S(2)}, u32[]{:S(2)}) %collective-permute-start.3) | collective-permute-done | bytes 393248 | tf_op jit(solution)/shard_map/ppermute | solution.py:19
  33.7 4.1 %shard_map.93 = bf16[512,256]{1,0:T(8,128)(2,1)S(1)} custom-call(bf16[1,3,3,6,128,256]{5,4,3,2,1,0:T(8,128)(2,1)S(1)} %maximum_bitcast_fusion.shifted_ref, bf16[27,256,256]{2,1,0:T(8,128)(2,1)} %taps_ref.3), custom_call_target="tpu_custom_call" | custom-call | flops 1811939328 | bytes 7340032 | tf_op jit(solution)/shard_map/pallas_call | solution.py:89
  37.8 1.0 fusion.3
  38.8 37.6 %all_to_all.10 = bf16[16,64,768]{2,1,0:T(8,128)(2,1)} all-to-all(bf16[16,64,768]{2,1,0:T(8,128)(2,1)S(1)} %bitcast.63), channel_id=1, replica_groups=mesh['dp'=16,'expert'=16] {'expert'}, dimensions={0} | all-to-all | bytes 3145728 | tf_op jit(solution)/shard_map/all_to_all | solution.py:219
  76.4 17.5 %shard_map.94 = (bf16[1024,768]{1,0:T(8,128)(2,1)}, bf16[16,768,128]{2,1,0:T(8,128)(2,1)}) custom-call(bf16[1024,768]{1,0:T(8,128)(2,1)} %bitcast.62, bf16[512,2048]{1,0:T(8,128)(2,1)} %bitcast.67, bf16[2048,256]{1,0:T(8,128)(2,1)} %bitcast.68), custom_call_target="tpu_custom_call" | custom-call | flops 9663676416 | bytes 9437184 | tf_op jit(solution)/shard_map/pallas_call | solution.py:159
  93.9 3.4 %fusion.25 = (bf16[8,768,128]{2,1,0:T(8,128)(2,1)}, bf16[8,768,128]{2,1,0:T(8,128)(2,1)S(1)}) fusion(bf16[16,768,128]{2,1,0:T(8,128)(2,1)} %get-tuple-element.7), kind=kLoop, calls=%fused_computation.51 | loop fusion | bytes 6291456 | tf_op jit(solution)/shard_map/slice | solution.py:42
  97.3 6.7 %all-to-all-start.1 = ((bf16[16,64,768]{2,1,0:T(8,128)(2,1)}), bf16[16,64,768]{2,1,0:T(8,128)(2,1)S(1)}, u32[]{:S(2)}, u32[]{:S(2)}) async-start(bf16[16,64,768]{2,1,0:T(8,128)(2,1)} %bitcast.61), calls=%async_computation.1 | async-start | bytes 3145728 | tf_op jit(solution)/shard_map/all_to_all | solution.py:223
  103.9 1.7 convert_add_fusion
  105.8 6.1 %collective-permute-start.9 = (bf16[2,2,768,128]{3,2,1,0:T(8,128)(2,1)S(1)}, bf16[2,2,768,128]{3,2,1,0:T(8,128)(2,1)S(1)}, u32[]{:S(2)}, u32[]{:S(2)}) collective-permute-start(bf16[2,2,768,128]{3,2,1,0:T(8,128)(2,1)S(1)} %fusion.12), channel_id=1, source_target_pairs={{0,32},{16,48},{32,0},{48,16},{64,96},{80,112},{96,64},{112,80},{1... | collective-permute-start | bytes 2359304 | tf_op jit(solution)/shard_map/ppermute | solution.py:47
  111.9 17.3 %collective-permute-done.9 = bf16[2,2,768,128]{3,2,1,0:T(8,128)(2,1)S(1)} collective-permute-done((bf16[2,2,768,128]{3,2,1,0:T(8,128)(2,1)S(1)}, bf16[2,2,768,128]{3,2,1,0:T(8,128)(2,1)S(1)}, u32[]{:S(2)}, u32[]{:S(2)}) %collective-permute-start.9) | collective-permute-done | bytes 786464 | tf_op jit(solution)/shard_map/ppermute | solution.py:47
  129.4 1.7 collective-permute-start.10
  131.2 9.3 %collective-permute-done.10 = bf16[2,768,128]{2,1,0:T(8,128)(2,1)S(1)} collective-permute-done((bf16[2,768,128]{2,1,0:T(8,128)(2,1)S(1)}, bf16[2,768,128]{2,1,0:T(8,128)(2,1)S(1)}, u32[]{:S(2)}, u32[]{:S(2)}) %collective-permute-start.10) | collective-permute-done | bytes 393248 | tf_op jit(solution)/shard_map/ppermute | solution.py:47
  140.7 0.8 fusion.6
  141.5 5.2 %collective-permute-start.4 = (bf16[1,1,128,256]{3,2,1,0:T(8,128)(2,1)S(1)}, bf16[1,1,128,256]{3,2,1,0:T(8,128)(2,1)S(1)}, u32[]{:S(2)}, u32[]{:S(2)}) collective-permute-start(bf16[1,1,128,256]{3,2,1,0:T(8,128)(2,1)S(1)} %get-tuple-element.20), channel_id=1, source_target_pairs={{0,1},{1,2},{2,3},{3,4},{4,5},{5,6},{6,7},{7,8},{8,9},{9,10},{10,1... | collective-permute-start | bytes 196616 | tf_op jit(solution)/shard_map/ppermute | solution.py:18
  146.7 1.9 %collective-permute-start.5 = (bf16[1,1,128,256]{3,2,1,0:T(8,128)(2,1)S(1)}, bf16[1,1,128,256]{3,2,1,0:T(8,128)(2,1)S(1)}, u32[]{:S(2)}, u32[]{:S(2)}) collective-permute-start(bf16[1,1,128,256]{3,2,1,0:T(8,128)(2,1)S(1)} %get-tuple-element.21), channel_id=1, source_target_pairs={{1,0},{2,1},{3,2},{4,3},{5,4},{6,5},{7,6},{8,7},{9,8},{10,9},{11,1... | collective-permute-start | bytes 196616 | tf_op jit(solution)/shard_map/ppermute | solution.py:19
  148.7 0.8 copy.12
  149.4 6.5 %collective-permute-done.5 = bf16[1,1,128,256]{3,2,1,0:T(8,128)(2,1)S(1)} collective-permute-done((bf16[1,1,128,256]{3,2,1,0:T(8,128)(2,1)S(1)}, bf16[1,1,128,256]{3,2,1,0:T(8,128)(2,1)S(1)}, u32[]{:S(2)}, u32[]{:S(2)}) %collective-permute-start.5) | collective-permute-done | bytes 65568 | tf_op jit(solution)/shard_map/ppermute | solution.py:19
  156.0 8.1 %collective-permute-start.6 = (bf16[1,6,128,256]{3,2,1,0:T(8,128)(2,1)S(1)}, bf16[1,6,128,256]{3,2,1,0:T(8,128)(2,1)S(1)}, u32[]{:S(2)}, u32[]{:S(2)}) collective-permute-start(bf16[1,6,128,256]{3,2,1,0:T(8,128)(2,1)S(1)} %pad_maximum_fusion.2), channel_id=1, source_target_pairs={{0,16},{16,32},{32,48},{48,64},{64,80},{80,96},{96,112},{112,128},... | collective-permute-start | bytes 1179656 | tf_op jit(solution)/shard_map/ppermute | solution.py:18
  164.1 1.9 %collective-permute-start.7 = (bf16[1,6,128,256]{3,2,1,0:T(8,128)(2,1)S(1)}, bf16[1,6,128,256]{3,2,1,0:T(8,128)(2,1)S(1)}, u32[]{:S(2)}, u32[]{:S(2)}) collective-permute-start(bf16[1,6,128,256]{3,2,1,0:T(8,128)(2,1)S(1)} %pad_maximum_fusion.2), channel_id=1, source_target_pairs={{16,0},{32,16},{48,32},{64,48},{80,64},{96,80},{112,96},{128,112},... | collective-permute-start | bytes 1179656 | tf_op jit(solution)/shard_map/ppermute | solution.py:19
  166.0 0.7 slice_bitcast_fusion.7
  166.8 1.6 fusion.5
  168.8 6.5 %collective-permute-done.7 = bf16[1,6,128,256]{3,2,1,0:T(8,128)(2,1)S(1)} collective-permute-done((bf16[1,6,128,256]{3,2,1,0:T(8,128)(2,1)S(1)}, bf16[1,6,128,256]{3,2,1,0:T(8,128)(2,1)S(1)}, u32[]{:S(2)}, u32[]{:S(2)}) %collective-permute-start.7) | collective-permute-done | bytes 393248 | tf_op jit(solution)/shard_map/ppermute | solution.py:19
  176.7 4.7 %shard_map.95 = bf16[512,256]{1,0:T(8,128)(2,1)} custom-call(bf16[1,3,3,6,128,256]{5,4,3,2,1,0:T(8,128)(2,1)S(1)} %maximum_bitcast_fusion.1.shifted_ref, bf16[27,256,256]{2,1,0:T(8,128)(2,1)} %taps_ref.3), custom_call_target="tpu_custom_call" | custom-call | flops 1811939328 | bytes 7340032 | tf_op jit(solution)/shard_map/pallas_call | solution.py:89
  (29 shorter events, 4.6 us)
Async XLA Ops:
  1.5 8.1 %collective-permute-start = (bf16[1,1,128,256]{3,2,1,0:T(8,128)(2,1)S(1)}, bf16[1,1,128,256]{3,2,1,0:T(8,128)(2,1)S(1)}, u32[]{:S(2)}, u32[]{:S(2)}) collective-permute-start(bf16[1,1,128,256]{3,2,1,0:T(8,128)(2,1)S(1)} %get-tuple-element.23), channel_id=1, source_target_pairs={{0,1},{1,2},{2,3},{3,4},{4,5},{5,6},{6,7},{7,8},{8,9},{9,10},{10,1... | collective-permute-start | bytes 196616 | tf_op jit(solution)/shard_map/ppermute | solution.py:18
  7.5 9.8 %collective-permute-start.1 = (bf16[1,1,128,256]{3,2,1,0:T(8,128)(2,1)S(1)}, bf16[1,1,128,256]{3,2,1,0:T(8,128)(2,1)S(1)}, u32[]{:S(2)}, u32[]{:S(2)}) collective-permute-start(bf16[1,1,128,256]{3,2,1,0:T(8,128)(2,1)S(1)} %get-tuple-element.22), channel_id=1, source_target_pairs={{1,0},{2,1},{3,2},{4,3},{5,4},{6,5},{7,6},{8,7},{9,8},{10,9},{11,1... | collective-permute-start | bytes 196616 | tf_op jit(solution)/shard_map/ppermute | solution.py:19
  17.4 8.5 %collective-permute-start.2 = (bf16[1,6,128,256]{3,2,1,0:T(8,128)(2,1)S(1)}, bf16[1,6,128,256]{3,2,1,0:T(8,128)(2,1)S(1)}, u32[]{:S(2)}, u32[]{:S(2)}) collective-permute-start(bf16[1,6,128,256]{3,2,1,0:T(8,128)(2,1)S(1)} %constant_dynamic-update-slice_fusion), channel_id=1, source_target_pairs={{0,16},{16,32},{32,48},{48,64},{64,80},{80,96},{96,112},{112,128},... | collective-permute-start | bytes 1179656 | tf_op jit(solution)/shard_map/ppermute | solution.py:18
  21.2 11.2 %collective-permute-start.3 = (bf16[1,6,128,256]{3,2,1,0:T(8,128)(2,1)S(1)}, bf16[1,6,128,256]{3,2,1,0:T(8,128)(2,1)S(1)}, u32[]{:S(2)}, u32[]{:S(2)}) collective-permute-start(bf16[1,6,128,256]{3,2,1,0:T(8,128)(2,1)S(1)} %constant_dynamic-update-slice_fusion), channel_id=1, source_target_pairs={{16,0},{32,16},{48,32},{64,48},{80,64},{96,80},{112,96},{128,112},... | collective-permute-start | bytes 1179656 | tf_op jit(solution)/shard_map/ppermute | solution.py:19
  33.7 4.1 %copy-start = (bf16[1,4,128,512]{3,2,1,0:T(8,128)(2,1)S(1)}, bf16[1,4,128,512]{3,2,1,0:T(8,128)(2,1)}, u32[]{:S(2)}) copy-start(bf16[1,4,128,512]{3,2,1,0:T(8,128)(2,1)} %param.6) | copy-start | bytes 1572868
  97.3 6.7 %collective-permute-start.8 = (bf16[2,2,2,768,128]{4,3,2,1,0:T(8,128)(2,1)}, bf16[2,2,2,768,128]{4,3,2,1,0:T(8,128)(2,1)}, u32[]{:S(2)}, u32[]{:S(2)}) collective-permute-start(bf16[2,2,2,768,128]{4,3,2,1,0:T(8,128)(2,1)} %bitcast.20), channel_id=1, source_target_pairs={{0,16},{16,0},{32,48},{48,32},{64,80},{80,64},{96,112},{112,96},{1... | collective-permute-start | bytes 4718600 | tf_op jit(solution)/shard_map/ppermute | solution.py:47
  97.3 43.4 %all-to-all-start.1 = ((bf16[16,64,768]{2,1,0:T(8,128)(2,1)}), bf16[16,64,768]{2,1,0:T(8,128)(2,1)S(1)}, u32[]{:S(2)}, u32[]{:S(2)}) async-start(bf16[16,64,768]{2,1,0:T(8,128)(2,1)} %bitcast.61), calls=%async_computation.1 | async-start | bytes 3145728 | tf_op jit(solution)/shard_map/all_to_all | solution.py:223
  105.8 23.4 %collective-permute-start.9 = (bf16[2,2,768,128]{3,2,1,0:T(8,128)(2,1)S(1)}, bf16[2,2,768,128]{3,2,1,0:T(8,128)(2,1)S(1)}, u32[]{:S(2)}, u32[]{:S(2)}) collective-permute-start(bf16[2,2,768,128]{3,2,1,0:T(8,128)(2,1)S(1)} %fusion.12), channel_id=1, source_target_pairs={{0,32},{16,48},{32,0},{48,16},{64,96},{80,112},{96,64},{112,80},{1... | collective-permute-start | bytes 2359304 | tf_op jit(solution)/shard_map/ppermute | solution.py:47
  129.4 11.0 %collective-permute-start.10 = (bf16[2,768,128]{2,1,0:T(8,128)(2,1)S(1)}, bf16[2,768,128]{2,1,0:T(8,128)(2,1)S(1)}, u32[]{:S(2)}, u32[]{:S(2)}) collective-permute-start(bf16[2,768,128]{2,1,0:T(8,128)(2,1)S(1)} %fusion.18), channel_id=1, source_target_pairs={{0,64},{16,80},{32,96},{48,112},{64,0},{80,16},{96,32},{112,48},{1... | collective-permute-start | bytes 1179656 | tf_op jit(solution)/shard_map/ppermute | solution.py:47
  140.6 8.1 %collective-permute-start.11 = (bf16[768,128]{1,0:T(8,128)(2,1)S(1)}, bf16[768,128]{1,0:T(8,128)(2,1)S(1)}, u32[]{:S(2)}, u32[]{:S(2)}) collective-permute-start(bf16[768,128]{1,0:T(8,128)(2,1)S(1)} %fusion.20), channel_id=1, source_target_pairs={{0,128},{16,144},{32,160},{48,176},{64,192},{80,208},{96,224},{112... | collective-permute-start | bytes 589832 | tf_op jit(solution)/shard_map/ppermute | solution.py:47
  141.5 8.0 %collective-permute-start.4 = (bf16[1,1,128,256]{3,2,1,0:T(8,128)(2,1)S(1)}, bf16[1,1,128,256]{3,2,1,0:T(8,128)(2,1)S(1)}, u32[]{:S(2)}, u32[]{:S(2)}) collective-permute-start(bf16[1,1,128,256]{3,2,1,0:T(8,128)(2,1)S(1)} %get-tuple-element.20), channel_id=1, source_target_pairs={{0,1},{1,2},{2,3},{3,4},{4,5},{5,6},{6,7},{7,8},{8,9},{9,10},{10,1... | collective-permute-start | bytes 196616 | tf_op jit(solution)/shard_map/ppermute | solution.py:18
  146.7 9.2 %collective-permute-start.5 = (bf16[1,1,128,256]{3,2,1,0:T(8,128)(2,1)S(1)}, bf16[1,1,128,256]{3,2,1,0:T(8,128)(2,1)S(1)}, u32[]{:S(2)}, u32[]{:S(2)}) collective-permute-start(bf16[1,1,128,256]{3,2,1,0:T(8,128)(2,1)S(1)} %get-tuple-element.21), channel_id=1, source_target_pairs={{1,0},{2,1},{3,2},{4,3},{5,4},{6,5},{7,6},{8,7},{9,8},{10,9},{11,1... | collective-permute-start | bytes 196616 | tf_op jit(solution)/shard_map/ppermute | solution.py:19
  156.0 12.8 %collective-permute-start.6 = (bf16[1,6,128,256]{3,2,1,0:T(8,128)(2,1)S(1)}, bf16[1,6,128,256]{3,2,1,0:T(8,128)(2,1)S(1)}, u32[]{:S(2)}, u32[]{:S(2)}) collective-permute-start(bf16[1,6,128,256]{3,2,1,0:T(8,128)(2,1)S(1)} %pad_maximum_fusion.2), channel_id=1, source_target_pairs={{0,16},{16,32},{32,48},{48,64},{64,80},{80,96},{96,112},{112,128},... | collective-permute-start | bytes 1179656 | tf_op jit(solution)/shard_map/ppermute | solution.py:18
  164.1 11.2 %collective-permute-start.7 = (bf16[1,6,128,256]{3,2,1,0:T(8,128)(2,1)S(1)}, bf16[1,6,128,256]{3,2,1,0:T(8,128)(2,1)S(1)}, u32[]{:S(2)}, u32[]{:S(2)}) collective-permute-start(bf16[1,6,128,256]{3,2,1,0:T(8,128)(2,1)S(1)} %pad_maximum_fusion.2), channel_id=1, source_target_pairs={{16,0},{32,16},{48,32},{64,48},{80,64},{96,80},{112,96},{128,112},... | collective-permute-start | bytes 1179656 | tf_op jit(solution)/shard_map/ppermute | solution.py:19

commit v19 on v18

--- a/solution.py
+++ b/solution.py
@@ -213,8 +213,9 @@
 
     flat_feats = feats.reshape(patch_count, feat_width)
     field_rows = conv_block(cotangent, kernel, True)
-    local = jnp.concatenate([flat_feats, field_rows], axis=1)
-    outbound = jnp.dot(route, local, preferred_element_type=jnp.float32).astype(jnp.bfloat16)
+    sent_feats = jnp.dot(route, flat_feats, preferred_element_type=jnp.float32).astype(jnp.bfloat16)
+    sent_grads = jnp.dot(route, field_rows, preferred_element_type=jnp.float32).astype(jnp.bfloat16)
+    outbound = jnp.concatenate([sent_feats, sent_grads], axis=1)
     both = feat_width + channels
     inbound = lax.all_to_all(
         outbound.reshape(experts, capacity, both), "expert", split_axis=0, concat_axis=0, tiled=True

time: 183 us -> 186 us (1.016)
  matrix products: 4.38 us -> 7.03 us
  starting transfers between devices: 45.8 us -> 43.7 us
    ppermute x4, starting transfers between devices: 23.2 us -> 20 us  [extended(): before = lax.ppermute(last, axis, up)]
    all_to_all x1, waiting for transfers between devices: 0.01 us -> 2.89 us  [per_device(): lax.all_to_all(back.reshape(experts, capacity, both), 'expert', split_axi...]
    ppermute x4, waiting for transfers between devices: 26.2 us -> 23.7 us  [extended(): after = lax.ppermute(first, axis, down)]
  transfers between devices with their start and end apart: 13 -> 13, of which waited for: 9 -> 8; matrix products, arithmetic and copies ran while one was open for 5% -> 6% of each run, Pallas kernels for 0% -> 0%
where the time goes in v19:
time: 186 us; the launch traced here: 184 us
  waiting for transfers between devices  54.3 us (29%)
  starting transfers between devices  43.7 us (23%)
  blocking collectives  37.9 us (20%)
  Pallas kernels  26.2 us (14%)
  local copies, waits for them, and re-layouts  9.79 us (5%)
  matrix products  7.03 us (4%)
  other arithmetic  4.21 us (2%)
    all_to_all x1, blocking collectives, per_device(): lax.all_to_all(outbound.reshape(experts, capacity, both), 'expert', split...  37.9 us
    ppermute x4, waiting for transfers between devices, tree_scatter(): got = lax.ppermute(send.astype(jnp.bfloat16), 'dp', pairs)  26.8 us
    ppermute x4, waiting for transfers between devices, extended(): after = lax.ppermute(first, axis, down)  23.7 us
    ppermute x4, starting transfers between devices, extended(): before = lax.ppermute(last, axis, up)  20 us
    pallas_call x1, Pallas kernels, expert(): pl.pallas_call(functools.partial(expert_kernel, cols), grid=(hidden // ch...  17.5 us
    ppermute x4, starting transfers between devices, extended(): after = lax.ppermute(first, axis, down)  9.09 us
    pallas_call x2, Pallas kernels, conv_block(): pl.pallas_call(functools.partial(conv_kernel, flip), out_shape=jax.ShapeD...  8.72 us
    ppermute x4, starting transfers between devices, tree_scatter(): got = lax.ppermute(send.astype(jnp.bfloat16), 'dp', pairs)  7.32 us
  transfers between devices with their start and end apart: 13, of which 8 were waited for; matrix products, arithmetic and copies ran while one was open for 6% of the time, Pallas kernels for 0%

profile of v19, /device:TPU:95, one launch (start us, length us, event | category | flops | bytes accessed | tf_op | source)
XLA Modules:
  0.0 184.0 jit_solution(17957265780985446653)
XLA Ops:
  0.6 0.9 fusion.26
  1.6 6.0 %collective-permute-start = (bf16[1,1,128,256]{3,2,1,0:T(8,128)(2,1)S(1)}, bf16[1,1,128,256]{3,2,1,0:T(8,128)(2,1)S(1)}, u32[]{:S(2)}, u32[]{:S(2)}) collective-permute-start(bf16[1,1,128,256]{3,2,1,0:T(8,128)(2,1)S(1)} %get-tuple-element.23), channel_id=1, source_target_pairs={{0,1},{1,2},{2,3},{3,4},{4,5},{5,6},{6,7},{7,8},{8,9},{9,10},{10,1... | collective-permute-start | bytes 196616 | tf_op jit(solution)/shard_map/ppermute | solution.py:18
  7.6 1.9 %collective-permute-start.1 = (bf16[1,1,128,256]{3,2,1,0:T(8,128)(2,1)S(1)}, bf16[1,1,128,256]{3,2,1,0:T(8,128)(2,1)S(1)}, u32[]{:S(2)}, u32[]{:S(2)}) collective-permute-start(bf16[1,1,128,256]{3,2,1,0:T(8,128)(2,1)S(1)} %get-tuple-element.22), channel_id=1, source_target_pairs={{1,0},{2,1},{3,2},{4,3},{5,4},{6,5},{7,6},{8,7},{9,8},{10,9},{11,1... | collective-permute-start | bytes 196616 | tf_op jit(solution)/shard_map/ppermute | solution.py:19
  9.5 1.0 fusion.9
  10.6 1.0 constant_dynamic-update-slice_fusion.1
  11.6 5.9 %collective-permute-done.1 = bf16[1,1,128,256]{3,2,1,0:T(8,128)(2,1)S(1)} collective-permute-done((bf16[1,1,128,256]{3,2,1,0:T(8,128)(2,1)S(1)}, bf16[1,1,128,256]{3,2,1,0:T(8,128)(2,1)S(1)}, u32[]{:S(2)}, u32[]{:S(2)}) %collective-permute-start.1) | collective-permute-done | bytes 65568 | tf_op jit(solution)/shard_map/ppermute | solution.py:19
  17.5 3.8 %collective-permute-start.2 = (bf16[1,6,128,256]{3,2,1,0:T(8,128)(2,1)S(1)}, bf16[1,6,128,256]{3,2,1,0:T(8,128)(2,1)S(1)}, u32[]{:S(2)}, u32[]{:S(2)}) collective-permute-start(bf16[1,6,128,256]{3,2,1,0:T(8,128)(2,1)S(1)} %constant_dynamic-update-slice_fusion), channel_id=1, source_target_pairs={{0,16},{16,32},{32,48},{48,64},{64,80},{80,96},{96,112},{112,128},... | collective-permute-start | bytes 1179656 | tf_op jit(solution)/shard_map/ppermute | solution.py:18
  21.3 2.3 %collective-permute-start.3 = (bf16[1,6,128,256]{3,2,1,0:T(8,128)(2,1)S(1)}, bf16[1,6,128,256]{3,2,1,0:T(8,128)(2,1)S(1)}, u32[]{:S(2)}, u32[]{:S(2)}) collective-permute-start(bf16[1,6,128,256]{3,2,1,0:T(8,128)(2,1)S(1)} %constant_dynamic-update-slice_fusion), channel_id=1, source_target_pairs={{16,0},{32,16},{48,32},{64,48},{80,64},{96,80},{112,96},{128,112},... | collective-permute-start | bytes 1179656 | tf_op jit(solution)/shard_map/ppermute | solution.py:19
  24.3 0.8 fusion.5
  25.1 0.9 collective-permute-done.2
  26.0 6.5 %collective-permute-done.3 = bf16[1,6,128,256]{3,2,1,0:T(8,128)(2,1)S(1)} collective-permute-done((bf16[1,6,128,256]{3,2,1,0:T(8,128)(2,1)S(1)}, bf16[1,6,128,256]{3,2,1,0:T(8,128)(2,1)S(1)}, u32[]{:S(2)}, u32[]{:S(2)}) %collective-permute-start.3) | collective-permute-done | bytes 393248 | tf_op jit(solution)/shard_map/ppermute | solution.py:19
  33.7 4.0 %shard_map.93 = bf16[512,256]{1,0:T(8,128)(2,1)S(1)} custom-call(bf16[1,3,3,6,128,256]{5,4,3,2,1,0:T(8,128)(2,1)S(1)} %maximum_bitcast_fusion.shifted_ref, bf16[27,256,256]{2,1,0:T(8,128)(2,1)} %taps_ref.3), custom_call_target="tpu_custom_call" | custom-call | flops 1811939328 | bytes 7340032 | tf_op jit(solution)/shard_map/pallas_call | solution.py:89
  38.5 1.6 copy.13
  40.1 37.9 %all_to_all.10 = bf16[16,64,768]{2,1,0:T(8,128)(2,1)} all-to-all(bf16[16,64,768]{2,1,0:T(8,128)(2,1)} %bitcast.57), channel_id=1, replica_groups=mesh['dp'=16,'expert'=16] {'expert'}, dimensions={0} | all-to-all | bytes 3145728 | tf_op jit(solution)/shard_map/all_to_all | solution.py:220
  78.0 17.5 %shard_map.94 = (bf16[1024,768]{1,0:T(8,128)(2,1)}, bf16[16,768,128]{2,1,0:T(8,128)(2,1)}) custom-call(bf16[1024,768]{1,0:T(8,128)(2,1)} %bitcast.64, bf16[512,2048]{1,0:T(8,128)(2,1)} %bitcast.68, bf16[2048,256]{1,0:T(8,128)(2,1)} %bitcast.69), custom_call_target="tpu_custom_call" | custom-call | flops 9663676416 | bytes 9437184 | tf_op jit(solution)/shard_map/pallas_call | solution.py:159
  95.5 3.4 %fusion.24 = (bf16[8,768,128]{2,1,0:T(8,128)(2,1)}, bf16[8,768,128]{2,1,0:T(8,128)(2,1)S(1)}) fusion(bf16[16,768,128]{2,1,0:T(8,128)(2,1)} %get-tuple-element.7), kind=kLoop, calls=%fused_computation.51 | loop fusion | bytes 6291456 | tf_op jit(solution)/shard_map/slice | solution.py:42
  98.9 7.3 %all-to-all-start.1 = ((bf16[16,64,768]{2,1,0:T(8,128)(2,1)}), bf16[16,64,768]{2,1,0:T(8,128)(2,1)}, u32[]{:S(2)}, u32[]{:S(2)}) async-start(bf16[16,64,768]{2,1,0:T(8,128)(2,1)} %bitcast.63), calls=%async_computation.1 | async-start | bytes 3145728 | tf_op jit(solution)/shard_map/all_to_all | solution.py:224
  106.2 1.7 convert_add_fusion
  108.0 5.4 %collective-permute-start.9 = (bf16[2,2,768,128]{3,2,1,0:T(8,128)(2,1)S(1)}, bf16[2,2,768,128]{3,2,1,0:T(8,128)(2,1)S(1)}, u32[]{:S(2)}, u32[]{:S(2)}) collective-permute-start(bf16[2,2,768,128]{3,2,1,0:T(8,128)(2,1)S(1)} %fusion.15), channel_id=1, source_target_pairs={{0,32},{16,48},{32,0},{48,16},{64,96},{80,112},{96,64},{112,80},{1... | collective-permute-start | bytes 2359304 | tf_op jit(solution)/shard_map/ppermute | solution.py:47
  113.4 17.4 %collective-permute-done.9 = bf16[2,2,768,128]{3,2,1,0:T(8,128)(2,1)S(1)} collective-permute-done((bf16[2,2,768,128]{3,2,1,0:T(8,128)(2,1)S(1)}, bf16[2,2,768,128]{3,2,1,0:T(8,128)(2,1)S(1)}, u32[]{:S(2)}, u32[]{:S(2)}) %collective-permute-start.9) | collective-permute-done | bytes 786464 | tf_op jit(solution)/shard_map/ppermute | solution.py:47
  131.1 1.8 collective-permute-start.10
  132.9 9.4 %collective-permute-done.10 = bf16[2,768,128]{2,1,0:T(8,128)(2,1)S(1)} collective-permute-done((bf16[2,768,128]{2,1,0:T(8,128)(2,1)S(1)}, bf16[2,768,128]{2,1,0:T(8,128)(2,1)S(1)}, u32[]{:S(2)}, u32[]{:S(2)}) %collective-permute-start.10) | collective-permute-done | bytes 393248 | tf_op jit(solution)/shard_map/ppermute | solution.py:47
  142.5 2.9 %all-to-all-done.1 = bf16[16,64,768]{2,1,0:T(8,128)(2,1)} async-done(((bf16[16,64,768]{2,1,0:T(8,128)(2,1)}), bf16[16,64,768]{2,1,0:T(8,128)(2,1)}, u32[]{:S(2)}, u32[]{:S(2)}) %all-to-all-start.1) | async-done | bytes 1572896 | tf_op jit(solution)/shard_map/all_to_all | solution.py:224
  145.4 1.8 fusion.8
  147.2 2.3 %collective-permute-start.4 = (bf16[1,1,128,256]{3,2,1,0:T(8,128)(2,1)S(1)}, bf16[1,1,128,256]{3,2,1,0:T(8,128)(2,1)S(1)}, u32[]{:S(2)}, u32[]{:S(2)}) collective-permute-start(bf16[1,1,128,256]{3,2,1,0:T(8,128)(2,1)S(1)} %get-tuple-element.20), channel_id=1, source_target_pairs={{0,1},{1,2},{2,3},{3,4},{4,5},{5,6},{6,7},{7,8},{8,9},{9,10},{10,1... | collective-permute-start | bytes 196616 | tf_op jit(solution)/shard_map/ppermute | solution.py:18
  149.6 3.0 %collective-permute-start.5 = (bf16[1,1,128,256]{3,2,1,0:T(8,128)(2,1)S(1)}, bf16[1,1,128,256]{3,2,1,0:T(8,128)(2,1)S(1)}, u32[]{:S(2)}, u32[]{:S(2)}) collective-permute-start(bf16[1,1,128,256]{3,2,1,0:T(8,128)(2,1)S(1)} %get-tuple-element.21), channel_id=1, source_target_pairs={{1,0},{2,1},{3,2},{4,3},{5,4},{6,5},{7,6},{8,7},{9,8},{10,9},{11,1... | collective-permute-start | bytes 196616 | tf_op jit(solution)/shard_map/ppermute | solution.py:19
  153.4 5.5 %collective-permute-done.5 = bf16[1,1,128,256]{3,2,1,0:T(8,128)(2,1)S(1)} collective-permute-done((bf16[1,1,128,256]{3,2,1,0:T(8,128)(2,1)S(1)}, bf16[1,1,128,256]{3,2,1,0:T(8,128)(2,1)S(1)}, u32[]{:S(2)}, u32[]{:S(2)}) %collective-permute-start.5) | collective-permute-done | bytes 65568 | tf_op jit(solution)/shard_map/ppermute | solution.py:19
  159.0 7.8 %collective-permute-start.6 = (bf16[1,6,128,256]{3,2,1,0:T(8,128)(2,1)S(1)}, bf16[1,6,128,256]{3,2,1,0:T(8,128)(2,1)S(1)}, u32[]{:S(2)}, u32[]{:S(2)}) collective-permute-start(bf16[1,6,128,256]{3,2,1,0:T(8,128)(2,1)S(1)} %pad_maximum_fusion.3), channel_id=1, source_target_pairs={{0,16},{16,32},{32,48},{48,64},{64,80},{80,96},{96,112},{112,128},... | collective-permute-start | bytes 1179656 | tf_op jit(solution)/shard_map/ppermute | solution.py:18
  166.8 1.9 %collective-permute-start.7 = (bf16[1,6,128,256]{3,2,1,0:T(8,128)(2,1)S(1)}, bf16[1,6,128,256]{3,2,1,0:T(8,128)(2,1)S(1)}, u32[]{:S(2)}, u32[]{:S(2)}) collective-permute-start(bf16[1,6,128,256]{3,2,1,0:T(8,128)(2,1)S(1)} %pad_maximum_fusion.3), channel_id=1, source_target_pairs={{16,0},{32,16},{48,32},{64,48},{80,64},{96,80},{112,96},{128,112},... | collective-permute-start | bytes 1179656 | tf_op jit(solution)/shard_map/ppermute | solution.py:19
  169.4 2.8 %fusion.6 = bf16[512,512]{1,0:T(8,128)(2,1)} fusion(bf16[1024,768]{1,0:T(8,128)(2,1)} %bitcast.11, s32[512]{0:T(512)S(1)} %add_add_fusion), kind=kOutput, calls=%fused_computation.13 | convolution fusion | flops 537657344 | bytes 1574912 | tf_op jit(solution)/shard_map/dot_general | solution.py:233
  172.2 5.8 %collective-permute-done.7 = bf16[1,6,128,256]{3,2,1,0:T(8,128)(2,1)S(1)} collective-permute-done((bf16[1,6,128,256]{3,2,1,0:T(8,128)(2,1)S(1)}, bf16[1,6,128,256]{3,2,1,0:T(8,128)(2,1)S(1)}, u32[]{:S(2)}, u32[]{:S(2)}) %collective-permute-start.7) | collective-permute-done | bytes 393248 | tf_op jit(solution)/shard_map/ppermute | solution.py:19
  179.3 4.7 %shard_map.95 = bf16[512,256]{1,0:T(8,128)(2,1)} custom-call(bf16[1,3,3,6,128,256]{5,4,3,2,1,0:T(8,128)(2,1)S(1)} %maximum_bitcast_fusion.1.shifted_ref, bf16[27,256,256]{2,1,0:T(8,128)(2,1)} %taps_ref.3), custom_call_target="tpu_custom_call" | custom-call | flops 1811939328 | bytes 7340032 | tf_op jit(solution)/shard_map/pallas_call | solution.py:89
  (32 shorter events, 6.1 us)
Async XLA Ops:
  0.6 23.7 %copy-start = (bf16[1,4,128,512]{3,2,1,0:T(8,128)(2,1)S(1)}, bf16[1,4,128,512]{3,2,1,0:T(8,128)(2,1)}, u32[]{:S(2)}) copy-start(bf16[1,4,128,512]{3,2,1,0:T(8,128)(2,1)} %param.6) | copy-start | bytes 1572868
  1.6 9.0 %collective-permute-start = (bf16[1,1,128,256]{3,2,1,0:T(8,128)(2,1)S(1)}, bf16[1,1,128,256]{3,2,1,0:T(8,128)(2,1)S(1)}, u32[]{:S(2)}, u32[]{:S(2)}) collective-permute-start(bf16[1,1,128,256]{3,2,1,0:T(8,128)(2,1)S(1)} %get-tuple-element.23), channel_id=1, source_target_pairs={{0,1},{1,2},{2,3},{3,4},{4,5},{5,6},{6,7},{7,8},{8,9},{9,10},{10,1... | collective-permute-start | bytes 196616 | tf_op jit(solution)/shard_map/ppermute | solution.py:18
  7.6 9.8 %collective-permute-start.1 = (bf16[1,1,128,256]{3,2,1,0:T(8,128)(2,1)S(1)}, bf16[1,1,128,256]{3,2,1,0:T(8,128)(2,1)S(1)}, u32[]{:S(2)}, u32[]{:S(2)}) collective-permute-start(bf16[1,1,128,256]{3,2,1,0:T(8,128)(2,1)S(1)} %get-tuple-element.22), channel_id=1, source_target_pairs={{1,0},{2,1},{3,2},{4,3},{5,4},{6,5},{7,6},{8,7},{9,8},{10,9},{11,1... | collective-permute-start | bytes 196616 | tf_op jit(solution)/shard_map/ppermute | solution.py:19
  17.5 8.5 %collective-permute-start.2 = (bf16[1,6,128,256]{3,2,1,0:T(8,128)(2,1)S(1)}, bf16[1,6,128,256]{3,2,1,0:T(8,128)(2,1)S(1)}, u32[]{:S(2)}, u32[]{:S(2)}) collective-permute-start(bf16[1,6,128,256]{3,2,1,0:T(8,128)(2,1)S(1)} %constant_dynamic-update-slice_fusion), channel_id=1, source_target_pairs={{0,16},{16,32},{32,48},{48,64},{64,80},{80,96},{96,112},{112,128},... | collective-permute-start | bytes 1179656 | tf_op jit(solution)/shard_map/ppermute | solution.py:18
  21.3 11.2 %collective-permute-start.3 = (bf16[1,6,128,256]{3,2,1,0:T(8,128)(2,1)S(1)}, bf16[1,6,128,256]{3,2,1,0:T(8,128)(2,1)S(1)}, u32[]{:S(2)}, u32[]{:S(2)}) collective-permute-start(bf16[1,6,128,256]{3,2,1,0:T(8,128)(2,1)S(1)} %constant_dynamic-update-slice_fusion), channel_id=1, source_target_pairs={{16,0},{32,16},{48,32},{64,48},{80,64},{96,80},{112,96},{128,112},... | collective-permute-start | bytes 1179656 | tf_op jit(solution)/shard_map/ppermute | solution.py:19
  98.9 7.3 %collective-permute-start.8 = (bf16[2,2,2,768,128]{4,3,2,1,0:T(8,128)(2,1)}, bf16[2,2,2,768,128]{4,3,2,1,0:T(8,128)(2,1)}, u32[]{:S(2)}, u32[]{:S(2)}) collective-permute-start(bf16[2,2,2,768,128]{4,3,2,1,0:T(8,128)(2,1)} %bitcast.20), channel_id=1, source_target_pairs={{0,16},{16,0},{32,48},{48,32},{64,80},{80,64},{96,112},{112,96},{1... | collective-permute-start | bytes 4718600 | tf_op jit(solution)/shard_map/ppermute | solution.py:47
  98.9 46.5 %all-to-all-start.1 = ((bf16[16,64,768]{2,1,0:T(8,128)(2,1)}), bf16[16,64,768]{2,1,0:T(8,128)(2,1)}, u32[]{:S(2)}, u32[]{:S(2)}) async-start(bf16[16,64,768]{2,1,0:T(8,128)(2,1)} %bitcast.63), calls=%async_computation.1 | async-start | bytes 3145728 | tf_op jit(solution)/shard_map/all_to_all | solution.py:224
  108.0 22.8 %collective-permute-start.9 = (bf16[2,2,768,128]{3,2,1,0:T(8,128)(2,1)S(1)}, bf16[2,2,768,128]{3,2,1,0:T(8,128)(2,1)S(1)}, u32[]{:S(2)}, u32[]{:S(2)}) collective-permute-start(bf16[2,2,768,128]{3,2,1,0:T(8,128)(2,1)S(1)} %fusion.15), channel_id=1, source_target_pairs={{0,32},{16,48},{32,0},{48,16},{64,96},{80,112},{96,64},{112,80},{1... | collective-permute-start | bytes 2359304 | tf_op jit(solution)/shard_map/ppermute | solution.py:47
  131.1 11.2 %collective-permute-start.10 = (bf16[2,768,128]{2,1,0:T(8,128)(2,1)S(1)}, bf16[2,768,128]{2,1,0:T(8,128)(2,1)S(1)}, u32[]{:S(2)}, u32[]{:S(2)}) collective-permute-start(bf16[2,768,128]{2,1,0:T(8,128)(2,1)S(1)} %fusion.18), channel_id=1, source_target_pairs={{0,64},{16,80},{32,96},{48,112},{64,0},{80,16},{96,32},{112,48},{1... | collective-permute-start | bytes 1179656 | tf_op jit(solution)/shard_map/ppermute | solution.py:47
  142.4 10.1 %collective-permute-start.11 = (bf16[768,128]{1,0:T(8,128)(2,1)S(1)}, bf16[768,128]{1,0:T(8,128)(2,1)S(1)}, u32[]{:S(2)}, u32[]{:S(2)}) collective-permute-start(bf16[768,128]{1,0:T(8,128)(2,1)S(1)} %fusion.20), channel_id=1, source_target_pairs={{0,128},{16,144},{32,160},{48,176},{64,192},{80,208},{96,224},{112... | collective-permute-start | bytes 589832 | tf_op jit(solution)/shard_map/ppermute | solution.py:47
  147.2 6.1 %collective-permute-start.4 = (bf16[1,1,128,256]{3,2,1,0:T(8,128)(2,1)S(1)}, bf16[1,1,128,256]{3,2,1,0:T(8,128)(2,1)S(1)}, u32[]{:S(2)}, u32[]{:S(2)}) collective-permute-start(bf16[1,1,128,256]{3,2,1,0:T(8,128)(2,1)S(1)} %get-tuple-element.20), channel_id=1, source_target_pairs={{0,1},{1,2},{2,3},{3,4},{4,5},{5,6},{6,7},{7,8},{8,9},{9,10},{10,1... | collective-permute-start | bytes 196616 | tf_op jit(solution)/shard_map/ppermute | solution.py:18
  149.6 9.3 %collective-permute-start.5 = (bf16[1,1,128,256]{3,2,1,0:T(8,128)(2,1)S(1)}, bf16[1,1,128,256]{3,2,1,0:T(8,128)(2,1)S(1)}, u32[]{:S(2)}, u32[]{:S(2)}) collective-permute-start(bf16[1,1,128,256]{3,2,1,0:T(8,128)(2,1)S(1)} %get-tuple-element.21), channel_id=1, source_target_pairs={{1,0},{2,1},{3,2},{4,3},{5,4},{6,5},{7,6},{8,7},{9,8},{10,9},{11,1... | collective-permute-start | bytes 196616 | tf_op jit(solution)/shard_map/ppermute | solution.py:19
  159.0 13.2 %collective-permute-start.6 = (bf16[1,6,128,256]{3,2,1,0:T(8,128)(2,1)S(1)}, bf16[1,6,128,256]{3,2,1,0:T(8,128)(2,1)S(1)}, u32[]{:S(2)}, u32[]{:S(2)}) collective-permute-start(bf16[1,6,128,256]{3,2,1,0:T(8,128)(2,1)S(1)} %pad_maximum_fusion.3), channel_id=1, source_target_pairs={{0,16},{16,32},{32,48},{48,64},{64,80},{80,96},{96,112},{112,128},... | collective-permute-start | bytes 1179656 | tf_op jit(solution)/shard_map/ppermute | solution.py:18
  166.8 11.2 %collective-permute-start.7 = (bf16[1,6,128,256]{3,2,1,0:T(8,128)(2,1)S(1)}, bf16[1,6,128,256]{3,2,1,0:T(8,128)(2,1)S(1)}, u32[]{:S(2)}, u32[]{:S(2)}) collective-permute-start(bf16[1,6,128,256]{3,2,1,0:T(8,128)(2,1)S(1)} %pad_maximum_fusion.3), channel_id=1, source_target_pairs={{16,0},{32,16},{48,32},{64,48},{80,64},{96,80},{112,96},{128,112},... | collective-permute-start | bytes 1179656 | tf_op jit(solution)/shard_map/ppermute | solution.py:19
